TPU v7x, 128 devices: a whole 4x4x4 slice. The times are simulated.
128 devices in a mesh: seq: 16 (over z_hi, y, core), chan: 8 (over x, z_lo).
Axes of the slice: x: 4, y: 4, z: 4 (z_hi: 2, z_lo: 2; z = z_hi * 2 + z_lo), core: 2. Of those that a mesh axis runs over, the one named last changes fastest.
Arguments:
- query_rows: bfloat16 [2048, 8192], P('seq', 'chan'), may hold values from -6 to 6
- key_rows: bfloat16 [2048, 8192], P('seq', 'chan'), may hold values from -6 to 6
- value_rows: bfloat16 [2048, 8192], P('seq', 'chan'), may hold values from -6 to 6
- grad_rows: bfloat16 [2048, 8192], P('seq', 'chan'), may hold values from -21 to 21
- filters: bfloat16 [512, 128], P('chan'), may hold values from -0.5 to 0.5
- span_order: int32 [32], replicated, may hold values from 0 to 31, as said below
Outputs:
- gated_out: bfloat16 [2048, 8192], P('seq', 'chan')
- grad_query: bfloat16 [2048, 8192], P('seq', 'chan')
- grad_key: bfloat16 [2048, 8192], P('seq', 'chan')
- grad_value: bfloat16 [2048, 8192], P('seq', 'chan')
- filter_grad: float32 [512, 128], P('chan')
Inputs may be any that keep to these rules, and one draw needn't show every extreme that they name: span_order names every span once. Slot s lies on seq index s // 2, and span c is owned by seq index c // 2. Seq index i holds a span p below 16 in slot 2 * i and span 32 - 1 - p in slot 2 * i + 1; which p each index holds is drawn. No seq index holds two spans of one owner.
All inputs are finite; a program needn't handle non-finite values.
Results may differ from a plain program's by a relative error of at most 0.0085.
Values may be sent and summed in bfloat16 or wider, within the bound.
No kernel may reach another device: no remote copies, remote signals or barrier semaphores. Data moves between devices by JAX's collectives and lax.ppermute only.
A program may use at most 128 MiB of HBM per device.

v0:
```python
import math

import jax
import jax.numpy as jnp
import numpy as np
from jax import lax
from jax.sharding import PartitionSpec as P

CPD = 2
MOST = 1


def from_behind(array, axis, by):
    size = lax.axis_size(axis)
    pairs = [(i, i + by) for i in range(size) if 0 <= i + by < size]
    return lax.ppermute(array, axis, pairs)


def band_tables(filters):
    taps = filters.shape[1]
    offsets = (np.arange(taps)[:, None] - np.arange(taps)[None, :]) % taps
    below = np.arange(taps)[:, None] >= np.arange(taps)[None, :]
    lookup = filters[:, offsets]
    zeroed = jnp.zeros_like(lookup)
    return (jnp.where(below, lookup, zeroed), jnp.where(below, zeroed, lookup))


def times_rounded(left, right):
    return (left.astype(jnp.float32) * right.astype(jnp.float32)).astype(jnp.bfloat16)


def route_plan(span_order, device, per_device, devices, capacity):
    owner_grid = (span_order // per_device).reshape(devices, per_device)
    position = jnp.arange(per_device, dtype=jnp.int32)
    earlier = (owner_grid[:, :, None] == owner_grid[:, None, :]) & (
        position[None, None, :] < position[None, :, None]
    )
    ranks = jnp.sum(earlier.astype(jnp.int32), axis=2)
    send_key = owner_grid * capacity + ranks
    arrive_key = (jnp.arange(devices, dtype=jnp.int32)[:, None] * capacity + ranks).reshape(-1)
    my_keys = lax.dynamic_index_in_dim(send_key, device, 0, keepdims=False)
    buffer_slots = jnp.arange(devices * capacity, dtype=jnp.int32)
    hits = my_keys[None, :] == buffer_slots[:, None]
    fill_slot = jnp.sum(jnp.where(hits, position[None, :], 0), axis=1)
    fill_valid = jnp.any(hits, axis=1)
    wanted = device * per_device + position
    owned = span_order[None, :] == wanted[:, None]
    take_slot = jnp.sum(jnp.where(owned, arrive_key[None, :], 0), axis=1)
    back_hits = take_slot[None, :] == buffer_slots[:, None]
    back_slot = jnp.sum(jnp.where(back_hits, position[None, :], 0), axis=1)
    back_valid = jnp.any(back_hits, axis=1)
    return (fill_slot, fill_valid, take_slot, back_slot, back_valid, my_keys)


def pack_rows(block, slot_index, valid, per_device):
    channels = block.shape[1]
    pieces = block.reshape(per_device, -1, channels)
    picked = jnp.take(pieces, slot_index, axis=0)
    picked = jnp.where(valid[:, None, None], picked, jnp.zeros_like(picked))
    return picked.reshape(-1, channels)


def unpack_rows(received, slot_index, count):
    channels = received.shape[1]
    pieces = received.reshape(count, -1, channels)
    return jnp.take(pieces, slot_index, axis=0).reshape(-1, channels)


def forward_conv(source, tail_rows, main_band, wrap_band, group_size):
    taps = main_band.shape[1]
    row_count, channels = source.shape
    extended = jnp.concatenate([jnp.zeros((1, channels), source.dtype), tail_rows, source], axis=0)
    tile_grid = extended.reshape(row_count // taps + 1, taps, channels // group_size, group_size)
    result = jnp.einsum(
        "gab,tbgc->tagc", main_band, tile_grid[1:], preferred_element_type=jnp.float32
    )
    result = result + jnp.einsum(
        "gab,tbgc->tagc", wrap_band, tile_grid[:-1], preferred_element_type=jnp.float32
    )
    return (result.reshape(row_count, channels), tile_grid)


def backward_conv(source, head_rows, main_band, wrap_band, group_size):
    taps = main_band.shape[1]
    row_count, channels = source.shape
    extended = jnp.concatenate([source, head_rows, jnp.zeros((1, channels), source.dtype)], axis=0)
    tile_grid = extended.reshape(row_count // taps + 1, taps, channels // group_size, group_size)
    result = jnp.einsum(
        "gba,tbgc->tagc", main_band, tile_grid[:-1], preferred_element_type=jnp.float32
    )
    result = result + jnp.einsum(
        "gba,tbgc->tagc", wrap_band, tile_grid[1:], preferred_element_type=jnp.float32
    )
    return result.reshape(row_count, channels)


def filter_terms(gated_grad, z_grid, group_size):
    taps = z_grid.shape[1]
    tile_count = z_grid.shape[0] - 1
    grad_tiles = gated_grad.reshape(tile_count, taps, -1, group_size)
    windows = jnp.concatenate([z_grid[:-1], z_grid[1:]], axis=1)
    products = jnp.einsum("tagc,tbgc->gab", grad_tiles, windows, preferred_element_type=jnp.float32)
    groups = products.shape[0]
    flattened = products.reshape(groups, 2 * taps * taps)
    padded = jnp.concatenate([flattened, jnp.zeros((groups, taps), jnp.float32)], axis=1)
    padded = padded.reshape(groups, taps, 2 * taps + 1)
    diagonals = jnp.sum(padded[:, :, 1 : taps + 1], axis=1)
    return diagonals[:, ::-1]


def shards(query_rows, key_rows, value_rows, grad_rows, filters, span_order):
    device = lax.axis_index("seq")
    devices = lax.axis_size("seq")
    row_count = query_rows.shape[0]
    taps = filters.shape[1]
    group_size = query_rows.shape[1] // filters.shape[0]
    capacity = MOST
    per_device = CPD
    slot_total = devices * capacity
    fill_slot, fill_valid, take_slot, back_slot, back_valid, my_keys = route_plan(
        span_order, device, per_device, devices, capacity
    )
    main_band, wrap_band = band_tables(filters)
    moved = (
        lax.all_to_all(
            pack_rows(query_rows, fill_slot, fill_valid, per_device),
            "seq",
            split_axis=0,
            concat_axis=0,
            tiled=True,
        ),
        lax.all_to_all(
            pack_rows(key_rows, fill_slot, fill_valid, per_device),
            "seq",
            split_axis=0,
            concat_axis=0,
            tiled=True,
        ),
        lax.all_to_all(
            pack_rows(value_rows, fill_slot, fill_valid, per_device),
            "seq",
            split_axis=0,
            concat_axis=0,
            tiled=True,
        ),
        lax.all_to_all(
            pack_rows(grad_rows, fill_slot, fill_valid, per_device),
            "seq",
            split_axis=0,
            concat_axis=0,
            tiled=True,
        ),
    )
    owner_query = unpack_rows(moved[0], take_slot, slot_total)
    owner_key = unpack_rows(moved[1], take_slot, slot_total)
    owner_value = unpack_rows(moved[2], take_slot, slot_total)
    owner_grad = unpack_rows(moved[3], take_slot, slot_total)
    mixed_kv = times_rounded(owner_key, owner_value)
    gated_grad = times_rounded(owner_grad, owner_query)
    tail_rows = from_behind(mixed_kv[row_count - taps + 1 :], "seq", 1)
    head_rows = from_behind(gated_grad[: taps - 1], "seq", -1)
    conv, z_grid = forward_conv(mixed_kv, tail_rows, main_band, wrap_band, group_size)
    convolved = conv.astype(jnp.bfloat16)
    dmixed = backward_conv(gated_grad, head_rows, main_band, wrap_band, group_size).astype(
        jnp.bfloat16
    )
    partial_grad = filter_terms(gated_grad, z_grid, group_size)
    total_grad = lax.psum(partial_grad, "seq")
    squares = lax.psum(jnp.sum(total_grad * total_grad), "chan")
    limit = math.sqrt(filters.shape[0] * lax.axis_size("chan") * taps)
    factor = jnp.minimum(1.0, limit * lax.rsqrt(squares + 1e-06))
    filter_grad = factor * total_grad
    returned = (
        lax.all_to_all(
            pack_rows(times_rounded(owner_query, convolved), back_slot, back_valid, per_device),
            "seq",
            split_axis=0,
            concat_axis=0,
            tiled=True,
        ),
        lax.all_to_all(
            pack_rows(times_rounded(owner_grad, convolved), back_slot, back_valid, per_device),
            "seq",
            split_axis=0,
            concat_axis=0,
            tiled=True,
        ),
        lax.all_to_all(
            pack_rows(times_rounded(dmixed, owner_value), back_slot, back_valid, per_device),
            "seq",
            split_axis=0,
            concat_axis=0,
            tiled=True,
        ),
        lax.all_to_all(
            pack_rows(times_rounded(dmixed, owner_key), back_slot, back_valid, per_device),
            "seq",
            split_axis=0,
            concat_axis=0,
            tiled=True,
        ),
    )
    gated_out = unpack_rows(returned[0], my_keys, slot_total)
    grad_query = unpack_rows(returned[1], my_keys, slot_total)
    grad_key = unpack_rows(returned[2], my_keys, slot_total)
    grad_value = unpack_rows(returned[3], my_keys, slot_total)
    return (gated_out, grad_query, grad_key, grad_value, filter_grad)


def solution(mesh):
    return jax.shard_map(
        shards,
        mesh=mesh,
        in_specs=(
            P("seq", "chan"),
            P("seq", "chan"),
            P("seq", "chan"),
            P("seq", "chan"),
            P("chan", None),
            P(),
        ),
        out_specs=(
            P("seq", "chan"),
            P("seq", "chan"),
            P("seq", "chan"),
            P("seq", "chan"),
            P("chan", None),
        ),
        check_vma=False,
    )
```

profile of v0, /device:TPU:0, one launch (start us, length us, event | category | flops | bytes accessed | tf_op | source)
XLA Modules:
  0.0 469.5 jit_solution(11138940141483297728)
XLA Ops:
  3.0 2.0 gather_fusion.5
  5.0 2.0 gather_fusion.3
  7.1 2.0 gather_fusion.1
  9.0 4.3 select_select_fusion.3
  13.4 37.1 %all_to_all.48 = bf16[16,64,1024]{2,1,0:T(8,128)(2,1)} all-to-all(bf16[16,64,1024]{2,1,0:T(8,128)(2,1)S(1)} %get-tuple-element.16), channel_id=1, replica_groups=mesh['seq'=16,'chan'=8] {'seq'}, dimensions={0} | all-to-all | bytes 4194304 | tf_op jit(solution)/shard_map/all_to_all | solution.py:146
  50.4 32.5 %all_to_all.49 = bf16[16,64,1024]{2,1,0:T(8,128)(2,1)} all-to-all(bf16[16,64,1024]{2,1,0:T(8,128)(2,1)S(1)} %get-tuple-element.17), channel_id=1, replica_groups=mesh['seq'=16,'chan'=8] {'seq'}, dimensions={0} | all-to-all | bytes 4194304 | tf_op jit(solution)/shard_map/all_to_all | solution.py:132
  82.9 32.5 %all_to_all.50 = bf16[16,64,1024]{2,1,0:T(8,128)(2,1)} all-to-all(bf16[16,64,1024]{2,1,0:T(8,128)(2,1)S(1)} %get-tuple-element.19), channel_id=1, replica_groups=mesh['seq'=16,'chan'=8] {'seq'}, dimensions={0} | all-to-all | bytes 4194304 | tf_op jit(solution)/shard_map/all_to_all | solution.py:125
  115.4 3.8 all-to-all-start.2
  119.6 57.4 %gather_fusion = bf16[16384,64]{1,0:T(8,128)(2,1)} fusion(bf16[64,128]{0,1:T(8,128)(2,1)S(1)} %copy.56, s32[16384]{0:T(1024)S(1)} %broadcast_clamp_fusion), kind=kCustom, calls=%fused_computation.16 | custom fusion | bytes 4259840 | tf_op jit(solution)/shard_map/gather | solution.py:23
  177.0 5.6 %copy.57 = bf16[128,128,64]{1,0,2:T(8,128)(2,1)} copy(bf16[128,128,64]{2,1,0:T(8,128)(2,1)} %bitcast.97) | data formatting | bytes 4194304 | tf_op jit(solution)/shard_map/gather | solution.py:23
  183.1 2.2 gather_fusion.10
  185.2 2.2 gather_fusion.2
  187.4 0.9 fusion.47
  188.3 1.3 copy.62
  189.6 1.3 collective-permute-start.1
  191.1 3.0 gather_fusion.4
  194.1 1.3 gather_fusion.6
  195.3 3.2 fusion.4
  198.5 1.1 copy.69
  199.8 1.7 fusion.35
  203.3 0.8 slice.61
  204.0 3.7 collective-permute-start
  207.8 1.0 convert_element_type.154
  209.4 2.0 gather_fusion.13
  211.4 3.6 fusion.6
  215.0 1.1 copy.68
  216.3 3.8 fusion.26
  220.1 2.6 reshape.257
  222.7 2.1 copy.60
  224.9 1.3 fusion.46
  226.2 2.0 gather_fusion.11
  228.2 2.0 gather_fusion.7
  230.2 4.3 select_select_fusion
  234.5 37.4 %all_to_all.51 = bf16[16,64,1024]{2,1,0:T(8,128)(2,1)} all-to-all(bf16[16,64,1024]{2,1,0:T(8,128)(2,1)S(1)} %get-tuple-element.12), channel_id=1, replica_groups=mesh['seq'=16,'chan'=8] {'seq'}, dimensions={0} | all-to-all | bytes 4194304 | tf_op jit(solution)/shard_map/all_to_all | solution.py:195
  271.9 32.5 %all_to_all.52 = bf16[16,64,1024]{2,1,0:T(8,128)(2,1)} all-to-all(bf16[16,64,1024]{2,1,0:T(8,128)(2,1)S(1)} %get-tuple-element.13), channel_id=1, replica_groups=mesh['seq'=16,'chan'=8] {'seq'}, dimensions={0} | all-to-all | bytes 4194304 | tf_op jit(solution)/shard_map/all_to_all | solution.py:181
  304.4 32.5 %all_to_all.53 = bf16[16,64,1024]{2,1,0:T(8,128)(2,1)} all-to-all(bf16[16,64,1024]{2,1,0:T(8,128)(2,1)S(1)} %get-tuple-element.14), channel_id=1, replica_groups=mesh['seq'=16,'chan'=8] {'seq'}, dimensions={0} | all-to-all | bytes 4194304 | tf_op jit(solution)/shard_map/all_to_all | solution.py:188
  336.9 4.0 all-to-all-start.3
  341.3 1.3 fusion.48
  342.6 4.7 %copy.70 = f32[8,8,128,256]{3,1,2,0:T(8,128)S(1)} copy(f32[8,8,128,256]{3,2,1,0:T(8,128)S(1)} %bitcast.93) | data formatting | bytes 16777216
  347.3 3.8 concatenate.17
  351.1 14.1 %reshape.256 = f32[64,128,257]{2,1,0:T(8,128)} reshape(f32[64,32896]{1,0:T(8,128)} %concatenate.17) | data formatting | bytes 16842752 | tf_op jit(solution)/shard_map/reshape | solution.py:106
  365.2 4.5 slice_reduce_fusion
  369.8 69.8 %psum.14 = f32[64,128]{1,0:T(8,128)S(1)} all-reduce(f32[64,128]{1,0:T(8,128)S(1)} %rev.3), channel_id=1, replica_groups=mesh['seq'=16,'chan'=8] {'seq'}, use_global_device_ids=true, to_apply=%region_7.10 | all-reduce | flops 8192 | bytes 65536 | tf_op jit(solution)/shard_map/psum | solution.py:168
  440.3 19.8 %psum.15 = f32[]{:T(128)} all-reduce(f32[]{:T(128)} %multiply_reduce_fusion), channel_id=1, replica_groups=mesh['seq'=16,'chan'=8] {'chan'}, use_global_device_ids=true, to_apply=%region_9.12 | all-reduce | flops 1 | bytes 8 | tf_op jit(solution)/shard_map/psum | solution.py:169
  461.4 2.2 gather_fusion.16
  463.6 2.2 gather_fusion.12
  465.7 2.2 gather_fusion.14
  468.5 1.1 broadcast_select_fusion.6
  (83 shorter events, 8.1 us)
Async XLA Ops:
  0.6 1.4 copy-start
  2.0 1.0 copy-start.2
  3.0 2.0 copy-start.3
  5.0 2.0 copy-start.4
  115.4 3.9 copy-start.14
  115.4 4.1 copy-start.15
  115.4 78.6 %all-to-all-start.2 = ((bf16[16,64,1024]{2,1,0:T(8,128)(2,1)}), bf16[16,64,1024]{2,1,0:T(8,128)(2,1)S(1)}, u32[]{:S(2)}, u32[]{:S(2)}) async-start(bf16[16,64,1024]{2,1,0:T(8,128)(2,1)} %get-tuple-element.18), calls=%async_computation.2 | async-start | bytes 4194304 | tf_op jit(solution)/shard_map/all_to_all | solution.py:139
  177.0 5.6 %copy-start.16 = (s32[32]{0:T(128)S(1)}, s32[32]{0:T(128)}, u32[]{:S(2)}) copy-start(s32[32]{0:T(128)} %param.18) | copy-start | bytes 388
  185.2 10.1 %copy-start.17 = (pred[128,128]{1,0:T(32,128)(4,1)S(1)}, pred[128,128]{1,0:T(32,128)(4,1)}, u32[]{:S(2)}) copy-start(pred[128,128]{1,0:T(32,128)(4,1)} %constant.72.clone) | copy-start | bytes 49156
  187.4 11.1 %copy-start.5 = (bf16[2,64,1024]{2,1,0:T(8,128)(2,1)}, bf16[2,64,1024]{2,1,0:T(8,128)(2,1)S(1)}, u32[]{:S(2)}) copy-start(bf16[2,64,1024]{2,1,0:T(8,128)(2,1)S(1)} %gather_fusion.2) | copy-start | bytes 786436
  189.6 9.0 %collective-permute-start.1 = (bf16[127,1024]{1,0:T(8,128)(2,1)}, bf16[127,1024]{1,0:T(8,128)(2,1)}, u32[]{:S(2)}, u32[]{:S(2)}) collective-permute-start(bf16[127,1024]{1,0:T(8,128)(2,1)} %bitcast.86), channel_id=1, source_target_pairs={{8,0},{16,8},{24,16},{32,24},{40,32},{48,40},{56,48},{64,56},{72,6... | collective-permute-start | bytes 780296 | tf_op jit(solution)/shard_map/ppermute | solution.py:16
  191.1 7.4 %copy-start.7 = (bf16[128,64,16]{0,2,1:T(8,128)(2,1)}, bf16[128,64,16]{0,2,1:T(8,128)(2,1)S(1)}, u32[]{:S(2)}) copy-start(bf16[128,64,16]{0,2,1:T(8,128)(2,1)S(1)} %convert_element_type.165) | copy-start | bytes 786436
  195.3 4.4 copy-start.6
  201.4 1.1 copy-start.11
  201.4 1.1 copy-start.12
  204.0 11.0 %collective-permute-start = (bf16[127,1024]{1,0:T(8,128)(2,1)}, bf16[127,1024]{1,0:T(8,128)(2,1)}, u32[]{:S(2)}, u32[]{:S(2)}) collective-permute-start(bf16[127,1024]{1,0:T(8,128)(2,1)} %slice.61), channel_id=1, source_target_pairs={{0,8},{8,16},{16,24},{24,32},{32,40},{40,48},{48,56},{56,64},{64,7... | collective-permute-start | bytes 780296 | tf_op jit(solution)/shard_map/ppermute | solution.py:16
  209.4 2.0 copy-start.13
  216.3 6.4 %copy-start.9 = (bf16[128,1024]{0,1:T(8,128)(2,1)}, bf16[128,1024]{0,1:T(8,128)(2,1)S(1)}, u32[]{:S(2)}) copy-start(bf16[128,1024]{0,1:T(8,128)(2,1)S(1)} %concatenate.14.clone) | copy-start | bytes 786436
  336.9 4.3 copy-start.8
  336.9 4.3 copy-start.10
  336.9 131.0 %all-to-all-start.3 = ((bf16[16,64,1024]{2,1,0:T(8,128)(2,1)}), bf16[16,64,1024]{2,1,0:T(8,128)(2,1)S(1)}, u32[]{:S(2)}, u32[]{:S(2)}) async-start(bf16[16,64,1024]{2,1,0:T(8,128)(2,1)} %get-tuple-element.15), calls=%async_computation.3 | async-start | bytes 4194304 | tf_op jit(solution)/shard_map/all_to_all | solution.py:174
  460.8 8.8 %copy-start.1 = (bf16[128,1024]{1,0:T(8,128)(2,1)S(1)}, bf16[128,1024]{1,0:T(8,128)(2,1)}, u32[]{:S(2)}) copy-start(bf16[128,1024]{1,0:T(8,128)(2,1)} %param.16) | copy-start | bytes 786436
where the time goes:
time: 471 us; the launch traced here: 470 us
  blocking collectives  294 us (62%)
  local copies, waits for them, and re-layouts  128 us (27%)
  other arithmetic  19.3 us (4%)
  matrix products  13.5 us (3%)
  starting transfers between devices  12.9 us (3%)
    psum x1, blocking collectives, shards(): total_grad = lax.psum(partial_grad, 'seq')  69.8 us
    gather x2, local copies, waits for them, and re-layouts, band_tables(): lookup = filters[:, offsets]  63 us
    all_to_all x1, blocking collectives, shards(): lax.all_to_all(pack_rows(times_rounded(dmixed, owner_key), back_slot, bac...  37.4 us
    all_to_all x1, blocking collectives, shards(): lax.all_to_all(pack_rows(grad_rows, fill_slot, fill_valid, per_device), '...  37.1 us
    all_to_all x1, blocking collectives, shards(): lax.all_to_all(pack_rows(times_rounded(dmixed, owner_value), back_slot, b...  32.5 us
    all_to_all x1, blocking collectives, shards(): lax.all_to_all(pack_rows(times_rounded(owner_grad, convolved), back_slot,...  32.5 us
    all_to_all x1, blocking collectives, shards(): lax.all_to_all(pack_rows(query_rows, fill_slot, fill_valid, per_device),...  32.5 us
    all_to_all x1, blocking collectives, shards(): lax.all_to_all(pack_rows(key_rows, fill_slot, fill_valid, per_device), 's...  32.5 us
  transfers between devices with their start and end apart: 4, of which 0 were waited for; matrix products, arithmetic and copies ran while one was open for 26% of the time, Pallas kernels for 0%

commit v1 on v0

v1 whole, which is shorter than its diff:
```python
import math

import jax
import jax.numpy as jnp
from jax import lax
from jax.sharding import PartitionSpec as P


def times_rounded(left, right):
    return (left.astype(jnp.float32) * right.astype(jnp.float32)).astype(jnp.bfloat16)


def band_select(taps, out_rows, window, lead):
    j = lax.broadcasted_iota(jnp.int32, (taps, out_rows, window), 0)
    a = lax.broadcasted_iota(jnp.int32, (taps, out_rows, window), 1)
    w = lax.broadcasted_iota(jnp.int32, (taps, out_rows, window), 2)
    return (w == lead + a - j).astype(jnp.bfloat16)


def shards(query_rows, key_rows, value_rows, grad_rows, filters, span_order):
    device = lax.axis_index("seq")
    devices = lax.axis_size("seq")
    rows, channels = query_rows.shape
    spans = span_order.shape[0]
    span_rows = rows * devices // spans
    per_device = rows // span_rows
    taps = filters.shape[1]
    groups = filters.shape[0]
    group_size = channels // groups
    halo = -(-(taps - 1) // span_rows)
    lead = halo * span_rows
    window = lead + span_rows

    mixed = times_rounded(key_rows, value_rows)
    gated = times_rounded(grad_rows, query_rows)
    gathered = lax.all_gather(jnp.stack([mixed, gated]), "seq", axis=0, tiled=False)
    mixed_blocks = gathered[:, 0].reshape(spans, span_rows, channels)
    gated_blocks = gathered[:, 1].reshape(spans, span_rows, channels)

    slot_of = jnp.zeros((spans,), jnp.int32).at[span_order].set(jnp.arange(spans, dtype=jnp.int32))
    mine = lax.dynamic_slice_in_dim(span_order, device * per_device, per_device)
    step = jnp.arange(halo, dtype=jnp.int32)
    before = mine[:, None] - halo + step[None, :]
    after = mine[:, None] + 1 + step[None, :]

    def pick(blocks, wanted):
        valid = (wanted >= 0) & (wanted < spans)
        slots = slot_of[jnp.clip(wanted, 0, spans - 1)].reshape(-1)
        taken = jnp.take(blocks, slots, axis=0).reshape(per_device, halo, span_rows, channels)
        return jnp.where(valid[:, :, None, None], taken, jnp.zeros_like(taken))

    own_mixed = mixed.reshape(per_device, span_rows, channels)
    own_gated = gated.reshape(per_device, span_rows, channels)
    mixed_window = jnp.concatenate(
        [pick(mixed_blocks, before).reshape(per_device, lead, channels), own_mixed], axis=1
    )
    gated_window = jnp.concatenate(
        [own_gated, pick(gated_blocks, after).reshape(per_device, lead, channels)], axis=1
    )
    mixed_window = mixed_window.reshape(per_device, window, groups, group_size)
    gated_window = gated_window.reshape(per_device, window, groups, group_size)

    select_fwd = band_select(taps, span_rows, window, lead)
    fwd_band = jnp.einsum(
        "gj,jaw->gaw", filters, select_fwd, preferred_element_type=jnp.float32
    ).astype(jnp.bfloat16)
    bwd_band = jnp.einsum(
        "gj,jau->gau", filters, _bwd_select(taps, span_rows, window),
        preferred_element_type=jnp.float32,
    ).astype(jnp.bfloat16)

    conv = jnp.einsum("gaw,swgc->sagc", fwd_band, mixed_window, preferred_element_type=jnp.float32)
    convolved = conv.reshape(rows, channels).astype(jnp.bfloat16)
    adjoint = jnp.einsum("gau,sugc->sagc", bwd_band, gated_window, preferred_element_type=jnp.float32)
    dmixed = adjoint.reshape(rows, channels).astype(jnp.bfloat16)

    own_gated_g = own_gated.reshape(per_device, span_rows, groups, group_size)
    corr = jnp.einsum(
        "sagc,swgc->gaw", own_gated_g, mixed_window, preferred_element_type=jnp.float32
    )
    partial_grad = jnp.einsum(
        "gaw,jaw->gj", corr, select_fwd.astype(jnp.float32), precision=lax.Precision.HIGHEST
    )
    total_grad = lax.psum(partial_grad, "seq")
    squares = lax.psum(jnp.sum(total_grad * total_grad), "chan")
    limit = math.sqrt(groups * lax.axis_size("chan") * taps)
    factor = jnp.minimum(1.0, limit / jnp.sqrt(squares + 1e-06))
    filter_grad = factor * total_grad

    gated_out = times_rounded(query_rows, convolved)
    grad_query = times_rounded(grad_rows, convolved)
    grad_key = times_rounded(dmixed, value_rows)
    grad_value = times_rounded(dmixed, key_rows)
    return (gated_out, grad_query, grad_key, grad_value, filter_grad)


def _bwd_select(taps, out_rows, window):
    j = lax.broadcasted_iota(jnp.int32, (taps, out_rows, window), 0)
    a = lax.broadcasted_iota(jnp.int32, (taps, out_rows, window), 1)
    u = lax.broadcasted_iota(jnp.int32, (taps, out_rows, window), 2)
    return (u == a + j).astype(jnp.bfloat16)


def solution(mesh):
    return jax.shard_map(
        shards,
        mesh=mesh,
        in_specs=(
            P("seq", "chan"),
            P("seq", "chan"),
            P("seq", "chan"),
            P("seq", "chan"),
            P("chan", None),
            P(),
        ),
        out_specs=(
            P("seq", "chan"),
            P("seq", "chan"),
            P("seq", "chan"),
            P("seq", "chan"),
            P("chan", None),
        ),
        check_vma=False,
    )
```

time: 471 us -> 216 us (0.46)
  blocking collectives: 294 us -> 85.7 us
  local copies, waits for them, and re-layouts: 128 us -> 29.9 us
  waiting for transfers between devices: 0.01 us -> 63.9 us
  other arithmetic: 19.3 us -> 2.32 us
  between operations: 1.75 us -> 15 us
  starting transfers between devices: 12.9 us -> 0.04 us
  matrix products: 13.5 us -> 19.1 us
    all_to_all x6 -> x0, blocking collectives: 205 us -> none  [the longest x1 37.4 us: shards(): lax.all_to_all(pack_rows(times_rounded(dmixed, owner_key), back_slot, bac...]
    gather x18 -> x4, local copies, waits for them, and re-layouts: 92 us -> 6.81 us  [the longest x2 5.53 us: pick(): jnp.take(blocks, slots, axis=0)]
    all_gather x0 -> x1, waiting for transfers between devices: none -> 63.9 us  [shards(): lax.all_gather(jnp.stack([mixed, gated]), 'seq', axis=0, tiled=False)]
    reshape x1 -> x2, local copies, waits for them, and re-layouts: 14.1 us -> 0.96 us  [pick(): jnp.take(blocks, slots, axis=0)]
    select_n x8, other arithmetic: 10.4 us -> 0.47 us  [the longest x4 0.24 us: pick(): jnp.take(blocks, slots, axis=0)]
    all_to_all x2 -> x0, starting transfers between devices: 7.88 us -> none  [the longest x1 4.03 us: shards(): lax.all_to_all(pack_rows(times_rounded(owner_query, convolved), back_slot...]
    dot_general x5 -> x6, matrix products: 13.5 us -> 19.1 us  [the longest x1 4.69 us: shards(): jnp.einsum('gaw,jaw->gj', corr, select_fwd.astype(jnp.float32), precision...]
    slice x1, local copies, waits for them, and re-layouts: 0.77 us -> 6.03 us  [shards(): gated_blocks = gathered[:, 1].reshape(spans, span_rows, channels)]
  transfers between devices with their start and end apart: 4 -> 1, of which waited for: 0 -> 1; matrix products, arithmetic and copies ran while one was open for 26% -> 5% of each run, Pallas kernels for 0% -> 0%
where the time goes in v1:
time: 216 us
  blocking collectives  85.7 us (40%)
  waiting for transfers between devices  63.9 us (30%)
  local copies, waits for them, and re-layouts  29.9 us (14%)
  matrix products  19.1 us (9%)
  between operations  15 us (7%)
  other arithmetic  2.32 us (1%)
    psum x1, blocking collectives, shards(): total_grad = lax.psum(partial_grad, 'seq')  65.4 us
    all_gather x1, waiting for transfers between devices, shards(): lax.all_gather(jnp.stack([mixed, gated]), 'seq', axis=0, tiled=False)  63.9 us
    psum x1, blocking collectives, shards(): squares = lax.psum(jnp.sum(total_grad * total_grad), 'chan')  20.2 us
    unnamed x16, local copies, waits for them, and re-layouts  7.91 us
    slice x1, local copies, waits for them, and re-layouts, shards(): gated_blocks = gathered[:, 1].reshape(spans, span_rows, channels)  6.03 us
    gather x2, local copies, waits for them, and re-layouts, pick(): jnp.take(blocks, slots, axis=0)  5.53 us
    dot_general x1, matrix products, shards(): jnp.einsum('gaw,jaw->gj', corr, select_fwd.astype(jnp.float32), precision...  4.69 us
  transfers between devices with their start and end apart: 1, of which 1 were waited for; matrix products, arithmetic and copies ran while one was open for 5% of the time, Pallas kernels for 0%

profile of v1, /device:TPU:0, one launch (start us, length us, event | category | flops | bytes accessed | tf_op | source)
XLA Modules:
  0.0 216.0 jit_solution(9747535979950176930)
XLA Ops:
  7.2 1.1 copy.64
  8.4 1.1 copy.65
  9.5 1.1 copy.63
  10.6 1.1 copy.66
  12.0 1.1 copy.67
  13.1 0.2 concatenate.12
  13.3 0.2 concatenate.14
  13.6 0.1 broadcast_add_fusion
  13.7 0.1 compare_select_fusion
  13.7 0.1 reshape.209
  14.0 0.1 broadcast_in_dim.42
  14.1 0.9 copy.70
  15.0 0.1 reshape.217
  15.1 0.7 scatter_custom_fusion
  15.8 0.6 gather_fusion
  16.4 0.6 gather_fusion.1
  17.0 0.9 copy.75
  18.0 3.2 %convert_bitcast_fusion = bf16[64,64,192,1]{2,0,1,3:T(8,128)(2,1)} fusion(bf16[64,128]{1,0:T(8,128)(2,1)S(1)} %copy-done), kind=kOutput, calls=%fused_computation.18 | convolution fusion | flops 205258752 | bytes 1589248 | tf_op jit(solution)/shard_map/gj,jau->gau/dot_general | solution.py:67
  21.1 3.5 %convert_bitcast_fusion.1 = bf16[64,64,192,1]{2,0,1,3:T(8,128)(2,1)} fusion(s32[64]{0:T(128)S(1)} %iota_add_fusion, bf16[64,128]{1,0:T(8,128)(2,1)S(1)} %copy-done), kind=kOutput, calls=%fused_computation.19 | convolution fusion | flops 205258752 | bytes 1589504 | tf_op jit(solution)/shard_map/gj,jaw->gaw/dot_general | solution.py:64
  24.6 63.9 %all-gather.3.cloned.1.call-done = bf16[32,128,1024]{2,1,0:T(8,128)(2,1)} async-done(((bf16[2,128,1024]{2,1,0:T(8,128)(2,1)}), bf16[32,128,1024]{2,1,0:T(8,128)(2,1)}) %all-gather.3.cloned.1.call-update) | async-done | bytes 8388624 | tf_op jit(solution)/shard_map/all_gather | solution.py:36
  88.6 6.0 %fusion.48 = (bf16[16,1,128,1024]{3,2,1,0:T(8,128)(2,1)}, bf16[16,1,128,1024]{3,2,1,0:T(8,128)(2,1)}) fusion(bf16[16,2,128,1024]{3,2,1,0:T(8,128)(2,1)} %bitcast.43), kind=kLoop, calls=%fused_computation.74 | loop fusion | bytes 16777216 | tf_op jit(solution)/shard_map/slice | solution.py:38
  94.6 2.8 %gather_fusion.2 = bf16[4,64,1024]{2,1,0:T(8,128)(2,1)S(1)} fusion(bf16[32,64,1024]{2,1,0:T(8,128)(2,1)} %bitcast.45, s32[1024]{0:T(1024)S(1)} %pad_clamp_fusion.2), kind=kCustom, calls=%fused_computation.clone | custom fusion | bytes 1048592 | tf_op jit(solution)/shard_map/jit(_take)/gather | solution.py:49
  97.4 0.1 broadcast_select_fusion.1
  97.5 0.7 copy.68
  98.2 0.5 reshape.186
  98.8 1.9 convolution_bitcast_fusion
  100.7 4.7 %fusion.28 = f32[64,128]{1,0:T(8,128)S(1)} fusion(s32[64]{0:T(128)S(1)} %iota_add_fusion, f32[64,64,192]{2,1,0:T(8,128)S(1)} %convolution_bitcast_fusion), kind=kOutput, calls=%fused_computation.26 | convolution fusion | flops 1211105280 | bytes 3178752 | tf_op jit(solution)/shard_map/gaw,jaw->gj/dot_general | solution.py:81
  105.4 65.4 %psum.14 = f32[64,128]{1,0:T(8,128)S(1)} all-reduce(f32[64,128]{1,0:T(8,128)S(1)} %fusion.28), channel_id=1, replica_groups=mesh['seq'=16,'chan'=8] {'seq'}, use_global_device_ids=true, to_apply=%region_1.3 | all-reduce | flops 8192 | bytes 65536 | tf_op jit(solution)/shard_map/psum | solution.py:84
  170.8 0.6 multiply_reduce_fusion
  171.5 0.1 broadcast_in_dim.46
  171.6 20.2 %psum.15 = f32[]{:T(128)} all-reduce(f32[]{:T(128)} %multiply_reduce_fusion), channel_id=1, replica_groups=mesh['seq'=16,'chan'=8] {'chan'}, use_global_device_ids=true, to_apply=%region_3.5 | all-reduce | flops 1 | bytes 8 | tf_op jit(solution)/shard_map/psum | solution.py:85
  192.5 0.6 broadcast_multiply_fusion
  193.1 2.9 %fusion.16 = f32[2,64,64,16]{1,3,0,2:T(8,128)S(1)} fusion(bf16[64,64,192,1]{2,0,1,3:T(8,128)(2,1)} %convert_bitcast_fusion.1, bf16[2,64,64,16]{1,3,0,2:T(8,128)(2,1)S(1)} %copy-done.1, bf16[2,128,64,16]{1,3,0,2:T(8,128)(2,1)S(1)} %copy_select_fusion.1), kind=kOutput, calls=%fused_computation.22 | convolution fusion | flops 52166656 | bytes 2883584 | tf_op jit(solution)/shard_map/gaw,swgc->sagc/dot_general | solution.py:72
  196.0 0.5 copy.72
  196.6 0.6 reshape.189
  197.2 0.1 fusion.39
  197.3 0.9 copy.80
  198.1 0.9 copy.81
  199.0 2.8 %gather_fusion.3 = bf16[4,64,1024]{2,1,0:T(8,128)(2,1)S(1)} fusion(bf16[32,64,1024]{2,1,0:T(8,128)(2,1)} %bitcast.44, s32[1024]{0:T(1024)S(1)} %pad_clamp_fusion), kind=kCustom, calls=%fused_computation.1.clone | custom fusion | bytes 1048592 | tf_op jit(solution)/shard_map/jit(_take)/gather | solution.py:49
  201.8 0.1 broadcast_select_fusion
  201.9 0.7 copy.73
  202.6 0.5 reshape.188
  203.2 3.0 %fusion.25 = f32[2,64,64,16]{1,3,0,2:T(8,128)S(1)} fusion(bf16[64,64,192,1]{2,0,1,3:T(8,128)(2,1)} %convert_bitcast_fusion, bf16[2,128,64,16]{1,3,0,2:T(8,128)(2,1)S(1)} %copy_select_fusion, bf16[2,64,64,16]{1,3,0,2:T(8,128)(2,1)S(1)} %copy-done.2), kind=kOutput, calls=%fused_computation.25 | convolution fusion | flops 52166656 | bytes 2883584 | tf_op jit(solution)/shard_map/gau,sugc->sagc/dot_general | solution.py:74
  206.2 0.6 copy.77
  206.7 0.6 reshape.190
  207.3 0.1 fusion.35
  207.4 0.8 copy.82
  208.3 0.8 copy.83
  (29 shorter events, 0.7 us)
Async XLA Ops:
  7.2 10.8 %copy-start = (bf16[64,128]{1,0:T(8,128)(2,1)S(1)}, bf16[64,128]{1,0:T(8,128)(2,1)}, u32[]{:S(2)}) copy-start(bf16[64,128]{1,0:T(8,128)(2,1)} %param.12) | copy-start | bytes 49156
  7.2 6.4 %copy-start.3 = (s32[32]{0:T(128)S(1)}, s32[32]{0:T(128)}, u32[]{:S(2)}) copy-start(s32[32]{0:T(128)} %param.13) | copy-start | bytes 388
  7.2 81.4 %all-gather.3.cloned.1.call-start = ((), (), s32[]{:S(2)}) async-start(), calls=%async_computation | async-start | bytes 8912896 | tf_op jit(solution)/shard_map/all_gather | solution.py:36
  98.8 94.3 %copy-start.1 = (bf16[2,64,64,16]{1,3,0,2:T(8,128)(2,1)S(1)}, bf16[2,64,64,16]{1,3,0,2:T(8,128)(2,1)}, u32[]{:S(2)}) copy-start(bf16[2,64,64,16]{1,3,0,2:T(8,128)(2,1)} %copy.70) | copy-start | bytes 786436
  197.1 6.0 %copy-start.2 = (bf16[2,64,64,16]{1,3,0,2:T(8,128)(2,1)S(1)}, bf16[2,64,64,16]{1,3,0,2:T(8,128)(2,1)}, u32[]{:S(2)}) copy-start(bf16[2,64,64,16]{1,3,0,2:T(8,128)(2,1)} %copy.75) | copy-start | bytes 786436
Sparse Core Ops, SparseCore 0:
  13.2 75.3 all-gather.2

commit v2 on v1

--- a/solution.py
+++ b/solution.py
@@ -81,10 +81,16 @@
     partial_grad = jnp.einsum(
         "gaw,jaw->gj", corr, select_fwd.astype(jnp.float32), precision=lax.Precision.HIGHEST
     )
-    total_grad = lax.psum(partial_grad, "seq")
-    squares = lax.psum(jnp.sum(total_grad * total_grad), "chan")
-    limit = math.sqrt(groups * lax.axis_size("chan") * taps)
+    lanes = lax.axis_size("chan")
+    slot = lax.axis_index("chan")
+    placed = jnp.where(
+        (jnp.arange(lanes) == slot)[:, None, None], partial_grad[None], jnp.zeros_like(partial_grad)[None]
+    )
+    every_grad = lax.psum(placed, ("seq", "chan"))
+    squares = jnp.sum(every_grad * every_grad)
+    limit = math.sqrt(groups * lanes * taps)
     factor = jnp.minimum(1.0, limit / jnp.sqrt(squares + 1e-06))
+    total_grad = lax.dynamic_index_in_dim(every_grad, slot, 0, keepdims=False)
     filter_grad = factor * total_grad
 
     gated_out = times_rounded(query_rows, convolved)

time: 216 us -> 259 us (1.20)
  waiting for transfers between devices: 63.9 us -> 188 us
  blocking collectives: 85.7 us -> 0 us
    psum x0 -> x1, waiting for transfers between devices: none -> 125 us  [shards(): every_grad = lax.psum(placed, ('seq', 'chan'))]
    psum x2 -> x0, blocking collectives: 85.7 us -> none  [the longest x1 65.4 us: shards(): total_grad = lax.psum(partial_grad, 'seq')]
  transfers between devices with their start and end apart: 1 -> 2, of which waited for: 1 -> 2; matrix products, arithmetic and copies ran while one was open for 5% -> 11% of each run, Pallas kernels for 0% -> 0%
where the time goes in v2:
time: 259 us; the launch traced here: 258 us
  waiting for transfers between devices  188 us (73%)
  local copies, waits for them, and re-layouts  30.1 us (12%)
  matrix products  19 us (7%)
  between operations  15 us (6%)
  other arithmetic  4.89 us (2%)
    psum x1, waiting for transfers between devices, shards(): every_grad = lax.psum(placed, ('seq', 'chan'))  125 us
    all_gather x1, waiting for transfers between devices, shards(): lax.all_gather(jnp.stack([mixed, gated]), 'seq', axis=0, tiled=False)  63.8 us
    unnamed x16, local copies, waits for them, and re-layouts  7.9 us
    slice x1, local copies, waits for them, and re-layouts, shards(): gated_blocks = gathered[:, 1].reshape(spans, span_rows, channels)  6.02 us
    gather x2, local copies, waits for them, and re-layouts, pick(): jnp.take(blocks, slots, axis=0)  5.61 us
  transfers between devices with their start and end apart: 2, of which 2 were waited for; matrix products, arithmetic and copies ran while one was open for 11% of the time, Pallas kernels for 0%

profile of v2, /device:TPU:0, one launch (start us, length us, event | category | flops | bytes accessed | tf_op | source)
XLA Modules:
  0.0 257.5 jit_solution(3051047460860267110)
XLA Ops:
  7.2 1.1 copy.64
  8.4 1.1 copy.65
  9.5 1.1 copy.63
  10.6 1.1 copy.66
  12.0 1.0 copy.67
  13.1 0.2 concatenate.12
  13.3 0.2 concatenate.14
  13.6 0.1 broadcast_add_fusion
  13.7 0.1 compare_select_fusion
  13.8 0.1 reshape.216
  14.0 0.1 broadcast_in_dim.68
  14.1 0.9 copy.70
  15.0 0.1 reshape.224
  15.1 0.7 scatter_custom_fusion
  15.8 0.6 gather_fusion
  16.4 0.6 gather_fusion.1
  17.1 0.1 broadcast_in_dim.72
  17.2 0.9 copy.75
  18.2 3.2 %convert_bitcast_fusion = bf16[64,64,192,1]{2,0,1,3:T(8,128)(2,1)} fusion(bf16[64,128]{1,0:T(8,128)(2,1)S(1)} %copy-done), kind=kOutput, calls=%fused_computation.18 | convolution fusion | flops 205258752 | bytes 1589248 | tf_op jit(solution)/shard_map/gj,jau->gau/dot_general | solution.py:67
  21.3 3.5 %convert_bitcast_fusion.1 = bf16[64,64,192,1]{2,0,1,3:T(8,128)(2,1)} fusion(s32[64]{0:T(128)S(1)} %iota_add_fusion, bf16[64,128]{1,0:T(8,128)(2,1)S(1)} %copy-done), kind=kOutput, calls=%fused_computation.19 | convolution fusion | flops 205258752 | bytes 1589504 | tf_op jit(solution)/shard_map/gj,jaw->gaw/dot_general | solution.py:64
  24.9 63.8 %all-gather.3.cloned.1.call-done = bf16[32,128,1024]{2,1,0:T(8,128)(2,1)} async-done(((bf16[2,128,1024]{2,1,0:T(8,128)(2,1)}), bf16[32,128,1024]{2,1,0:T(8,128)(2,1)}) %all-gather.3.cloned.1.call-update) | async-done | bytes 8388624 | tf_op jit(solution)/shard_map/all_gather | solution.py:36
  88.6 6.0 %fusion.48 = (bf16[16,1,128,1024]{3,2,1,0:T(8,128)(2,1)}, bf16[16,1,128,1024]{3,2,1,0:T(8,128)(2,1)}) fusion(bf16[16,2,128,1024]{3,2,1,0:T(8,128)(2,1)} %bitcast.45), kind=kLoop, calls=%fused_computation.76 | loop fusion | bytes 16777216 | tf_op jit(solution)/shard_map/slice | solution.py:38
  94.6 2.8 %gather_fusion.2 = bf16[4,64,1024]{2,1,0:T(8,128)(2,1)S(1)} fusion(bf16[32,64,1024]{2,1,0:T(8,128)(2,1)} %bitcast.47, s32[1024]{0:T(1024)S(1)} %pad_clamp_fusion.2), kind=kCustom, calls=%fused_computation.clone | custom fusion | bytes 1048592 | tf_op jit(solution)/shard_map/jit(_take)/gather | solution.py:49
  97.4 0.1 broadcast_select_fusion.1
  97.5 0.7 copy.68
  98.2 0.5 reshape.193
  98.8 1.8 convolution_bitcast_fusion
  100.6 4.6 %fusion.28 = f32[64,128]{1,0:T(8,128)S(1)} fusion(s32[64]{0:T(128)S(1)} %iota_add_fusion, f32[64,64,192]{2,1,0:T(8,128)S(1)} %convolution_bitcast_fusion), kind=kOutput, calls=%fused_computation.26 | convolution fusion | flops 1211105280 | bytes 3178752 | tf_op jit(solution)/shard_map/gaw,jaw->gj/dot_general | solution.py:81
  105.3 0.8 broadcast_select_fusion.2
  106.1 2.9 %fusion.16 = f32[2,64,64,16]{1,3,0,2:T(8,128)S(1)} fusion(bf16[64,64,192,1]{2,0,1,3:T(8,128)(2,1)} %convert_bitcast_fusion.1, bf16[2,64,64,16]{1,3,0,2:T(8,128)(2,1)S(1)} %copy-done.1, bf16[2,128,64,16]{1,3,0,2:T(8,128)(2,1)S(1)} %copy_select_fusion.1), kind=kOutput, calls=%fused_computation.22 | convolution fusion | flops 52166656 | bytes 2883584 | tf_op jit(solution)/shard_map/gaw,swgc->sagc/dot_general | solution.py:72
  109.0 0.5 copy.72
  109.6 0.6 reshape.196
  110.2 0.1 fusion.39
  110.3 2.8 %gather_fusion.3 = bf16[4,64,1024]{2,1,0:T(8,128)(2,1)S(1)} fusion(bf16[32,64,1024]{2,1,0:T(8,128)(2,1)} %bitcast.46, s32[1024]{0:T(1024)S(1)} %pad_clamp_fusion), kind=kCustom, calls=%fused_computation.1.clone | custom fusion | bytes 1048592 | tf_op jit(solution)/shard_map/jit(_take)/gather | solution.py:49
  113.1 0.1 broadcast_select_fusion
  113.2 0.9 copy.73
  114.2 0.5 reshape.195
  114.8 3.0 %fusion.25 = f32[2,64,64,16]{1,3,0,2:T(8,128)S(1)} fusion(bf16[64,64,192,1]{2,0,1,3:T(8,128)(2,1)} %convert_bitcast_fusion, bf16[2,128,64,16]{1,3,0,2:T(8,128)(2,1)S(1)} %copy_select_fusion, bf16[2,64,64,16]{1,3,0,2:T(8,128)(2,1)S(1)} %copy-done.2), kind=kOutput, calls=%fused_computation.25 | convolution fusion | flops 52166656 | bytes 2883584 | tf_op jit(solution)/shard_map/gau,sugc->sagc/dot_general | solution.py:74
  117.7 0.6 copy.77
  118.3 0.6 reshape.197
  118.9 0.1 fusion.35
  119.0 0.9 copy.80
  119.8 0.8 copy.81
  120.7 0.8 copy.82
  121.5 0.8 copy.83
  122.4 124.6 %all-reduce.2.cloned.1.call-done = f32[8,64,128]{2,1,0:T(8,128)} async-done(((f32[8,64,128]{2,1,0:T(8,128)}), f32[8,64,128]{2,1,0:T(8,128)}) %all-reduce.2.cloned.1.call-update) | async-done | bytes 262160 | tf_op jit(solution)/shard_map/psum | solution.py:89
  247.0 1.6 multiply_reduce_fusion
  249.3 1.4 multiply_bitcast_fusion
  (32 shorter events, 0.8 us)
Async XLA Ops:
  7.2 11.0 %copy-start = (bf16[64,128]{1,0:T(8,128)(2,1)S(1)}, bf16[64,128]{1,0:T(8,128)(2,1)}, u32[]{:S(2)}) copy-start(bf16[64,128]{1,0:T(8,128)(2,1)} %param.12) | copy-start | bytes 49156
  7.2 6.4 %copy-start.3 = (s32[32]{0:T(128)S(1)}, s32[32]{0:T(128)}, u32[]{:S(2)}) copy-start(s32[32]{0:T(128)} %param.13) | copy-start | bytes 388
  7.2 81.4 %all-gather.3.cloned.1.call-start = ((), (), s32[]{:S(2)}) async-start(), calls=%async_computation.1 | async-start | bytes 8912896 | tf_op jit(solution)/shard_map/all_gather | solution.py:36
  13.0 234.0 %all-reduce.2.cloned.1.call-start = ((), (), s32[]{:S(2)}) async-start(), calls=%async_computation | async-start | bytes 524288 | tf_op jit(solution)/shard_map/psum | solution.py:89
  100.6 5.5 %copy-start.1 = (bf16[2,64,64,16]{1,3,0,2:T(8,128)(2,1)S(1)}, bf16[2,64,64,16]{1,3,0,2:T(8,128)(2,1)}, u32[]{:S(2)}) copy-start(bf16[2,64,64,16]{1,3,0,2:T(8,128)(2,1)} %copy.70) | copy-start | bytes 786436
  110.3 4.5 %copy-start.2 = (bf16[2,64,64,16]{1,3,0,2:T(8,128)(2,1)S(1)}, bf16[2,64,64,16]{1,3,0,2:T(8,128)(2,1)}, u32[]{:S(2)}) copy-start(bf16[2,64,64,16]{1,3,0,2:T(8,128)(2,1)} %copy.75) | copy-start | bytes 786436
Sparse Core Ops, SparseCore 0:
  13.2 75.3 all-gather.2
  106.2 140.7 all-reduce.1

commit v3 on v1

--- a/solution.py
+++ b/solution.py
@@ -18,8 +18,8 @@
 
 
 def shards(query_rows, key_rows, value_rows, grad_rows, filters, span_order):
-    device = lax.axis_index("seq")
-    devices = lax.axis_size("seq")
+    device = lax.axis_index(SEQ)
+    devices = lax.axis_size(SEQ)
     rows, channels = query_rows.shape
     spans = span_order.shape[0]
     span_rows = rows * devices // spans
@@ -33,9 +33,13 @@
 
     mixed = times_rounded(key_rows, value_rows)
     gated = times_rounded(grad_rows, query_rows)
-    gathered = lax.all_gather(jnp.stack([mixed, gated]), "seq", axis=0, tiled=False)
-    mixed_blocks = gathered[:, 0].reshape(spans, span_rows, channels)
-    gated_blocks = gathered[:, 1].reshape(spans, span_rows, channels)
+    across = lax.all_gather(jnp.stack([mixed, gated]), CHIPS, axis=0, tiled=False)
+    gathered = lax.all_gather(across, CORE, axis=0, tiled=False)
+    cores = lax.axis_size(CORE)
+    chips = devices // cores
+    gathered = gathered.reshape(cores, chips, 2, per_device, span_rows, channels)
+    mixed_blocks = gathered[:, :, 0].reshape(spans, span_rows, channels)
+    gated_blocks = gathered[:, :, 1].reshape(spans, span_rows, channels)
 
     slot_of = jnp.zeros((spans,), jnp.int32).at[span_order].set(jnp.arange(spans, dtype=jnp.int32))
     mine = lax.dynamic_slice_in_dim(span_order, device * per_device, per_device)
@@ -46,6 +50,8 @@
     def pick(blocks, wanted):
         valid = (wanted >= 0) & (wanted < spans)
         slots = slot_of[jnp.clip(wanted, 0, spans - 1)].reshape(-1)
+        holder = slots // per_device
+        slots = ((holder % cores) * chips + holder // cores) * per_device + slots % per_device
         taken = jnp.take(blocks, slots, axis=0).reshape(per_device, halo, span_rows, channels)
         return jnp.where(valid[:, :, None, None], taken, jnp.zeros_like(taken))
 
@@ -81,9 +87,13 @@
     partial_grad = jnp.einsum(
         "gaw,jaw->gj", corr, select_fwd.astype(jnp.float32), precision=lax.Precision.HIGHEST
     )
-    total_grad = lax.psum(partial_grad, "seq")
-    squares = lax.psum(jnp.sum(total_grad * total_grad), "chan")
-    limit = math.sqrt(groups * lax.axis_size("chan") * taps)
+    total_grad = partial_grad
+    for axis in SEQ[::-1]:
+        total_grad = lax.psum(total_grad, axis)
+    squares = jnp.sum(total_grad * total_grad)
+    for axis in CHAN[::-1]:
+        squares = lax.psum(squares, axis)
+    limit = math.sqrt(groups * lax.axis_size(CHAN) * taps)
     factor = jnp.minimum(1.0, limit / jnp.sqrt(squares + 1e-06))
     filter_grad = factor * total_grad
 
@@ -101,24 +111,21 @@
     return (u == a + j).astype(jnp.bfloat16)
 
 
+SEQ = ("zh", "y", "core")
+CHAN = ("x", "zl")
+CHIPS = ("zh", "y")
+CORE = "core"
+
+
 def solution(mesh):
+    seq_size, chan_size = mesh.devices.shape
+    split = mesh.devices.reshape(2, seq_size // 4, 2, chan_size // 2, 2)
+    fine = jax.sharding.Mesh(split, SEQ + CHAN)
+    rows = P(SEQ, CHAN)
     return jax.shard_map(
         shards,
-        mesh=mesh,
-        in_specs=(
-            P("seq", "chan"),
-            P("seq", "chan"),
-            P("seq", "chan"),
-            P("seq", "chan"),
-            P("chan", None),
-            P(),
-        ),
-        out_specs=(
-            P("seq", "chan"),
-            P("seq", "chan"),
-            P("seq", "chan"),
-            P("seq", "chan"),
-            P("chan", None),
-        ),
+        mesh=fine,
+        in_specs=(rows, rows, rows, rows, P(CHAN, None), P()),
+        out_specs=(rows, rows, rows, rows, P(CHAN, None)),
         check_vma=False,
     )

time: 216 us -> 201 us (0.931)
  blocking collectives: 85.7 us -> 49 us
  waiting for transfers between devices: 63.9 us -> 85.4 us
    psum x2 -> x5, blocking collectives: 85.7 us -> 49 us  [the longest x3 32.4 us: shards(): total_grad = lax.psum(total_grad, axis)]
    all_gather x1 -> x2, waiting for transfers between devices: 63.9 us -> 85.4 us  [the longest x1 74.3 us: shards(): lax.all_gather(jnp.stack([mixed, gated]), CHIPS, axis=0, tiled=False)]
  transfers between devices with their start and end apart: 1 -> 2, of which waited for: 1 -> 2; matrix products, arithmetic and copies ran while one was open for 5% -> 5% of each run, Pallas kernels for 0% -> 0%
where the time goes in v3:
time: 201 us; the launch traced here: 200 us
  waiting for transfers between devices  85.4 us (42%)
  blocking collectives  49 us (24%)
  local copies, waits for them, and re-layouts  29.1 us (14%)
  matrix products  19.4 us (10%)
  between operations  15.1 us (8%)
  other arithmetic  2.33 us (1%)
    all_gather x1, waiting for transfers between devices, shards(): lax.all_gather(jnp.stack([mixed, gated]), CHIPS, axis=0, tiled=False)  74.3 us
    psum x3, blocking collectives, shards(): total_grad = lax.psum(total_grad, axis)  32.4 us
    psum x2, blocking collectives, shards(): squares = lax.psum(squares, axis)  16.6 us
    all_gather x1, waiting for transfers between devices, shards(): gathered = lax.all_gather(across, CORE, axis=0, tiled=False)  11.1 us
    unnamed x16, local copies, waits for them, and re-layouts  7.9 us
    slice x1, local copies, waits for them, and re-layouts, shards(): gated_blocks = gathered[:, :, 1].reshape(spans, span_rows, channels)  6.15 us
    gather x2, local copies, waits for them, and re-layouts, pick(): jnp.take(blocks, slots, axis=0)  5.53 us
    dot_general x1, matrix products, shards(): jnp.einsum('gaw,jaw->gj', corr, select_fwd.astype(jnp.float32), precision...  4.69 us
  transfers between devices with their start and end apart: 2, of which 2 were waited for; matrix products, arithmetic and copies ran while one was open for 5% of the time, Pallas kernels for 0%

profile of v3, /device:TPU:0, one launch (start us, length us, event | category | flops | bytes accessed | tf_op | source)
XLA Modules:
  0.0 200.4 jit_solution(10462531638418293397)
XLA Ops:
  7.2 1.1 copy.47
  8.4 1.1 copy.48
  9.5 1.1 copy.46
  10.6 1.1 copy.49
  12.0 1.0 copy.50
  13.0 74.3 %all-gather.5.cloned.1.call-done = bf16[16,128,1024]{2,1,0:T(8,128)(2,1)} async-done(((bf16[2,128,1024]{2,1,0:T(8,128)(2,1)}), bf16[16,128,1024]{2,1,0:T(8,128)(2,1)}) %all-gather.5.cloned.1.call-update) | async-done | bytes 4194320 | tf_op jit(solution)/shard_map/all_gather | solution.py:36
  87.4 0.2 concatenate.12
  87.6 0.2 concatenate.14
  88.0 0.1 reshape.213
  88.3 0.1 broadcast_in_dim.42
  88.4 0.9 copy.53
  89.3 0.7 scatter_custom_fusion
  90.0 0.6 gather_fusion
  90.7 0.6 gather_fusion.1
  91.4 3.1 %convert_bitcast_fusion = bf16[64,64,192,1]{2,0,1,3:T(8,128)(2,1)} fusion(bf16[64,128]{1,0:T(8,128)(2,1)S(1)} %copy-done), kind=kOutput, calls=%fused_computation.18 | convolution fusion | flops 205258752 | bytes 1589248 | tf_op jit(solution)/shard_map/gj,jau->gau/dot_general | solution.py:73
  94.5 3.5 %convert_bitcast_fusion.1 = bf16[64,64,192,1]{2,0,1,3:T(8,128)(2,1)} fusion(s32[64]{0:T(128)S(1)} %iota_add_fusion, bf16[64,128]{1,0:T(8,128)(2,1)S(1)} %copy-done), kind=kOutput, calls=%fused_computation.19 | convolution fusion | flops 205258752 | bytes 1589504 | tf_op jit(solution)/shard_map/gj,jaw->gaw/dot_general | solution.py:70
  98.1 11.1 %all-gather.7.cloned.1.call-done = bf16[16,2,128,1024]{3,2,1,0:T(8,128)(2,1)} async-done(((bf16[8,2,128,1024]{3,2,1,0:T(8,128)(2,1)}), bf16[16,2,128,1024]{3,2,1,0:T(8,128)(2,1)}) %all-gather.7.cloned.1.call-update) | async-done | bytes 8388624 | tf_op jit(solution)/shard_map/all_gather | solution.py:37
  109.2 6.2 %fusion.54 = (bf16[2,8,1,2,64,1024]{5,4,3,2,1,0:T(8,128)(2,1)}, bf16[2,8,1,2,64,1024]{5,4,3,2,1,0:T(8,128)(2,1)}) fusion(bf16[2,8,2,2,64,1024]{5,4,3,2,1,0:T(8,128)(2,1)} %bitcast.44), kind=kLoop, calls=%fused_computation.100 | loop fusion | bytes 16777216 | tf_op jit(solution)/shard_map/slice | solution.py:42
  115.3 2.8 %gather_fusion.2 = bf16[4,64,1024]{2,1,0:T(8,128)(2,1)S(1)} fusion(bf16[32,64,1024]{2,1,0:T(8,128)(2,1)} %bitcast.46, s32[1024]{0:T(1024)S(1)} %pad_clamp_fusion.2), kind=kCustom, calls=%fused_computation.clone | custom fusion | bytes 1048592 | tf_op jit(solution)/shard_map/jit(_take)/gather | solution.py:55
  118.1 0.1 broadcast_select_fusion.1
  118.2 0.7 copy.51
  119.0 0.5 reshape.190
  119.5 2.0 convolution_bitcast_fusion
  121.5 4.7 %fusion.28 = f32[64,128]{1,0:T(8,128)S(1)} fusion(s32[64]{0:T(128)S(1)} %iota_add_fusion, f32[64,64,192]{2,1,0:T(8,128)S(1)} %convolution_bitcast_fusion), kind=kOutput, calls=%fused_computation.26 | convolution fusion | flops 1211105280 | bytes 3178752 | tf_op jit(solution)/shard_map/gaw,jaw->gj/dot_general | solution.py:87
  126.2 3.7 %psum.35 = f32[64,128]{1,0:T(8,128)S(1)} all-reduce(f32[64,128]{1,0:T(8,128)S(1)} %fusion.28), channel_id=1, replica_groups=mesh['zh'=2,'y'=4,'core'=2,'x'=4,'zl'=2] {'core'}, use_global_device_ids=true, to_apply=%region_1.3 | all-reduce | flops 8192 | bytes 65536 | tf_op jit(solution)/shard_map/psum | solution.py:92
  130.0 17.2 %psum.36 = f32[64,128]{1,0:T(8,128)S(1)} all-reduce(f32[64,128]{1,0:T(8,128)S(1)} %psum.35), channel_id=1, replica_groups=mesh['zh'=2,'y'=4,'core'=2,'x'=4,'zl'=2] {'y'}, use_global_device_ids=true, to_apply=%region_2.4 | all-reduce | flops 8192 | bytes 65536 | tf_op jit(solution)/shard_map/psum | solution.py:92
  147.1 11.5 %psum.37 = f32[64,128]{1,0:T(8,128)S(1)} all-reduce(f32[64,128]{1,0:T(8,128)S(1)} %psum.36), channel_id=1, replica_groups=mesh['zh'=2,'y'=4,'core'=2,'x'=4,'zl'=2] {'zh'}, use_global_device_ids=true, to_apply=%region_3.5 | all-reduce | flops 8192 | bytes 65536 | tf_op jit(solution)/shard_map/psum | solution.py:92
  158.6 0.6 multiply_reduce_fusion
  159.3 5.6 %psum.38 = f32[]{:T(128)} all-reduce(f32[]{:T(128)} %multiply_reduce_fusion), channel_id=1, replica_groups=mesh['zh'=2,'y'=4,'core'=2,'x'=4,'zl'=2] {'zl'}, use_global_device_ids=true, to_apply=%region_5.7 | all-reduce | flops 1 | bytes 8 | tf_op jit(solution)/shard_map/psum | solution.py:95
  165.0 0.1 broadcast_in_dim.46
  165.0 11.0 %psum.39 = f32[]{:T(128)} all-reduce(f32[]{:T(128)} %psum.38), channel_id=1, replica_groups=mesh['zh'=2,'y'=4,'core'=2,'x'=4,'zl'=2] {'x'}, use_global_device_ids=true, to_apply=%region_6.8 | all-reduce | flops 1 | bytes 8 | tf_op jit(solution)/shard_map/psum | solution.py:95
  176.8 0.6 broadcast_multiply_fusion
  177.4 2.8 %gather_fusion.3 = bf16[4,64,1024]{2,1,0:T(8,128)(2,1)S(1)} fusion(bf16[32,64,1024]{2,1,0:T(8,128)(2,1)} %bitcast.45, s32[1024]{0:T(1024)S(1)} %pad_clamp_fusion), kind=kCustom, calls=%fused_computation.1.clone | custom fusion | bytes 1048592 | tf_op jit(solution)/shard_map/jit(_take)/gather | solution.py:55
  180.2 0.1 broadcast_select_fusion
  180.3 0.7 copy.56
  181.0 0.5 reshape.192
  181.6 3.0 %fusion.25 = f32[2,64,64,16]{1,3,0,2:T(8,128)S(1)} fusion(bf16[64,64,192,1]{2,0,1,3:T(8,128)(2,1)} %convert_bitcast_fusion, bf16[2,128,64,16]{1,3,0,2:T(8,128)(2,1)S(1)} %copy_select_fusion, bf16[2,64,64,16]{1,3,0,2:T(8,128)(2,1)S(1)} %copy.58), kind=kOutput, calls=%fused_computation.25 | convolution fusion | flops 52166656 | bytes 2883584 | tf_op jit(solution)/shard_map/gau,sugc->sagc/dot_general | solution.py:80
  184.5 0.6 copy.60
  185.1 0.6 reshape.194
  185.7 0.1 fusion.35
  185.8 0.9 copy.65
  186.6 0.8 copy.66
  187.5 3.1 %fusion.16 = f32[2,64,64,16]{1,3,0,2:T(8,128)S(1)} fusion(bf16[64,64,192,1]{2,0,1,3:T(8,128)(2,1)} %convert_bitcast_fusion.1, bf16[2,64,64,16]{1,3,0,2:T(8,128)(2,1)S(1)} %copy-done.1, bf16[2,128,64,16]{1,3,0,2:T(8,128)(2,1)} %copy-done.2), kind=kOutput, calls=%fused_computation.22 | convolution fusion | flops 52166656 | bytes 2883584 | tf_op jit(solution)/shard_map/gaw,swgc->sagc/dot_general | solution.py:78
  190.6 0.5 copy.55
  191.1 0.6 reshape.193
  191.7 0.1 fusion.39
  191.8 0.9 copy.63
  192.7 0.8 copy.64
  (33 shorter events, 1.1 us)
Async XLA Ops:
  7.2 84.2 %copy-start = (bf16[64,128]{1,0:T(8,128)(2,1)S(1)}, bf16[64,128]{1,0:T(8,128)(2,1)}, u32[]{:S(2)}) copy-start(bf16[64,128]{1,0:T(8,128)(2,1)} %param.12) | copy-start | bytes 49156
  7.2 80.1 %all-gather.5.cloned.1.call-start = ((), (), s32[]{:S(2)}) async-start(), calls=%async_computation | async-start | bytes 4718592 | tf_op jit(solution)/shard_map/all_gather | solution.py:36
  11.9 76.0 %copy-start.3 = (s32[32]{0:T(128)S(1)}, s32[32]{0:T(128)}, u32[]{:S(2)}) copy-start(s32[32]{0:T(128)} %param.13) | copy-start | bytes 388
  13.0 96.2 %all-gather.7.cloned.1.call-start = ((), (), s32[]{:S(2)}) async-start(), calls=%async_computation.1 | async-start | bytes 12582912 | tf_op jit(solution)/shard_map/all_gather | solution.py:37
  119.5 6.7 %copy-start.2 = (bf16[2,128,64,16]{1,3,0,2:T(8,128)(2,1)}, bf16[2,128,64,16]{1,3,0,2:T(8,128)(2,1)S(1)}, u32[]{:S(2)}) copy-start(bf16[2,128,64,16]{1,3,0,2:T(8,128)(2,1)S(1)} %copy_select_fusion.1) | copy-start | bytes 1572868
  184.5 3.0 %copy-start.1 = (bf16[2,64,64,16]{1,3,0,2:T(8,128)(2,1)S(1)}, bf16[2,64,64,16]{1,3,0,2:T(8,128)(2,1)}, u32[]{:S(2)}) copy-start(bf16[2,64,64,16]{1,3,0,2:T(8,128)(2,1)} %copy.53) | copy-start | bytes 786436
Sparse Core Ops, SparseCore 0:
  13.1 74.1 all-gather.4
  89.0 20.1 all-gather.6

commit v4 on v1

--- a/solution.py
+++ b/solution.py
@@ -8,6 +8,16 @@
 
 def times_rounded(left, right):
     return (left.astype(jnp.float32) * right.astype(jnp.float32)).astype(jnp.bfloat16)
+
+
+def butterfly_sum(value, axis):
+    size = lax.axis_size(axis)
+    bit = 1
+    while bit < size:
+        pairs = [(i, i ^ bit) for i in range(size)]
+        value = value + lax.ppermute(value, axis, pairs)
+        bit *= 2
+    return value
 
 
 def band_select(taps, out_rows, window, lead):
@@ -33,9 +43,8 @@
 
     mixed = times_rounded(key_rows, value_rows)
     gated = times_rounded(grad_rows, query_rows)
-    gathered = lax.all_gather(jnp.stack([mixed, gated]), "seq", axis=0, tiled=False)
-    mixed_blocks = gathered[:, 0].reshape(spans, span_rows, channels)
-    gated_blocks = gathered[:, 1].reshape(spans, span_rows, channels)
+    mixed_blocks = lax.all_gather(mixed, "seq", axis=0, tiled=True).reshape(spans, span_rows, channels)
+    gated_blocks = lax.all_gather(gated, "seq", axis=0, tiled=True).reshape(spans, span_rows, channels)
 
     slot_of = jnp.zeros((spans,), jnp.int32).at[span_order].set(jnp.arange(spans, dtype=jnp.int32))
     mine = lax.dynamic_slice_in_dim(span_order, device * per_device, per_device)
@@ -81,8 +90,8 @@
     partial_grad = jnp.einsum(
         "gaw,jaw->gj", corr, select_fwd.astype(jnp.float32), precision=lax.Precision.HIGHEST
     )
-    total_grad = lax.psum(partial_grad, "seq")
-    squares = lax.psum(jnp.sum(total_grad * total_grad), "chan")
+    total_grad = butterfly_sum(partial_grad, "seq")
+    squares = butterfly_sum(jnp.sum(total_grad * total_grad), "chan")
     limit = math.sqrt(groups * lax.axis_size("chan") * taps)
     factor = jnp.minimum(1.0, limit / jnp.sqrt(squares + 1e-06))
     filter_grad = factor * total_grad

time: 216 us -> 192 us (0.89)
  blocking collectives: 85.7 us -> 0 us
  waiting for transfers between devices: 63.9 us -> 118 us
  starting transfers between devices: 0.04 us -> 12 us
  local copies, waits for them, and re-layouts: 29.9 us -> 25.9 us
  matrix products: 19.1 us -> 15.2 us
    psum x2 -> x0, blocking collectives: 85.7 us -> none  [the longest x1 65.4 us: shards(): total_grad = lax.psum(partial_grad, 'seq')]
    all_gather x1 -> x2, waiting for transfers between devices: 63.9 us -> 108 us  [the longest x1 55.3 us: shards(): lax.all_gather(gated, 'seq', axis=0, tiled=True)]
    ppermute x0 -> x7, starting transfers between devices: none -> 12 us  [butterfly_sum(): value = value + lax.ppermute(value, axis, pairs)]
    ppermute x0 -> x7, waiting for transfers between devices: none -> 9.97 us  [butterfly_sum(): value = value + lax.ppermute(value, axis, pairs)]
    all_gather x0 -> x1, local copies, waits for them, and re-layouts: none -> 6.44 us  [shards(): lax.all_gather(gated, 'seq', axis=0, tiled=True)]
    slice x1 -> x0, local copies, waits for them, and re-layouts: 6.03 us -> none  [shards(): gated_blocks = gathered[:, 1].reshape(spans, span_rows, channels)]
    unnamed x16 -> x12, local copies, waits for them, and re-layouts: 7.91 us -> 3.96 us
  transfers between devices with their start and end apart: 1 -> 9, of which waited for: 1 -> 9; matrix products, arithmetic and copies ran while one was open for 5% -> 8% of each run, Pallas kernels for 0% -> 0%
where the time goes in v4:
time: 192 us
  waiting for transfers between devices  118 us (61%)
  local copies, waits for them, and re-layouts  25.9 us (13%)
  between operations  17.1 us (9%)
  matrix products  15.2 us (8%)
  starting transfers between devices  12 us (6%)
  other arithmetic  3.79 us (2%)
    all_gather x1, waiting for transfers between devices, shards(): lax.all_gather(gated, 'seq', axis=0, tiled=True)  55.3 us
    all_gather x1, waiting for transfers between devices, shards(): lax.all_gather(mixed, 'seq', axis=0, tiled=True)  52.4 us
    ppermute x7, starting transfers between devices, butterfly_sum(): value = value + lax.ppermute(value, axis, pairs)  12 us
    ppermute x7, waiting for transfers between devices, butterfly_sum(): value = value + lax.ppermute(value, axis, pairs)  9.97 us
    all_gather x1, local copies, waits for them, and re-layouts, shards(): lax.all_gather(gated, 'seq', axis=0, tiled=True)  6.44 us
    gather x2, local copies, waits for them, and re-layouts, pick(): jnp.take(blocks, slots, axis=0)  5.53 us
    dot_general x1, matrix products, shards(): jnp.einsum('gaw,jaw->gj', corr, select_fwd.astype(jnp.float32), precision...  4.69 us
    unnamed x12, local copies, waits for them, and re-layouts  3.96 us
  transfers between devices with their start and end apart: 9, of which 9 were waited for; matrix products, arithmetic and copies ran while one was open for 8% of the time, Pallas kernels for 0%

profile of v4, /device:TPU:0, one launch (start us, length us, event | category | flops | bytes accessed | tf_op | source)
XLA Modules:
  0.0 191.7 jit_solution(11736809673204109536)
XLA Ops:
  7.2 1.1 copy.25
  8.4 1.1 copy.32
  9.5 0.8 fusion.39
  10.3 1.2 concatenate.14
  12.1 0.7 scatter_custom_fusion
  12.8 0.6 gather_fusion.1
  13.5 3.2 %convert_bitcast_fusion = bf16[64,64,192,1]{2,0,1,3:T(8,128)(2,1)} fusion(bf16[64,128]{1,0:T(8,128)(2,1)S(1)} %copy-done), kind=kOutput, calls=%fused_computation.18 | convolution fusion | flops 205258752 | bytes 1589248 | tf_op jit(solution)/shard_map/gj,jau->gau/dot_general | solution.py:76
  16.7 55.3 %all-gather.5.cloned.1.call-done = bf16[2048,1024]{0,1:T(8,128)(2,1)} async-done(((bf16[128,1024]{0,1:T(8,128)(2,1)}), bf16[2048,1024]{0,1:T(8,128)(2,1)}) %all-gather.5.cloned.1.call-update) | async-done | bytes 4194320 | tf_op jit(solution)/shard_map/all_gather | solution.py:47
  72.0 6.4 %copy.33 = bf16[2048,1024]{1,0:T(8,128)(2,1)} copy(bf16[2048,1024]{0,1:T(8,128)(2,1)} %all-gather.5.cloned.1.call-done) | data formatting | bytes 8388608 | tf_op jit(solution)/shard_map/all_gather | solution.py:47
  78.5 2.8 %gather_fusion.3 = bf16[4,64,1024]{2,1,0:T(8,128)(2,1)S(1)} fusion(bf16[32,64,1024]{2,1,0:T(8,128)(2,1)} %bitcast.40, s32[1024]{0:T(1024)S(1)} %pad_clamp_fusion), kind=kCustom, calls=%fused_computation.1.clone | custom fusion | bytes 1048592 | tf_op jit(solution)/shard_map/jit(_take)/gather | solution.py:58
  81.4 0.7 copy.34
  82.1 0.5 reshape.196
  82.6 3.0 %fusion.25 = f32[2,64,64,16]{1,3,0,2:T(8,128)S(1)} fusion(bf16[64,64,192,1]{2,0,1,3:T(8,128)(2,1)} %convert_bitcast_fusion, bf16[2,128,64,16]{1,3,0,2:T(8,128)(2,1)S(1)} %copy_select_fusion, bf16[2,64,64,16]{1,3,0,2:T(8,128)(2,1)S(1)} %copy.36), kind=kOutput, calls=%fused_computation.25 | convolution fusion | flops 52166656 | bytes 2883584 | tf_op jit(solution)/shard_map/gau,sugc->sagc/dot_general | solution.py:83
  85.6 0.5 copy.38
  86.2 0.6 reshape.198
  86.8 0.2 copy.39
  87.0 1.0 fusion.35
  88.1 0.6 gather_fusion
  88.9 1.1 copy.28
  90.1 0.3 concatenate.12
  90.4 52.4 %all-gather.3.cloned.1.call-done = bf16[2048,1024]{1,0:T(8,128)(2,1)} async-done(((bf16[128,1024]{1,0:T(8,128)(2,1)}), bf16[2048,1024]{1,0:T(8,128)(2,1)}) %all-gather.3.cloned.1.call-update) | async-done | bytes 4194320 | tf_op jit(solution)/shard_map/all_gather | solution.py:46
  142.8 2.8 %gather_fusion.2 = bf16[4,64,1024]{2,1,0:T(8,128)(2,1)S(1)} fusion(bf16[32,64,1024]{2,1,0:T(8,128)(2,1)} %bitcast.41, s32[1024]{0:T(1024)S(1)} %pad_clamp_fusion.2), kind=kCustom, calls=%fused_computation.clone | custom fusion | bytes 1048592 | tf_op jit(solution)/shard_map/jit(_take)/gather | solution.py:58
  145.7 0.7 copy.26
  146.4 0.5 reshape.193
  147.0 0.8 convolution_bitcast_fusion
  147.8 4.7 %fusion.28 = f32[64,128]{1,0:T(8,128)S(1)} fusion(s32[64]{0:T(128)S(1)} %iota_add_fusion, f32[64,64,192]{2,1,0:T(8,128)S(1)} %convolution_bitcast_fusion), kind=kOutput, calls=%fused_computation.26 | convolution fusion | flops 1211105280 | bytes 3178752 | tf_op jit(solution)/shard_map/gaw,jaw->gj/dot_general | solution.py:90
  152.5 0.3 collective-permute-start
  152.8 1.0 collective-permute-done
  153.8 1.2 collective-permute-start.1
  154.9 2.2 %convert_bitcast_fusion.1 = bf16[64,64,192,1]{2,0,1,3:T(8,128)(2,1)S(1)} fusion(s32[64]{0:T(128)S(1)} %iota_add_fusion, bf16[64,128]{1,0:T(8,128)(2,1)S(1)} %copy-done), kind=kOutput, calls=%fused_computation.19 | convolution fusion | flops 205258752 | bytes 1589504 | tf_op jit(solution)/shard_map/gj,jaw->gaw/dot_general | solution.py:73
  157.1 0.5 collective-permute-done.1
  157.7 2.2 %collective-permute-start.2 = (f32[64,128]{1,0:T(8,128)S(1)}, f32[64,128]{1,0:T(8,128)S(1)}, u32[]{:S(2)}, u32[]{:S(2)}) collective-permute-start(f32[64,128]{1,0:T(8,128)S(1)} %add.156), channel_id=1, source_target_pairs={{0,32},{8,40},{16,48},{24,56},{32,0},{40,8},{48,16},{56,24},{64,96... | collective-permute-start | bytes 98312 | tf_op jit(solution)/shard_map/ppermute | solution.py:18
  159.9 1.3 fusion.16
  161.2 0.5 copy.31
  161.8 0.6 reshape.197
  162.4 0.7 collective-permute-done.2
  163.1 0.4 collective-permute-start.3
  163.6 0.9 copy.43
  164.4 0.8 copy.44
  165.3 3.2 %collective-permute-done.3 = f32[64,128]{1,0:T(8,128)S(1)} collective-permute-done((f32[64,128]{1,0:T(8,128)S(1)}, f32[64,128]{1,0:T(8,128)S(1)}, u32[]{:S(2)}, u32[]{:S(2)}) %collective-permute-start.3) | collective-permute-done | bytes 32800 | tf_op jit(solution)/shard_map/ppermute | solution.py:18
  168.5 0.6 multiply_reduce_fusion
  169.1 0.7 collective-permute-start.4
  169.8 3.0 %collective-permute-done.4 = f32[]{:T(128)} collective-permute-done((f32[]{:T(128)}, f32[]{:T(128)}, u32[]{:S(2)}, u32[]{:S(2)}) %collective-permute-start.4) | collective-permute-done | bytes 36 | tf_op jit(solution)/shard_map/ppermute | solution.py:18
  174.1 2.8 %collective-permute-start.5 = (f32[]{:T(128)}, f32[]{:T(128)}, u32[]{:S(2)}, u32[]{:S(2)}) collective-permute-start(f32[]{:T(128)} %add.159), channel_id=1, source_target_pairs={{0,2},{1,3},{2,0},{3,1},{4,6},{5,7},{6,4},{7,5},{8,10},{9,11},{10,... | collective-permute-start | bytes 20 | tf_op jit(solution)/shard_map/ppermute | solution.py:18
  177.0 0.8 collective-permute-done.5
  178.4 4.4 %collective-permute-start.6 = (f32[]{:T(128)}, f32[]{:T(128)}, u32[]{:S(2)}, u32[]{:S(2)}) collective-permute-start(f32[]{:T(128)} %add.160), channel_id=1, source_target_pairs={{0,4},{1,5},{2,6},{3,7},{4,0},{5,1},{6,2},{7,3},{8,12},{9,13},{10,... | collective-permute-start | bytes 20 | tf_op jit(solution)/shard_map/ppermute | solution.py:18
  182.8 0.8 collective-permute-done.6
  184.3 0.6 broadcast_multiply_fusion
  (42 shorter events, 1.6 us)
Async XLA Ops:
  7.2 6.3 %copy-start = (bf16[64,128]{1,0:T(8,128)(2,1)S(1)}, bf16[64,128]{1,0:T(8,128)(2,1)}, u32[]{:S(2)}) copy-start(bf16[64,128]{1,0:T(8,128)(2,1)} %param.12) | copy-start | bytes 49156
  7.2 4.4 %copy-start.3 = (s32[32]{0:T(128)S(1)}, s32[32]{0:T(128)}, u32[]{:S(2)}) copy-start(s32[32]{0:T(128)} %param.13) | copy-start | bytes 388
  7.2 64.8 %all-gather.5.cloned.1.call-start = ((), (), s32[]{:S(2)}) async-start(), calls=%async_computation.1 | async-start | bytes 4456448 | tf_op jit(solution)/shard_map/all_gather | solution.py:47
  10.3 132.5 %all-gather.3.cloned.1.call-start = ((), (), s32[]{:S(2)}) async-start(), calls=%async_computation | async-start | bytes 4456448 | tf_op jit(solution)/shard_map/all_gather | solution.py:46
  85.6 1.4 copy-start.1
  85.6 1.4 copy-start.2
  152.5 1.3 collective-permute-start
  153.8 3.9 %collective-permute-start.1 = (f32[64,128]{1,0:T(8,128)S(1)}, f32[64,128]{1,0:T(8,128)S(1)}, u32[]{:S(2)}, u32[]{:S(2)}) collective-permute-start(f32[64,128]{1,0:T(8,128)S(1)} %add.155), channel_id=1, source_target_pairs={{0,16},{8,24},{16,0},{24,8},{32,48},{40,56},{48,32},{56,40},{64,80... | collective-permute-start | bytes 98312 | tf_op jit(solution)/shard_map/ppermute | solution.py:18
  157.7 5.4 %collective-permute-start.2 = (f32[64,128]{1,0:T(8,128)S(1)}, f32[64,128]{1,0:T(8,128)S(1)}, u32[]{:S(2)}, u32[]{:S(2)}) collective-permute-start(f32[64,128]{1,0:T(8,128)S(1)} %add.156), channel_id=1, source_target_pairs={{0,32},{8,40},{16,48},{24,56},{32,0},{40,8},{48,16},{56,24},{64,96... | collective-permute-start | bytes 98312 | tf_op jit(solution)/shard_map/ppermute | solution.py:18
  163.1 5.4 %collective-permute-start.3 = (f32[64,128]{1,0:T(8,128)S(1)}, f32[64,128]{1,0:T(8,128)S(1)}, u32[]{:S(2)}, u32[]{:S(2)}) collective-permute-start(f32[64,128]{1,0:T(8,128)S(1)} %add.157), channel_id=1, source_target_pairs={{0,64},{8,72},{16,80},{24,88},{32,96},{40,104},{48,112},{56,120},{... | collective-permute-start | bytes 98312 | tf_op jit(solution)/shard_map/ppermute | solution.py:18
  169.1 3.7 %collective-permute-start.4 = (f32[]{:T(128)}, f32[]{:T(128)}, u32[]{:S(2)}, u32[]{:S(2)}) collective-permute-start(f32[]{:T(128)} %get-tuple-element.16), channel_id=1, source_target_pairs={{0,1},{1,0},{2,3},{3,2},{4,5},{5,4},{6,7},{7,6},{8,9},{9,8},{10,11... | collective-permute-start | bytes 20 | tf_op jit(solution)/shard_map/ppermute | solution.py:18
  174.1 3.6 %collective-permute-start.5 = (f32[]{:T(128)}, f32[]{:T(128)}, u32[]{:S(2)}, u32[]{:S(2)}) collective-permute-start(f32[]{:T(128)} %add.159), channel_id=1, source_target_pairs={{0,2},{1,3},{2,0},{3,1},{4,6},{5,7},{6,4},{7,5},{8,10},{9,11},{10,... | collective-permute-start | bytes 20 | tf_op jit(solution)/shard_map/ppermute | solution.py:18
  178.4 5.1 %collective-permute-start.6 = (f32[]{:T(128)}, f32[]{:T(128)}, u32[]{:S(2)}, u32[]{:S(2)}) collective-permute-start(f32[]{:T(128)} %add.160), channel_id=1, source_target_pairs={{0,4},{1,5},{2,6},{3,7},{4,0},{5,1},{6,2},{7,3},{8,12},{9,13},{10,... | collective-permute-start | bytes 20 | tf_op jit(solution)/shard_map/ppermute | solution.py:18
Sparse Core Ops, SparseCore 0:
  10.8 61.1 all-gather.4
  88.1 54.6 all-gather.2

commit v5 on v4

--- a/solution.py
+++ b/solution.py
@@ -43,8 +43,9 @@
 
     mixed = times_rounded(key_rows, value_rows)
     gated = times_rounded(grad_rows, query_rows)
-    mixed_blocks = lax.all_gather(mixed, "seq", axis=0, tiled=True).reshape(spans, span_rows, channels)
-    gated_blocks = lax.all_gather(gated, "seq", axis=0, tiled=True).reshape(spans, span_rows, channels)
+    gathered = lax.all_gather(jnp.stack([mixed, gated]), "seq", axis=0, tiled=False)
+    mixed_blocks = gathered[:, 0].reshape(spans, span_rows, channels)
+    gated_blocks = gathered[:, 1].reshape(spans, span_rows, channels)
 
     slot_of = jnp.zeros((spans,), jnp.int32).at[span_order].set(jnp.arange(spans, dtype=jnp.int32))
     mine = lax.dynamic_slice_in_dim(span_order, device * per_device, per_device)

time: 192 us -> 153 us (0.80)
  waiting for transfers between devices: 118 us -> 70.5 us
  local copies, waits for them, and re-layouts: 25.9 us -> 31.1 us
  matrix products: 15.2 us -> 19.6 us
    all_gather x2 -> x1, waiting for transfers between devices: 108 us -> 63.8 us  [shards(): lax.all_gather(jnp.stack([mixed, gated]), 'seq', axis=0, tiled=False)]
    all_gather x1 -> x0, local copies, waits for them, and re-layouts: 6.44 us -> none  [shards(): lax.all_gather(gated, 'seq', axis=0, tiled=True)]
    slice x0 -> x1, local copies, waits for them, and re-layouts: none -> 6.06 us  [shards(): gated_blocks = gathered[:, 1].reshape(spans, span_rows, channels)]
    unnamed x12 -> x20, local copies, waits for them, and re-layouts: 3.96 us -> 7.91 us
    ppermute x7, waiting for transfers between devices: 9.97 us -> 6.71 us  [butterfly_sum(): value = value + lax.ppermute(value, axis, pairs)]
  transfers between devices with their start and end apart: 9 -> 8, of which waited for: 9 -> 6; matrix products, arithmetic and copies ran while one was open for 8% -> 19% of each run, Pallas kernels for 0% -> 0%
where the time goes in v5:
time: 153 us; the launch traced here: 152 us
  waiting for transfers between devices  70.5 us (46%)
  local copies, waits for them, and re-layouts  31.1 us (20%)
  matrix products  19.6 us (13%)
  between operations  17.1 us (11%)
  starting transfers between devices  11.4 us (7%)
  other arithmetic  2.32 us (2%)
    all_gather x1, waiting for transfers between devices, shards(): lax.all_gather(jnp.stack([mixed, gated]), 'seq', axis=0, tiled=False)  63.8 us
    ppermute x7, starting transfers between devices, butterfly_sum(): value = value + lax.ppermute(value, axis, pairs)  11.3 us
    unnamed x20, local copies, waits for them, and re-layouts  7.91 us
    ppermute x7, waiting for transfers between devices, butterfly_sum(): value = value + lax.ppermute(value, axis, pairs)  6.71 us
    slice x1, local copies, waits for them, and re-layouts, shards(): gated_blocks = gathered[:, 1].reshape(spans, span_rows, channels)  6.06 us
    gather x2, local copies, waits for them, and re-layouts, pick(): jnp.take(blocks, slots, axis=0)  5.59 us
    dot_general x1, matrix products, shards(): jnp.einsum('gaw,jaw->gj', corr, select_fwd.astype(jnp.float32), precision...  4.69 us
    dot_general x1, matrix products, shards(): jnp.einsum('gau,sugc->sagc', bwd_band, gated_window, preferred_element_ty...  3.95 us
  transfers between devices with their start and end apart: 8, of which 6 were waited for; matrix products, arithmetic and copies ran while one was open for 19% of the time, Pallas kernels for 0%

profile of v5, /device:TPU:0, one launch (start us, length us, event | category | flops | bytes accessed | tf_op | source)
XLA Modules:
  0.0 152.1 jit_solution(329173691057268655)
XLA Ops:
  7.2 1.1 copy.64
  8.4 1.1 copy.65
  9.5 1.1 copy.63
  10.6 1.1 copy.66
  12.0 1.1 copy.67
  13.1 0.2 concatenate.12
  13.3 0.2 concatenate.14
  14.1 0.9 copy.70
  15.0 0.7 scatter_custom_fusion
  15.7 0.6 gather_fusion
  16.4 0.6 gather_fusion.1
  17.2 0.9 copy.75
  18.1 3.2 %convert_bitcast_fusion = bf16[64,64,192,1]{2,0,1,3:T(8,128)(2,1)} fusion(bf16[64,128]{1,0:T(8,128)(2,1)S(1)} %copy-done), kind=kOutput, calls=%fused_computation.18 | convolution fusion | flops 205258752 | bytes 1589248 | tf_op jit(solution)/shard_map/gj,jau->gau/dot_general | solution.py:77
  21.3 3.5 %convert_bitcast_fusion.1 = bf16[64,64,192,1]{2,0,1,3:T(8,128)(2,1)} fusion(s32[64]{0:T(128)S(1)} %iota_add_fusion, bf16[64,128]{1,0:T(8,128)(2,1)S(1)} %copy-done), kind=kOutput, calls=%fused_computation.19 | convolution fusion | flops 205258752 | bytes 1589504 | tf_op jit(solution)/shard_map/gj,jaw->gaw/dot_general | solution.py:74
  24.8 63.8 %all-gather.3.cloned.1.call-done = bf16[32,128,1024]{2,1,0:T(8,128)(2,1)} async-done(((bf16[2,128,1024]{2,1,0:T(8,128)(2,1)}), bf16[32,128,1024]{2,1,0:T(8,128)(2,1)}) %all-gather.3.cloned.1.call-update) | async-done | bytes 8388624 | tf_op jit(solution)/shard_map/all_gather | solution.py:46
  88.6 6.1 %fusion.48 = (bf16[16,1,128,1024]{3,2,1,0:T(8,128)(2,1)}, bf16[16,1,128,1024]{3,2,1,0:T(8,128)(2,1)}) fusion(bf16[16,2,128,1024]{3,2,1,0:T(8,128)(2,1)} %bitcast.43), kind=kLoop, calls=%fused_computation.74 | loop fusion | bytes 16777216 | tf_op jit(solution)/shard_map/slice | solution.py:48
  94.6 2.8 %gather_fusion.2 = bf16[4,64,1024]{2,1,0:T(8,128)(2,1)S(1)} fusion(bf16[32,64,1024]{2,1,0:T(8,128)(2,1)} %bitcast.45, s32[1024]{0:T(1024)S(1)} %pad_clamp_fusion.2), kind=kCustom, calls=%fused_computation.clone | custom fusion | bytes 1048592 | tf_op jit(solution)/shard_map/jit(_take)/gather | solution.py:59
  97.5 0.7 copy.68
  98.2 0.5 reshape.186
  98.8 2.0 %convolution_bitcast_fusion = f32[64,64,192]{2,1,0:T(8,128)S(1)} fusion(bf16[2,64,64,16]{1,3,0,2:T(8,128)(2,1)} %copy.70, bf16[2,128,64,16]{1,3,0,2:T(8,128)(2,1)S(1)} %copy_select_fusion.1, bf16[2,64,64,16]{1,0,3,2:T(2,128)(2,1)S(1)} %concatenate.14), kind=kOutput, calls=%fused_computation.13 | convolution fusion | flops 51904512 | bytes 4194304 | tf_op jit(solution)/shard_map/sagc,swgc->gaw/dot_general | solution.py:88
  100.8 4.7 %fusion.28 = f32[64,128]{1,0:T(8,128)S(1)} fusion(s32[64]{0:T(128)S(1)} %iota_add_fusion, f32[64,64,192]{2,1,0:T(8,128)S(1)} %convolution_bitcast_fusion), kind=kOutput, calls=%fused_computation.26 | convolution fusion | flops 1211105280 | bytes 3178752 | tf_op jit(solution)/shard_map/gaw,jaw->gj/dot_general | solution.py:91
  105.5 0.5 collective-permute-start
  106.0 2.3 %fusion.16 = f32[2,64,64,16]{1,3,0,2:T(8,128)} fusion(bf16[64,64,192,1]{2,0,1,3:T(8,128)(2,1)S(1)} %copy-done.5, bf16[2,64,64,16]{1,3,0,2:T(8,128)(2,1)S(1)} %copy-done.1, bf16[2,128,64,16]{1,3,0,2:T(8,128)(2,1)S(1)} %copy_select_fusion.1), kind=kOutput, calls=%fused_computation.22 | convolution fusion | flops 52166656 | bytes 2883584 | tf_op jit(solution)/shard_map/gaw,swgc->sagc/dot_general | solution.py:82
  108.3 2.8 %gather_fusion.3 = bf16[4,64,1024]{2,1,0:T(8,128)(2,1)S(1)} fusion(bf16[32,64,1024]{2,1,0:T(8,128)(2,1)} %bitcast.44, s32[1024]{0:T(1024)S(1)} %pad_clamp_fusion), kind=kCustom, calls=%fused_computation.1.clone | custom fusion | bytes 1048592 | tf_op jit(solution)/shard_map/jit(_take)/gather | solution.py:59
  111.3 0.7 copy.73
  112.0 0.5 reshape.188
  112.6 0.2 collective-permute-start.1
  112.8 4.0 %fusion.25 = f32[2,64,64,16]{1,3,0,2:T(8,128)} fusion(bf16[64,64,192,1]{2,0,1,3:T(8,128)(2,1)} %convert_bitcast_fusion, bf16[2,128,64,16]{1,3,0,2:T(8,128)(2,1)S(1)} %copy_select_fusion, bf16[2,64,64,16]{1,3,0,2:T(8,128)(2,1)S(1)} %copy-done.3), kind=kOutput, calls=%fused_computation.25 | convolution fusion | flops 52166656 | bytes 2883584 | tf_op jit(solution)/shard_map/gau,sugc->sagc/dot_general | solution.py:84
  116.8 0.5 copy.72
  117.3 0.6 reshape.189
  118.0 2.4 %collective-permute-start.2 = (f32[64,128]{1,0:T(8,128)S(1)}, f32[64,128]{1,0:T(8,128)S(1)}, u32[]{:S(2)}, u32[]{:S(2)}) collective-permute-start(f32[64,128]{1,0:T(8,128)S(1)} %add.156), channel_id=1, source_target_pairs={{0,32},{8,40},{16,48},{24,56},{32,0},{40,8},{48,16},{56,24},{64,96... | collective-permute-start | bytes 98312 | tf_op jit(solution)/shard_map/ppermute | solution.py:18
  120.4 1.8 %copy.77 = f32[2,64,64,16]{1,0,3,2:T(2,128)S(1)} copy(f32[2,64,64,16]{1,3,0,2:T(8,128)} %fusion.25) | data formatting | bytes 1048576 | tf_op jit(solution)/shard_map/convert_element_type | solution.py:10
  122.2 0.6 reshape.190
  122.8 0.7 collective-permute-done.2
  123.5 0.4 collective-permute-start.3
  124.0 0.9 copy.80
  124.8 0.8 copy.81
  125.7 0.8 copy.82
  126.5 0.8 copy.83
  127.4 1.5 %collective-permute-done.3 = f32[64,128]{1,0:T(8,128)S(1)} collective-permute-done((f32[64,128]{1,0:T(8,128)S(1)}, f32[64,128]{1,0:T(8,128)S(1)}, u32[]{:S(2)}, u32[]{:S(2)}) %collective-permute-start.3) | collective-permute-done | bytes 32800 | tf_op jit(solution)/shard_map/ppermute | solution.py:18
  128.9 0.6 multiply_reduce_fusion
  129.5 0.7 collective-permute-start.4
  130.1 3.0 %collective-permute-done.4 = f32[]{:T(128)} collective-permute-done((f32[]{:T(128)}, f32[]{:T(128)}, u32[]{:S(2)}, u32[]{:S(2)}) %collective-permute-start.4) | collective-permute-done | bytes 36 | tf_op jit(solution)/shard_map/ppermute | solution.py:18
  134.5 2.8 %collective-permute-start.5 = (f32[]{:T(128)}, f32[]{:T(128)}, u32[]{:S(2)}, u32[]{:S(2)}) collective-permute-start(f32[]{:T(128)} %add.159), channel_id=1, source_target_pairs={{0,2},{1,3},{2,0},{3,1},{4,6},{5,7},{6,4},{7,5},{8,10},{9,11},{10,... | collective-permute-start | bytes 20 | tf_op jit(solution)/shard_map/ppermute | solution.py:18
  137.3 0.8 collective-permute-done.5
  138.8 4.4 %collective-permute-start.6 = (f32[]{:T(128)}, f32[]{:T(128)}, u32[]{:S(2)}, u32[]{:S(2)}) collective-permute-start(f32[]{:T(128)} %add.160), channel_id=1, source_target_pairs={{0,4},{1,5},{2,6},{3,7},{4,0},{5,1},{6,2},{7,3},{8,12},{9,13},{10,... | collective-permute-start | bytes 20 | tf_op jit(solution)/shard_map/ppermute | solution.py:18
  143.1 0.7 collective-permute-done.6
  144.6 0.6 broadcast_multiply_fusion
  (48 shorter events, 1.7 us)
Async XLA Ops:
  7.2 10.9 %copy-start = (bf16[64,128]{1,0:T(8,128)(2,1)S(1)}, bf16[64,128]{1,0:T(8,128)(2,1)}, u32[]{:S(2)}) copy-start(bf16[64,128]{1,0:T(8,128)(2,1)} %param.12) | copy-start | bytes 49156
  7.2 6.4 %copy-start.4 = (s32[32]{0:T(128)S(1)}, s32[32]{0:T(128)}, u32[]{:S(2)}) copy-start(s32[32]{0:T(128)} %param.13) | copy-start | bytes 388
  7.2 81.4 %all-gather.3.cloned.1.call-start = ((), (), s32[]{:S(2)}) async-start(), calls=%async_computation | async-start | bytes 8912896 | tf_op jit(solution)/shard_map/all_gather | solution.py:46
  98.8 7.2 %copy-start.1 = (bf16[2,64,64,16]{1,3,0,2:T(8,128)(2,1)S(1)}, bf16[2,64,64,16]{1,3,0,2:T(8,128)(2,1)}, u32[]{:S(2)}) copy-start(bf16[2,64,64,16]{1,3,0,2:T(8,128)(2,1)} %copy.70) | copy-start | bytes 786436
  98.8 7.2 %copy-start.5 = (bf16[64,64,192,1]{2,0,1,3:T(8,128)(2,1)S(1)}, bf16[64,64,192,1]{2,0,1,3:T(8,128)(2,1)}, u32[]{:S(2)}) copy-start(bf16[64,64,192,1]{2,0,1,3:T(8,128)(2,1)} %convert_bitcast_fusion.1) | copy-start | bytes 4718596
  105.5 7.1 %collective-permute-start = (f32[64,128]{1,0:T(8,128)S(1)}, f32[64,128]{1,0:T(8,128)S(1)}, u32[]{:S(2)}, u32[]{:S(2)}) collective-permute-start(f32[64,128]{1,0:T(8,128)S(1)} %fusion.28), channel_id=1, source_target_pairs={{0,8},{8,0},{16,24},{24,16},{32,40},{40,32},{48,56},{56,48},{64,72... | collective-permute-start | bytes 98312 | tf_op jit(solution)/shard_map/ppermute | solution.py:18
  108.3 4.5 %copy-start.3 = (bf16[2,64,64,16]{1,3,0,2:T(8,128)(2,1)S(1)}, bf16[2,64,64,16]{1,3,0,2:T(8,128)(2,1)}, u32[]{:S(2)}) copy-start(bf16[2,64,64,16]{1,3,0,2:T(8,128)(2,1)} %copy.75) | copy-start | bytes 786436
  112.5 4.3 %copy-start.2 = (f32[2,64,64,16]{1,3,0,2:T(8,128)S(1)}, f32[2,64,64,16]{1,3,0,2:T(8,128)}, u32[]{:S(2)}) copy-start(f32[2,64,64,16]{1,3,0,2:T(8,128)} %fusion.16) | copy-start | bytes 1572868
  112.6 5.3 %collective-permute-start.1 = (f32[64,128]{1,0:T(8,128)S(1)}, f32[64,128]{1,0:T(8,128)S(1)}, u32[]{:S(2)}, u32[]{:S(2)}) collective-permute-start(f32[64,128]{1,0:T(8,128)S(1)} %add.155), channel_id=1, source_target_pairs={{0,16},{8,24},{16,0},{24,8},{32,48},{40,56},{48,32},{56,40},{64,80... | collective-permute-start | bytes 98312 | tf_op jit(solution)/shard_map/ppermute | solution.py:18
  118.0 5.5 %collective-permute-start.2 = (f32[64,128]{1,0:T(8,128)S(1)}, f32[64,128]{1,0:T(8,128)S(1)}, u32[]{:S(2)}, u32[]{:S(2)}) collective-permute-start(f32[64,128]{1,0:T(8,128)S(1)} %add.156), channel_id=1, source_target_pairs={{0,32},{8,40},{16,48},{24,56},{32,0},{40,8},{48,16},{56,24},{64,96... | collective-permute-start | bytes 98312 | tf_op jit(solution)/shard_map/ppermute | solution.py:18
  123.5 5.4 %collective-permute-start.3 = (f32[64,128]{1,0:T(8,128)S(1)}, f32[64,128]{1,0:T(8,128)S(1)}, u32[]{:S(2)}, u32[]{:S(2)}) collective-permute-start(f32[64,128]{1,0:T(8,128)S(1)} %add.157), channel_id=1, source_target_pairs={{0,64},{8,72},{16,80},{24,88},{32,96},{40,104},{48,112},{56,120},{... | collective-permute-start | bytes 98312 | tf_op jit(solution)/shard_map/ppermute | solution.py:18
  129.5 3.7 %collective-permute-start.4 = (f32[]{:T(128)}, f32[]{:T(128)}, u32[]{:S(2)}, u32[]{:S(2)}) collective-permute-start(f32[]{:T(128)} %get-tuple-element.21), channel_id=1, source_target_pairs={{0,1},{1,0},{2,3},{3,2},{4,5},{5,4},{6,7},{7,6},{8,9},{9,8},{10,11... | collective-permute-start | bytes 20 | tf_op jit(solution)/shard_map/ppermute | solution.py:18
  134.5 3.6 %collective-permute-start.5 = (f32[]{:T(128)}, f32[]{:T(128)}, u32[]{:S(2)}, u32[]{:S(2)}) collective-permute-start(f32[]{:T(128)} %add.159), channel_id=1, source_target_pairs={{0,2},{1,3},{2,0},{3,1},{4,6},{5,7},{6,4},{7,5},{8,10},{9,11},{10,... | collective-permute-start | bytes 20 | tf_op jit(solution)/shard_map/ppermute | solution.py:18
  138.8 5.1 %collective-permute-start.6 = (f32[]{:T(128)}, f32[]{:T(128)}, u32[]{:S(2)}, u32[]{:S(2)}) collective-permute-start(f32[]{:T(128)} %add.160), channel_id=1, source_target_pairs={{0,4},{1,5},{2,6},{3,7},{4,0},{5,1},{6,2},{7,3},{8,12},{9,13},{10,... | collective-permute-start | bytes 20 | tf_op jit(solution)/shard_map/ppermute | solution.py:18
Sparse Core Ops, SparseCore 0:
  13.2 75.3 all-gather.2

commit v6 on v5

--- a/solution.py
+++ b/solution.py
@@ -44,8 +44,7 @@
     mixed = times_rounded(key_rows, value_rows)
     gated = times_rounded(grad_rows, query_rows)
     gathered = lax.all_gather(jnp.stack([mixed, gated]), "seq", axis=0, tiled=False)
-    mixed_blocks = gathered[:, 0].reshape(spans, span_rows, channels)
-    gated_blocks = gathered[:, 1].reshape(spans, span_rows, channels)
+    blocks = gathered.reshape(devices * 2 * per_device, span_rows, channels)
 
     slot_of = jnp.zeros((spans,), jnp.int32).at[span_order].set(jnp.arange(spans, dtype=jnp.int32))
     mine = lax.dynamic_slice_in_dim(span_order, device * per_device, per_device)
@@ -53,19 +52,20 @@
     before = mine[:, None] - halo + step[None, :]
     after = mine[:, None] + 1 + step[None, :]
 
-    def pick(blocks, wanted):
+    def pick(which, wanted):
         valid = (wanted >= 0) & (wanted < spans)
         slots = slot_of[jnp.clip(wanted, 0, spans - 1)].reshape(-1)
+        slots = ((slots // per_device) * 2 + which) * per_device + slots % per_device
         taken = jnp.take(blocks, slots, axis=0).reshape(per_device, halo, span_rows, channels)
         return jnp.where(valid[:, :, None, None], taken, jnp.zeros_like(taken))
 
     own_mixed = mixed.reshape(per_device, span_rows, channels)
     own_gated = gated.reshape(per_device, span_rows, channels)
     mixed_window = jnp.concatenate(
-        [pick(mixed_blocks, before).reshape(per_device, lead, channels), own_mixed], axis=1
+        [pick(0, before).reshape(per_device, lead, channels), own_mixed], axis=1
     )
     gated_window = jnp.concatenate(
-        [own_gated, pick(gated_blocks, after).reshape(per_device, lead, channels)], axis=1
+        [own_gated, pick(1, after).reshape(per_device, lead, channels)], axis=1
     )
     mixed_window = mixed_window.reshape(per_device, window, groups, group_size)
     gated_window = gated_window.reshape(per_device, window, groups, group_size)

time: 153 us -> 153 us (level)
  other arithmetic: 2.32 us -> 5.21 us
  waiting for transfers between devices: 70.5 us -> 73.2 us
  matrix products: 19.6 us -> 17.1 us
  local copies, waits for them, and re-layouts: 31.1 us -> 28.7 us
    slice x1 -> x0, local copies, waits for them, and re-layouts: 6.06 us -> none  [shards(): gated_blocks = gathered[:, 1].reshape(spans, span_rows, channels)]
    gather x2, local copies, waits for them, and re-layouts: 5.59 us -> 8.73 us  [pick(): jnp.take(blocks, slots, axis=0)]
    ppermute x7, waiting for transfers between devices: 6.71 us -> 9.58 us  [butterfly_sum(): value = value + lax.ppermute(value, axis, pairs)]
    select_n x4 -> x2, other arithmetic: 0.24 us -> 2.08 us  [pick(): jnp.take(blocks, slots, axis=0)]
    dot_general x1, matrix products: 3.95 us -> 2.39 us  [shards(): jnp.einsum('gau,sugc->sagc', bwd_band, gated_window, preferred_element_ty...]
    unnamed x20 -> x22, local copies, waits for them, and re-layouts: 7.91 us -> 7.92 us
  transfers between devices with their start and end apart: 8 -> 8, of which waited for: 6 -> 8; matrix products, arithmetic and copies ran while one was open for 19% -> 13% of each run, Pallas kernels for 0% -> 0%
where the time goes in v6:
time: 153 us; the launch traced here: 152 us
  waiting for transfers between devices  73.2 us (48%)
  local copies, waits for them, and re-layouts  28.7 us (19%)
  matrix products  17.1 us (11%)
  between operations  16.7 us (11%)
  starting transfers between devices  11.1 us (7%)
  other arithmetic  5.21 us (3%)
    all_gather x1, waiting for transfers between devices, shards(): lax.all_gather(jnp.stack([mixed, gated]), 'seq', axis=0, tiled=False)  63.6 us
    ppermute x7, starting transfers between devices, butterfly_sum(): value = value + lax.ppermute(value, axis, pairs)  11.1 us
    ppermute x7, waiting for transfers between devices, butterfly_sum(): value = value + lax.ppermute(value, axis, pairs)  9.58 us
    gather x2, local copies, waits for them, and re-layouts, pick(): jnp.take(blocks, slots, axis=0)  8.73 us
    unnamed x22, local copies, waits for them, and re-layouts  7.92 us
    dot_general x1, matrix products, shards(): jnp.einsum('gaw,jaw->gj', corr, select_fwd.astype(jnp.float32), precision...  4.7 us
    dot_general x1, matrix products, shards(): jnp.einsum('gj,jaw->gaw', filters, select_fwd, preferred_element_type=jnp...  3.53 us
    dot_general x1, matrix products, shards(): jnp.einsum('gj,jau->gau', filters, _bwd_select(taps, span_rows, window),...  3.22 us
  transfers between devices with their start and end apart: 8, of which 8 were waited for; matrix products, arithmetic and copies ran while one was open for 13% of the time, Pallas kernels for 0%

profile of v6, /device:TPU:0, one launch (start us, length us, event | category | flops | bytes accessed | tf_op | source)
XLA Modules:
  0.0 152.1 jit_solution(12418135602895910702)
XLA Ops:
  7.2 1.1 copy.43
  8.4 1.1 copy.44
  9.5 1.1 copy.45
  10.6 1.1 copy.46
  12.0 1.0 copy.47
  13.3 0.2 concatenate.12
  14.3 0.7 scatter_custom_fusion
  15.0 0.6 gather_fusion
  15.6 0.6 gather_fusion.1
  16.2 0.9 copy.55
  17.2 0.9 copy.50
  18.1 3.2 %convert_bitcast_fusion = bf16[64,64,192,1]{2,0,1,3:T(8,128)(2,1)} fusion(bf16[64,128]{1,0:T(8,128)(2,1)S(1)} %copy-done), kind=kOutput, calls=%fused_computation.18 | convolution fusion | flops 205258752 | bytes 1589248 | tf_op jit(solution)/shard_map/gj,jau->gau/dot_general | solution.py:77
  21.4 3.5 %convert_bitcast_fusion.1 = bf16[64,64,192,1]{2,0,1,3:T(8,128)(2,1)} fusion(s32[64]{0:T(128)S(1)} %iota_add_fusion, bf16[64,128]{1,0:T(8,128)(2,1)S(1)} %copy-done), kind=kOutput, calls=%fused_computation.19 | convolution fusion | flops 205258752 | bytes 1589504 | tf_op jit(solution)/shard_map/gj,jaw->gaw/dot_general | solution.py:74
  24.9 63.6 %all-gather.3.cloned.1.call-done = bf16[32,128,1024]{2,1,0:T(8,128)(2,1)} async-done(((bf16[2,128,1024]{2,1,0:T(8,128)(2,1)}), bf16[32,128,1024]{2,1,0:T(8,128)(2,1)}) %all-gather.3.cloned.1.call-update) | async-done | bytes 8388624 | tf_op jit(solution)/shard_map/all_gather | solution.py:46
  88.5 4.0 %gather_fusion.3 = bf16[4,64,1024]{2,1,0:T(8,128)(2,1)S(1)} fusion(bf16[64,64,1024]{2,1,0:T(8,128)(2,1)} %bitcast.44, s32[1024]{0:T(1024)S(1)} %pad_clamp_fusion), kind=kCustom, calls=%fused_computation.1.clone | custom fusion | bytes 1048592 | tf_op jit(solution)/shard_map/jit(_take)/gather | solution.py:59
  92.5 4.8 %gather_fusion.2 = bf16[4,64,1024]{2,1,0:T(8,128)(2,1)} fusion(bf16[64,64,1024]{2,1,0:T(8,128)(2,1)} %bitcast.45, s32[1024]{0:T(1024)S(1)} %pad_clamp_fusion.2), kind=kCustom, calls=%fused_computation.clone | custom fusion | bytes 1048592 | tf_op jit(solution)/shard_map/jit(_take)/gather | solution.py:59
  97.4 0.7 copy.53
  98.1 0.5 reshape.192
  98.6 2.0 %broadcast_select_fusion.1 = bf16[4,64,1024]{2,1,0:T(8,128)(2,1)} fusion(bf16[4,64,1024]{2,1,0:T(8,128)(2,1)} %gather_fusion.2, pred[4]{0:T(512)(128)(4,1)S(1)} %get-tuple-element.20), kind=kLoop, calls=%fused_computation.47 | loop fusion | flops 262144 | bytes 1048580 | tf_op jit(solution)/shard_map/jit(_take)/select_n | solution.py:59
  100.6 1.6 %copy.48 = bf16[4,64,1024]{1,0,2:T(4,128)(2,1)S(1)} copy(bf16[4,64,1024]{2,1,0:T(8,128)(2,1)} %broadcast_select_fusion.1) | data formatting | bytes 1048576 | tf_op jit(solution)/shard_map/jit(_take)/select_n | solution.py:59
  102.2 1.3 reshape.190
  103.5 1.1 copy_select_fusion.1
  104.6 2.0 %convolution_bitcast_fusion = f32[64,64,192]{2,1,0:T(8,128)S(1)} fusion(bf16[2,64,64,16]{1,3,0,2:T(8,128)(2,1)} %copy.50, bf16[2,128,64,16]{1,3,0,2:T(8,128)(2,1)S(1)} %copy_select_fusion.1, bf16[2,64,64,16]{1,0,3,2:T(2,128)(2,1)S(1)} %concatenate.14), kind=kOutput, calls=%fused_computation.13 | convolution fusion | flops 51904512 | bytes 4194304 | tf_op jit(solution)/shard_map/sagc,swgc->gaw/dot_general | solution.py:88
  106.6 1.3 fusion.16
  107.9 4.7 %fusion.28 = f32[64,128]{1,0:T(8,128)S(1)} fusion(s32[64]{0:T(128)S(1)} %iota_add_fusion, f32[64,64,192]{2,1,0:T(8,128)S(1)} %convolution_bitcast_fusion), kind=kOutput, calls=%fused_computation.26 | convolution fusion | flops 1211105280 | bytes 3178752 | tf_op jit(solution)/shard_map/gaw,jaw->gj/dot_general | solution.py:91
  112.6 0.5 collective-permute-start
  113.2 0.9 collective-permute-done
  114.2 2.4 %fusion.25 = f32[2,64,64,16]{1,3,0,2:T(8,128)} fusion(bf16[64,64,192,1]{2,0,1,3:T(8,128)(2,1)S(1)} %copy-done.5, bf16[2,128,64,16]{1,3,0,2:T(8,128)(2,1)S(1)} %copy_select_fusion, bf16[2,64,64,16]{1,3,0,2:T(8,128)(2,1)S(1)} %copy-done.3), kind=kOutput, calls=%fused_computation.25 | convolution fusion | flops 52166656 | bytes 2883584 | tf_op jit(solution)/shard_map/gau,sugc->sagc/dot_general | solution.py:84
  116.6 0.5 copy.52
  117.2 0.6 reshape.193
  118.0 2.2 %collective-permute-start.2 = (f32[64,128]{1,0:T(8,128)S(1)}, f32[64,128]{1,0:T(8,128)S(1)}, u32[]{:S(2)}, u32[]{:S(2)}) collective-permute-start(f32[64,128]{1,0:T(8,128)S(1)} %add.182), channel_id=1, source_target_pairs={{0,32},{8,40},{16,48},{24,56},{32,0},{40,8},{48,16},{56,24},{64,96... | collective-permute-start | bytes 98312 | tf_op jit(solution)/shard_map/ppermute | solution.py:18
  120.3 0.5 copy.57
  120.8 0.6 reshape.194
  121.4 2.0 %collective-permute-done.2 = f32[64,128]{1,0:T(8,128)S(1)} collective-permute-done((f32[64,128]{1,0:T(8,128)S(1)}, f32[64,128]{1,0:T(8,128)S(1)}, u32[]{:S(2)}, u32[]{:S(2)}) %collective-permute-start.2) | collective-permute-done | bytes 32800 | tf_op jit(solution)/shard_map/ppermute | solution.py:18
  123.4 0.4 collective-permute-start.3
  123.9 0.9 copy.61
  124.7 0.8 copy.60
  125.6 0.8 copy.63
  126.4 0.8 copy.62
  127.3 1.5 %collective-permute-done.3 = f32[64,128]{1,0:T(8,128)S(1)} collective-permute-done((f32[64,128]{1,0:T(8,128)S(1)}, f32[64,128]{1,0:T(8,128)S(1)}, u32[]{:S(2)}, u32[]{:S(2)}) %collective-permute-start.3) | collective-permute-done | bytes 32800 | tf_op jit(solution)/shard_map/ppermute | solution.py:18
  128.8 0.6 multiply_reduce_fusion
  129.4 0.7 collective-permute-start.4
  130.1 3.2 %collective-permute-done.4 = f32[]{:T(128)} collective-permute-done((f32[]{:T(128)}, f32[]{:T(128)}, u32[]{:S(2)}, u32[]{:S(2)}) %collective-permute-start.4) | collective-permute-done | bytes 36 | tf_op jit(solution)/shard_map/ppermute | solution.py:18
  134.5 2.8 %collective-permute-start.5 = (f32[]{:T(128)}, f32[]{:T(128)}, u32[]{:S(2)}, u32[]{:S(2)}) collective-permute-start(f32[]{:T(128)} %add.185), channel_id=1, source_target_pairs={{0,2},{1,3},{2,0},{3,1},{4,6},{5,7},{6,4},{7,5},{8,10},{9,11},{10,... | collective-permute-start | bytes 20 | tf_op jit(solution)/shard_map/ppermute | solution.py:18
  137.3 0.9 collective-permute-done.5
  138.8 4.4 %collective-permute-start.6 = (f32[]{:T(128)}, f32[]{:T(128)}, u32[]{:S(2)}, u32[]{:S(2)}) collective-permute-start(f32[]{:T(128)} %add.186), channel_id=1, source_target_pairs={{0,4},{1,5},{2,6},{3,7},{4,0},{5,1},{6,2},{7,3},{8,12},{9,13},{10,... | collective-permute-start | bytes 20 | tf_op jit(solution)/shard_map/ppermute | solution.py:18
  143.1 0.9 collective-permute-done.6
  144.6 0.6 broadcast_multiply_fusion
  (47 shorter events, 2.1 us)
Async XLA Ops:
  7.2 11.0 %copy-start = (bf16[64,128]{1,0:T(8,128)(2,1)S(1)}, bf16[64,128]{1,0:T(8,128)(2,1)}, u32[]{:S(2)}) copy-start(bf16[64,128]{1,0:T(8,128)(2,1)} %param.12) | copy-start | bytes 49156
  7.2 81.4 %all-gather.3.cloned.1.call-start = ((), (), s32[]{:S(2)}) async-start(), calls=%async_computation | async-start | bytes 8912896 | tf_op jit(solution)/shard_map/all_gather | solution.py:46
  11.9 1.6 %copy-start.4 = (s32[32]{0:T(128)S(1)}, s32[32]{0:T(128)}, u32[]{:S(2)}) copy-start(s32[32]{0:T(128)} %param.13) | copy-start | bytes 388
  104.6 2.0 %copy-start.1 = (bf16[2,64,64,16]{1,3,0,2:T(8,128)(2,1)S(1)}, bf16[2,64,64,16]{1,3,0,2:T(8,128)(2,1)}, u32[]{:S(2)}) copy-start(bf16[2,64,64,16]{1,3,0,2:T(8,128)(2,1)} %copy.50) | copy-start | bytes 786436
  104.6 2.0 %copy-start.6 = (bf16[64,64,192,1]{2,0,1,3:T(8,128)(2,1)S(1)}, bf16[64,64,192,1]{2,0,1,3:T(8,128)(2,1)}, u32[]{:S(2)}) copy-start(bf16[64,64,192,1]{2,0,1,3:T(8,128)(2,1)} %convert_bitcast_fusion.1) | copy-start | bytes 4718596
  107.9 6.4 %copy-start.3 = (bf16[2,64,64,16]{1,3,0,2:T(8,128)(2,1)S(1)}, bf16[2,64,64,16]{1,3,0,2:T(8,128)(2,1)}, u32[]{:S(2)}) copy-start(bf16[2,64,64,16]{1,3,0,2:T(8,128)(2,1)} %copy.55) | copy-start | bytes 786436
  107.9 6.4 %copy-start.5 = (bf16[64,64,192,1]{2,0,1,3:T(8,128)(2,1)S(1)}, bf16[64,64,192,1]{2,0,1,3:T(8,128)(2,1)}, u32[]{:S(2)}) copy-start(bf16[64,64,192,1]{2,0,1,3:T(8,128)(2,1)} %convert_bitcast_fusion) | copy-start | bytes 4718596
  112.6 1.5 collective-permute-start
  114.1 3.9 %collective-permute-start.1 = (f32[64,128]{1,0:T(8,128)S(1)}, f32[64,128]{1,0:T(8,128)S(1)}, u32[]{:S(2)}, u32[]{:S(2)}) collective-permute-start(f32[64,128]{1,0:T(8,128)S(1)} %add.181), channel_id=1, source_target_pairs={{0,16},{8,24},{16,0},{24,8},{32,48},{40,56},{48,32},{56,40},{64,80... | collective-permute-start | bytes 98312 | tf_op jit(solution)/shard_map/ppermute | solution.py:18
  117.8 2.5 %copy-start.2 = (f32[2,64,64,16]{1,3,0,2:T(8,128)S(1)}, f32[2,64,64,16]{1,3,0,2:T(8,128)}, u32[]{:S(2)}) copy-start(f32[2,64,64,16]{1,3,0,2:T(8,128)} %fusion.25) | copy-start | bytes 1572868
  118.0 5.4 %collective-permute-start.2 = (f32[64,128]{1,0:T(8,128)S(1)}, f32[64,128]{1,0:T(8,128)S(1)}, u32[]{:S(2)}, u32[]{:S(2)}) collective-permute-start(f32[64,128]{1,0:T(8,128)S(1)} %add.182), channel_id=1, source_target_pairs={{0,32},{8,40},{16,48},{24,56},{32,0},{40,8},{48,16},{56,24},{64,96... | collective-permute-start | bytes 98312 | tf_op jit(solution)/shard_map/ppermute | solution.py:18
  123.4 5.4 %collective-permute-start.3 = (f32[64,128]{1,0:T(8,128)S(1)}, f32[64,128]{1,0:T(8,128)S(1)}, u32[]{:S(2)}, u32[]{:S(2)}) collective-permute-start(f32[64,128]{1,0:T(8,128)S(1)} %add.183), channel_id=1, source_target_pairs={{0,64},{8,72},{16,80},{24,88},{32,96},{40,104},{48,112},{56,120},{... | collective-permute-start | bytes 98312 | tf_op jit(solution)/shard_map/ppermute | solution.py:18
  129.4 3.8 %collective-permute-start.4 = (f32[]{:T(128)}, f32[]{:T(128)}, u32[]{:S(2)}, u32[]{:S(2)}) collective-permute-start(f32[]{:T(128)} %get-tuple-element.16), channel_id=1, source_target_pairs={{0,1},{1,0},{2,3},{3,2},{4,5},{5,4},{6,7},{7,6},{8,9},{9,8},{10,11... | collective-permute-start | bytes 20 | tf_op jit(solution)/shard_map/ppermute | solution.py:18
  134.5 3.8 %collective-permute-start.5 = (f32[]{:T(128)}, f32[]{:T(128)}, u32[]{:S(2)}, u32[]{:S(2)}) collective-permute-start(f32[]{:T(128)} %add.185), channel_id=1, source_target_pairs={{0,2},{1,3},{2,0},{3,1},{4,6},{5,7},{6,4},{7,5},{8,10},{9,11},{10,... | collective-permute-start | bytes 20 | tf_op jit(solution)/shard_map/ppermute | solution.py:18
  138.8 5.3 %collective-permute-start.6 = (f32[]{:T(128)}, f32[]{:T(128)}, u32[]{:S(2)}, u32[]{:S(2)}) collective-permute-start(f32[]{:T(128)} %add.186), channel_id=1, source_target_pairs={{0,4},{1,5},{2,6},{3,7},{4,0},{5,1},{6,2},{7,3},{8,12},{9,13},{10,... | collective-permute-start | bytes 20 | tf_op jit(solution)/shard_map/ppermute | solution.py:18
Sparse Core Ops, SparseCore 0:
  13.1 75.3 all-gather.2

commit v7 on v6

--- a/solution.py
+++ b/solution.py
@@ -12,11 +12,18 @@
 
 def butterfly_sum(value, axis):
     size = lax.axis_size(axis)
+
+    def swap(v, mask):
+        return lax.ppermute(v, axis, [(i, i ^ mask) for i in range(size)])
+
     bit = 1
     while bit < size:
-        pairs = [(i, i ^ bit) for i in range(size)]
-        value = value + lax.ppermute(value, axis, pairs)
-        bit *= 2
+        if bit * 4 <= size:
+            value = (value + swap(value, bit)) + (swap(value, 2 * bit) + swap(value, 3 * bit))
+            bit *= 4
+        else:
+            value = value + swap(value, bit)
+            bit *= 2
     return value
 
 

time: 153 us -> 150 us (0.980)
  waiting for transfers between devices: 73.2 us -> 66.9 us
  starting transfers between devices: 11.1 us -> 16.4 us
  other arithmetic: 5.21 us -> 2.34 us
  matrix products: 17.1 us -> 19.8 us
  local copies, waits for them, and re-layouts: 28.7 us -> 26.2 us
    ppermute x7 -> x10, waiting for transfers between devices: 9.58 us -> 3.2 us  [swap(): return lax.ppermute(v, axis, [(i, i ^ mask) for i in range(size)])]
    ppermute x7 -> x10, starting transfers between devices: 11.1 us -> 16.4 us  [swap(): return lax.ppermute(v, axis, [(i, i ^ mask) for i in range(size)])]
    dot_general x1, matrix products: 1.3 us -> 3.23 us  [shards(): jnp.einsum('gaw,swgc->sagc', fwd_band, mixed_window, preferred_element_ty...]
    select_n x2, other arithmetic: 2.08 us -> 0.23 us  [pick(): jnp.take(blocks, slots, axis=0)]
    unnamed x22 -> x14, local copies, waits for them, and re-layouts: 7.92 us -> 7.9 us
  transfers between devices with their start and end apart: 8 -> 11, of which waited for: 8 -> 3; matrix products, arithmetic and copies ran while one was open for 13% -> 20% of each run, Pallas kernels for 0% -> 0%
where the time goes in v7:
time: 150 us; the launch traced here: 149 us
  waiting for transfers between devices  66.9 us (45%)
  local copies, waits for them, and re-layouts  26.2 us (17%)
  matrix products  19.8 us (13%)
  between operations  17.6 us (12%)
  starting transfers between devices  16.4 us (11%)
  other arithmetic  2.34 us (2%)
    all_gather x1, waiting for transfers between devices, shards(): lax.all_gather(jnp.stack([mixed, gated]), 'seq', axis=0, tiled=False)  63.6 us
    ppermute x10, starting transfers between devices, swap(): return lax.ppermute(v, axis, [(i, i ^ mask) for i in range(size)])  16.4 us
    gather x2, local copies, waits for them, and re-layouts, pick(): jnp.take(blocks, slots, axis=0)  7.92 us
    unnamed x14, local copies, waits for them, and re-layouts  7.9 us
    dot_general x1, matrix products, shards(): jnp.einsum('gaw,jaw->gj', corr, select_fwd.astype(jnp.float32), precision...  4.69 us
    dot_general x1, matrix products, shards(): jnp.einsum('gj,jaw->gaw', filters, select_fwd, preferred_element_type=jnp...  3.54 us
    dot_general x1, matrix products, shards(): jnp.einsum('gaw,swgc->sagc', fwd_band, mixed_window, preferred_element_ty...  3.23 us
    dot_general x1, matrix products, shards(): jnp.einsum('gj,jau->gau', filters, _bwd_select(taps, span_rows, window),...  3.23 us
  transfers between devices with their start and end apart: 11, of which 3 were waited for; matrix products, arithmetic and copies ran while one was open for 20% of the time, Pallas kernels for 0%

profile of v7, /device:TPU:0, one launch (start us, length us, event | category | flops | bytes accessed | tf_op | source)
XLA Modules:
  0.0 149.3 jit_solution(6854829107349361860)
XLA Ops:
  7.2 1.1 copy.43
  8.4 1.1 copy.44
  9.5 1.1 copy.45
  10.6 1.1 copy.46
  12.0 1.0 copy.47
  13.0 0.2 concatenate.14
  13.3 0.2 concatenate.12
  14.3 0.7 scatter_custom_fusion
  15.0 0.6 gather_fusion
  15.6 0.6 gather_fusion.1
  16.3 0.9 copy.55
  17.2 0.9 copy.50
  18.1 3.2 %convert_bitcast_fusion = bf16[64,64,192,1]{2,0,1,3:T(8,128)(2,1)} fusion(bf16[64,128]{1,0:T(8,128)(2,1)S(1)} %copy-done), kind=kOutput, calls=%fused_computation.18 | convolution fusion | flops 205258752 | bytes 1589248 | tf_op jit(solution)/shard_map/gj,jau->gau/dot_general | solution.py:84
  21.4 3.5 %convert_bitcast_fusion.1 = bf16[64,64,192,1]{2,0,1,3:T(8,128)(2,1)} fusion(s32[64]{0:T(128)S(1)} %iota_add_fusion, bf16[64,128]{1,0:T(8,128)(2,1)S(1)} %copy-done), kind=kOutput, calls=%fused_computation.19 | convolution fusion | flops 205258752 | bytes 1589504 | tf_op jit(solution)/shard_map/gj,jaw->gaw/dot_general | solution.py:81
  24.9 63.6 %all-gather.3.cloned.1.call-done = bf16[32,128,1024]{2,1,0:T(8,128)(2,1)} async-done(((bf16[2,128,1024]{2,1,0:T(8,128)(2,1)}), bf16[32,128,1024]{2,1,0:T(8,128)(2,1)}) %all-gather.3.cloned.1.call-update) | async-done | bytes 8388624 | tf_op jit(solution)/shard_map/all_gather | solution.py:53
  88.5 4.0 %gather_fusion.2 = bf16[4,64,1024]{2,1,0:T(8,128)(2,1)S(1)} fusion(bf16[64,64,1024]{2,1,0:T(8,128)(2,1)} %bitcast.44, s32[1024]{0:T(1024)S(1)} %pad_clamp_fusion.2), kind=kCustom, calls=%fused_computation.clone | custom fusion | bytes 1048592 | tf_op jit(solution)/shard_map/jit(_take)/gather | solution.py:66
  92.5 0.1 broadcast_select_fusion.1
  92.6 0.7 copy.48
  93.3 0.5 reshape.190
  93.9 2.0 %convolution_bitcast_fusion = f32[64,64,192]{2,1,0:T(8,128)S(1)} fusion(bf16[2,64,64,16]{1,3,0,2:T(8,128)(2,1)} %copy.50, bf16[2,128,64,16]{1,3,0,2:T(8,128)(2,1)S(1)} %copy_select_fusion.1, bf16[2,64,64,16]{1,0,3,2:T(2,128)(2,1)S(1)} %concatenate.14), kind=kOutput, calls=%fused_computation.13 | convolution fusion | flops 51904512 | bytes 4194304 | tf_op jit(solution)/shard_map/sagc,swgc->gaw/dot_general | solution.py:95
  95.9 4.7 %fusion.28 = f32[64,128]{1,0:T(8,128)S(1)} fusion(s32[64]{0:T(128)S(1)} %iota_add_fusion, f32[64,64,192]{2,1,0:T(8,128)S(1)} %convolution_bitcast_fusion), kind=kOutput, calls=%fused_computation.26 | convolution fusion | flops 1211105280 | bytes 3178752 | tf_op jit(solution)/shard_map/gaw,jaw->gj/dot_general | solution.py:98
  100.7 1.9 %collective-permute-start.1 = (f32[64,128]{1,0:T(8,128)S(1)}, f32[64,128]{1,0:T(8,128)S(1)}, u32[]{:S(2)}, u32[]{:S(2)}) collective-permute-start(f32[64,128]{1,0:T(8,128)S(1)} %fusion.28), channel_id=1, source_target_pairs={{0,16},{8,24},{16,0},{24,8},{32,48},{40,56},{48,32},{56,40},{64,80... | collective-permute-start | bytes 98312 | tf_op jit(solution)/shard_map/ppermute | solution.py:17
  102.6 4.0 %gather_fusion.3 = bf16[4,64,1024]{2,1,0:T(8,128)(2,1)S(1)} fusion(bf16[64,64,1024]{2,1,0:T(8,128)(2,1)} %bitcast.45, s32[1024]{0:T(1024)S(1)} %pad_clamp_fusion), kind=kCustom, calls=%fused_computation.1.clone | custom fusion | bytes 1048592 | tf_op jit(solution)/shard_map/jit(_take)/gather | solution.py:66
  106.6 0.1 broadcast_select_fusion
  106.7 0.7 copy.53
  107.4 0.5 reshape.192
  107.9 3.2 %fusion.16 = f32[2,64,64,16]{1,3,0,2:T(8,128)S(1)} fusion(bf16[64,64,192,1]{2,0,1,3:T(8,128)(2,1)} %convert_bitcast_fusion.1, bf16[2,64,64,16]{1,3,0,2:T(8,128)(2,1)} %copy.50, bf16[2,128,64,16]{1,3,0,2:T(8,128)(2,1)} %copy-done.1), kind=kOutput, calls=%fused_computation.22 | convolution fusion | flops 52166656 | bytes 2883584 | tf_op jit(solution)/shard_map/gaw,swgc->sagc/dot_general | solution.py:89
  111.1 0.5 copy.52
  111.7 0.6 reshape.193
  112.3 3.1 %fusion.25 = f32[2,64,64,16]{1,3,0,2:T(8,128)S(1)} fusion(bf16[64,64,192,1]{2,0,1,3:T(8,128)(2,1)} %convert_bitcast_fusion, bf16[2,128,64,16]{1,3,0,2:T(8,128)(2,1)S(1)} %copy_select_fusion, bf16[2,64,64,16]{1,3,0,2:T(8,128)(2,1)} %copy.55), kind=kOutput, calls=%fused_computation.25 | convolution fusion | flops 52166656 | bytes 2883584 | tf_op jit(solution)/shard_map/gau,sugc->sagc/dot_general | solution.py:91
  115.5 0.1 fusion.39
  115.6 0.5 copy.57
  116.1 0.6 reshape.194
  116.8 1.3 collective-permute-start.5
  118.1 3.2 %collective-permute-start.4 = (f32[64,128]{1,0:T(8,128)S(1)}, f32[64,128]{1,0:T(8,128)S(1)}, u32[]{:S(2)}, u32[]{:S(2)}) collective-permute-start(f32[64,128]{1,0:T(8,128)S(1)} %add_add_fusion.1), channel_id=1, source_target_pairs={{0,64},{8,72},{16,80},{24,88},{32,96},{40,104},{48,112},{56,120},{... | collective-permute-start | bytes 98312 | tf_op jit(solution)/shard_map/ppermute | solution.py:17
  121.2 2.1 %collective-permute-start.3 = (f32[64,128]{1,0:T(8,128)S(1)}, f32[64,128]{1,0:T(8,128)S(1)}, u32[]{:S(2)}, u32[]{:S(2)}) collective-permute-start(f32[64,128]{1,0:T(8,128)S(1)} %add_add_fusion.1), channel_id=1, source_target_pairs={{0,32},{8,40},{16,48},{24,56},{32,0},{40,8},{48,16},{56,24},{64,96... | collective-permute-start | bytes 98312 | tf_op jit(solution)/shard_map/ppermute | solution.py:17
  123.5 0.9 copy.61
  124.3 0.8 copy.60
  125.2 0.8 copy.63
  126.0 0.8 copy.62
  126.9 0.6 multiply_reduce_fusion
  127.5 1.6 %collective-permute-start.8 = (f32[]{:T(128)}, f32[]{:T(128)}, u32[]{:S(2)}, u32[]{:S(2)}) collective-permute-start(f32[]{:T(128)} %get-tuple-element.16), channel_id=1, source_target_pairs={{0,3},{1,2},{2,1},{3,0},{4,7},{5,6},{6,5},{7,4},{8,11},{9,10},{10,... | collective-permute-start | bytes 20 | tf_op jit(solution)/shard_map/ppermute | solution.py:17
  129.1 0.6 collective-permute-start.7
  129.6 1.4 collective-permute-start.6
  131.0 2.4 %collective-permute-done.6 = f32[]{:T(128)} collective-permute-done((f32[]{:T(128)}, f32[]{:T(128)}, u32[]{:S(2)}, u32[]{:S(2)}) %collective-permute-start.6) | collective-permute-done | bytes 36 | tf_op jit(solution)/shard_map/ppermute | solution.py:17
  136.0 4.4 %collective-permute-start.9 = (f32[]{:T(128)}, f32[]{:T(128)}, u32[]{:S(2)}, u32[]{:S(2)}) collective-permute-start(f32[]{:T(128)} %add.198), channel_id=1, source_target_pairs={{0,4},{1,5},{2,6},{3,7},{4,0},{5,1},{6,2},{7,3},{8,12},{9,13},{10,... | collective-permute-start | bytes 20 | tf_op jit(solution)/shard_map/ppermute | solution.py:17
  140.3 0.7 collective-permute-done.9
  141.8 0.6 broadcast_multiply_fusion
  (43 shorter events, 1.4 us)
Async XLA Ops:
  7.2 11.0 %copy-start = (bf16[64,128]{1,0:T(8,128)(2,1)S(1)}, bf16[64,128]{1,0:T(8,128)(2,1)}, u32[]{:S(2)}) copy-start(bf16[64,128]{1,0:T(8,128)(2,1)} %param.12) | copy-start | bytes 49156
  7.2 81.4 %all-gather.3.cloned.1.call-start = ((), (), s32[]{:S(2)}) async-start(), calls=%async_computation | async-start | bytes 8912896 | tf_op jit(solution)/shard_map/all_gather | solution.py:53
  11.9 1.6 %copy-start.2 = (s32[32]{0:T(128)S(1)}, s32[32]{0:T(128)}, u32[]{:S(2)}) copy-start(s32[32]{0:T(128)} %param.13) | copy-start | bytes 388
  93.9 2.0 %copy-start.1 = (bf16[2,128,64,16]{1,3,0,2:T(8,128)(2,1)}, bf16[2,128,64,16]{1,3,0,2:T(8,128)(2,1)S(1)}, u32[]{:S(2)}) copy-start(bf16[2,128,64,16]{1,3,0,2:T(8,128)(2,1)S(1)} %copy_select_fusion.1) | copy-start | bytes 1572868
  100.6 16.1 %collective-permute-start.2 = (f32[64,128]{1,0:T(8,128)S(1)}, f32[64,128]{1,0:T(8,128)S(1)}, u32[]{:S(2)}, u32[]{:S(2)}) collective-permute-start(f32[64,128]{1,0:T(8,128)S(1)} %fusion.28), channel_id=1, source_target_pairs={{0,24},{8,16},{16,8},{24,0},{32,56},{40,48},{48,40},{56,32},{64,88... | collective-permute-start | bytes 98312 | tf_op jit(solution)/shard_map/ppermute | solution.py:17
  100.7 16.0 %collective-permute-start.1 = (f32[64,128]{1,0:T(8,128)S(1)}, f32[64,128]{1,0:T(8,128)S(1)}, u32[]{:S(2)}, u32[]{:S(2)}) collective-permute-start(f32[64,128]{1,0:T(8,128)S(1)} %fusion.28), channel_id=1, source_target_pairs={{0,16},{8,24},{16,0},{24,8},{32,48},{40,56},{48,32},{56,40},{64,80... | collective-permute-start | bytes 98312 | tf_op jit(solution)/shard_map/ppermute | solution.py:17
  102.6 14.2 %collective-permute-start = (f32[64,128]{1,0:T(8,128)S(1)}, f32[64,128]{1,0:T(8,128)S(1)}, u32[]{:S(2)}, u32[]{:S(2)}) collective-permute-start(f32[64,128]{1,0:T(8,128)S(1)} %fusion.28), channel_id=1, source_target_pairs={{0,8},{8,0},{16,24},{24,16},{32,40},{40,32},{48,56},{56,48},{64,72... | collective-permute-start | bytes 98312 | tf_op jit(solution)/shard_map/ppermute | solution.py:17
  116.8 10.1 %collective-permute-start.5 = (f32[64,128]{1,0:T(8,128)S(1)}, f32[64,128]{1,0:T(8,128)S(1)}, u32[]{:S(2)}, u32[]{:S(2)}) collective-permute-start(f32[64,128]{1,0:T(8,128)S(1)} %add_add_fusion.1), channel_id=1, source_target_pairs={{0,96},{8,104},{16,112},{24,120},{32,64},{40,72},{48,80},{56,88},{... | collective-permute-start | bytes 98312 | tf_op jit(solution)/shard_map/ppermute | solution.py:17
  118.1 8.8 %collective-permute-start.4 = (f32[64,128]{1,0:T(8,128)S(1)}, f32[64,128]{1,0:T(8,128)S(1)}, u32[]{:S(2)}, u32[]{:S(2)}) collective-permute-start(f32[64,128]{1,0:T(8,128)S(1)} %add_add_fusion.1), channel_id=1, source_target_pairs={{0,64},{8,72},{16,80},{24,88},{32,96},{40,104},{48,112},{56,120},{... | collective-permute-start | bytes 98312 | tf_op jit(solution)/shard_map/ppermute | solution.py:17
  121.2 5.6 %collective-permute-start.3 = (f32[64,128]{1,0:T(8,128)S(1)}, f32[64,128]{1,0:T(8,128)S(1)}, u32[]{:S(2)}, u32[]{:S(2)}) collective-permute-start(f32[64,128]{1,0:T(8,128)S(1)} %add_add_fusion.1), channel_id=1, source_target_pairs={{0,32},{8,40},{16,48},{24,56},{32,0},{40,8},{48,16},{56,24},{64,96... | collective-permute-start | bytes 98312 | tf_op jit(solution)/shard_map/ppermute | solution.py:17
  127.5 7.2 %collective-permute-start.8 = (f32[]{:T(128)}, f32[]{:T(128)}, u32[]{:S(2)}, u32[]{:S(2)}) collective-permute-start(f32[]{:T(128)} %get-tuple-element.16), channel_id=1, source_target_pairs={{0,3},{1,2},{2,1},{3,0},{4,7},{5,6},{6,5},{7,4},{8,11},{9,10},{10,... | collective-permute-start | bytes 20 | tf_op jit(solution)/shard_map/ppermute | solution.py:17
  129.1 5.7 %collective-permute-start.7 = (f32[]{:T(128)}, f32[]{:T(128)}, u32[]{:S(2)}, u32[]{:S(2)}) collective-permute-start(f32[]{:T(128)} %get-tuple-element.16), channel_id=1, source_target_pairs={{0,2},{1,3},{2,0},{3,1},{4,6},{5,7},{6,4},{7,5},{8,10},{9,11},{10,... | collective-permute-start | bytes 20 | tf_op jit(solution)/shard_map/ppermute | solution.py:17
  129.6 3.8 %collective-permute-start.6 = (f32[]{:T(128)}, f32[]{:T(128)}, u32[]{:S(2)}, u32[]{:S(2)}) collective-permute-start(f32[]{:T(128)} %get-tuple-element.16), channel_id=1, source_target_pairs={{0,1},{1,0},{2,3},{3,2},{4,5},{5,4},{6,7},{7,6},{8,9},{9,8},{10,11... | collective-permute-start | bytes 20 | tf_op jit(solution)/shard_map/ppermute | solution.py:17
  136.0 5.1 %collective-permute-start.9 = (f32[]{:T(128)}, f32[]{:T(128)}, u32[]{:S(2)}, u32[]{:S(2)}) collective-permute-start(f32[]{:T(128)} %add.198), channel_id=1, source_target_pairs={{0,4},{1,5},{2,6},{3,7},{4,0},{5,1},{6,2},{7,3},{8,12},{9,13},{10,... | collective-permute-start | bytes 20 | tf_op jit(solution)/shard_map/ppermute | solution.py:17
Sparse Core Ops, SparseCore 0:
  13.1 75.3 all-gather.2

commit v8 on v7

--- a/solution.py
+++ b/solution.py
@@ -66,16 +66,10 @@
         taken = jnp.take(blocks, slots, axis=0).reshape(per_device, halo, span_rows, channels)
         return jnp.where(valid[:, :, None, None], taken, jnp.zeros_like(taken))
 
-    own_mixed = mixed.reshape(per_device, span_rows, channels)
-    own_gated = gated.reshape(per_device, span_rows, channels)
-    mixed_window = jnp.concatenate(
-        [pick(0, before).reshape(per_device, lead, channels), own_mixed], axis=1
-    )
-    gated_window = jnp.concatenate(
-        [own_gated, pick(1, after).reshape(per_device, lead, channels)], axis=1
-    )
-    mixed_window = mixed_window.reshape(per_device, window, groups, group_size)
-    gated_window = gated_window.reshape(per_device, window, groups, group_size)
+    own_mixed = mixed.reshape(per_device, span_rows, groups, group_size)
+    own_gated = gated.reshape(per_device, span_rows, groups, group_size)
+    halo_mixed = pick(0, before).reshape(per_device, lead, groups, group_size)
+    halo_gated = pick(1, after).reshape(per_device, lead, groups, group_size)
 
     select_fwd = band_select(taps, span_rows, window, lead)
     fwd_band = jnp.einsum(
@@ -86,17 +80,24 @@
         preferred_element_type=jnp.float32,
     ).astype(jnp.bfloat16)
 
-    conv = jnp.einsum("gaw,swgc->sagc", fwd_band, mixed_window, preferred_element_type=jnp.float32)
+    def band_apply(band, source):
+        return jnp.einsum("gaw,swgc->sagc", band, source, preferred_element_type=jnp.float32)
+
+    conv = band_apply(fwd_band[:, :, lead:], own_mixed) + band_apply(fwd_band[:, :, :lead], halo_mixed)
     convolved = conv.reshape(rows, channels).astype(jnp.bfloat16)
-    adjoint = jnp.einsum("gau,sugc->sagc", bwd_band, gated_window, preferred_element_type=jnp.float32)
+    adjoint = band_apply(bwd_band[:, :, :span_rows], own_gated) + band_apply(
+        bwd_band[:, :, span_rows:], halo_gated
+    )
     dmixed = adjoint.reshape(rows, channels).astype(jnp.bfloat16)
 
-    own_gated_g = own_gated.reshape(per_device, span_rows, groups, group_size)
-    corr = jnp.einsum(
-        "sagc,swgc->gaw", own_gated_g, mixed_window, preferred_element_type=jnp.float32
-    )
-    partial_grad = jnp.einsum(
-        "gaw,jaw->gj", corr, select_fwd.astype(jnp.float32), precision=lax.Precision.HIGHEST
+    def lag_sums(source, select):
+        corr = jnp.einsum("sagc,swgc->gaw", own_gated, source, preferred_element_type=jnp.float32)
+        return jnp.einsum(
+            "gaw,jaw->gj", corr, select.astype(jnp.float32), precision=lax.Precision.HIGH
+        )
+
+    partial_grad = lag_sums(own_mixed, select_fwd[:, :, lead:]) + lag_sums(
+        halo_mixed, select_fwd[:, :, :lead]
     )
     total_grad = butterfly_sum(partial_grad, "seq")
     squares = butterfly_sum(jnp.sum(total_grad * total_grad), "chan")

time: 150 us -> 158 us (1.053)
  local copies, waits for them, and re-layouts: 26.2 us -> 38.2 us
  other arithmetic: 2.34 us -> 9.65 us
  waiting for transfers between devices: 66.9 us -> 60.2 us
  matrix products: 19.8 us -> 14.8 us
    all_gather x1, waiting for transfers between devices: 63.6 us -> 57 us  [shards(): lax.all_gather(jnp.stack([mixed, gated]), 'seq', axis=0, tiled=False)]
    reshape x2, local copies, waits for them, and re-layouts: 0.96 us -> 6.21 us  [pick(): jnp.take(blocks, slots, axis=0)]
    select_n x2, other arithmetic: 0.15 us -> 3.05 us  [pick(): return jnp.where(valid[:, :, None, None], taken, jnp.zeros_like(taken))]
    concatenate x4 -> x0, local copies, waits for them, and re-layouts: 2.28 us -> none  [the longest x2 1.16 us: shards(): jnp.concatenate([own_gated, pick(1, after).reshape(per_device, lead, chan...]
    dot_general x4 -> x8, matrix products: 13.1 us -> 10.8 us  [the longest x4 5.95 us: band_apply(): jnp.einsum('gaw,swgc->sagc', band, source, preferred_element_type=jnp.flo...]
    select_n x2, other arithmetic: 0.23 us -> 2.31 us  [pick(): jnp.take(blocks, slots, axis=0)]
    slice x0 -> x4, local copies, waits for them, and re-layouts: none -> 2.01 us  [the longest x1 1.19 us: shards(): fwd_band[:, :, :lead]]
    gather x2, local copies, waits for them, and re-layouts: 7.92 us -> 9.73 us  [pick(): jnp.take(blocks, slots, axis=0)]
  transfers between devices with their start and end apart: 11 -> 11, of which waited for: 3 -> 3; matrix products, arithmetic and copies ran while one was open for 20% -> 25% of each run, Pallas kernels for 0% -> 0%
where the time goes in v8:
time: 158 us; the launch traced here: 157 us
  waiting for transfers between devices  60.2 us (38%)
  local copies, waits for them, and re-layouts  38.2 us (24%)
  between operations  17.8 us (11%)
  starting transfers between devices  16.4 us (10%)
  matrix products  14.8 us (9%)
  other arithmetic  9.65 us (6%)
    all_gather x1, waiting for transfers between devices, shards(): lax.all_gather(jnp.stack([mixed, gated]), 'seq', axis=0, tiled=False)  57 us
    ppermute x10, starting transfers between devices, swap(): return lax.ppermute(v, axis, [(i, i ^ mask) for i in range(size)])  16.4 us
    gather x2, local copies, waits for them, and re-layouts, pick(): jnp.take(blocks, slots, axis=0)  9.73 us
    unnamed x30, local copies, waits for them, and re-layouts  9.6 us
    reshape x2, local copies, waits for them, and re-layouts, pick(): jnp.take(blocks, slots, axis=0)  6.21 us
    dot_general x4, matrix products, band_apply(): jnp.einsum('gaw,swgc->sagc', band, source, preferred_element_type=jnp.flo...  5.95 us
    dot_general x2, matrix products, lag_sums(): jnp.einsum('gaw,jaw->gj', corr, select.astype(jnp.float32), precision=lax...  3.88 us
    ppermute x10, waiting for transfers between devices, swap(): return lax.ppermute(v, axis, [(i, i ^ mask) for i in range(size)])  3.2 us
  transfers between devices with their start and end apart: 11, of which 3 were waited for; matrix products, arithmetic and copies ran while one was open for 25% of the time, Pallas kernels for 0%

profile of v8, /device:TPU:0, one launch (start us, length us, event | category | flops | bytes accessed | tf_op | source)
XLA Modules:
  0.0 157.1 jit_solution(18085739204166638943)
XLA Ops:
  7.2 1.1 copy.62
  8.4 1.2 copy.63
  9.6 1.1 copy.64
  10.7 1.2 copy.67
  12.2 1.0 copy.68
  14.0 0.7 broadcast_in_dim.46
  15.1 0.7 scatter_custom_fusion
  15.8 0.6 gather_fusion
  16.4 0.6 gather_fusion.1
  17.6 0.6 pad_clamp_fusion
  18.7 1.2 subtract_compare_fusion
  20.0 1.2 copy-done.1
  21.2 1.9 %fusion.18 = f32[64,128]{1,0:T(8,128)S(1)} fusion(pred[128,64,192]{0,2,1:T(32,128)(4,1)S(1)} %subtract_compare_fusion, f32[64,64,64]{2,1,0:T(8,128)S(1)} %convolution_bitcast_fusion.1), kind=kOutput, calls=%fused_computation.27 | convolution fusion | flops 201326592 | bytes 2654208 | tf_op jit(solution)/shard_map/gaw,jaw->gj/dot_general | solution.py:95
  23.0 2.2 %convert_bitcast_fusion.1 = bf16[64,64,192]{2,0,1:T(8,128)(2,1)S(1)} fusion(s32[64]{0:T(128)S(1)} %iota_add_fusion, bf16[64,128]{1,0:T(8,128)(2,1)S(1)} %copy-done), kind=kOutput, calls=%fused_computation.14 | convolution fusion | flops 205258752 | bytes 1589504 | tf_op jit(solution)/shard_map/gj,jaw->gaw/dot_general | solution.py:75
  25.2 1.2 slice_bitcast_fusion.2
  26.6 1.8 %convert_bitcast_fusion = bf16[64,64,192]{2,0,1:T(8,128)(2,1)S(1)} fusion(bf16[64,128]{1,0:T(8,128)(2,1)S(1)} %copy-done), kind=kOutput, calls=%fused_computation.13 | convolution fusion | flops 205258752 | bytes 1589248 | tf_op jit(solution)/shard_map/gj,jau->gau/dot_general | solution.py:78
  29.1 1.8 %fusion.32 = f32[64,2,16,64]{3,2,1,0:T(8,128)} fusion(bf16[64,64,64,1]{2,0,1,3:T(8,128)(2,1)S(1)} %slice_bitcast_fusion.3, bf16[2,64,64,16]{1,0,3,2:T(2,128)(2,1)S(1)} %reshape.182), kind=kOutput, calls=%fused_computation.37 | convolution fusion | flops 16777216 | bytes 1310720 | tf_op jit(solution)/shard_map/gaw,swgc->sagc/dot_general | solution.py:84
  30.9 0.8 fusion.29
  31.8 57.0 %all-gather.3.cloned.1.call-done = bf16[32,128,1024]{2,1,0:T(8,128)(2,1)} async-done(((bf16[2,128,1024]{2,1,0:T(8,128)(2,1)}), bf16[32,128,1024]{2,1,0:T(8,128)(2,1)}) %all-gather.3.cloned.1.call-update) | async-done | bytes 8388624 | tf_op jit(solution)/shard_map/all_gather | solution.py:53
  88.8 4.8 %gather_fusion.2 = bf16[4,64,1024]{2,1,0:T(8,128)(2,1)} fusion(bf16[64,64,1024]{2,1,0:T(8,128)(2,1)} %bitcast.55, s32[1024]{0:T(1024)S(1)} %pad_clamp_fusion.2), kind=kCustom, calls=%fused_computation.clone | custom fusion | bytes 1048592 | tf_op jit(solution)/shard_map/jit(_take)/gather | solution.py:66
  93.6 1.2 broadcast_select_fusion.3
  94.7 1.6 %copy.69 = bf16[4,64,1024]{1,0,2:T(4,128)(2,1)} copy(bf16[4,64,1024]{2,1,0:T(8,128)(2,1)S(1)} %broadcast_select_fusion.3) | data formatting | bytes 1048576 | tf_op jit(solution)/shard_map/jit(_take)/select_n | solution.py:66
  96.4 3.1 %reshape.185 = bf16[2,128,64,16]{1,0,3,2:T(2,128)(2,1)} reshape(bf16[4,64,1024]{1,0,2:T(4,128)(2,1)} %copy.69) | data formatting | bytes 1048576 | tf_op jit(solution)/shard_map/reshape | solution.py:66
  99.5 1.6 %broadcast_select_fusion.1 = bf16[2,128,64,16]{1,0,3,2:T(2,128)(2,1)S(1)} fusion(bf16[2,128,64,16]{1,0,3,2:T(2,128)(2,1)} %reshape.185, pred[2,128]{1,0:T(4,128)(4,1)S(1)} %broadcast_in_dim.42), kind=kLoop, calls=%fused_computation.40 | loop fusion | flops 262144 | bytes 1048832 | tf_op jit(solution)/shard_map/jit(_where)/select_n | solution.py:67
  101.6 2.0 %fusion.23 = f32[64,128]{1,0:T(8,128)S(1)} fusion(f32[64,128]{1,0:T(8,128)S(1)} %fusion.18, pred[128,64,192]{0,2,1:T(32,128)(4,1)S(1)} %copy-done.2, f32[64,64,128]{2,1,0:T(8,128)S(1)} %convolution_bitcast_fusion), kind=kOutput, calls=%fused_computation.28 | convolution fusion | flops 402661376 | bytes 3211264 | tf_op jit(solution)/shard_map/gaw,jaw->gj/dot_general | solution.py:95
  103.7 1.9 %collective-permute-start.1 = (f32[64,128]{1,0:T(8,128)S(1)}, f32[64,128]{1,0:T(8,128)S(1)}, u32[]{:S(2)}, u32[]{:S(2)}) collective-permute-start(f32[64,128]{1,0:T(8,128)S(1)} %fusion.23), channel_id=1, source_target_pairs={{0,16},{8,24},{16,0},{24,8},{32,48},{40,56},{48,32},{56,40},{64,80... | collective-permute-start | bytes 98312 | tf_op jit(solution)/shard_map/ppermute | solution.py:17
  105.5 5.0 %gather_fusion.3 = bf16[4,64,1024]{2,1,0:T(8,128)(2,1)} fusion(bf16[64,64,1024]{2,1,0:T(8,128)(2,1)} %bitcast.56, s32[1024]{0:T(1024)} %pad_clamp_fusion), kind=kCustom, calls=%fused_computation.1.clone | custom fusion | bytes 1048592 | tf_op jit(solution)/shard_map/jit(_take)/gather | solution.py:66
  110.5 1.2 broadcast_select_fusion.2
  111.6 1.4 copy.75
  113.1 3.1 %reshape.188 = bf16[2,128,64,16]{1,0,3,2:T(2,128)(2,1)} reshape(bf16[4,64,1024]{1,0,2:T(4,128)(2,1)} %copy.75) | data formatting | bytes 1048576 | tf_op jit(solution)/shard_map/reshape | solution.py:66
  116.2 2.4 %fusion.12 = f32[2,64,64,16]{1,3,0,2:T(8,128)S(1)} fusion(f32[64,2,16,64]{3,2,1,0:T(8,128)} %fusion.32, bf16[64,64,128,1]{2,0,1,3:T(8,128)(2,1)} %slice_bitcast_fusion.2, bf16[2,128,64,16]{1,0,3,2:T(2,128)(2,1)S(1)} %broadcast_select_fusion.1), kind=kOutput, calls=%fused_computation.25 | convolution fusion | flops 33947648 | bytes 2621440 | tf_op jit(solution)/shard_map/gaw,swgc->sagc/dot_general | solution.py:84
  119.1 1.4 reshape.189
  120.5 1.5 broadcast_select_fusion
  122.0 0.9 fusion.10
  124.5 1.3 collective-permute-start.5
  125.8 3.2 %collective-permute-start.4 = (f32[64,128]{1,0:T(8,128)S(1)}, f32[64,128]{1,0:T(8,128)S(1)}, u32[]{:S(2)}, u32[]{:S(2)}) collective-permute-start(f32[64,128]{1,0:T(8,128)S(1)} %add_add_fusion.1), channel_id=1, source_target_pairs={{0,64},{8,72},{16,80},{24,88},{32,96},{40,104},{48,112},{56,120},{... | collective-permute-start | bytes 98312 | tf_op jit(solution)/shard_map/ppermute | solution.py:17
  129.0 2.1 %collective-permute-start.3 = (f32[64,128]{1,0:T(8,128)S(1)}, f32[64,128]{1,0:T(8,128)S(1)}, u32[]{:S(2)}, u32[]{:S(2)}) collective-permute-start(f32[64,128]{1,0:T(8,128)S(1)} %add_add_fusion.1), channel_id=1, source_target_pairs={{0,32},{8,40},{16,48},{24,56},{32,0},{40,8},{48,16},{56,24},{64,96... | collective-permute-start | bytes 98312 | tf_op jit(solution)/shard_map/ppermute | solution.py:17
  131.2 0.9 copy.87
  132.0 0.8 copy.86
  132.9 0.8 copy.89
  133.7 0.8 copy.88
  134.6 0.6 multiply_reduce_fusion
  135.2 1.6 collective-permute-start.8
  137.3 1.4 collective-permute-start.6
  138.7 2.4 %collective-permute-done.6 = f32[]{:T(128)} collective-permute-done((f32[]{:T(128)}, f32[]{:T(128)}, u32[]{:S(2)}, u32[]{:S(2)}) %collective-permute-start.6) | collective-permute-done | bytes 36 | tf_op jit(solution)/shard_map/ppermute | solution.py:17
  143.8 4.4 %collective-permute-start.9 = (f32[]{:T(128)}, f32[]{:T(128)}, u32[]{:S(2)}, u32[]{:S(2)}) collective-permute-start(f32[]{:T(128)} %add.214), channel_id=1, source_target_pairs={{0,4},{1,5},{2,6},{3,7},{4,0},{5,1},{6,2},{7,3},{8,12},{9,13},{10,... | collective-permute-start | bytes 20 | tf_op jit(solution)/shard_map/ppermute | solution.py:17
  148.2 0.8 collective-permute-done.9
  149.6 0.6 broadcast_multiply_fusion
  (66 shorter events, 6.6 us)
Async XLA Ops:
  7.2 15.9 %copy-start = (bf16[64,128]{1,0:T(8,128)(2,1)S(1)}, bf16[64,128]{1,0:T(8,128)(2,1)}, u32[]{:S(2)}) copy-start(bf16[64,128]{1,0:T(8,128)(2,1)} %param.12) | copy-start | bytes 49156
  7.2 81.6 %all-gather.3.cloned.1.call-start = ((), (), s32[]{:S(2)}) async-start(), calls=%async_computation | async-start | bytes 8912896 | tf_op jit(solution)/shard_map/all_gather | solution.py:53
  8.4 3.8 %copy-start.5 = (bf16[128,1024]{0,1:T(8,128)(2,1)}, bf16[128,1024]{0,1:T(8,128)(2,1)S(1)}, u32[]{:S(2)}) copy-start(bf16[128,1024]{0,1:T(8,128)(2,1)S(1)} %copy.62) | copy-start | bytes 786436
  10.7 2.5 %copy-start.3 = (bf16[128,1024]{0,1:T(8,128)(2,1)}, bf16[128,1024]{0,1:T(8,128)(2,1)S(1)}, u32[]{:S(2)}) copy-start(bf16[128,1024]{0,1:T(8,128)(2,1)S(1)} %copy.64) | copy-start | bytes 786436
  11.9 1.3 copy-start.7
  12.1 1.7 %copy-start.10 = (s32[32]{0:T(128)S(1)}, s32[32]{0:T(128)}, u32[]{:S(2)}) copy-start(s32[32]{0:T(128)} %param.13) | copy-start | bytes 388
  20.0 1.2 copy-start.1
  99.5 2.1 %copy-start.2 = (pred[128,64,192]{0,2,1:T(32,128)(4,1)S(1)}, pred[128,64,192]{0,2,1:T(32,128)(4,1)}, u32[]{:S(2)}) copy-start(pred[128,64,192]{0,2,1:T(32,128)(4,1)} %copy-done.1) | copy-start | bytes 4718596
  103.6 20.9 %collective-permute-start.2 = (f32[64,128]{1,0:T(8,128)S(1)}, f32[64,128]{1,0:T(8,128)S(1)}, u32[]{:S(2)}, u32[]{:S(2)}) collective-permute-start(f32[64,128]{1,0:T(8,128)S(1)} %fusion.23), channel_id=1, source_target_pairs={{0,24},{8,16},{16,8},{24,0},{32,56},{40,48},{48,40},{56,32},{64,88... | collective-permute-start | bytes 98312 | tf_op jit(solution)/shard_map/ppermute | solution.py:17
  103.7 20.8 %collective-permute-start.1 = (f32[64,128]{1,0:T(8,128)S(1)}, f32[64,128]{1,0:T(8,128)S(1)}, u32[]{:S(2)}, u32[]{:S(2)}) collective-permute-start(f32[64,128]{1,0:T(8,128)S(1)} %fusion.23), channel_id=1, source_target_pairs={{0,16},{8,24},{16,0},{24,8},{32,48},{40,56},{48,32},{56,40},{64,80... | collective-permute-start | bytes 98312 | tf_op jit(solution)/shard_map/ppermute | solution.py:17
  105.5 19.0 %collective-permute-start = (f32[64,128]{1,0:T(8,128)S(1)}, f32[64,128]{1,0:T(8,128)S(1)}, u32[]{:S(2)}, u32[]{:S(2)}) collective-permute-start(f32[64,128]{1,0:T(8,128)S(1)} %fusion.23), channel_id=1, source_target_pairs={{0,8},{8,0},{16,24},{24,16},{32,40},{40,32},{48,56},{56,48},{64,72... | collective-permute-start | bytes 98312 | tf_op jit(solution)/shard_map/ppermute | solution.py:17
  122.0 1.0 copy-start.6
  122.0 1.0 copy-start.8
  122.0 1.2 copy-start.9
  123.3 7.8 %copy-start.4 = (bf16[128,1024]{0,1:T(8,128)(2,1)S(1)}, bf16[128,1024]{0,1:T(8,128)(2,1)}, u32[]{:S(2)}) copy-start(bf16[128,1024]{0,1:T(8,128)(2,1)} %copy-done.3) | copy-start | bytes 786436
  124.5 10.1 %collective-permute-start.5 = (f32[64,128]{1,0:T(8,128)S(1)}, f32[64,128]{1,0:T(8,128)S(1)}, u32[]{:S(2)}, u32[]{:S(2)}) collective-permute-start(f32[64,128]{1,0:T(8,128)S(1)} %add_add_fusion.1), channel_id=1, source_target_pairs={{0,96},{8,104},{16,112},{24,120},{32,64},{40,72},{48,80},{56,88},{... | collective-permute-start | bytes 98312 | tf_op jit(solution)/shard_map/ppermute | solution.py:17
  125.8 8.8 %collective-permute-start.4 = (f32[64,128]{1,0:T(8,128)S(1)}, f32[64,128]{1,0:T(8,128)S(1)}, u32[]{:S(2)}, u32[]{:S(2)}) collective-permute-start(f32[64,128]{1,0:T(8,128)S(1)} %add_add_fusion.1), channel_id=1, source_target_pairs={{0,64},{8,72},{16,80},{24,88},{32,96},{40,104},{48,112},{56,120},{... | collective-permute-start | bytes 98312 | tf_op jit(solution)/shard_map/ppermute | solution.py:17
  129.0 5.7 %collective-permute-start.3 = (f32[64,128]{1,0:T(8,128)S(1)}, f32[64,128]{1,0:T(8,128)S(1)}, u32[]{:S(2)}, u32[]{:S(2)}) collective-permute-start(f32[64,128]{1,0:T(8,128)S(1)} %add_add_fusion.1), channel_id=1, source_target_pairs={{0,32},{8,40},{16,48},{24,56},{32,0},{40,8},{48,16},{56,24},{64,96... | collective-permute-start | bytes 98312 | tf_op jit(solution)/shard_map/ppermute | solution.py:17
  135.2 7.2 %collective-permute-start.8 = (f32[]{:T(128)}, f32[]{:T(128)}, u32[]{:S(2)}, u32[]{:S(2)}) collective-permute-start(f32[]{:T(128)} %get-tuple-element.16), channel_id=1, source_target_pairs={{0,3},{1,2},{2,1},{3,0},{4,7},{5,6},{6,5},{7,4},{8,11},{9,10},{10,... | collective-permute-start | bytes 20 | tf_op jit(solution)/shard_map/ppermute | solution.py:17
  136.8 5.7 %collective-permute-start.7 = (f32[]{:T(128)}, f32[]{:T(128)}, u32[]{:S(2)}, u32[]{:S(2)}) collective-permute-start(f32[]{:T(128)} %get-tuple-element.16), channel_id=1, source_target_pairs={{0,2},{1,3},{2,0},{3,1},{4,6},{5,7},{6,4},{7,5},{8,10},{9,11},{10,... | collective-permute-start | bytes 20 | tf_op jit(solution)/shard_map/ppermute | solution.py:17
  137.3 3.8 %collective-permute-start.6 = (f32[]{:T(128)}, f32[]{:T(128)}, u32[]{:S(2)}, u32[]{:S(2)}) collective-permute-start(f32[]{:T(128)} %get-tuple-element.16), channel_id=1, source_target_pairs={{0,1},{1,0},{2,3},{3,2},{4,5},{5,4},{6,7},{7,6},{8,9},{9,8},{10,11... | collective-permute-start | bytes 20 | tf_op jit(solution)/shard_map/ppermute | solution.py:17
  143.8 5.1 %collective-permute-start.9 = (f32[]{:T(128)}, f32[]{:T(128)}, u32[]{:S(2)}, u32[]{:S(2)}) collective-permute-start(f32[]{:T(128)} %add.214), channel_id=1, source_target_pairs={{0,4},{1,5},{2,6},{3,7},{4,0},{5,1},{6,2},{7,3},{8,12},{9,13},{10,... | collective-permute-start | bytes 20 | tf_op jit(solution)/shard_map/ppermute | solution.py:17
Sparse Core Ops, SparseCore 0:
  13.4 75.3 all-gather.2

commit v9 on v7

--- a/solution.py
+++ b/solution.py
@@ -96,7 +96,7 @@
         "sagc,swgc->gaw", own_gated_g, mixed_window, preferred_element_type=jnp.float32
     )
     partial_grad = jnp.einsum(
-        "gaw,jaw->gj", corr, select_fwd.astype(jnp.float32), precision=lax.Precision.HIGHEST
+        "gaw,jaw->gj", corr, select_fwd.astype(jnp.float32), precision=lax.Precision.HIGH
     )
     total_grad = butterfly_sum(partial_grad, "seq")
     squares = butterfly_sum(jnp.sum(total_grad * total_grad), "chan")

time: 150 us -> 149 us (level)
  no operation moved by 1% of the time
where the time goes in v9:
time: 149 us
  waiting for transfers between devices  66.9 us (45%)
  local copies, waits for them, and re-layouts  26.2 us (18%)
  matrix products  19.1 us (13%)
  between operations  17.6 us (12%)
  starting transfers between devices  16.4 us (11%)
  other arithmetic  2.34 us (2%)
    all_gather x1, waiting for transfers between devices, shards(): lax.all_gather(jnp.stack([mixed, gated]), 'seq', axis=0, tiled=False)  63.6 us
    ppermute x10, starting transfers between devices, swap(): return lax.ppermute(v, axis, [(i, i ^ mask) for i in range(size)])  16.4 us
    gather x2, local copies, waits for them, and re-layouts, pick(): jnp.take(blocks, slots, axis=0)  7.92 us
    unnamed x14, local copies, waits for them, and re-layouts  7.9 us
    dot_general x1, matrix products, shards(): jnp.einsum('gaw,jaw->gj', corr, select_fwd.astype(jnp.float32), precision...  3.92 us
    dot_general x1, matrix products, shards(): jnp.einsum('gj,jaw->gaw', filters, select_fwd, preferred_element_type=jnp...  3.54 us
    dot_general x1, matrix products, shards(): jnp.einsum('gaw,swgc->sagc', fwd_band, mixed_window, preferred_element_ty...  3.23 us
    dot_general x1, matrix products, shards(): jnp.einsum('gj,jau->gau', filters, _bwd_select(taps, span_rows, window),...  3.23 us
  transfers between devices with their start and end apart: 11, of which 3 were waited for; matrix products, arithmetic and copies ran while one was open for 20% of the time, Pallas kernels for 0%

profile of v9, /device:TPU:0, one launch (start us, length us, event | category | flops | bytes accessed | tf_op | source)
XLA Modules:
  0.0 148.5 jit_solution(17575460117184730370)
XLA Ops:
  7.2 1.1 copy.43
  8.4 1.1 copy.44
  9.5 1.1 copy.45
  10.6 1.1 copy.46
  12.0 1.0 copy.47
  13.0 0.2 concatenate.14
  13.3 0.2 concatenate.12
  14.3 0.7 scatter_custom_fusion
  15.0 0.6 gather_fusion
  15.6 0.6 gather_fusion.1
  16.3 0.9 copy.55
  17.2 0.9 copy.50
  18.1 3.2 %convert_bitcast_fusion = bf16[64,64,192,1]{2,0,1,3:T(8,128)(2,1)} fusion(bf16[64,128]{1,0:T(8,128)(2,1)S(1)} %copy-done), kind=kOutput, calls=%fused_computation.18 | convolution fusion | flops 205258752 | bytes 1589248 | tf_op jit(solution)/shard_map/gj,jau->gau/dot_general | solution.py:84
  21.4 3.5 %convert_bitcast_fusion.1 = bf16[64,64,192,1]{2,0,1,3:T(8,128)(2,1)} fusion(s32[64]{0:T(128)S(1)} %iota_add_fusion, bf16[64,128]{1,0:T(8,128)(2,1)S(1)} %copy-done), kind=kOutput, calls=%fused_computation.19 | convolution fusion | flops 205258752 | bytes 1589504 | tf_op jit(solution)/shard_map/gj,jaw->gaw/dot_general | solution.py:81
  24.9 63.6 %all-gather.3.cloned.1.call-done = bf16[32,128,1024]{2,1,0:T(8,128)(2,1)} async-done(((bf16[2,128,1024]{2,1,0:T(8,128)(2,1)}), bf16[32,128,1024]{2,1,0:T(8,128)(2,1)}) %all-gather.3.cloned.1.call-update) | async-done | bytes 8388624 | tf_op jit(solution)/shard_map/all_gather | solution.py:53
  88.5 4.0 %gather_fusion.2 = bf16[4,64,1024]{2,1,0:T(8,128)(2,1)S(1)} fusion(bf16[64,64,1024]{2,1,0:T(8,128)(2,1)} %bitcast.44, s32[1024]{0:T(1024)S(1)} %pad_clamp_fusion.2), kind=kCustom, calls=%fused_computation.clone | custom fusion | bytes 1048592 | tf_op jit(solution)/shard_map/jit(_take)/gather | solution.py:66
  92.5 0.1 broadcast_select_fusion.1
  92.6 0.7 copy.48
  93.3 0.5 reshape.190
  93.9 2.0 %convolution_bitcast_fusion = f32[64,64,192]{2,1,0:T(8,128)S(1)} fusion(bf16[2,64,64,16]{1,3,0,2:T(8,128)(2,1)} %copy.50, bf16[2,128,64,16]{1,3,0,2:T(8,128)(2,1)S(1)} %copy_select_fusion.1, bf16[2,64,64,16]{1,0,3,2:T(2,128)(2,1)S(1)} %concatenate.14), kind=kOutput, calls=%fused_computation.13 | convolution fusion | flops 51904512 | bytes 4194304 | tf_op jit(solution)/shard_map/sagc,swgc->gaw/dot_general | solution.py:95
  95.9 3.9 %fusion.28 = f32[64,128]{1,0:T(8,128)S(1)} fusion(s32[64]{0:T(128)S(1)} %iota_add_fusion, f32[64,64,192]{2,1,0:T(8,128)S(1)} %convolution_bitcast_fusion), kind=kOutput, calls=%fused_computation.26 | convolution fusion | flops 607125504 | bytes 3178752 | tf_op jit(solution)/shard_map/gaw,jaw->gj/dot_general | solution.py:98
  100.0 1.9 %collective-permute-start.1 = (f32[64,128]{1,0:T(8,128)S(1)}, f32[64,128]{1,0:T(8,128)S(1)}, u32[]{:S(2)}, u32[]{:S(2)}) collective-permute-start(f32[64,128]{1,0:T(8,128)S(1)} %fusion.28), channel_id=1, source_target_pairs={{0,16},{8,24},{16,0},{24,8},{32,48},{40,56},{48,32},{56,40},{64,80... | collective-permute-start | bytes 98312 | tf_op jit(solution)/shard_map/ppermute | solution.py:17
  101.8 4.0 %gather_fusion.3 = bf16[4,64,1024]{2,1,0:T(8,128)(2,1)S(1)} fusion(bf16[64,64,1024]{2,1,0:T(8,128)(2,1)} %bitcast.45, s32[1024]{0:T(1024)S(1)} %pad_clamp_fusion), kind=kCustom, calls=%fused_computation.1.clone | custom fusion | bytes 1048592 | tf_op jit(solution)/shard_map/jit(_take)/gather | solution.py:66
  105.8 0.1 broadcast_select_fusion
  105.9 0.7 copy.53
  106.6 0.5 reshape.192
  107.1 3.2 %fusion.16 = f32[2,64,64,16]{1,3,0,2:T(8,128)S(1)} fusion(bf16[64,64,192,1]{2,0,1,3:T(8,128)(2,1)} %convert_bitcast_fusion.1, bf16[2,64,64,16]{1,3,0,2:T(8,128)(2,1)} %copy.50, bf16[2,128,64,16]{1,3,0,2:T(8,128)(2,1)} %copy-done.1), kind=kOutput, calls=%fused_computation.22 | convolution fusion | flops 52166656 | bytes 2883584 | tf_op jit(solution)/shard_map/gaw,swgc->sagc/dot_general | solution.py:89
  110.3 0.5 copy.52
  110.9 0.6 reshape.193
  111.6 3.1 %fusion.25 = f32[2,64,64,16]{1,3,0,2:T(8,128)S(1)} fusion(bf16[64,64,192,1]{2,0,1,3:T(8,128)(2,1)} %convert_bitcast_fusion, bf16[2,128,64,16]{1,3,0,2:T(8,128)(2,1)S(1)} %copy_select_fusion, bf16[2,64,64,16]{1,3,0,2:T(8,128)(2,1)} %copy.55), kind=kOutput, calls=%fused_computation.25 | convolution fusion | flops 52166656 | bytes 2883584 | tf_op jit(solution)/shard_map/gau,sugc->sagc/dot_general | solution.py:91
  114.7 0.1 fusion.39
  114.8 0.5 copy.57
  115.4 0.6 reshape.194
  116.0 1.3 collective-permute-start.5
  117.3 3.1 %collective-permute-start.4 = (f32[64,128]{1,0:T(8,128)S(1)}, f32[64,128]{1,0:T(8,128)S(1)}, u32[]{:S(2)}, u32[]{:S(2)}) collective-permute-start(f32[64,128]{1,0:T(8,128)S(1)} %add_add_fusion.1), channel_id=1, source_target_pairs={{0,64},{8,72},{16,80},{24,88},{32,96},{40,104},{48,112},{56,120},{... | collective-permute-start | bytes 98312 | tf_op jit(solution)/shard_map/ppermute | solution.py:17
  120.5 2.1 %collective-permute-start.3 = (f32[64,128]{1,0:T(8,128)S(1)}, f32[64,128]{1,0:T(8,128)S(1)}, u32[]{:S(2)}, u32[]{:S(2)}) collective-permute-start(f32[64,128]{1,0:T(8,128)S(1)} %add_add_fusion.1), channel_id=1, source_target_pairs={{0,32},{8,40},{16,48},{24,56},{32,0},{40,8},{48,16},{56,24},{64,96... | collective-permute-start | bytes 98312 | tf_op jit(solution)/shard_map/ppermute | solution.py:17
  122.7 0.9 copy.61
  123.5 0.8 copy.60
  124.4 0.8 copy.63
  125.2 0.8 copy.62
  126.1 0.6 multiply_reduce_fusion
  126.7 1.6 %collective-permute-start.8 = (f32[]{:T(128)}, f32[]{:T(128)}, u32[]{:S(2)}, u32[]{:S(2)}) collective-permute-start(f32[]{:T(128)} %get-tuple-element.16), channel_id=1, source_target_pairs={{0,3},{1,2},{2,1},{3,0},{4,7},{5,6},{6,5},{7,4},{8,11},{9,10},{10,... | collective-permute-start | bytes 20 | tf_op jit(solution)/shard_map/ppermute | solution.py:17
  128.3 0.6 collective-permute-start.7
  128.8 1.4 collective-permute-start.6
  130.2 2.4 %collective-permute-done.6 = f32[]{:T(128)} collective-permute-done((f32[]{:T(128)}, f32[]{:T(128)}, u32[]{:S(2)}, u32[]{:S(2)}) %collective-permute-start.6) | collective-permute-done | bytes 36 | tf_op jit(solution)/shard_map/ppermute | solution.py:17
  135.2 4.4 %collective-permute-start.9 = (f32[]{:T(128)}, f32[]{:T(128)}, u32[]{:S(2)}, u32[]{:S(2)}) collective-permute-start(f32[]{:T(128)} %add.198), channel_id=1, source_target_pairs={{0,4},{1,5},{2,6},{3,7},{4,0},{5,1},{6,2},{7,3},{8,12},{9,13},{10,... | collective-permute-start | bytes 20 | tf_op jit(solution)/shard_map/ppermute | solution.py:17
  139.5 0.7 collective-permute-done.9
  141.0 0.6 broadcast_multiply_fusion
  (43 shorter events, 1.4 us)
Async XLA Ops:
  7.2 11.0 %copy-start = (bf16[64,128]{1,0:T(8,128)(2,1)S(1)}, bf16[64,128]{1,0:T(8,128)(2,1)}, u32[]{:S(2)}) copy-start(bf16[64,128]{1,0:T(8,128)(2,1)} %param.12) | copy-start | bytes 49156
  7.2 81.4 %all-gather.3.cloned.1.call-start = ((), (), s32[]{:S(2)}) async-start(), calls=%async_computation | async-start | bytes 8912896 | tf_op jit(solution)/shard_map/all_gather | solution.py:53
  11.9 1.6 %copy-start.2 = (s32[32]{0:T(128)S(1)}, s32[32]{0:T(128)}, u32[]{:S(2)}) copy-start(s32[32]{0:T(128)} %param.13) | copy-start | bytes 388
  93.9 2.0 %copy-start.1 = (bf16[2,128,64,16]{1,3,0,2:T(8,128)(2,1)}, bf16[2,128,64,16]{1,3,0,2:T(8,128)(2,1)S(1)}, u32[]{:S(2)}) copy-start(bf16[2,128,64,16]{1,3,0,2:T(8,128)(2,1)S(1)} %copy_select_fusion.1) | copy-start | bytes 1572868
  99.9 16.1 %collective-permute-start.2 = (f32[64,128]{1,0:T(8,128)S(1)}, f32[64,128]{1,0:T(8,128)S(1)}, u32[]{:S(2)}, u32[]{:S(2)}) collective-permute-start(f32[64,128]{1,0:T(8,128)S(1)} %fusion.28), channel_id=1, source_target_pairs={{0,24},{8,16},{16,8},{24,0},{32,56},{40,48},{48,40},{56,32},{64,88... | collective-permute-start | bytes 98312 | tf_op jit(solution)/shard_map/ppermute | solution.py:17
  100.0 16.0 %collective-permute-start.1 = (f32[64,128]{1,0:T(8,128)S(1)}, f32[64,128]{1,0:T(8,128)S(1)}, u32[]{:S(2)}, u32[]{:S(2)}) collective-permute-start(f32[64,128]{1,0:T(8,128)S(1)} %fusion.28), channel_id=1, source_target_pairs={{0,16},{8,24},{16,0},{24,8},{32,48},{40,56},{48,32},{56,40},{64,80... | collective-permute-start | bytes 98312 | tf_op jit(solution)/shard_map/ppermute | solution.py:17
  101.8 14.2 %collective-permute-start = (f32[64,128]{1,0:T(8,128)S(1)}, f32[64,128]{1,0:T(8,128)S(1)}, u32[]{:S(2)}, u32[]{:S(2)}) collective-permute-start(f32[64,128]{1,0:T(8,128)S(1)} %fusion.28), channel_id=1, source_target_pairs={{0,8},{8,0},{16,24},{24,16},{32,40},{40,32},{48,56},{56,48},{64,72... | collective-permute-start | bytes 98312 | tf_op jit(solution)/shard_map/ppermute | solution.py:17
  116.0 10.1 %collective-permute-start.5 = (f32[64,128]{1,0:T(8,128)S(1)}, f32[64,128]{1,0:T(8,128)S(1)}, u32[]{:S(2)}, u32[]{:S(2)}) collective-permute-start(f32[64,128]{1,0:T(8,128)S(1)} %add_add_fusion.1), channel_id=1, source_target_pairs={{0,96},{8,104},{16,112},{24,120},{32,64},{40,72},{48,80},{56,88},{... | collective-permute-start | bytes 98312 | tf_op jit(solution)/shard_map/ppermute | solution.py:17
  117.3 8.8 %collective-permute-start.4 = (f32[64,128]{1,0:T(8,128)S(1)}, f32[64,128]{1,0:T(8,128)S(1)}, u32[]{:S(2)}, u32[]{:S(2)}) collective-permute-start(f32[64,128]{1,0:T(8,128)S(1)} %add_add_fusion.1), channel_id=1, source_target_pairs={{0,64},{8,72},{16,80},{24,88},{32,96},{40,104},{48,112},{56,120},{... | collective-permute-start | bytes 98312 | tf_op jit(solution)/shard_map/ppermute | solution.py:17
  120.5 5.6 %collective-permute-start.3 = (f32[64,128]{1,0:T(8,128)S(1)}, f32[64,128]{1,0:T(8,128)S(1)}, u32[]{:S(2)}, u32[]{:S(2)}) collective-permute-start(f32[64,128]{1,0:T(8,128)S(1)} %add_add_fusion.1), channel_id=1, source_target_pairs={{0,32},{8,40},{16,48},{24,56},{32,0},{40,8},{48,16},{56,24},{64,96... | collective-permute-start | bytes 98312 | tf_op jit(solution)/shard_map/ppermute | solution.py:17
  126.7 7.2 %collective-permute-start.8 = (f32[]{:T(128)}, f32[]{:T(128)}, u32[]{:S(2)}, u32[]{:S(2)}) collective-permute-start(f32[]{:T(128)} %get-tuple-element.16), channel_id=1, source_target_pairs={{0,3},{1,2},{2,1},{3,0},{4,7},{5,6},{6,5},{7,4},{8,11},{9,10},{10,... | collective-permute-start | bytes 20 | tf_op jit(solution)/shard_map/ppermute | solution.py:17
  128.3 5.7 %collective-permute-start.7 = (f32[]{:T(128)}, f32[]{:T(128)}, u32[]{:S(2)}, u32[]{:S(2)}) collective-permute-start(f32[]{:T(128)} %get-tuple-element.16), channel_id=1, source_target_pairs={{0,2},{1,3},{2,0},{3,1},{4,6},{5,7},{6,4},{7,5},{8,10},{9,11},{10,... | collective-permute-start | bytes 20 | tf_op jit(solution)/shard_map/ppermute | solution.py:17
  128.8 3.8 %collective-permute-start.6 = (f32[]{:T(128)}, f32[]{:T(128)}, u32[]{:S(2)}, u32[]{:S(2)}) collective-permute-start(f32[]{:T(128)} %get-tuple-element.16), channel_id=1, source_target_pairs={{0,1},{1,0},{2,3},{3,2},{4,5},{5,4},{6,7},{7,6},{8,9},{9,8},{10,11... | collective-permute-start | bytes 20 | tf_op jit(solution)/shard_map/ppermute | solution.py:17
  135.2 5.1 %collective-permute-start.9 = (f32[]{:T(128)}, f32[]{:T(128)}, u32[]{:S(2)}, u32[]{:S(2)}) collective-permute-start(f32[]{:T(128)} %add.198), channel_id=1, source_target_pairs={{0,4},{1,5},{2,6},{3,7},{4,0},{5,1},{6,2},{7,3},{8,12},{9,13},{10,... | collective-permute-start | bytes 20 | tf_op jit(solution)/shard_map/ppermute | solution.py:17
Sparse Core Ops, SparseCore 0:
  13.1 75.3 all-gather.2

commit v10 on v9

--- a/solution.py
+++ b/solution.py
@@ -104,10 +104,13 @@
     factor = jnp.minimum(1.0, limit / jnp.sqrt(squares + 1e-06))
     filter_grad = factor * total_grad
 
-    gated_out = times_rounded(query_rows, convolved)
-    grad_query = times_rounded(grad_rows, convolved)
-    grad_key = times_rounded(dmixed, value_rows)
-    grad_value = times_rounded(dmixed, key_rows)
+    late_query, late_key, late_value, late_grad = lax.optimization_barrier(
+        (query_rows, key_rows, value_rows, grad_rows)
+    )
+    gated_out = times_rounded(late_query, convolved)
+    grad_query = times_rounded(late_grad, convolved)
+    grad_key = times_rounded(dmixed, late_value)
+    grad_value = times_rounded(dmixed, late_key)
     return (gated_out, grad_query, grad_key, grad_value, filter_grad)
 
 

time: 149 us -> 144 us (0.966)
  waiting for transfers between devices: 66.9 us -> 63.4 us
  other arithmetic: 2.34 us -> 5.68 us
  local copies, waits for them, and re-layouts: 26.2 us -> 23.5 us
  matrix products: 19.1 us -> 17.4 us
    unnamed x14 -> x28, local copies, waits for them, and re-layouts: 7.9 us -> 3.47 us
    all_gather x1, waiting for transfers between devices: 63.6 us -> 60.3 us  [shards(): lax.all_gather(jnp.stack([mixed, gated]), 'seq', axis=0, tiled=False)]
    optimization_barrier x0 -> x4, local copies, waits for them, and re-layouts: none -> 2.7 us  [shards(): lax.optimization_barrier((query_rows, key_rows, value_rows, grad_rows))]
    convert_element_type x4, other arithmetic: 0.37 us -> 2.41 us  [times_rounded(): (left.astype(jnp.float32) * right.astype(jnp.float32)).astype(jnp.bfloat16)]
  transfers between devices with their start and end apart: 11 -> 11, of which waited for: 3 -> 3; matrix products, arithmetic and copies ran while one was open for 20% -> 22% of each run, Pallas kernels for 0% -> 0%
where the time goes in v10:
time: 144 us
  waiting for transfers between devices  63.4 us (44%)
  local copies, waits for them, and re-layouts  23.5 us (16%)
  between operations  17.7 us (12%)
  matrix products  17.4 us (12%)
  starting transfers between devices  16.4 us (11%)
  other arithmetic  5.68 us (4%)
    all_gather x1, waiting for transfers between devices, shards(): lax.all_gather(jnp.stack([mixed, gated]), 'seq', axis=0, tiled=False)  60.3 us
    ppermute x10, starting transfers between devices, swap(): return lax.ppermute(v, axis, [(i, i ^ mask) for i in range(size)])  16.4 us
    gather x2, local copies, waits for them, and re-layouts, pick(): jnp.take(blocks, slots, axis=0)  7.92 us
    dot_general x1, matrix products, shards(): jnp.einsum('gaw,jaw->gj', corr, select_fwd.astype(jnp.float32), precision...  3.92 us
    dot_general x1, matrix products, shards(): jnp.einsum('gj,jaw->gaw', filters, select_fwd, preferred_element_type=jnp...  3.54 us
    unnamed x28, local copies, waits for them, and re-layouts  3.47 us
    dot_general x1, matrix products, shards(): jnp.einsum('gj,jau->gau', filters, _bwd_select(taps, span_rows, window),...  3.23 us
    ppermute x10, waiting for transfers between devices, swap(): return lax.ppermute(v, axis, [(i, i ^ mask) for i in range(size)])  3.06 us
  transfers between devices with their start and end apart: 11, of which 3 were waited for; matrix products, arithmetic and copies ran while one was open for 22% of the time, Pallas kernels for 0%

profile of v10, /device:TPU:0, one launch (start us, length us, event | category | flops | bytes accessed | tf_op | source)
XLA Modules:
  0.0 144.1 jit_solution(12269833661224612699)
XLA Ops:
  7.2 1.1 multiply_convert_fusion.4
  8.3 1.1 multiply_convert_fusion.5
  9.4 0.8 pad_maximum_fusion.3
  10.9 0.6 broadcast_in_dim.46
  11.9 0.7 scatter_custom_fusion
  12.6 0.6 gather_fusion
  13.3 0.6 gather_fusion.1
  13.9 0.2 concatenate.12
  14.3 0.2 concatenate.14
  14.5 0.8 copy.49
  15.4 0.8 copy.56
  16.2 0.2 copy.63
  16.4 0.8 copy.64
  17.2 0.9 copy.60
  18.2 0.5 compare_and_fusion
  18.7 3.2 %convert_bitcast_fusion = bf16[64,64,192,1]{2,0,1,3:T(8,128)(2,1)} fusion(bf16[64,128]{1,0:T(8,128)(2,1)S(1)} %copy-done), kind=kOutput, calls=%fused_computation.18 | convolution fusion | flops 205258752 | bytes 1589248 | tf_op jit(solution)/shard_map/gj,jau->gau/dot_general | solution.py:84
  22.0 3.5 %convert_bitcast_fusion.1 = bf16[64,64,192,1]{2,0,1,3:T(8,128)(2,1)} fusion(s32[64]{0:T(128)S(1)} %iota_add_fusion, bf16[64,128]{1,0:T(8,128)(2,1)S(1)} %copy-done), kind=kOutput, calls=%fused_computation.19 | convolution fusion | flops 205258752 | bytes 1589504 | tf_op jit(solution)/shard_map/gj,jaw->gaw/dot_general | solution.py:81
  25.5 60.3 %all-gather.3.cloned.1.call-done = bf16[32,128,1024]{2,1,0:T(8,128)(2,1)} async-done(((bf16[2,128,1024]{2,1,0:T(8,128)(2,1)}), bf16[32,128,1024]{2,1,0:T(8,128)(2,1)}) %all-gather.3.cloned.1.call-update) | async-done | bytes 8388624 | tf_op jit(solution)/shard_map/all_gather | solution.py:53
  85.8 4.0 %gather_fusion.2 = bf16[4,64,1024]{2,1,0:T(8,128)(2,1)S(1)} fusion(bf16[64,64,1024]{2,1,0:T(8,128)(2,1)} %bitcast.44, s32[1024]{0:T(1024)S(1)} %pad_clamp_fusion.2), kind=kCustom, calls=%fused_computation.clone | custom fusion | bytes 1048592 | tf_op jit(solution)/shard_map/jit(_take)/gather | solution.py:66
  89.9 0.7 copy.50
  90.7 0.5 reshape.190
  91.2 0.8 convolution_bitcast_fusion
  92.0 3.9 %fusion.28 = f32[64,128]{1,0:T(8,128)S(1)} fusion(s32[64]{0:T(128)S(1)} %iota_add_fusion, f32[64,64,192]{2,1,0:T(8,128)S(1)} %convolution_bitcast_fusion), kind=kOutput, calls=%fused_computation.26 | convolution fusion | flops 607125504 | bytes 3178752 | tf_op jit(solution)/shard_map/gaw,jaw->gj/dot_general | solution.py:98
  96.0 1.9 %collective-permute-start.1 = (f32[64,128]{1,0:T(8,128)S(1)}, f32[64,128]{1,0:T(8,128)S(1)}, u32[]{:S(2)}, u32[]{:S(2)}) collective-permute-start(f32[64,128]{1,0:T(8,128)S(1)} %fusion.28), channel_id=1, source_target_pairs={{0,16},{8,24},{16,0},{24,8},{32,48},{40,56},{48,32},{56,40},{64,80... | collective-permute-start | bytes 98312 | tf_op jit(solution)/shard_map/ppermute | solution.py:17
  97.9 4.0 %gather_fusion.3 = bf16[4,64,1024]{2,1,0:T(8,128)(2,1)S(1)} fusion(bf16[64,64,1024]{2,1,0:T(8,128)(2,1)} %bitcast.45, s32[1024]{0:T(1024)S(1)} %pad_clamp_fusion), kind=kCustom, calls=%fused_computation.1.clone | custom fusion | bytes 1048592 | tf_op jit(solution)/shard_map/jit(_take)/gather | solution.py:66
  102.0 0.7 copy.58
  102.7 0.5 reshape.192
  103.2 2.9 %fusion.16 = f32[2,64,64,16]{1,3,0,2:T(8,128)S(1)} fusion(bf16[64,64,192,1]{2,0,1,3:T(8,128)(2,1)} %convert_bitcast_fusion.1, bf16[2,64,64,16]{1,3,0,2:T(8,128)(2,1)S(1)} %copy.53, bf16[2,128,64,16]{1,3,0,2:T(8,128)(2,1)S(1)} %copy_select_fusion.1), kind=kOutput, calls=%fused_computation.22 | convolution fusion | flops 52166656 | bytes 2883584 | tf_op jit(solution)/shard_map/gaw,swgc->sagc/dot_general | solution.py:89
  106.1 0.5 copy.55
  106.6 0.6 reshape.193
  107.3 3.0 %fusion.25 = f32[2,64,64,16]{1,3,0,2:T(8,128)S(1)} fusion(bf16[64,64,192,1]{2,0,1,3:T(8,128)(2,1)} %convert_bitcast_fusion, bf16[2,128,64,16]{1,3,0,2:T(8,128)(2,1)S(1)} %copy_select_fusion, bf16[2,64,64,16]{1,3,0,2:T(8,128)(2,1)S(1)} %copy-done.8), kind=kOutput, calls=%fused_computation.25 | convolution fusion | flops 52166656 | bytes 2883584 | tf_op jit(solution)/shard_map/gau,sugc->sagc/dot_general | solution.py:91
  110.5 0.5 copy.62
  111.1 0.6 reshape.194
  111.7 1.3 collective-permute-start.5
  113.0 3.1 %collective-permute-start.4 = (f32[64,128]{1,0:T(8,128)S(1)}, f32[64,128]{1,0:T(8,128)S(1)}, u32[]{:S(2)}, u32[]{:S(2)}) collective-permute-start(f32[64,128]{1,0:T(8,128)S(1)} %add_add_fusion.1), channel_id=1, source_target_pairs={{0,64},{8,72},{16,80},{24,88},{32,96},{40,104},{48,112},{56,120},{... | collective-permute-start | bytes 98312 | tf_op jit(solution)/shard_map/ppermute | solution.py:17
  116.2 2.1 %collective-permute-start.3 = (f32[64,128]{1,0:T(8,128)S(1)}, f32[64,128]{1,0:T(8,128)S(1)}, u32[]{:S(2)}, u32[]{:S(2)}) collective-permute-start(f32[64,128]{1,0:T(8,128)S(1)} %add_add_fusion.1), channel_id=1, source_target_pairs={{0,32},{8,40},{16,48},{24,56},{32,0},{40,8},{48,16},{56,24},{64,96... | collective-permute-start | bytes 98312 | tf_op jit(solution)/shard_map/ppermute | solution.py:17
  118.4 0.9 copy.68
  119.2 0.8 copy.67
  120.1 0.8 copy.70
  120.9 0.8 copy.69
  121.8 0.6 multiply_reduce_fusion
  122.4 1.6 %collective-permute-start.8 = (f32[]{:T(128)}, f32[]{:T(128)}, u32[]{:S(2)}, u32[]{:S(2)}) collective-permute-start(f32[]{:T(128)} %get-tuple-element.29), channel_id=1, source_target_pairs={{0,3},{1,2},{2,1},{3,0},{4,7},{5,6},{6,5},{7,4},{8,11},{9,10},{10,... | collective-permute-start | bytes 20 | tf_op jit(solution)/shard_map/ppermute | solution.py:17
  124.0 0.6 collective-permute-start.7
  124.5 1.4 collective-permute-start.6
  125.9 2.3 %collective-permute-done.6 = f32[]{:T(128)} collective-permute-done((f32[]{:T(128)}, f32[]{:T(128)}, u32[]{:S(2)}, u32[]{:S(2)}) %collective-permute-start.6) | collective-permute-done | bytes 36 | tf_op jit(solution)/shard_map/ppermute | solution.py:17
  130.8 4.4 %collective-permute-start.9 = (f32[]{:T(128)}, f32[]{:T(128)}, u32[]{:S(2)}, u32[]{:S(2)}) collective-permute-start(f32[]{:T(128)} %add.198), channel_id=1, source_target_pairs={{0,4},{1,5},{2,6},{3,7},{4,0},{5,1},{6,2},{7,3},{8,12},{9,13},{10,... | collective-permute-start | bytes 20 | tf_op jit(solution)/shard_map/ppermute | solution.py:17
  135.1 0.8 collective-permute-done.9
  136.6 0.6 broadcast_multiply_fusion
  (62 shorter events, 1.9 us)
Async XLA Ops:
  7.2 11.6 %copy-start = (bf16[64,128]{1,0:T(8,128)(2,1)S(1)}, bf16[64,128]{1,0:T(8,128)(2,1)}, u32[]{:S(2)}) copy-start(bf16[64,128]{1,0:T(8,128)(2,1)} %param.12) | copy-start | bytes 49156
  7.2 3.5 %copy-start.11 = (s32[32]{0:T(128)S(1)}, s32[32]{0:T(128)}, u32[]{:S(2)}) copy-start(s32[32]{0:T(128)} %param.13) | copy-start | bytes 388
  7.2 78.7 %all-gather.3.cloned.1.call-start = ((), (), s32[]{:S(2)}) async-start(), calls=%async_computation | async-start | bytes 8912896 | tf_op jit(solution)/shard_map/all_gather | solution.py:53
  13.3 1.2 copy-start.1
  13.3 2.1 %copy-start.2 = (bf16[128,1024]{1,0:T(8,128)(2,1)S(1)}, bf16[128,1024]{1,0:T(8,128)(2,1)}, u32[]{:S(2)}) copy-start(bf16[128,1024]{1,0:T(8,128)(2,1)} %param.11) | copy-start | bytes 786436
  13.9 2.3 %copy-start.3 = (bf16[128,1024]{1,0:T(8,128)(2,1)S(1)}, bf16[128,1024]{1,0:T(8,128)(2,1)}, u32[]{:S(2)}) copy-start(bf16[128,1024]{1,0:T(8,128)(2,1)} %param.10) | copy-start | bytes 786436
  13.9 2.5 %copy-start.4 = (bf16[128,1024]{1,0:T(8,128)(2,1)S(1)}, bf16[128,1024]{1,0:T(8,128)(2,1)}, u32[]{:S(2)}) copy-start(bf16[128,1024]{1,0:T(8,128)(2,1)} %param.9) | copy-start | bytes 786436
  92.0 9.9 %copy-start.10 = (pred[4]{0:T(512)(128)(4,1)S(1)}, pred[4]{0:T(512)(128)(4,1)}, u32[]{:S(2)}) copy-start(pred[4]{0:T(512)(128)(4,1)} %get-tuple-element.31) | copy-start | bytes 16
  95.9 15.7 %collective-permute-start.2 = (f32[64,128]{1,0:T(8,128)S(1)}, f32[64,128]{1,0:T(8,128)S(1)}, u32[]{:S(2)}, u32[]{:S(2)}) collective-permute-start(f32[64,128]{1,0:T(8,128)S(1)} %fusion.28), channel_id=1, source_target_pairs={{0,24},{8,16},{16,8},{24,0},{32,56},{40,48},{48,40},{56,32},{64,88... | collective-permute-start | bytes 98312 | tf_op jit(solution)/shard_map/ppermute | solution.py:17
  96.0 15.6 %collective-permute-start.1 = (f32[64,128]{1,0:T(8,128)S(1)}, f32[64,128]{1,0:T(8,128)S(1)}, u32[]{:S(2)}, u32[]{:S(2)}) collective-permute-start(f32[64,128]{1,0:T(8,128)S(1)} %fusion.28), channel_id=1, source_target_pairs={{0,16},{8,24},{16,0},{24,8},{32,48},{40,56},{48,32},{56,40},{64,80... | collective-permute-start | bytes 98312 | tf_op jit(solution)/shard_map/ppermute | solution.py:17
  97.9 13.8 %collective-permute-start = (f32[64,128]{1,0:T(8,128)S(1)}, f32[64,128]{1,0:T(8,128)S(1)}, u32[]{:S(2)}, u32[]{:S(2)}) collective-permute-start(f32[64,128]{1,0:T(8,128)S(1)} %fusion.28), channel_id=1, source_target_pairs={{0,8},{8,0},{16,24},{24,16},{32,40},{40,32},{48,56},{56,48},{64,72... | collective-permute-start | bytes 98312 | tf_op jit(solution)/shard_map/ppermute | solution.py:17
  106.1 1.1 copy-start.9
  106.1 1.2 copy-start.8
  107.3 3.1 %copy-start.6 = (bf16[128,1024]{0,1:T(8,128)(2,1)S(1)}, bf16[128,1024]{0,1:T(8,128)(2,1)}, u32[]{:S(2)}) copy-start(bf16[128,1024]{0,1:T(8,128)(2,1)} %copy.49) | copy-start | bytes 786436
  107.3 3.1 %copy-start.7 = (bf16[128,1024]{0,1:T(8,128)(2,1)S(1)}, bf16[128,1024]{0,1:T(8,128)(2,1)}, u32[]{:S(2)}) copy-start(bf16[128,1024]{0,1:T(8,128)(2,1)} %copy.56) | copy-start | bytes 786436
  110.5 7.8 %copy-start.5 = (bf16[128,1024]{0,1:T(8,128)(2,1)S(1)}, bf16[128,1024]{0,1:T(8,128)(2,1)}, u32[]{:S(2)}) copy-start(bf16[128,1024]{0,1:T(8,128)(2,1)} %copy.64) | copy-start | bytes 786436
  111.7 10.1 %collective-permute-start.5 = (f32[64,128]{1,0:T(8,128)S(1)}, f32[64,128]{1,0:T(8,128)S(1)}, u32[]{:S(2)}, u32[]{:S(2)}) collective-permute-start(f32[64,128]{1,0:T(8,128)S(1)} %add_add_fusion.1), channel_id=1, source_target_pairs={{0,96},{8,104},{16,112},{24,120},{32,64},{40,72},{48,80},{56,88},{... | collective-permute-start | bytes 98312 | tf_op jit(solution)/shard_map/ppermute | solution.py:17
  113.0 8.8 %collective-permute-start.4 = (f32[64,128]{1,0:T(8,128)S(1)}, f32[64,128]{1,0:T(8,128)S(1)}, u32[]{:S(2)}, u32[]{:S(2)}) collective-permute-start(f32[64,128]{1,0:T(8,128)S(1)} %add_add_fusion.1), channel_id=1, source_target_pairs={{0,64},{8,72},{16,80},{24,88},{32,96},{40,104},{48,112},{56,120},{... | collective-permute-start | bytes 98312 | tf_op jit(solution)/shard_map/ppermute | solution.py:17
  116.2 5.6 %collective-permute-start.3 = (f32[64,128]{1,0:T(8,128)S(1)}, f32[64,128]{1,0:T(8,128)S(1)}, u32[]{:S(2)}, u32[]{:S(2)}) collective-permute-start(f32[64,128]{1,0:T(8,128)S(1)} %add_add_fusion.1), channel_id=1, source_target_pairs={{0,32},{8,40},{16,48},{24,56},{32,0},{40,8},{48,16},{56,24},{64,96... | collective-permute-start | bytes 98312 | tf_op jit(solution)/shard_map/ppermute | solution.py:17
  122.4 7.0 %collective-permute-start.8 = (f32[]{:T(128)}, f32[]{:T(128)}, u32[]{:S(2)}, u32[]{:S(2)}) collective-permute-start(f32[]{:T(128)} %get-tuple-element.29), channel_id=1, source_target_pairs={{0,3},{1,2},{2,1},{3,0},{4,7},{5,6},{6,5},{7,4},{8,11},{9,10},{10,... | collective-permute-start | bytes 20 | tf_op jit(solution)/shard_map/ppermute | solution.py:17
  124.0 5.5 %collective-permute-start.7 = (f32[]{:T(128)}, f32[]{:T(128)}, u32[]{:S(2)}, u32[]{:S(2)}) collective-permute-start(f32[]{:T(128)} %get-tuple-element.29), channel_id=1, source_target_pairs={{0,2},{1,3},{2,0},{3,1},{4,6},{5,7},{6,4},{7,5},{8,10},{9,11},{10,... | collective-permute-start | bytes 20 | tf_op jit(solution)/shard_map/ppermute | solution.py:17
  124.5 3.7 %collective-permute-start.6 = (f32[]{:T(128)}, f32[]{:T(128)}, u32[]{:S(2)}, u32[]{:S(2)}) collective-permute-start(f32[]{:T(128)} %get-tuple-element.29), channel_id=1, source_target_pairs={{0,1},{1,0},{2,3},{3,2},{4,5},{5,4},{6,7},{7,6},{8,9},{9,8},{10,11... | collective-permute-start | bytes 20 | tf_op jit(solution)/shard_map/ppermute | solution.py:17
  130.8 5.1 %collective-permute-start.9 = (f32[]{:T(128)}, f32[]{:T(128)}, u32[]{:S(2)}, u32[]{:S(2)}) collective-permute-start(f32[]{:T(128)} %add.198), channel_id=1, source_target_pairs={{0,4},{1,5},{2,6},{3,7},{4,0},{5,1},{6,2},{7,3},{8,12},{9,13},{10,... | collective-permute-start | bytes 20 | tf_op jit(solution)/shard_map/ppermute | solution.py:17
Sparse Core Ops, SparseCore 0:
  10.4 75.3 all-gather.2

commit v11 on v10

--- a/solution.py
+++ b/solution.py
@@ -10,20 +10,21 @@
     return (left.astype(jnp.float32) * right.astype(jnp.float32)).astype(jnp.bfloat16)
 
 
+def swap(value, axis, mask):
+    size = lax.axis_size(axis)
+    return lax.ppermute(value, axis, [(i, i ^ mask) for i in range(size)])
+
+
+def radix_round(value, axis, bit):
+    if bit * 4 <= lax.axis_size(axis):
+        return (value + swap(value, axis, bit)) + (swap(value, axis, 2 * bit) + swap(value, axis, 3 * bit)), bit * 4
+    return value + swap(value, axis, bit), bit * 2
+
+
 def butterfly_sum(value, axis):
-    size = lax.axis_size(axis)
-
-    def swap(v, mask):
-        return lax.ppermute(v, axis, [(i, i ^ mask) for i in range(size)])
-
     bit = 1
-    while bit < size:
-        if bit * 4 <= size:
-            value = (value + swap(value, bit)) + (swap(value, 2 * bit) + swap(value, 3 * bit))
-            bit *= 4
-        else:
-            value = value + swap(value, bit)
-            bit *= 2
+    while bit < lax.axis_size(axis):
+        value, bit = radix_round(value, axis, bit)
     return value
 
 
@@ -59,7 +60,7 @@
     before = mine[:, None] - halo + step[None, :]
     after = mine[:, None] + 1 + step[None, :]
 
-    def pick(which, wanted):
+    def pick(blocks, which, wanted):
         valid = (wanted >= 0) & (wanted < spans)
         slots = slot_of[jnp.clip(wanted, 0, spans - 1)].reshape(-1)
         slots = ((slots // per_device) * 2 + which) * per_device + slots % per_device
@@ -69,13 +70,9 @@
     own_mixed = mixed.reshape(per_device, span_rows, channels)
     own_gated = gated.reshape(per_device, span_rows, channels)
     mixed_window = jnp.concatenate(
-        [pick(0, before).reshape(per_device, lead, channels), own_mixed], axis=1
-    )
-    gated_window = jnp.concatenate(
-        [own_gated, pick(1, after).reshape(per_device, lead, channels)], axis=1
+        [pick(blocks, 0, before).reshape(per_device, lead, channels), own_mixed], axis=1
     )
     mixed_window = mixed_window.reshape(per_device, window, groups, group_size)
-    gated_window = gated_window.reshape(per_device, window, groups, group_size)
 
     select_fwd = band_select(taps, span_rows, window, lead)
     fwd_band = jnp.einsum(
@@ -88,9 +85,6 @@
 
     conv = jnp.einsum("gaw,swgc->sagc", fwd_band, mixed_window, preferred_element_type=jnp.float32)
     convolved = conv.reshape(rows, channels).astype(jnp.bfloat16)
-    adjoint = jnp.einsum("gau,sugc->sagc", bwd_band, gated_window, preferred_element_type=jnp.float32)
-    dmixed = adjoint.reshape(rows, channels).astype(jnp.bfloat16)
-
     own_gated_g = own_gated.reshape(per_device, span_rows, groups, group_size)
     corr = jnp.einsum(
         "sagc,swgc->gaw", own_gated_g, mixed_window, preferred_element_type=jnp.float32
@@ -98,15 +92,23 @@
     partial_grad = jnp.einsum(
         "gaw,jaw->gj", corr, select_fwd.astype(jnp.float32), precision=lax.Precision.HIGH
     )
-    total_grad = butterfly_sum(partial_grad, "seq")
+    total_grad, bit = radix_round(partial_grad, "seq", 1)
+    total_grad, late_blocks = lax.optimization_barrier((total_grad, blocks))
+    gated_window = jnp.concatenate(
+        [own_gated, pick(late_blocks, 1, after).reshape(per_device, lead, channels)], axis=1
+    ).reshape(per_device, window, groups, group_size)
+    adjoint = jnp.einsum("gau,sugc->sagc", bwd_band, gated_window, preferred_element_type=jnp.float32)
+    dmixed = adjoint.reshape(rows, channels).astype(jnp.bfloat16)
+    while bit < devices:
+        total_grad, bit = radix_round(total_grad, "seq", bit)
+    total_grad, late_query, late_key, late_value, late_grad = lax.optimization_barrier(
+        (total_grad, query_rows, key_rows, value_rows, grad_rows)
+    )
     squares = butterfly_sum(jnp.sum(total_grad * total_grad), "chan")
     limit = math.sqrt(groups * lax.axis_size("chan") * taps)
     factor = jnp.minimum(1.0, limit / jnp.sqrt(squares + 1e-06))
     filter_grad = factor * total_grad
 
-    late_query, late_key, late_value, late_grad = lax.optimization_barrier(
-        (query_rows, key_rows, value_rows, grad_rows)
-    )
     gated_out = times_rounded(late_query, convolved)
     grad_query = times_rounded(late_grad, convolved)
     grad_key = times_rounded(dmixed, late_value)

time: 144 us -> 141 us (0.979)
  local copies, waits for them, and re-layouts: 23.5 us -> 20.1 us
  waiting for transfers between devices: 63.4 us -> 65.7 us
  matrix products: 17.4 us -> 15.7 us
    all_gather x1, waiting for transfers between devices: 60.3 us -> 64.9 us  [shards(): lax.all_gather(jnp.stack([mixed, gated]), 'seq', axis=0, tiled=False)]
    ppermute x10, waiting for transfers between devices: 3.06 us -> 0.77 us  [swap(): return lax.ppermute(value, axis, [(i, i ^ mask) for i in range(size)])]
    optimization_barrier x4, local copies, waits for them, and re-layouts: 2.7 us -> 0.67 us  [shards(): lax.optimization_barrier((total_grad, query_rows, key_rows, value_rows, g...]
    dot_general x1, matrix products: 2.89 us -> 1.33 us  [shards(): jnp.einsum('gaw,swgc->sagc', fwd_band, mixed_window, preferred_element_ty...]
    unnamed x28 -> x18, local copies, waits for them, and re-layouts: 3.47 us -> 3.43 us
  transfers between devices with their start and end apart: 11 -> 11, of which waited for: 3 -> 2; matrix products, arithmetic and copies ran while one was open for 22% -> 19% of each run, Pallas kernels for 0% -> 0%
where the time goes in v11:
time: 141 us
  waiting for transfers between devices  65.7 us (47%)
  local copies, waits for them, and re-layouts  20.1 us (14%)
  between operations  17.7 us (13%)
  starting transfers between devices  16.4 us (12%)
  matrix products  15.7 us (11%)
  other arithmetic  5.24 us (4%)
    all_gather x1, waiting for transfers between devices, shards(): lax.all_gather(jnp.stack([mixed, gated]), 'seq', axis=0, tiled=False)  64.9 us
    ppermute x10, starting transfers between devices, swap(): return lax.ppermute(value, axis, [(i, i ^ mask) for i in range(size)])  16.4 us
    gather x2, local copies, waits for them, and re-layouts, pick(): jnp.take(blocks, slots, axis=0)  7.92 us
    dot_general x1, matrix products, shards(): jnp.einsum('gaw,jaw->gj', corr, select_fwd.astype(jnp.float32), precision...  3.92 us
    dot_general x1, matrix products, shards(): jnp.einsum('gj,jaw->gaw', filters, select_fwd, preferred_element_type=jnp...  3.53 us
    unnamed x18, local copies, waits for them, and re-layouts  3.43 us
    dot_general x1, matrix products, shards(): jnp.einsum('gj,jau->gau', filters, _bwd_select(taps, span_rows, window),...  3.23 us
    dot_general x1, matrix products, shards(): jnp.einsum('gau,sugc->sagc', bwd_band, gated_window, preferred_element_ty...  2.95 us
  transfers between devices with their start and end apart: 11, of which 2 were waited for; matrix products, arithmetic and copies ran while one was open for 19% of the time, Pallas kernels for 0%

profile of v11, /device:TPU:0, one launch (start us, length us, event | category | flops | bytes accessed | tf_op | source)
XLA Modules:
  0.0 140.8 jit_solution(9225731005280992454)
XLA Ops:
  7.2 1.1 multiply_convert_fusion.4
  8.3 1.1 multiply_convert_fusion.5
  9.4 0.9 pad_maximum_fusion.3
  10.4 0.2 copy.52
  10.5 0.2 copy.49
  11.2 0.2 concatenate.10
  11.6 0.2 reshape_reshape.3
  11.9 0.7 scatter_custom_fusion
  12.6 0.6 gather_fusion
  13.2 0.6 gather_fusion.1
  14.2 3.2 %convert_bitcast_fusion = bf16[64,64,192,1]{2,0,1,3:T(8,128)(2,1)} fusion(bf16[64,128]{1,0:T(8,128)(2,1)S(1)} %copy-done), kind=kOutput, calls=%fused_computation.18 | convolution fusion | flops 205258752 | bytes 1589248 | tf_op jit(solution)/shard_map/gj,jau->gau/dot_general | solution.py:81
  17.4 3.5 %convert_bitcast_fusion.1 = bf16[64,64,192,1]{2,0,1,3:T(8,128)(2,1)} fusion(s32[64]{0:T(128)S(1)} %iota_add_fusion, bf16[64,128]{1,0:T(8,128)(2,1)S(1)} %copy-done), kind=kOutput, calls=%fused_computation.19 | convolution fusion | flops 205258752 | bytes 1589504 | tf_op jit(solution)/shard_map/gj,jaw->gaw/dot_general | solution.py:78
  21.0 64.9 %all-gather.3.cloned.1.call-done = bf16[32,128,1024]{2,1,0:T(8,128)(2,1)} async-done(((bf16[2,128,1024]{2,1,0:T(8,128)(2,1)}), bf16[32,128,1024]{2,1,0:T(8,128)(2,1)}) %all-gather.3.cloned.1.call-update) | async-done | bytes 8388624 | tf_op jit(solution)/shard_map/all_gather | solution.py:54
  85.9 4.0 %gather_fusion.2 = bf16[4,64,1024]{2,1,0:T(8,128)(2,1)S(1)} fusion(bf16[64,64,1024]{2,1,0:T(8,128)(2,1)} %bitcast.43, s32[1024]{0:T(1024)S(1)} %pad_clamp_fusion.2), kind=kCustom, calls=%fused_computation.clone | custom fusion | bytes 1048592 | tf_op jit(solution)/shard_map/jit(_take)/gather | solution.py:67
  90.0 0.7 copy.50
  90.7 0.5 reshape.190
  91.3 0.8 convolution_bitcast_fusion
  92.0 3.9 %fusion.28 = f32[64,128]{1,0:T(8,128)S(1)} fusion(s32[64]{0:T(128)S(1)} %iota_add_fusion, f32[64,64,192]{2,1,0:T(8,128)S(1)} %convolution_bitcast_fusion), kind=kOutput, calls=%fused_computation.26 | convolution fusion | flops 607125504 | bytes 3178752 | tf_op jit(solution)/shard_map/gaw,jaw->gj/dot_general | solution.py:92
  96.0 0.3 collective-permute-start
  96.3 0.2 collective-permute-start.1
  96.4 1.5 %collective-permute-start.2 = (f32[64,128]{1,0:T(8,128)S(1)}, f32[64,128]{1,0:T(8,128)S(1)}, u32[]{:S(2)}, u32[]{:S(2)}) collective-permute-start(f32[64,128]{1,0:T(8,128)S(1)} %fusion.28), channel_id=1, source_target_pairs={{0,24},{8,16},{16,8},{24,0},{32,56},{40,48},{48,40},{56,32},{64,88... | collective-permute-start | bytes 98312 | tf_op jit(solution)/shard_map/ppermute | solution.py:15
  97.9 1.3 fusion.16
  99.2 0.5 copy.58
  99.8 0.6 reshape.193
  100.4 1.9 %collective-permute-start.3 = (f32[64,128]{1,0:T(8,128)S(1)}, f32[64,128]{1,0:T(8,128)S(1)}, u32[]{:S(2)}, u32[]{:S(2)}) collective-permute-start(f32[64,128]{1,0:T(8,128)S(1)} %add_add_fusion.1), channel_id=1, source_target_pairs={{0,32},{8,40},{16,48},{24,56},{32,0},{40,8},{48,16},{56,24},{64,96... | collective-permute-start | bytes 98312 | tf_op jit(solution)/shard_map/ppermute | solution.py:15
  102.3 0.4 collective-permute-start.4
  102.7 4.3 %collective-permute-start.5 = (f32[64,128]{1,0:T(8,128)S(1)}, f32[64,128]{1,0:T(8,128)S(1)}, u32[]{:S(2)}, u32[]{:S(2)}) collective-permute-start(f32[64,128]{1,0:T(8,128)S(1)} %add_add_fusion.1), channel_id=1, source_target_pairs={{0,96},{8,104},{16,112},{24,120},{32,64},{40,72},{48,80},{56,88},{... | collective-permute-start | bytes 98312 | tf_op jit(solution)/shard_map/ppermute | solution.py:15
  107.0 4.0 %gather_fusion.3 = bf16[4,64,1024]{2,1,0:T(8,128)(2,1)S(1)} fusion(bf16[64,64,1024]{2,1,0:T(8,128)(2,1)} %bitcast.44, s32[1024]{0:T(1024)S(1)} %pad_clamp_fusion), kind=kCustom, calls=%fused_computation.1.clone | custom fusion | bytes 1048592 | tf_op jit(solution)/shard_map/jit(_take)/gather | solution.py:67
  111.1 0.7 copy.60
  111.8 0.5 reshape.192
  112.4 3.0 %fusion.25 = f32[2,64,64,16]{1,3,0,2:T(8,128)S(1)} fusion(bf16[64,64,192,1]{2,0,1,3:T(8,128)(2,1)} %convert_bitcast_fusion, bf16[2,128,64,16]{1,3,0,2:T(8,128)(2,1)S(1)} %copy_select_fusion, bf16[2,64,64,16]{1,3,0,2:T(8,128)(2,1)S(1)} %copy.54), kind=kOutput, calls=%fused_computation.25 | convolution fusion | flops 52166656 | bytes 2883584 | tf_op jit(solution)/shard_map/gau,sugc->sagc/dot_general | solution.py:100
  115.3 0.5 copy.64
  115.9 0.6 reshape.194
  116.5 0.6 multiply_reduce_fusion
  117.1 1.5 %collective-permute-start.7 = (f32[]{:T(128)}, f32[]{:T(128)}, u32[]{:S(2)}, u32[]{:S(2)}) collective-permute-start(f32[]{:T(128)} %multiply_reduce_fusion), channel_id=1, source_target_pairs={{0,2},{1,3},{2,0},{3,1},{4,6},{5,7},{6,4},{7,5},{8,10},{9,11},{10,... | collective-permute-start | bytes 20 | tf_op jit(solution)/shard_map/ppermute | solution.py:15
  118.6 0.6 collective-permute-start.8
  119.3 1.4 collective-permute-start.6
  120.6 0.2 copy.65
  120.8 0.2 copy.66
  121.1 0.9 copy.69
  122.0 0.8 copy.70
  122.8 0.2 copy.56
  123.0 0.2 copy.59
  123.3 0.9 copy.67
  124.1 0.8 copy.68
  127.5 4.4 %collective-permute-start.9 = (f32[]{:T(128)}, f32[]{:T(128)}, u32[]{:S(2)}, u32[]{:S(2)}) collective-permute-start(f32[]{:T(128)} %add.198), channel_id=1, source_target_pairs={{0,4},{1,5},{2,6},{3,7},{4,0},{5,1},{6,2},{7,3},{8,12},{9,13},{10,... | collective-permute-start | bytes 20 | tf_op jit(solution)/shard_map/ppermute | solution.py:15
  131.9 0.7 collective-permute-done.9
  133.3 0.6 broadcast_multiply_fusion
  (53 shorter events, 1.7 us)
Async XLA Ops:
  7.2 7.0 %copy-start = (bf16[64,128]{1,0:T(8,128)(2,1)S(1)}, bf16[64,128]{1,0:T(8,128)(2,1)}, u32[]{:S(2)}) copy-start(bf16[64,128]{1,0:T(8,128)(2,1)} %param.12) | copy-start | bytes 49156
  7.2 3.5 %copy-start.5 = (s32[32]{0:T(128)S(1)}, s32[32]{0:T(128)}, u32[]{:S(2)}) copy-start(s32[32]{0:T(128)} %param.13) | copy-start | bytes 388
  7.2 78.7 %all-gather.3.cloned.1.call-start = ((), (), s32[]{:S(2)}) async-start(), calls=%async_computation | async-start | bytes 8912896 | tf_op jit(solution)/shard_map/all_gather | solution.py:54
  92.0 5.9 %copy-start.6 = (bf16[64,64,192,1]{2,0,1,3:T(8,128)(2,1)S(1)}, bf16[64,64,192,1]{2,0,1,3:T(8,128)(2,1)}, u32[]{:S(2)}) copy-start(bf16[64,64,192,1]{2,0,1,3:T(8,128)(2,1)} %convert_bitcast_fusion.1) | copy-start | bytes 4718596
  96.0 4.4 %collective-permute-start = (f32[64,128]{1,0:T(8,128)S(1)}, f32[64,128]{1,0:T(8,128)S(1)}, u32[]{:S(2)}, u32[]{:S(2)}) collective-permute-start(f32[64,128]{1,0:T(8,128)S(1)} %fusion.28), channel_id=1, source_target_pairs={{0,8},{8,0},{16,24},{24,16},{32,40},{40,32},{48,56},{56,48},{64,72... | collective-permute-start | bytes 98312 | tf_op jit(solution)/shard_map/ppermute | solution.py:15
  96.3 4.1 %collective-permute-start.1 = (f32[64,128]{1,0:T(8,128)S(1)}, f32[64,128]{1,0:T(8,128)S(1)}, u32[]{:S(2)}, u32[]{:S(2)}) collective-permute-start(f32[64,128]{1,0:T(8,128)S(1)} %fusion.28), channel_id=1, source_target_pairs={{0,16},{8,24},{16,0},{24,8},{32,48},{40,56},{48,32},{56,40},{64,80... | collective-permute-start | bytes 98312 | tf_op jit(solution)/shard_map/ppermute | solution.py:15
  96.4 3.9 %collective-permute-start.2 = (f32[64,128]{1,0:T(8,128)S(1)}, f32[64,128]{1,0:T(8,128)S(1)}, u32[]{:S(2)}, u32[]{:S(2)}) collective-permute-start(f32[64,128]{1,0:T(8,128)S(1)} %fusion.28), channel_id=1, source_target_pairs={{0,24},{8,16},{16,8},{24,0},{32,56},{40,48},{48,40},{56,32},{64,88... | collective-permute-start | bytes 98312 | tf_op jit(solution)/shard_map/ppermute | solution.py:15
  100.4 16.1 %collective-permute-start.3 = (f32[64,128]{1,0:T(8,128)S(1)}, f32[64,128]{1,0:T(8,128)S(1)}, u32[]{:S(2)}, u32[]{:S(2)}) collective-permute-start(f32[64,128]{1,0:T(8,128)S(1)} %add_add_fusion.1), channel_id=1, source_target_pairs={{0,32},{8,40},{16,48},{24,56},{32,0},{40,8},{48,16},{56,24},{64,96... | collective-permute-start | bytes 98312 | tf_op jit(solution)/shard_map/ppermute | solution.py:15
  102.3 14.2 %collective-permute-start.4 = (f32[64,128]{1,0:T(8,128)S(1)}, f32[64,128]{1,0:T(8,128)S(1)}, u32[]{:S(2)}, u32[]{:S(2)}) collective-permute-start(f32[64,128]{1,0:T(8,128)S(1)} %add_add_fusion.1), channel_id=1, source_target_pairs={{0,64},{8,72},{16,80},{24,88},{32,96},{40,104},{48,112},{56,120},{... | collective-permute-start | bytes 98312 | tf_op jit(solution)/shard_map/ppermute | solution.py:15
  102.7 13.8 %collective-permute-start.5 = (f32[64,128]{1,0:T(8,128)S(1)}, f32[64,128]{1,0:T(8,128)S(1)}, u32[]{:S(2)}, u32[]{:S(2)}) collective-permute-start(f32[64,128]{1,0:T(8,128)S(1)} %add_add_fusion.1), channel_id=1, source_target_pairs={{0,96},{8,104},{16,112},{24,120},{32,64},{40,72},{48,80},{56,88},{... | collective-permute-start | bytes 98312 | tf_op jit(solution)/shard_map/ppermute | solution.py:15
  115.3 5.3 %copy-start.1 = (bf16[128,1024]{1,0:T(8,128)(2,1)S(1)}, bf16[128,1024]{1,0:T(8,128)(2,1)}, u32[]{:S(2)}) copy-start(bf16[128,1024]{1,0:T(8,128)(2,1)} %param.10) | copy-start | bytes 786436
  115.3 5.5 %copy-start.2 = (bf16[128,1024]{1,0:T(8,128)(2,1)S(1)}, bf16[128,1024]{1,0:T(8,128)(2,1)}, u32[]{:S(2)}) copy-start(bf16[128,1024]{1,0:T(8,128)(2,1)} %param.9) | copy-start | bytes 786436
  116.5 6.3 %copy-start.3 = (bf16[128,1024]{1,0:T(8,128)(2,1)S(1)}, bf16[128,1024]{1,0:T(8,128)(2,1)}, u32[]{:S(2)}) copy-start(bf16[128,1024]{1,0:T(8,128)(2,1)} %param.8) | copy-start | bytes 786436
  117.1 5.8 %copy-start.4 = (bf16[128,1024]{1,0:T(8,128)(2,1)S(1)}, bf16[128,1024]{1,0:T(8,128)(2,1)}, u32[]{:S(2)}) copy-start(bf16[128,1024]{1,0:T(8,128)(2,1)} %param.11) | copy-start | bytes 786436
  117.1 9.1 %collective-permute-start.7 = (f32[]{:T(128)}, f32[]{:T(128)}, u32[]{:S(2)}, u32[]{:S(2)}) collective-permute-start(f32[]{:T(128)} %multiply_reduce_fusion), channel_id=1, source_target_pairs={{0,2},{1,3},{2,0},{3,1},{4,6},{5,7},{6,4},{7,5},{8,10},{9,11},{10,... | collective-permute-start | bytes 20 | tf_op jit(solution)/shard_map/ppermute | solution.py:15
  118.6 7.7 %collective-permute-start.8 = (f32[]{:T(128)}, f32[]{:T(128)}, u32[]{:S(2)}, u32[]{:S(2)}) collective-permute-start(f32[]{:T(128)} %multiply_reduce_fusion), channel_id=1, source_target_pairs={{0,3},{1,2},{2,1},{3,0},{4,7},{5,6},{6,5},{7,4},{8,11},{9,10},{10,... | collective-permute-start | bytes 20 | tf_op jit(solution)/shard_map/ppermute | solution.py:15
  119.3 5.7 %collective-permute-start.6 = (f32[]{:T(128)}, f32[]{:T(128)}, u32[]{:S(2)}, u32[]{:S(2)}) collective-permute-start(f32[]{:T(128)} %multiply_reduce_fusion), channel_id=1, source_target_pairs={{0,1},{1,0},{2,3},{3,2},{4,5},{5,4},{6,7},{7,6},{8,9},{9,8},{10,11... | collective-permute-start | bytes 20 | tf_op jit(solution)/shard_map/ppermute | solution.py:15
  127.5 5.1 %collective-permute-start.9 = (f32[]{:T(128)}, f32[]{:T(128)}, u32[]{:S(2)}, u32[]{:S(2)}) collective-permute-start(f32[]{:T(128)} %add.198), channel_id=1, source_target_pairs={{0,4},{1,5},{2,6},{3,7},{4,0},{5,1},{6,2},{7,3},{8,12},{9,13},{10,... | collective-permute-start | bytes 20 | tf_op jit(solution)/shard_map/ppermute | solution.py:15
Sparse Core Ops, SparseCore 0:
  10.5 75.3 all-gather.2

commit v12 on v11

--- a/solution.py
+++ b/solution.py
@@ -92,11 +92,12 @@
     partial_grad = jnp.einsum(
         "gaw,jaw->gj", corr, select_fwd.astype(jnp.float32), precision=lax.Precision.HIGH
     )
-    total_grad, bit = radix_round(partial_grad, "seq", 1)
-    total_grad, late_blocks = lax.optimization_barrier((total_grad, blocks))
+    partial_grad, late_blocks = lax.optimization_barrier((partial_grad, blocks))
     gated_window = jnp.concatenate(
         [own_gated, pick(late_blocks, 1, after).reshape(per_device, lead, channels)], axis=1
     ).reshape(per_device, window, groups, group_size)
+    total_grad, bit = radix_round(partial_grad, "seq", 1)
+    total_grad, gated_window = lax.optimization_barrier((total_grad, gated_window))
     adjoint = jnp.einsum("gau,sugc->sagc", bwd_band, gated_window, preferred_element_type=jnp.float32)
     dmixed = adjoint.reshape(rows, channels).astype(jnp.bfloat16)
     while bit < devices:

time: 141 us -> 143 us (1.014)
  matrix products: 15.7 us -> 17.4 us
    dot_general x1, matrix products: 1.33 us -> 2.89 us  [shards(): jnp.einsum('gaw,swgc->sagc', fwd_band, mixed_window, preferred_element_ty...]
    unnamed x18 -> x20, local copies, waits for them, and re-layouts: 3.43 us -> 3.51 us
  transfers between devices with their start and end apart: 11 -> 11, of which waited for: 2 -> 2; matrix products, arithmetic and copies ran while one was open for 19% -> 20% of each run, Pallas kernels for 0% -> 0%
where the time goes in v12:
time: 143 us
  waiting for transfers between devices  65.7 us (46%)
  local copies, waits for them, and re-layouts  20.1 us (14%)
  between operations  17.7 us (12%)
  matrix products  17.4 us (12%)
  starting transfers between devices  16.4 us (11%)
  other arithmetic  5.74 us (4%)
    all_gather x1, waiting for transfers between devices, shards(): lax.all_gather(jnp.stack([mixed, gated]), 'seq', axis=0, tiled=False)  64.9 us
    ppermute x10, starting transfers between devices, swap(): return lax.ppermute(value, axis, [(i, i ^ mask) for i in range(size)])  16.4 us
    gather x2, local copies, waits for them, and re-layouts, pick(): jnp.take(blocks, slots, axis=0)  7.92 us
    dot_general x1, matrix products, shards(): jnp.einsum('gaw,jaw->gj', corr, select_fwd.astype(jnp.float32), precision...  3.92 us
    dot_general x1, matrix products, shards(): jnp.einsum('gj,jaw->gaw', filters, select_fwd, preferred_element_type=jnp...  3.54 us
    unnamed x20, local copies, waits for them, and re-layouts  3.51 us
    dot_general x1, matrix products, shards(): jnp.einsum('gj,jau->gau', filters, _bwd_select(taps, span_rows, window),...  3.24 us
    dot_general x1, matrix products, shards(): jnp.einsum('gau,sugc->sagc', bwd_band, gated_window, preferred_element_ty...  3.08 us
  transfers between devices with their start and end apart: 11, of which 2 were waited for; matrix products, arithmetic and copies ran while one was open for 20% of the time, Pallas kernels for 0%

profile of v12, /device:TPU:0, one launch (start us, length us, event | category | flops | bytes accessed | tf_op | source)
XLA Modules:
  0.0 143.1 jit_solution(10984836577932866082)
XLA Ops:
  7.2 1.1 multiply_convert_fusion.4
  8.3 1.1 multiply_convert_fusion.5
  9.4 0.9 pad_maximum_fusion.4
  10.4 0.2 copy.52
  10.5 0.2 copy.49
  11.2 0.2 concatenate.10
  11.6 0.2 reshape_reshape.3
  11.9 0.7 scatter_custom_fusion
  12.6 0.6 gather_fusion
  13.2 0.6 gather_fusion.1
  14.2 3.2 %convert_bitcast_fusion = bf16[64,64,192,1]{2,0,1,3:T(8,128)(2,1)} fusion(bf16[64,128]{1,0:T(8,128)(2,1)S(1)} %copy-done), kind=kOutput, calls=%fused_computation.18 | convolution fusion | flops 205258752 | bytes 1589248 | tf_op jit(solution)/shard_map/gj,jau->gau/dot_general | solution.py:81
  17.4 3.5 %convert_bitcast_fusion.1 = bf16[64,64,192,1]{2,0,1,3:T(8,128)(2,1)} fusion(s32[64]{0:T(128)S(1)} %iota_add_fusion, bf16[64,128]{1,0:T(8,128)(2,1)S(1)} %copy-done), kind=kOutput, calls=%fused_computation.19 | convolution fusion | flops 205258752 | bytes 1589504 | tf_op jit(solution)/shard_map/gj,jaw->gaw/dot_general | solution.py:78
  21.0 64.9 %all-gather.3.cloned.1.call-done = bf16[32,128,1024]{2,1,0:T(8,128)(2,1)} async-done(((bf16[2,128,1024]{2,1,0:T(8,128)(2,1)}), bf16[32,128,1024]{2,1,0:T(8,128)(2,1)}) %all-gather.3.cloned.1.call-update) | async-done | bytes 8388624 | tf_op jit(solution)/shard_map/all_gather | solution.py:54
  85.9 4.0 %gather_fusion.2 = bf16[4,64,1024]{2,1,0:T(8,128)(2,1)S(1)} fusion(bf16[64,64,1024]{2,1,0:T(8,128)(2,1)} %bitcast.44, s32[1024]{0:T(1024)S(1)} %pad_clamp_fusion.2), kind=kCustom, calls=%fused_computation.clone | custom fusion | bytes 1048592 | tf_op jit(solution)/shard_map/jit(_take)/gather | solution.py:67
  90.0 0.7 copy.50
  90.7 0.5 reshape.190
  91.3 0.8 convolution_bitcast_fusion
  92.1 3.9 %fusion.28 = f32[64,128]{1,0:T(8,128)S(1)} fusion(s32[64]{0:T(128)S(1)} %iota_add_fusion, f32[64,64,192]{2,1,0:T(8,128)S(1)} %convolution_bitcast_fusion), kind=kOutput, calls=%fused_computation.26 | convolution fusion | flops 607125504 | bytes 3178752 | tf_op jit(solution)/shard_map/gaw,jaw->gj/dot_general | solution.py:92
  96.0 0.3 collective-permute-start
  96.3 0.2 collective-permute-start.1
  96.5 1.5 %collective-permute-start.2 = (f32[64,128]{1,0:T(8,128)S(1)}, f32[64,128]{1,0:T(8,128)S(1)}, u32[]{:S(2)}, u32[]{:S(2)}) collective-permute-start(f32[64,128]{1,0:T(8,128)S(1)} %fusion.28), channel_id=1, source_target_pairs={{0,24},{8,16},{16,8},{24,0},{32,56},{40,48},{48,40},{56,32},{64,88... | collective-permute-start | bytes 98312 | tf_op jit(solution)/shard_map/ppermute | solution.py:15
  98.0 4.0 %gather_fusion.3 = bf16[4,64,1024]{2,1,0:T(8,128)(2,1)S(1)} fusion(bf16[64,64,1024]{2,1,0:T(8,128)(2,1)} %bitcast.45, s32[1024]{0:T(1024)S(1)} %pad_clamp_fusion), kind=kCustom, calls=%fused_computation.1.clone | custom fusion | bytes 1048592 | tf_op jit(solution)/shard_map/jit(_take)/gather | solution.py:67
  102.1 0.7 copy.56
  102.8 0.5 reshape.192
  103.3 2.9 %fusion.16 = f32[2,64,64,16]{1,3,0,2:T(8,128)S(1)} fusion(bf16[64,64,192,1]{2,0,1,3:T(8,128)(2,1)} %convert_bitcast_fusion.1, bf16[2,64,64,16]{1,3,0,2:T(8,128)(2,1)S(1)} %copy.53, bf16[2,128,64,16]{1,3,0,2:T(8,128)(2,1)S(1)} %copy-done.2), kind=kOutput, calls=%fused_computation.22 | convolution fusion | flops 52166656 | bytes 2883584 | tf_op jit(solution)/shard_map/gaw,swgc->sagc/dot_general | solution.py:86
  106.3 0.5 pad_maximum_fusion.1
  106.8 0.5 copy.61
  107.3 0.6 reshape.193
  108.0 1.5 %collective-permute-start.3 = (f32[64,128]{1,0:T(8,128)S(1)}, f32[64,128]{1,0:T(8,128)S(1)}, u32[]{:S(2)}, u32[]{:S(2)}) collective-permute-start(f32[64,128]{1,0:T(8,128)S(1)} %add_add_fusion.1), channel_id=1, source_target_pairs={{0,32},{8,40},{16,48},{24,56},{32,0},{40,8},{48,16},{56,24},{64,96... | collective-permute-start | bytes 98312 | tf_op jit(solution)/shard_map/ppermute | solution.py:15
  109.4 0.4 collective-permute-start.4
  109.8 4.7 %collective-permute-start.5 = (f32[64,128]{1,0:T(8,128)S(1)}, f32[64,128]{1,0:T(8,128)S(1)}, u32[]{:S(2)}, u32[]{:S(2)}) collective-permute-start(f32[64,128]{1,0:T(8,128)S(1)} %add_add_fusion.1), channel_id=1, source_target_pairs={{0,96},{8,104},{16,112},{24,120},{32,64},{40,72},{48,80},{56,88},{... | collective-permute-start | bytes 98312 | tf_op jit(solution)/shard_map/ppermute | solution.py:15
  114.5 3.1 %fusion.25 = f32[2,64,64,16]{1,3,0,2:T(8,128)S(1)} fusion(bf16[2,192,64,16]{1,3,0,2:T(8,128)(2,1)S(1)} %pad_maximum_fusion.1, bf16[64,64,192,1]{2,0,1,3:T(8,128)(2,1)} %convert_bitcast_fusion), kind=kOutput, calls=%fused_computation.25 | convolution fusion | flops 50593792 | bytes 2883584 | tf_op jit(solution)/shard_map/gau,sugc->sagc/dot_general | solution.py:101
  117.6 0.5 copy.64
  118.2 0.6 reshape.194
  118.8 0.6 multiply_reduce_fusion
  119.4 1.5 %collective-permute-start.7 = (f32[]{:T(128)}, f32[]{:T(128)}, u32[]{:S(2)}, u32[]{:S(2)}) collective-permute-start(f32[]{:T(128)} %multiply_reduce_fusion), channel_id=1, source_target_pairs={{0,2},{1,3},{2,0},{3,1},{4,6},{5,7},{6,4},{7,5},{8,10},{9,11},{10,... | collective-permute-start | bytes 20 | tf_op jit(solution)/shard_map/ppermute | solution.py:15
  120.9 0.6 collective-permute-start.8
  121.5 1.4 collective-permute-start.6
  122.9 0.2 copy.65
  123.1 0.2 copy.66
  123.4 0.9 copy.69
  124.2 0.8 copy.70
  125.3 0.2 copy.62
  125.6 0.9 copy.67
  126.4 0.8 copy.68
  129.9 4.4 %collective-permute-start.9 = (f32[]{:T(128)}, f32[]{:T(128)}, u32[]{:S(2)}, u32[]{:S(2)}) collective-permute-start(f32[]{:T(128)} %add.198), channel_id=1, source_target_pairs={{0,4},{1,5},{2,6},{3,7},{4,0},{5,1},{6,2},{7,3},{8,12},{9,13},{10,... | collective-permute-start | bytes 20 | tf_op jit(solution)/shard_map/ppermute | solution.py:15
  134.2 0.8 collective-permute-done.9
  135.7 0.6 broadcast_multiply_fusion
  (56 shorter events, 1.9 us)
Async XLA Ops:
  7.2 7.0 %copy-start = (bf16[64,128]{1,0:T(8,128)(2,1)S(1)}, bf16[64,128]{1,0:T(8,128)(2,1)}, u32[]{:S(2)}) copy-start(bf16[64,128]{1,0:T(8,128)(2,1)} %param.12) | copy-start | bytes 49156
  7.2 3.5 %copy-start.7 = (s32[32]{0:T(128)S(1)}, s32[32]{0:T(128)}, u32[]{:S(2)}) copy-start(s32[32]{0:T(128)} %param.13) | copy-start | bytes 388
  7.2 78.7 %all-gather.3.cloned.1.call-start = ((), (), s32[]{:S(2)}) async-start(), calls=%async_computation | async-start | bytes 8912896 | tf_op jit(solution)/shard_map/all_gather | solution.py:54
  91.2 0.9 copy-start.1
  96.0 11.9 %collective-permute-start = (f32[64,128]{1,0:T(8,128)S(1)}, f32[64,128]{1,0:T(8,128)S(1)}, u32[]{:S(2)}, u32[]{:S(2)}) collective-permute-start(f32[64,128]{1,0:T(8,128)S(1)} %fusion.28), channel_id=1, source_target_pairs={{0,8},{8,0},{16,24},{24,16},{32,40},{40,32},{48,56},{56,48},{64,72... | collective-permute-start | bytes 98312 | tf_op jit(solution)/shard_map/ppermute | solution.py:15
  96.3 11.6 %collective-permute-start.1 = (f32[64,128]{1,0:T(8,128)S(1)}, f32[64,128]{1,0:T(8,128)S(1)}, u32[]{:S(2)}, u32[]{:S(2)}) collective-permute-start(f32[64,128]{1,0:T(8,128)S(1)} %fusion.28), channel_id=1, source_target_pairs={{0,16},{8,24},{16,0},{24,8},{32,48},{40,56},{48,32},{56,40},{64,80... | collective-permute-start | bytes 98312 | tf_op jit(solution)/shard_map/ppermute | solution.py:15
  96.5 11.4 %collective-permute-start.2 = (f32[64,128]{1,0:T(8,128)S(1)}, f32[64,128]{1,0:T(8,128)S(1)}, u32[]{:S(2)}, u32[]{:S(2)}) collective-permute-start(f32[64,128]{1,0:T(8,128)S(1)} %fusion.28), channel_id=1, source_target_pairs={{0,24},{8,16},{16,8},{24,0},{32,56},{40,48},{48,40},{56,32},{64,88... | collective-permute-start | bytes 98312 | tf_op jit(solution)/shard_map/ppermute | solution.py:15
  101.9 1.3 copy-start.2
  108.0 10.8 %collective-permute-start.3 = (f32[64,128]{1,0:T(8,128)S(1)}, f32[64,128]{1,0:T(8,128)S(1)}, u32[]{:S(2)}, u32[]{:S(2)}) collective-permute-start(f32[64,128]{1,0:T(8,128)S(1)} %add_add_fusion.1), channel_id=1, source_target_pairs={{0,32},{8,40},{16,48},{24,56},{32,0},{40,8},{48,16},{56,24},{64,96... | collective-permute-start | bytes 98312 | tf_op jit(solution)/shard_map/ppermute | solution.py:15
  109.4 9.3 %collective-permute-start.4 = (f32[64,128]{1,0:T(8,128)S(1)}, f32[64,128]{1,0:T(8,128)S(1)}, u32[]{:S(2)}, u32[]{:S(2)}) collective-permute-start(f32[64,128]{1,0:T(8,128)S(1)} %add_add_fusion.1), channel_id=1, source_target_pairs={{0,64},{8,72},{16,80},{24,88},{32,96},{40,104},{48,112},{56,120},{... | collective-permute-start | bytes 98312 | tf_op jit(solution)/shard_map/ppermute | solution.py:15
  109.8 9.0 %collective-permute-start.5 = (f32[64,128]{1,0:T(8,128)S(1)}, f32[64,128]{1,0:T(8,128)S(1)}, u32[]{:S(2)}, u32[]{:S(2)}) collective-permute-start(f32[64,128]{1,0:T(8,128)S(1)} %add_add_fusion.1), channel_id=1, source_target_pairs={{0,96},{8,104},{16,112},{24,120},{32,64},{40,72},{48,80},{56,88},{... | collective-permute-start | bytes 98312 | tf_op jit(solution)/shard_map/ppermute | solution.py:15
  117.6 5.3 %copy-start.3 = (bf16[128,1024]{1,0:T(8,128)(2,1)S(1)}, bf16[128,1024]{1,0:T(8,128)(2,1)}, u32[]{:S(2)}) copy-start(bf16[128,1024]{1,0:T(8,128)(2,1)} %param.10) | copy-start | bytes 786436
  117.6 5.5 %copy-start.4 = (bf16[128,1024]{1,0:T(8,128)(2,1)S(1)}, bf16[128,1024]{1,0:T(8,128)(2,1)}, u32[]{:S(2)}) copy-start(bf16[128,1024]{1,0:T(8,128)(2,1)} %param.9) | copy-start | bytes 786436
  118.8 6.3 %copy-start.5 = (bf16[128,1024]{1,0:T(8,128)(2,1)S(1)}, bf16[128,1024]{1,0:T(8,128)(2,1)}, u32[]{:S(2)}) copy-start(bf16[128,1024]{1,0:T(8,128)(2,1)} %param.8) | copy-start | bytes 786436
  119.4 5.8 %copy-start.6 = (bf16[128,1024]{1,0:T(8,128)(2,1)S(1)}, bf16[128,1024]{1,0:T(8,128)(2,1)}, u32[]{:S(2)}) copy-start(bf16[128,1024]{1,0:T(8,128)(2,1)} %param.11) | copy-start | bytes 786436
  119.4 9.2 %collective-permute-start.7 = (f32[]{:T(128)}, f32[]{:T(128)}, u32[]{:S(2)}, u32[]{:S(2)}) collective-permute-start(f32[]{:T(128)} %multiply_reduce_fusion), channel_id=1, source_target_pairs={{0,2},{1,3},{2,0},{3,1},{4,6},{5,7},{6,4},{7,5},{8,10},{9,11},{10,... | collective-permute-start | bytes 20 | tf_op jit(solution)/shard_map/ppermute | solution.py:15
  120.9 7.7 %collective-permute-start.8 = (f32[]{:T(128)}, f32[]{:T(128)}, u32[]{:S(2)}, u32[]{:S(2)}) collective-permute-start(f32[]{:T(128)} %multiply_reduce_fusion), channel_id=1, source_target_pairs={{0,3},{1,2},{2,1},{3,0},{4,7},{5,6},{6,5},{7,4},{8,11},{9,10},{10,... | collective-permute-start | bytes 20 | tf_op jit(solution)/shard_map/ppermute | solution.py:15
  121.5 5.7 %collective-permute-start.6 = (f32[]{:T(128)}, f32[]{:T(128)}, u32[]{:S(2)}, u32[]{:S(2)}) collective-permute-start(f32[]{:T(128)} %multiply_reduce_fusion), channel_id=1, source_target_pairs={{0,1},{1,0},{2,3},{3,2},{4,5},{5,4},{6,7},{7,6},{8,9},{9,8},{10,11... | collective-permute-start | bytes 20 | tf_op jit(solution)/shard_map/ppermute | solution.py:15
  129.9 5.1 %collective-permute-start.9 = (f32[]{:T(128)}, f32[]{:T(128)}, u32[]{:S(2)}, u32[]{:S(2)}) collective-permute-start(f32[]{:T(128)} %add.198), channel_id=1, source_target_pairs={{0,4},{1,5},{2,6},{3,7},{4,0},{5,1},{6,2},{7,3},{8,12},{9,13},{10,... | collective-permute-start | bytes 20 | tf_op jit(solution)/shard_map/ppermute | solution.py:15
Sparse Core Ops, SparseCore 0:
  10.5 75.3 all-gather.2

commit v13 on v11

--- a/solution.py
+++ b/solution.py
@@ -15,16 +15,16 @@
     return lax.ppermute(value, axis, [(i, i ^ mask) for i in range(size)])
 
 
-def radix_round(value, axis, bit):
-    if bit * 4 <= lax.axis_size(axis):
-        return (value + swap(value, axis, bit)) + (swap(value, axis, 2 * bit) + swap(value, axis, 3 * bit)), bit * 4
-    return value + swap(value, axis, bit), bit * 2
+def radix_round(value, axis, low, high=None):
+    if high is None:
+        return value + swap(value, axis, 1 << low)
+    one, two = 1 << low, 1 << high
+    return (value + swap(value, axis, one)) + (swap(value, axis, two) + swap(value, axis, one | two))
 
 
-def butterfly_sum(value, axis):
-    bit = 1
-    while bit < lax.axis_size(axis):
-        value, bit = radix_round(value, axis, bit)
+def butterfly_sum(value, axis, rounds):
+    for bits in rounds:
+        value = radix_round(value, axis, *bits)
     return value
 
 
@@ -89,22 +89,24 @@
     corr = jnp.einsum(
         "sagc,swgc->gaw", own_gated_g, mixed_window, preferred_element_type=jnp.float32
     )
+    corr_high = corr.astype(jnp.bfloat16)
+    corr_low = (corr - corr_high.astype(jnp.float32)).astype(jnp.bfloat16)
     partial_grad = jnp.einsum(
-        "gaw,jaw->gj", corr, select_fwd.astype(jnp.float32), precision=lax.Precision.HIGH
-    )
-    total_grad, bit = radix_round(partial_grad, "seq", 1)
+        "gaw,jaw->gj", corr_high, select_fwd, preferred_element_type=jnp.float32
+    ) + jnp.einsum("gaw,jaw->gj", corr_low, select_fwd, preferred_element_type=jnp.float32)
+    seq_rounds = ((0, 3), (1, 2))
+    total_grad = radix_round(partial_grad, "seq", *seq_rounds[0])
     total_grad, late_blocks = lax.optimization_barrier((total_grad, blocks))
     gated_window = jnp.concatenate(
         [own_gated, pick(late_blocks, 1, after).reshape(per_device, lead, channels)], axis=1
     ).reshape(per_device, window, groups, group_size)
     adjoint = jnp.einsum("gau,sugc->sagc", bwd_band, gated_window, preferred_element_type=jnp.float32)
     dmixed = adjoint.reshape(rows, channels).astype(jnp.bfloat16)
-    while bit < devices:
-        total_grad, bit = radix_round(total_grad, "seq", bit)
+    total_grad = butterfly_sum(total_grad, "seq", seq_rounds[1:])
     total_grad, late_query, late_key, late_value, late_grad = lax.optimization_barrier(
         (total_grad, query_rows, key_rows, value_rows, grad_rows)
     )
-    squares = butterfly_sum(jnp.sum(total_grad * total_grad), "chan")
+    squares = butterfly_sum(jnp.sum(total_grad * total_grad), "chan", ((1, 2), (0,)))
     limit = math.sqrt(groups * lax.axis_size("chan") * taps)
     factor = jnp.minimum(1.0, limit / jnp.sqrt(squares + 1e-06))
     filter_grad = factor * total_grad

time: 141 us -> 142 us (level)
  matrix products: 15.7 us -> 17.8 us
    dot_general x1 -> x2, matrix products: 3.92 us -> 5.97 us  [the longest x1 2.99 us: shards(): jnp.einsum('gaw,jaw->gj', corr_low, select_fwd, preferred_element_type=jn...]
where the time goes in v13:
time: 142 us
  waiting for transfers between devices  65.8 us (46%)
  local copies, waits for them, and re-layouts  20.1 us (14%)
  matrix products  17.8 us (13%)
  between operations  17.7 us (12%)
  starting transfers between devices  15.1 us (11%)
  other arithmetic  5.24 us (4%)
    all_gather x1, waiting for transfers between devices, shards(): lax.all_gather(jnp.stack([mixed, gated]), 'seq', axis=0, tiled=False)  64.9 us
    ppermute x10, starting transfers between devices, swap(): return lax.ppermute(value, axis, [(i, i ^ mask) for i in range(size)])  15.1 us
    gather x2, local copies, waits for them, and re-layouts, pick(): jnp.take(blocks, slots, axis=0)  7.92 us
    dot_general x1, matrix products, shards(): jnp.einsum('gj,jaw->gaw', filters, select_fwd, preferred_element_type=jnp...  3.54 us
    unnamed x18, local copies, waits for them, and re-layouts  3.43 us
    dot_general x1, matrix products, shards(): jnp.einsum('gj,jau->gau', filters, _bwd_select(taps, span_rows, window),...  3.24 us
    dot_general x1, matrix products, shards(): jnp.einsum('gaw,jaw->gj', corr_low, select_fwd, preferred_element_type=jn...  2.99 us
    dot_general x1, matrix products, shards(): jnp.einsum('gaw,jaw->gj', corr_high, select_fwd, preferred_element_type=j...  2.98 us
  transfers between devices with their start and end apart: 11, of which 2 were waited for; matrix products, arithmetic and copies ran while one was open for 19% of the time, Pallas kernels for 0%

profile of v13, /device:TPU:0, one launch (start us, length us, event | category | flops | bytes accessed | tf_op | source)
XLA Modules:
  0.0 141.8 jit_solution(7837083753137746138)
XLA Ops:
  7.2 1.1 multiply_convert_fusion.4
  8.3 1.1 multiply_convert_fusion.5
  9.4 0.9 pad_maximum_fusion.3
  10.4 0.2 copy.58
  10.5 0.2 copy.55
  11.2 0.2 concatenate.10
  11.6 0.2 reshape_reshape.3
  11.9 0.7 scatter_custom_fusion
  12.6 0.6 gather_fusion
  13.2 0.6 gather_fusion.1
  14.2 3.2 %convert_bitcast_fusion = bf16[64,64,192,1]{2,0,1,3:T(8,128)(2,1)} fusion(bf16[64,128]{1,0:T(8,128)(2,1)S(1)} %copy-done), kind=kOutput, calls=%fused_computation.23 | convolution fusion | flops 205258752 | bytes 1589248 | tf_op jit(solution)/shard_map/gj,jau->gau/dot_general | solution.py:81
  17.4 3.5 %convert_bitcast_fusion.1 = bf16[64,64,192,1]{2,0,1,3:T(8,128)(2,1)} fusion(s32[64]{0:T(128)S(1)} %iota_add_fusion, bf16[64,128]{1,0:T(8,128)(2,1)S(1)} %copy-done), kind=kOutput, calls=%fused_computation.24 | convolution fusion | flops 205258752 | bytes 1589504 | tf_op jit(solution)/shard_map/gj,jaw->gaw/dot_general | solution.py:78
  21.0 64.9 %all-gather.3.cloned.1.call-done = bf16[32,128,1024]{2,1,0:T(8,128)(2,1)} async-done(((bf16[2,128,1024]{2,1,0:T(8,128)(2,1)}), bf16[32,128,1024]{2,1,0:T(8,128)(2,1)}) %all-gather.3.cloned.1.call-update) | async-done | bytes 8388624 | tf_op jit(solution)/shard_map/all_gather | solution.py:54
  85.9 4.0 %gather_fusion.2 = bf16[4,64,1024]{2,1,0:T(8,128)(2,1)S(1)} fusion(bf16[64,64,1024]{2,1,0:T(8,128)(2,1)} %bitcast.51, s32[1024]{0:T(1024)S(1)} %pad_clamp_fusion.2), kind=kCustom, calls=%fused_computation.clone | custom fusion | bytes 1048592 | tf_op jit(solution)/shard_map/jit(_take)/gather | solution.py:67
  90.0 0.7 copy.56
  90.7 0.5 reshape.190
  91.2 0.8 fusion.4
  92.0 3.0 %fusion.32 = f32[64,128]{1,0:T(8,128)S(1)} fusion(s32[64]{0:T(128)S(1)} %iota_add_fusion, bf16[64,64,192]{2,1,0:T(8,128)(2,1)S(1)} %get-tuple-element.38), kind=kOutput, calls=%fused_computation.31 | convolution fusion | flops 204472320 | bytes 1605888 | tf_op jit(solution)/shard_map/gaw,jaw->gj/dot_general | solution.py:94
  95.0 3.0 %fusion.38 = f32[64,128]{1,0:T(8,128)S(1)} fusion(f32[64,128]{1,0:T(8,128)S(1)} %fusion.32, s32[64]{0:T(128)S(1)} %iota_add_fusion, bf16[64,64,192]{2,1,0:T(8,128)(2,1)S(1)} %get-tuple-element.37), kind=kOutput, calls=%fused_computation.33 | convolution fusion | flops 204480512 | bytes 1638656 | tf_op jit(solution)/shard_map/gaw,jaw->gj/dot_general | solution.py:96
  98.0 0.3 collective-permute-start
  98.3 0.4 collective-permute-start.1
  98.7 2.7 %collective-permute-start.2 = (f32[64,128]{1,0:T(8,128)S(1)}, f32[64,128]{1,0:T(8,128)S(1)}, u32[]{:S(2)}, u32[]{:S(2)}) collective-permute-start(f32[64,128]{1,0:T(8,128)S(1)} %fusion.38), channel_id=1, source_target_pairs={{0,72},{8,64},{16,88},{24,80},{32,104},{40,96},{48,120},{56,112},{... | collective-permute-start | bytes 98312 | tf_op jit(solution)/shard_map/ppermute | solution.py:15
  101.5 1.3 fusion.20
  102.8 0.5 copy.65
  103.4 0.6 reshape.193
  104.0 0.3 collective-permute-start.3
  104.2 2.3 %collective-permute-start.4 = (f32[64,128]{1,0:T(8,128)S(1)}, f32[64,128]{1,0:T(8,128)S(1)}, u32[]{:S(2)}, u32[]{:S(2)}) collective-permute-start(f32[64,128]{1,0:T(8,128)S(1)} %add_add_fusion.1), channel_id=1, source_target_pairs={{0,32},{8,40},{16,48},{24,56},{32,0},{40,8},{48,16},{56,24},{64,96... | collective-permute-start | bytes 98312 | tf_op jit(solution)/shard_map/ppermute | solution.py:15
  106.5 2.2 %collective-permute-start.5 = (f32[64,128]{1,0:T(8,128)S(1)}, f32[64,128]{1,0:T(8,128)S(1)}, u32[]{:S(2)}, u32[]{:S(2)}) collective-permute-start(f32[64,128]{1,0:T(8,128)S(1)} %add_add_fusion.1), channel_id=1, source_target_pairs={{0,48},{8,56},{16,32},{24,40},{32,16},{40,24},{48,0},{56,8},{64,11... | collective-permute-start | bytes 98312 | tf_op jit(solution)/shard_map/ppermute | solution.py:15
  108.8 4.0 %gather_fusion.3 = bf16[4,64,1024]{2,1,0:T(8,128)(2,1)S(1)} fusion(bf16[64,64,1024]{2,1,0:T(8,128)(2,1)} %bitcast.52, s32[1024]{0:T(1024)S(1)} %pad_clamp_fusion), kind=kCustom, calls=%fused_computation.1.clone | custom fusion | bytes 1048592 | tf_op jit(solution)/shard_map/jit(_take)/gather | solution.py:67
  112.9 0.7 copy.67
  113.6 0.5 reshape.192
  114.1 3.0 %fusion.29 = f32[2,64,64,16]{1,3,0,2:T(8,128)S(1)} fusion(bf16[64,64,192,1]{2,0,1,3:T(8,128)(2,1)} %convert_bitcast_fusion, bf16[2,128,64,16]{1,3,0,2:T(8,128)(2,1)S(1)} %copy_select_fusion, bf16[2,64,64,16]{1,3,0,2:T(8,128)(2,1)S(1)} %copy.60), kind=kOutput, calls=%fused_computation.30 | convolution fusion | flops 52166656 | bytes 2883584 | tf_op jit(solution)/shard_map/gau,sugc->sagc/dot_general | solution.py:103
  117.1 0.5 copy.71
  117.7 0.6 reshape.194
  118.3 0.6 multiply_reduce_fusion
  118.9 3.0 %collective-permute-start.7 = (f32[]{:T(128)}, f32[]{:T(128)}, u32[]{:S(2)}, u32[]{:S(2)}) collective-permute-start(f32[]{:T(128)} %multiply_reduce_fusion), channel_id=1, source_target_pairs={{0,4},{1,5},{2,6},{3,7},{4,0},{5,1},{6,2},{7,3},{8,12},{9,13},{10,... | collective-permute-start | bytes 20 | tf_op jit(solution)/shard_map/ppermute | solution.py:15
  121.9 1.2 collective-permute-start.8
  123.1 0.2 copy.72
  123.2 0.2 copy.73
  123.5 0.9 copy.76
  124.4 0.8 copy.77
  125.2 0.2 copy.63
  125.4 0.2 copy.66
  125.7 0.9 copy.74
  126.6 0.8 copy.75
  130.0 2.7 %collective-permute-start.9 = (f32[]{:T(128)}, f32[]{:T(128)}, u32[]{:S(2)}, u32[]{:S(2)}) collective-permute-start(f32[]{:T(128)} %add.204), channel_id=1, source_target_pairs={{0,1},{1,0},{2,3},{3,2},{4,5},{5,4},{6,7},{7,6},{8,9},{9,8},{10,11... | collective-permute-start | bytes 20 | tf_op jit(solution)/shard_map/ppermute | solution.py:15
  132.7 0.9 collective-permute-done.9
  134.3 0.6 broadcast_multiply_fusion
  (54 shorter events, 1.7 us)
Async XLA Ops:
  7.2 7.0 %copy-start = (bf16[64,128]{1,0:T(8,128)(2,1)S(1)}, bf16[64,128]{1,0:T(8,128)(2,1)}, u32[]{:S(2)}) copy-start(bf16[64,128]{1,0:T(8,128)(2,1)} %param.12) | copy-start | bytes 49156
  7.2 3.5 %copy-start.5 = (s32[32]{0:T(128)S(1)}, s32[32]{0:T(128)}, u32[]{:S(2)}) copy-start(s32[32]{0:T(128)} %param.13) | copy-start | bytes 388
  7.2 78.7 %all-gather.3.cloned.1.call-start = ((), (), s32[]{:S(2)}) async-start(), calls=%async_computation | async-start | bytes 8912896 | tf_op jit(solution)/shard_map/all_gather | solution.py:54
  95.0 6.5 %copy-start.6 = (bf16[64,64,192,1]{2,0,1,3:T(8,128)(2,1)S(1)}, bf16[64,64,192,1]{2,0,1,3:T(8,128)(2,1)}, u32[]{:S(2)}) copy-start(bf16[64,64,192,1]{2,0,1,3:T(8,128)(2,1)} %convert_bitcast_fusion.1) | copy-start | bytes 4718596
  98.0 5.9 %collective-permute-start = (f32[64,128]{1,0:T(8,128)S(1)}, f32[64,128]{1,0:T(8,128)S(1)}, u32[]{:S(2)}, u32[]{:S(2)}) collective-permute-start(f32[64,128]{1,0:T(8,128)S(1)} %fusion.38), channel_id=1, source_target_pairs={{0,8},{8,0},{16,24},{24,16},{32,40},{40,32},{48,56},{56,48},{64,72... | collective-permute-start | bytes 98312 | tf_op jit(solution)/shard_map/ppermute | solution.py:15
  98.3 5.6 %collective-permute-start.1 = (f32[64,128]{1,0:T(8,128)S(1)}, f32[64,128]{1,0:T(8,128)S(1)}, u32[]{:S(2)}, u32[]{:S(2)}) collective-permute-start(f32[64,128]{1,0:T(8,128)S(1)} %fusion.38), channel_id=1, source_target_pairs={{0,64},{8,72},{16,80},{24,88},{32,96},{40,104},{48,112},{56,120},{... | collective-permute-start | bytes 98312 | tf_op jit(solution)/shard_map/ppermute | solution.py:15
  98.7 5.2 %collective-permute-start.2 = (f32[64,128]{1,0:T(8,128)S(1)}, f32[64,128]{1,0:T(8,128)S(1)}, u32[]{:S(2)}, u32[]{:S(2)}) collective-permute-start(f32[64,128]{1,0:T(8,128)S(1)} %fusion.38), channel_id=1, source_target_pairs={{0,72},{8,64},{16,88},{24,80},{32,104},{40,96},{48,120},{56,112},{... | collective-permute-start | bytes 98312 | tf_op jit(solution)/shard_map/ppermute | solution.py:15
  104.0 14.3 %collective-permute-start.3 = (f32[64,128]{1,0:T(8,128)S(1)}, f32[64,128]{1,0:T(8,128)S(1)}, u32[]{:S(2)}, u32[]{:S(2)}) collective-permute-start(f32[64,128]{1,0:T(8,128)S(1)} %add_add_fusion.1), channel_id=1, source_target_pairs={{0,16},{8,24},{16,0},{24,8},{32,48},{40,56},{48,32},{56,40},{64,80... | collective-permute-start | bytes 98312 | tf_op jit(solution)/shard_map/ppermute | solution.py:15
  104.2 14.0 %collective-permute-start.4 = (f32[64,128]{1,0:T(8,128)S(1)}, f32[64,128]{1,0:T(8,128)S(1)}, u32[]{:S(2)}, u32[]{:S(2)}) collective-permute-start(f32[64,128]{1,0:T(8,128)S(1)} %add_add_fusion.1), channel_id=1, source_target_pairs={{0,32},{8,40},{16,48},{24,56},{32,0},{40,8},{48,16},{56,24},{64,96... | collective-permute-start | bytes 98312 | tf_op jit(solution)/shard_map/ppermute | solution.py:15
  106.5 11.8 %collective-permute-start.5 = (f32[64,128]{1,0:T(8,128)S(1)}, f32[64,128]{1,0:T(8,128)S(1)}, u32[]{:S(2)}, u32[]{:S(2)}) collective-permute-start(f32[64,128]{1,0:T(8,128)S(1)} %add_add_fusion.1), channel_id=1, source_target_pairs={{0,48},{8,56},{16,32},{24,40},{32,16},{40,24},{48,0},{56,8},{64,11... | collective-permute-start | bytes 98312 | tf_op jit(solution)/shard_map/ppermute | solution.py:15
  117.1 6.0 %copy-start.1 = (bf16[128,1024]{1,0:T(8,128)(2,1)S(1)}, bf16[128,1024]{1,0:T(8,128)(2,1)}, u32[]{:S(2)}) copy-start(bf16[128,1024]{1,0:T(8,128)(2,1)} %param.10) | copy-start | bytes 786436
  117.1 6.1 %copy-start.2 = (bf16[128,1024]{1,0:T(8,128)(2,1)S(1)}, bf16[128,1024]{1,0:T(8,128)(2,1)}, u32[]{:S(2)}) copy-start(bf16[128,1024]{1,0:T(8,128)(2,1)} %param.9) | copy-start | bytes 786436
  118.2 7.0 %copy-start.3 = (bf16[128,1024]{1,0:T(8,128)(2,1)S(1)}, bf16[128,1024]{1,0:T(8,128)(2,1)}, u32[]{:S(2)}) copy-start(bf16[128,1024]{1,0:T(8,128)(2,1)} %param.8) | copy-start | bytes 786436
  118.9 6.5 %copy-start.4 = (bf16[128,1024]{1,0:T(8,128)(2,1)S(1)}, bf16[128,1024]{1,0:T(8,128)(2,1)}, u32[]{:S(2)}) copy-start(bf16[128,1024]{1,0:T(8,128)(2,1)} %param.11) | copy-start | bytes 786436
  118.9 9.8 %collective-permute-start.7 = (f32[]{:T(128)}, f32[]{:T(128)}, u32[]{:S(2)}, u32[]{:S(2)}) collective-permute-start(f32[]{:T(128)} %multiply_reduce_fusion), channel_id=1, source_target_pairs={{0,4},{1,5},{2,6},{3,7},{4,0},{5,1},{6,2},{7,3},{8,12},{9,13},{10,... | collective-permute-start | bytes 20 | tf_op jit(solution)/shard_map/ppermute | solution.py:15
  121.9 6.9 %collective-permute-start.8 = (f32[]{:T(128)}, f32[]{:T(128)}, u32[]{:S(2)}, u32[]{:S(2)}) collective-permute-start(f32[]{:T(128)} %multiply_reduce_fusion), channel_id=1, source_target_pairs={{0,6},{1,7},{2,4},{3,5},{4,2},{5,3},{6,0},{7,1},{8,14},{9,15},{10,... | collective-permute-start | bytes 20 | tf_op jit(solution)/shard_map/ppermute | solution.py:15
  123.1 4.4 %collective-permute-start.6 = (f32[]{:T(128)}, f32[]{:T(128)}, u32[]{:S(2)}, u32[]{:S(2)}) collective-permute-start(f32[]{:T(128)} %multiply_reduce_fusion), channel_id=1, source_target_pairs={{0,2},{1,3},{2,0},{3,1},{4,6},{5,7},{6,4},{7,5},{8,10},{9,11},{10,... | collective-permute-start | bytes 20 | tf_op jit(solution)/shard_map/ppermute | solution.py:15
  130.0 3.6 %collective-permute-start.9 = (f32[]{:T(128)}, f32[]{:T(128)}, u32[]{:S(2)}, u32[]{:S(2)}) collective-permute-start(f32[]{:T(128)} %add.204), channel_id=1, source_target_pairs={{0,1},{1,0},{2,3},{3,2},{4,5},{5,4},{6,7},{7,6},{8,9},{9,8},{10,11... | collective-permute-start | bytes 20 | tf_op jit(solution)/shard_map/ppermute | solution.py:15
Sparse Core Ops, SparseCore 0:
  10.5 75.3 all-gather.2

commit v14 on v13

--- a/solution.py
+++ b/solution.py
@@ -89,23 +89,21 @@
     corr = jnp.einsum(
         "sagc,swgc->gaw", own_gated_g, mixed_window, preferred_element_type=jnp.float32
     )
-    corr_high = corr.astype(jnp.bfloat16)
-    corr_low = (corr - corr_high.astype(jnp.float32)).astype(jnp.bfloat16)
     partial_grad = jnp.einsum(
-        "gaw,jaw->gj", corr_high, select_fwd, preferred_element_type=jnp.float32
-    ) + jnp.einsum("gaw,jaw->gj", corr_low, select_fwd, preferred_element_type=jnp.float32)
+        "gaw,jaw->gj", corr, select_fwd.astype(jnp.float32), precision=lax.Precision.HIGH
+    )
     seq_rounds = ((0, 3), (1, 2))
     total_grad = radix_round(partial_grad, "seq", *seq_rounds[0])
     total_grad, late_blocks = lax.optimization_barrier((total_grad, blocks))
     gated_window = jnp.concatenate(
         [own_gated, pick(late_blocks, 1, after).reshape(per_device, lead, channels)], axis=1
     ).reshape(per_device, window, groups, group_size)
+    total_grad = butterfly_sum(total_grad, "seq", seq_rounds[1:])
+    total_grad, gated_window, late_query, late_key, late_value, late_grad = lax.optimization_barrier(
+        (total_grad, gated_window, query_rows, key_rows, value_rows, grad_rows)
+    )
     adjoint = jnp.einsum("gau,sugc->sagc", bwd_band, gated_window, preferred_element_type=jnp.float32)
     dmixed = adjoint.reshape(rows, channels).astype(jnp.bfloat16)
-    total_grad = butterfly_sum(total_grad, "seq", seq_rounds[1:])
-    total_grad, late_query, late_key, late_value, late_grad = lax.optimization_barrier(
-        (total_grad, query_rows, key_rows, value_rows, grad_rows)
-    )
     squares = butterfly_sum(jnp.sum(total_grad * total_grad), "chan", ((1, 2), (0,)))
     limit = math.sqrt(groups * lax.axis_size("chan") * taps)
     factor = jnp.minimum(1.0, limit / jnp.sqrt(squares + 1e-06))

time: 142 us -> 139 us (0.979)
  matrix products: 17.8 us -> 14.3 us
    dot_general x2 -> x1, matrix products: 5.97 us -> 3.92 us  [shards(): jnp.einsum('gaw,jaw->gj', corr, select_fwd.astype(jnp.float32), precision...]
    dot_general x1, matrix products: 2.95 us -> 1.49 us  [shards(): jnp.einsum('gau,sugc->sagc', bwd_band, gated_window, preferred_element_ty...]
    unnamed x18 -> x20, local copies, waits for them, and re-layouts: 3.43 us -> 3.44 us
where the time goes in v14:
time: 139 us
  waiting for transfers between devices  65.8 us (47%)
  local copies, waits for them, and re-layouts  20.1 us (14%)
  between operations  17.7 us (13%)
  starting transfers between devices  15.1 us (11%)
  matrix products  14.3 us (10%)
  other arithmetic  5.74 us (4%)
    all_gather x1, waiting for transfers between devices, shards(): lax.all_gather(jnp.stack([mixed, gated]), 'seq', axis=0, tiled=False)  64.9 us
    ppermute x10, starting transfers between devices, swap(): return lax.ppermute(value, axis, [(i, i ^ mask) for i in range(size)])  15.1 us
    gather x2, local copies, waits for them, and re-layouts, pick(): jnp.take(blocks, slots, axis=0)  7.92 us
    dot_general x1, matrix products, shards(): jnp.einsum('gaw,jaw->gj', corr, select_fwd.astype(jnp.float32), precision...  3.92 us
    dot_general x1, matrix products, shards(): jnp.einsum('gj,jaw->gaw', filters, select_fwd, preferred_element_type=jnp...  3.54 us
    unnamed x20, local copies, waits for them, and re-layouts  3.44 us
    dot_general x1, matrix products, shards(): jnp.einsum('gj,jau->gau', filters, _bwd_select(taps, span_rows, window),...  3.24 us
  transfers between devices with their start and end apart: 11, of which 2 were waited for; matrix products, arithmetic and copies ran while one was open for 19% of the time, Pallas kernels for 0%

profile of v14, /device:TPU:0, one launch (start us, length us, event | category | flops | bytes accessed | tf_op | source)
XLA Modules:
  0.0 138.8 jit_solution(6629380260283093949)
XLA Ops:
  7.2 1.1 multiply_convert_fusion.4
  8.3 1.1 multiply_convert_fusion.5
  9.4 0.9 pad_maximum_fusion.4
  10.4 0.2 copy.52
  10.5 0.2 copy.49
  11.2 0.2 concatenate.10
  11.6 0.2 reshape_reshape.3
  11.9 0.7 scatter_custom_fusion
  12.6 0.6 gather_fusion
  13.2 0.6 gather_fusion.1
  14.2 3.2 %convert_bitcast_fusion = bf16[64,64,192,1]{2,0,1,3:T(8,128)(2,1)} fusion(bf16[64,128]{1,0:T(8,128)(2,1)S(1)} %copy-done), kind=kOutput, calls=%fused_computation.18 | convolution fusion | flops 205258752 | bytes 1589248 | tf_op jit(solution)/shard_map/gj,jau->gau/dot_general | solution.py:81
  17.4 3.5 %convert_bitcast_fusion.1 = bf16[64,64,192,1]{2,0,1,3:T(8,128)(2,1)} fusion(s32[64]{0:T(128)S(1)} %iota_add_fusion, bf16[64,128]{1,0:T(8,128)(2,1)S(1)} %copy-done), kind=kOutput, calls=%fused_computation.19 | convolution fusion | flops 205258752 | bytes 1589504 | tf_op jit(solution)/shard_map/gj,jaw->gaw/dot_general | solution.py:78
  21.0 64.9 %all-gather.3.cloned.1.call-done = bf16[32,128,1024]{2,1,0:T(8,128)(2,1)} async-done(((bf16[2,128,1024]{2,1,0:T(8,128)(2,1)}), bf16[32,128,1024]{2,1,0:T(8,128)(2,1)}) %all-gather.3.cloned.1.call-update) | async-done | bytes 8388624 | tf_op jit(solution)/shard_map/all_gather | solution.py:54
  85.9 4.0 %gather_fusion.2 = bf16[4,64,1024]{2,1,0:T(8,128)(2,1)S(1)} fusion(bf16[64,64,1024]{2,1,0:T(8,128)(2,1)} %bitcast.44, s32[1024]{0:T(1024)S(1)} %pad_clamp_fusion.2), kind=kCustom, calls=%fused_computation.clone | custom fusion | bytes 1048592 | tf_op jit(solution)/shard_map/jit(_take)/gather | solution.py:67
  90.0 0.7 copy.50
  90.7 0.5 reshape.190
  91.2 0.8 convolution_bitcast_fusion
  92.0 3.9 %fusion.28 = f32[64,128]{1,0:T(8,128)S(1)} fusion(s32[64]{0:T(128)S(1)} %iota_add_fusion, f32[64,64,192]{2,1,0:T(8,128)S(1)} %convolution_bitcast_fusion), kind=kOutput, calls=%fused_computation.26 | convolution fusion | flops 607125504 | bytes 3178752 | tf_op jit(solution)/shard_map/gaw,jaw->gj/dot_general | solution.py:92
  96.0 0.3 collective-permute-start
  96.3 0.4 collective-permute-start.1
  96.7 2.7 %collective-permute-start.2 = (f32[64,128]{1,0:T(8,128)S(1)}, f32[64,128]{1,0:T(8,128)S(1)}, u32[]{:S(2)}, u32[]{:S(2)}) collective-permute-start(f32[64,128]{1,0:T(8,128)S(1)} %fusion.28), channel_id=1, source_target_pairs={{0,72},{8,64},{16,88},{24,80},{32,104},{40,96},{48,120},{56,112},{... | collective-permute-start | bytes 98312 | tf_op jit(solution)/shard_map/ppermute | solution.py:15
  99.4 1.3 fusion.16
  100.7 0.5 copy.61
  101.3 0.6 reshape.193
  101.9 0.3 collective-permute-start.3
  102.2 2.3 %collective-permute-start.4 = (f32[64,128]{1,0:T(8,128)S(1)}, f32[64,128]{1,0:T(8,128)S(1)}, u32[]{:S(2)}, u32[]{:S(2)}) collective-permute-start(f32[64,128]{1,0:T(8,128)S(1)} %add_add_fusion.1), channel_id=1, source_target_pairs={{0,32},{8,40},{16,48},{24,56},{32,0},{40,8},{48,16},{56,24},{64,96... | collective-permute-start | bytes 98312 | tf_op jit(solution)/shard_map/ppermute | solution.py:15
  104.5 2.2 %collective-permute-start.5 = (f32[64,128]{1,0:T(8,128)S(1)}, f32[64,128]{1,0:T(8,128)S(1)}, u32[]{:S(2)}, u32[]{:S(2)}) collective-permute-start(f32[64,128]{1,0:T(8,128)S(1)} %add_add_fusion.1), channel_id=1, source_target_pairs={{0,48},{8,56},{16,32},{24,40},{32,16},{40,24},{48,0},{56,8},{64,11... | collective-permute-start | bytes 98312 | tf_op jit(solution)/shard_map/ppermute | solution.py:15
  106.7 4.0 %gather_fusion.3 = bf16[4,64,1024]{2,1,0:T(8,128)(2,1)S(1)} fusion(bf16[64,64,1024]{2,1,0:T(8,128)(2,1)} %bitcast.45, s32[1024]{0:T(1024)S(1)} %pad_clamp_fusion), kind=kCustom, calls=%fused_computation.1.clone | custom fusion | bytes 1048592 | tf_op jit(solution)/shard_map/jit(_take)/gather | solution.py:67
  110.8 0.7 copy.56
  111.5 0.5 reshape.192
  112.1 0.5 pad_maximum_fusion.1
  112.6 0.6 multiply_reduce_fusion
  113.2 3.0 %collective-permute-start.7 = (f32[]{:T(128)}, f32[]{:T(128)}, u32[]{:S(2)}, u32[]{:S(2)}) collective-permute-start(f32[]{:T(128)} %multiply_reduce_fusion), channel_id=1, source_target_pairs={{0,4},{1,5},{2,6},{3,7},{4,0},{5,1},{6,2},{7,3},{8,12},{9,13},{10,... | collective-permute-start | bytes 20 | tf_op jit(solution)/shard_map/ppermute | solution.py:15
  116.2 1.2 collective-permute-start.8
  117.4 1.5 %fusion.25 = f32[2,64,64,16]{1,3,0,2:T(8,128)S(1)} fusion(bf16[2,192,64,16]{1,3,0,2:T(8,128)(2,1)S(1)} %pad_maximum_fusion.1, bf16[64,64,192,1]{2,0,1,3:T(8,128)(2,1)S(1)} %copy-done.1), kind=kOutput, calls=%fused_computation.25 | convolution fusion | flops 50593792 | bytes 2883584 | tf_op jit(solution)/shard_map/gau,sugc->sagc/dot_general | solution.py:105
  118.9 0.5 copy.64
  119.4 0.6 reshape.194
  120.1 0.2 copy.65
  120.2 0.2 copy.66
  120.5 0.9 copy.69
  121.4 0.8 copy.70
  122.2 0.2 copy.59
  122.4 0.2 copy.62
  122.7 0.9 copy.67
  123.6 0.8 copy.68
  127.0 2.7 %collective-permute-start.9 = (f32[]{:T(128)}, f32[]{:T(128)}, u32[]{:S(2)}, u32[]{:S(2)}) collective-permute-start(f32[]{:T(128)} %add.198), channel_id=1, source_target_pairs={{0,1},{1,0},{2,3},{3,2},{4,5},{5,4},{6,7},{7,6},{8,9},{9,8},{10,11... | collective-permute-start | bytes 20 | tf_op jit(solution)/shard_map/ppermute | solution.py:15
  129.7 0.9 collective-permute-done.9
  131.3 0.6 broadcast_multiply_fusion
  (56 shorter events, 1.7 us)
Async XLA Ops:
  7.2 7.0 %copy-start = (bf16[64,128]{1,0:T(8,128)(2,1)S(1)}, bf16[64,128]{1,0:T(8,128)(2,1)}, u32[]{:S(2)}) copy-start(bf16[64,128]{1,0:T(8,128)(2,1)} %param.12) | copy-start | bytes 49156
  7.2 3.5 %copy-start.6 = (s32[32]{0:T(128)S(1)}, s32[32]{0:T(128)}, u32[]{:S(2)}) copy-start(s32[32]{0:T(128)} %param.13) | copy-start | bytes 388
  7.2 78.7 %all-gather.3.cloned.1.call-start = ((), (), s32[]{:S(2)}) async-start(), calls=%async_computation | async-start | bytes 8912896 | tf_op jit(solution)/shard_map/all_gather | solution.py:54
  92.0 7.4 %copy-start.7 = (bf16[64,64,192,1]{2,0,1,3:T(8,128)(2,1)S(1)}, bf16[64,64,192,1]{2,0,1,3:T(8,128)(2,1)}, u32[]{:S(2)}) copy-start(bf16[64,64,192,1]{2,0,1,3:T(8,128)(2,1)} %convert_bitcast_fusion.1) | copy-start | bytes 4718596
  96.0 5.9 %collective-permute-start = (f32[64,128]{1,0:T(8,128)S(1)}, f32[64,128]{1,0:T(8,128)S(1)}, u32[]{:S(2)}, u32[]{:S(2)}) collective-permute-start(f32[64,128]{1,0:T(8,128)S(1)} %fusion.28), channel_id=1, source_target_pairs={{0,8},{8,0},{16,24},{24,16},{32,40},{40,32},{48,56},{56,48},{64,72... | collective-permute-start | bytes 98312 | tf_op jit(solution)/shard_map/ppermute | solution.py:15
  96.3 5.6 %collective-permute-start.1 = (f32[64,128]{1,0:T(8,128)S(1)}, f32[64,128]{1,0:T(8,128)S(1)}, u32[]{:S(2)}, u32[]{:S(2)}) collective-permute-start(f32[64,128]{1,0:T(8,128)S(1)} %fusion.28), channel_id=1, source_target_pairs={{0,64},{8,72},{16,80},{24,88},{32,96},{40,104},{48,112},{56,120},{... | collective-permute-start | bytes 98312 | tf_op jit(solution)/shard_map/ppermute | solution.py:15
  96.7 5.2 %collective-permute-start.2 = (f32[64,128]{1,0:T(8,128)S(1)}, f32[64,128]{1,0:T(8,128)S(1)}, u32[]{:S(2)}, u32[]{:S(2)}) collective-permute-start(f32[64,128]{1,0:T(8,128)S(1)} %fusion.28), channel_id=1, source_target_pairs={{0,72},{8,64},{16,88},{24,80},{32,104},{40,96},{48,120},{56,112},{... | collective-permute-start | bytes 98312 | tf_op jit(solution)/shard_map/ppermute | solution.py:15
  101.9 10.7 %collective-permute-start.3 = (f32[64,128]{1,0:T(8,128)S(1)}, f32[64,128]{1,0:T(8,128)S(1)}, u32[]{:S(2)}, u32[]{:S(2)}) collective-permute-start(f32[64,128]{1,0:T(8,128)S(1)} %add_add_fusion.1), channel_id=1, source_target_pairs={{0,16},{8,24},{16,0},{24,8},{32,48},{40,56},{48,32},{56,40},{64,80... | collective-permute-start | bytes 98312 | tf_op jit(solution)/shard_map/ppermute | solution.py:15
  102.2 10.4 %collective-permute-start.4 = (f32[64,128]{1,0:T(8,128)S(1)}, f32[64,128]{1,0:T(8,128)S(1)}, u32[]{:S(2)}, u32[]{:S(2)}) collective-permute-start(f32[64,128]{1,0:T(8,128)S(1)} %add_add_fusion.1), channel_id=1, source_target_pairs={{0,32},{8,40},{16,48},{24,56},{32,0},{40,8},{48,16},{56,24},{64,96... | collective-permute-start | bytes 98312 | tf_op jit(solution)/shard_map/ppermute | solution.py:15
  104.5 8.2 %collective-permute-start.5 = (f32[64,128]{1,0:T(8,128)S(1)}, f32[64,128]{1,0:T(8,128)S(1)}, u32[]{:S(2)}, u32[]{:S(2)}) collective-permute-start(f32[64,128]{1,0:T(8,128)S(1)} %add_add_fusion.1), channel_id=1, source_target_pairs={{0,48},{8,56},{16,32},{24,40},{32,16},{40,24},{48,0},{56,8},{64,11... | collective-permute-start | bytes 98312 | tf_op jit(solution)/shard_map/ppermute | solution.py:15
  112.0 5.4 %copy-start.1 = (bf16[64,64,192,1]{2,0,1,3:T(8,128)(2,1)S(1)}, bf16[64,64,192,1]{2,0,1,3:T(8,128)(2,1)}, u32[]{:S(2)}) copy-start(bf16[64,64,192,1]{2,0,1,3:T(8,128)(2,1)} %convert_bitcast_fusion) | copy-start | bytes 4718596
  113.2 12.5 %collective-permute-start.7 = (f32[]{:T(128)}, f32[]{:T(128)}, u32[]{:S(2)}, u32[]{:S(2)}) collective-permute-start(f32[]{:T(128)} %multiply_reduce_fusion), channel_id=1, source_target_pairs={{0,4},{1,5},{2,6},{3,7},{4,0},{5,1},{6,2},{7,3},{8,12},{9,13},{10,... | collective-permute-start | bytes 20 | tf_op jit(solution)/shard_map/ppermute | solution.py:15
  116.2 9.5 %collective-permute-start.8 = (f32[]{:T(128)}, f32[]{:T(128)}, u32[]{:S(2)}, u32[]{:S(2)}) collective-permute-start(f32[]{:T(128)} %multiply_reduce_fusion), channel_id=1, source_target_pairs={{0,6},{1,7},{2,4},{3,5},{4,2},{5,3},{6,0},{7,1},{8,14},{9,15},{10,... | collective-permute-start | bytes 20 | tf_op jit(solution)/shard_map/ppermute | solution.py:15
  117.4 7.0 %collective-permute-start.6 = (f32[]{:T(128)}, f32[]{:T(128)}, u32[]{:S(2)}, u32[]{:S(2)}) collective-permute-start(f32[]{:T(128)} %multiply_reduce_fusion), channel_id=1, source_target_pairs={{0,2},{1,3},{2,0},{3,1},{4,6},{5,7},{6,4},{7,5},{8,10},{9,11},{10,... | collective-permute-start | bytes 20 | tf_op jit(solution)/shard_map/ppermute | solution.py:15
  118.9 1.1 copy-start.2
  118.9 1.4 copy-start.3
  120.0 2.2 %copy-start.4 = (bf16[128,1024]{1,0:T(8,128)(2,1)S(1)}, bf16[128,1024]{1,0:T(8,128)(2,1)}, u32[]{:S(2)}) copy-start(bf16[128,1024]{1,0:T(8,128)(2,1)} %param.8) | copy-start | bytes 786436
  120.1 2.4 %copy-start.5 = (bf16[128,1024]{1,0:T(8,128)(2,1)S(1)}, bf16[128,1024]{1,0:T(8,128)(2,1)}, u32[]{:S(2)}) copy-start(bf16[128,1024]{1,0:T(8,128)(2,1)} %param.11) | copy-start | bytes 786436
  127.0 3.6 %collective-permute-start.9 = (f32[]{:T(128)}, f32[]{:T(128)}, u32[]{:S(2)}, u32[]{:S(2)}) collective-permute-start(f32[]{:T(128)} %add.198), channel_id=1, source_target_pairs={{0,1},{1,0},{2,3},{3,2},{4,5},{5,4},{6,7},{7,6},{8,9},{9,8},{10,11... | collective-permute-start | bytes 20 | tf_op jit(solution)/shard_map/ppermute | solution.py:15
Sparse Core Ops, SparseCore 0:
  10.5 75.3 all-gather.2

commit v15 on v14

--- a/solution.py
+++ b/solution.py
@@ -99,12 +99,14 @@
         [own_gated, pick(late_blocks, 1, after).reshape(per_device, lead, channels)], axis=1
     ).reshape(per_device, window, groups, group_size)
     total_grad = butterfly_sum(total_grad, "seq", seq_rounds[1:])
-    total_grad, gated_window, late_query, late_key, late_value, late_grad = lax.optimization_barrier(
-        (total_grad, gated_window, query_rows, key_rows, value_rows, grad_rows)
-    )
+    total_grad, gated_window = lax.optimization_barrier((total_grad, gated_window))
     adjoint = jnp.einsum("gau,sugc->sagc", bwd_band, gated_window, preferred_element_type=jnp.float32)
     dmixed = adjoint.reshape(rows, channels).astype(jnp.bfloat16)
-    squares = butterfly_sum(jnp.sum(total_grad * total_grad), "chan", ((1, 2), (0,)))
+    squares = radix_round(jnp.sum(total_grad * total_grad), "chan", 1, 2)
+    squares, late_query, late_key, late_value, late_grad = lax.optimization_barrier(
+        (squares, query_rows, key_rows, value_rows, grad_rows)
+    )
+    squares = radix_round(squares, "chan", 0)
     limit = math.sqrt(groups * lax.axis_size("chan") * taps)
     factor = jnp.minimum(1.0, limit / jnp.sqrt(squares + 1e-06))
     filter_grad = factor * total_grad

time: 139 us -> 139 us (level)
  transfers between devices with their start and end apart: 11 -> 11, of which waited for: 2 -> 2; matrix products, arithmetic and copies ran while one was open for 19% -> 18% of each run, Pallas kernels for 0% -> 0%
where the time goes in v15:
time: 139 us
  waiting for transfers between devices  65.9 us (47%)
  local copies, waits for them, and re-layouts  20.1 us (14%)
  between operations  17.7 us (13%)
  starting transfers between devices  15.1 us (11%)
  matrix products  14.3 us (10%)
  other arithmetic  5.74 us (4%)
    all_gather x1, waiting for transfers between devices, shards(): lax.all_gather(jnp.stack([mixed, gated]), 'seq', axis=0, tiled=False)  64.9 us
    ppermute x10, starting transfers between devices, swap(): return lax.ppermute(value, axis, [(i, i ^ mask) for i in range(size)])  15.1 us
    gather x2, local copies, waits for them, and re-layouts, pick(): jnp.take(blocks, slots, axis=0)  7.92 us
    dot_general x1, matrix products, shards(): jnp.einsum('gaw,jaw->gj', corr, select_fwd.astype(jnp.float32), precision...  3.92 us
    dot_general x1, matrix products, shards(): jnp.einsum('gj,jaw->gaw', filters, select_fwd, preferred_element_type=jnp...  3.54 us
    unnamed x20, local copies, waits for them, and re-layouts  3.44 us
    dot_general x1, matrix products, shards(): jnp.einsum('gj,jau->gau', filters, _bwd_select(taps, span_rows, window),...  3.24 us
  transfers between devices with their start and end apart: 11, of which 2 were waited for; matrix products, arithmetic and copies ran while one was open for 18% of the time, Pallas kernels for 0%

profile of v15, /device:TPU:0, one launch (start us, length us, event | category | flops | bytes accessed | tf_op | source)
XLA Modules:
  0.0 138.9 jit_solution(4990471809856798419)
XLA Ops:
  7.2 1.1 multiply_convert_fusion.4
  8.3 1.1 multiply_convert_fusion.5
  9.4 0.9 pad_maximum_fusion.4
  10.4 0.2 copy.52
  10.5 0.2 copy.49
  11.2 0.2 concatenate.10
  11.6 0.2 reshape_reshape.3
  11.9 0.7 scatter_custom_fusion
  12.6 0.6 gather_fusion
  13.2 0.6 gather_fusion.1
  14.2 3.2 %convert_bitcast_fusion = bf16[64,64,192,1]{2,0,1,3:T(8,128)(2,1)} fusion(bf16[64,128]{1,0:T(8,128)(2,1)S(1)} %copy-done), kind=kOutput, calls=%fused_computation.18 | convolution fusion | flops 205258752 | bytes 1589248 | tf_op jit(solution)/shard_map/gj,jau->gau/dot_general | solution.py:81
  17.4 3.5 %convert_bitcast_fusion.1 = bf16[64,64,192,1]{2,0,1,3:T(8,128)(2,1)} fusion(s32[64]{0:T(128)S(1)} %iota_add_fusion, bf16[64,128]{1,0:T(8,128)(2,1)S(1)} %copy-done), kind=kOutput, calls=%fused_computation.19 | convolution fusion | flops 205258752 | bytes 1589504 | tf_op jit(solution)/shard_map/gj,jaw->gaw/dot_general | solution.py:78
  21.0 64.9 %all-gather.3.cloned.1.call-done = bf16[32,128,1024]{2,1,0:T(8,128)(2,1)} async-done(((bf16[2,128,1024]{2,1,0:T(8,128)(2,1)}), bf16[32,128,1024]{2,1,0:T(8,128)(2,1)}) %all-gather.3.cloned.1.call-update) | async-done | bytes 8388624 | tf_op jit(solution)/shard_map/all_gather | solution.py:54
  85.9 4.0 %gather_fusion.2 = bf16[4,64,1024]{2,1,0:T(8,128)(2,1)S(1)} fusion(bf16[64,64,1024]{2,1,0:T(8,128)(2,1)} %bitcast.44, s32[1024]{0:T(1024)S(1)} %pad_clamp_fusion.2), kind=kCustom, calls=%fused_computation.clone | custom fusion | bytes 1048592 | tf_op jit(solution)/shard_map/jit(_take)/gather | solution.py:67
  90.0 0.7 copy.50
  90.7 0.5 reshape.190
  91.2 0.8 convolution_bitcast_fusion
  92.0 3.9 %fusion.28 = f32[64,128]{1,0:T(8,128)S(1)} fusion(s32[64]{0:T(128)S(1)} %iota_add_fusion, f32[64,64,192]{2,1,0:T(8,128)S(1)} %convolution_bitcast_fusion), kind=kOutput, calls=%fused_computation.26 | convolution fusion | flops 607125504 | bytes 3178752 | tf_op jit(solution)/shard_map/gaw,jaw->gj/dot_general | solution.py:92
  96.0 0.3 collective-permute-start
  96.3 0.4 collective-permute-start.1
  96.7 2.7 %collective-permute-start.2 = (f32[64,128]{1,0:T(8,128)S(1)}, f32[64,128]{1,0:T(8,128)S(1)}, u32[]{:S(2)}, u32[]{:S(2)}) collective-permute-start(f32[64,128]{1,0:T(8,128)S(1)} %fusion.28), channel_id=1, source_target_pairs={{0,72},{8,64},{16,88},{24,80},{32,104},{40,96},{48,120},{56,112},{... | collective-permute-start | bytes 98312 | tf_op jit(solution)/shard_map/ppermute | solution.py:15
  99.4 1.3 fusion.16
  100.7 0.5 copy.61
  101.3 0.6 reshape.193
  101.9 0.3 collective-permute-start.3
  102.2 2.3 %collective-permute-start.4 = (f32[64,128]{1,0:T(8,128)S(1)}, f32[64,128]{1,0:T(8,128)S(1)}, u32[]{:S(2)}, u32[]{:S(2)}) collective-permute-start(f32[64,128]{1,0:T(8,128)S(1)} %add_add_fusion.1), channel_id=1, source_target_pairs={{0,32},{8,40},{16,48},{24,56},{32,0},{40,8},{48,16},{56,24},{64,96... | collective-permute-start | bytes 98312 | tf_op jit(solution)/shard_map/ppermute | solution.py:15
  104.5 2.2 %collective-permute-start.5 = (f32[64,128]{1,0:T(8,128)S(1)}, f32[64,128]{1,0:T(8,128)S(1)}, u32[]{:S(2)}, u32[]{:S(2)}) collective-permute-start(f32[64,128]{1,0:T(8,128)S(1)} %add_add_fusion.1), channel_id=1, source_target_pairs={{0,48},{8,56},{16,32},{24,40},{32,16},{40,24},{48,0},{56,8},{64,11... | collective-permute-start | bytes 98312 | tf_op jit(solution)/shard_map/ppermute | solution.py:15
  106.7 4.0 %gather_fusion.3 = bf16[4,64,1024]{2,1,0:T(8,128)(2,1)S(1)} fusion(bf16[64,64,1024]{2,1,0:T(8,128)(2,1)} %bitcast.45, s32[1024]{0:T(1024)S(1)} %pad_clamp_fusion), kind=kCustom, calls=%fused_computation.1.clone | custom fusion | bytes 1048592 | tf_op jit(solution)/shard_map/jit(_take)/gather | solution.py:67
  110.8 0.7 copy.56
  111.5 0.5 reshape.192
  112.1 0.5 pad_maximum_fusion.1
  112.6 0.6 multiply_reduce_fusion
  113.2 3.0 %collective-permute-start.7 = (f32[]{:T(128)}, f32[]{:T(128)}, u32[]{:S(2)}, u32[]{:S(2)}) collective-permute-start(f32[]{:T(128)} %multiply_reduce_fusion), channel_id=1, source_target_pairs={{0,4},{1,5},{2,6},{3,7},{4,0},{5,1},{6,2},{7,3},{8,12},{9,13},{10,... | collective-permute-start | bytes 20 | tf_op jit(solution)/shard_map/ppermute | solution.py:15
  116.2 1.2 collective-permute-start.8
  117.4 1.5 %fusion.25 = f32[2,64,64,16]{1,3,0,2:T(8,128)S(1)} fusion(bf16[2,192,64,16]{1,3,0,2:T(8,128)(2,1)S(1)} %pad_maximum_fusion.1, bf16[64,64,192,1]{2,0,1,3:T(8,128)(2,1)S(1)} %copy-done.1), kind=kOutput, calls=%fused_computation.25 | convolution fusion | flops 50593792 | bytes 2883584 | tf_op jit(solution)/shard_map/gau,sugc->sagc/dot_general | solution.py:103
  118.9 0.5 copy.64
  119.4 0.6 reshape.194
  120.0 1.0 collective-permute-done.6
  123.7 2.7 %collective-permute-start.9 = (f32[]{:T(128)}, f32[]{:T(128)}, u32[]{:S(2)}, u32[]{:S(2)}) collective-permute-start(f32[]{:T(128)} %add.197), channel_id=1, source_target_pairs={{0,1},{1,0},{2,3},{3,2},{4,5},{5,4},{6,7},{7,6},{8,9},{9,8},{10,11... | collective-permute-start | bytes 20 | tf_op jit(solution)/shard_map/ppermute | solution.py:15
  126.4 0.2 copy.65
  126.6 0.2 copy.66
  126.8 0.9 copy.69
  127.7 0.8 copy.70
  128.5 0.2 copy.59
  128.7 0.2 copy.62
  129.0 0.9 copy.67
  129.9 0.8 copy.68
  131.4 0.6 broadcast_multiply_fusion
  (56 shorter events, 1.7 us)
Async XLA Ops:
  7.2 7.0 %copy-start = (bf16[64,128]{1,0:T(8,128)(2,1)S(1)}, bf16[64,128]{1,0:T(8,128)(2,1)}, u32[]{:S(2)}) copy-start(bf16[64,128]{1,0:T(8,128)(2,1)} %param.12) | copy-start | bytes 49156
  7.2 3.5 %copy-start.6 = (s32[32]{0:T(128)S(1)}, s32[32]{0:T(128)}, u32[]{:S(2)}) copy-start(s32[32]{0:T(128)} %param.13) | copy-start | bytes 388
  7.2 78.7 %all-gather.3.cloned.1.call-start = ((), (), s32[]{:S(2)}) async-start(), calls=%async_computation | async-start | bytes 8912896 | tf_op jit(solution)/shard_map/all_gather | solution.py:54
  92.0 7.4 %copy-start.7 = (bf16[64,64,192,1]{2,0,1,3:T(8,128)(2,1)S(1)}, bf16[64,64,192,1]{2,0,1,3:T(8,128)(2,1)}, u32[]{:S(2)}) copy-start(bf16[64,64,192,1]{2,0,1,3:T(8,128)(2,1)} %convert_bitcast_fusion.1) | copy-start | bytes 4718596
  96.0 5.9 %collective-permute-start = (f32[64,128]{1,0:T(8,128)S(1)}, f32[64,128]{1,0:T(8,128)S(1)}, u32[]{:S(2)}, u32[]{:S(2)}) collective-permute-start(f32[64,128]{1,0:T(8,128)S(1)} %fusion.28), channel_id=1, source_target_pairs={{0,8},{8,0},{16,24},{24,16},{32,40},{40,32},{48,56},{56,48},{64,72... | collective-permute-start | bytes 98312 | tf_op jit(solution)/shard_map/ppermute | solution.py:15
  96.3 5.6 %collective-permute-start.1 = (f32[64,128]{1,0:T(8,128)S(1)}, f32[64,128]{1,0:T(8,128)S(1)}, u32[]{:S(2)}, u32[]{:S(2)}) collective-permute-start(f32[64,128]{1,0:T(8,128)S(1)} %fusion.28), channel_id=1, source_target_pairs={{0,64},{8,72},{16,80},{24,88},{32,96},{40,104},{48,112},{56,120},{... | collective-permute-start | bytes 98312 | tf_op jit(solution)/shard_map/ppermute | solution.py:15
  96.7 5.2 %collective-permute-start.2 = (f32[64,128]{1,0:T(8,128)S(1)}, f32[64,128]{1,0:T(8,128)S(1)}, u32[]{:S(2)}, u32[]{:S(2)}) collective-permute-start(f32[64,128]{1,0:T(8,128)S(1)} %fusion.28), channel_id=1, source_target_pairs={{0,72},{8,64},{16,88},{24,80},{32,104},{40,96},{48,120},{56,112},{... | collective-permute-start | bytes 98312 | tf_op jit(solution)/shard_map/ppermute | solution.py:15
  101.9 10.7 %collective-permute-start.3 = (f32[64,128]{1,0:T(8,128)S(1)}, f32[64,128]{1,0:T(8,128)S(1)}, u32[]{:S(2)}, u32[]{:S(2)}) collective-permute-start(f32[64,128]{1,0:T(8,128)S(1)} %add_add_fusion.1), channel_id=1, source_target_pairs={{0,16},{8,24},{16,0},{24,8},{32,48},{40,56},{48,32},{56,40},{64,80... | collective-permute-start | bytes 98312 | tf_op jit(solution)/shard_map/ppermute | solution.py:15
  102.2 10.4 %collective-permute-start.4 = (f32[64,128]{1,0:T(8,128)S(1)}, f32[64,128]{1,0:T(8,128)S(1)}, u32[]{:S(2)}, u32[]{:S(2)}) collective-permute-start(f32[64,128]{1,0:T(8,128)S(1)} %add_add_fusion.1), channel_id=1, source_target_pairs={{0,32},{8,40},{16,48},{24,56},{32,0},{40,8},{48,16},{56,24},{64,96... | collective-permute-start | bytes 98312 | tf_op jit(solution)/shard_map/ppermute | solution.py:15
  104.5 8.2 %collective-permute-start.5 = (f32[64,128]{1,0:T(8,128)S(1)}, f32[64,128]{1,0:T(8,128)S(1)}, u32[]{:S(2)}, u32[]{:S(2)}) collective-permute-start(f32[64,128]{1,0:T(8,128)S(1)} %add_add_fusion.1), channel_id=1, source_target_pairs={{0,48},{8,56},{16,32},{24,40},{32,16},{40,24},{48,0},{56,8},{64,11... | collective-permute-start | bytes 98312 | tf_op jit(solution)/shard_map/ppermute | solution.py:15
  112.0 5.4 %copy-start.1 = (bf16[64,64,192,1]{2,0,1,3:T(8,128)(2,1)S(1)}, bf16[64,64,192,1]{2,0,1,3:T(8,128)(2,1)}, u32[]{:S(2)}) copy-start(bf16[64,64,192,1]{2,0,1,3:T(8,128)(2,1)} %convert_bitcast_fusion) | copy-start | bytes 4718596
  113.2 9.1 %collective-permute-start.7 = (f32[]{:T(128)}, f32[]{:T(128)}, u32[]{:S(2)}, u32[]{:S(2)}) collective-permute-start(f32[]{:T(128)} %multiply_reduce_fusion), channel_id=1, source_target_pairs={{0,4},{1,5},{2,6},{3,7},{4,0},{5,1},{6,2},{7,3},{8,12},{9,13},{10,... | collective-permute-start | bytes 20 | tf_op jit(solution)/shard_map/ppermute | solution.py:15
  116.2 6.2 %collective-permute-start.8 = (f32[]{:T(128)}, f32[]{:T(128)}, u32[]{:S(2)}, u32[]{:S(2)}) collective-permute-start(f32[]{:T(128)} %multiply_reduce_fusion), channel_id=1, source_target_pairs={{0,6},{1,7},{2,4},{3,5},{4,2},{5,3},{6,0},{7,1},{8,14},{9,15},{10,... | collective-permute-start | bytes 20 | tf_op jit(solution)/shard_map/ppermute | solution.py:15
  117.4 3.7 %collective-permute-start.6 = (f32[]{:T(128)}, f32[]{:T(128)}, u32[]{:S(2)}, u32[]{:S(2)}) collective-permute-start(f32[]{:T(128)} %multiply_reduce_fusion), channel_id=1, source_target_pairs={{0,2},{1,3},{2,0},{3,1},{4,6},{5,7},{6,4},{7,5},{8,10},{9,11},{10,... | collective-permute-start | bytes 20 | tf_op jit(solution)/shard_map/ppermute | solution.py:15
  118.9 7.5 %copy-start.2 = (bf16[128,1024]{1,0:T(8,128)(2,1)S(1)}, bf16[128,1024]{1,0:T(8,128)(2,1)}, u32[]{:S(2)}) copy-start(bf16[128,1024]{1,0:T(8,128)(2,1)} %param.10) | copy-start | bytes 786436
  118.9 7.7 %copy-start.3 = (bf16[128,1024]{1,0:T(8,128)(2,1)S(1)}, bf16[128,1024]{1,0:T(8,128)(2,1)}, u32[]{:S(2)}) copy-start(bf16[128,1024]{1,0:T(8,128)(2,1)} %param.9) | copy-start | bytes 786436
  120.0 8.5 %copy-start.4 = (bf16[128,1024]{1,0:T(8,128)(2,1)S(1)}, bf16[128,1024]{1,0:T(8,128)(2,1)}, u32[]{:S(2)}) copy-start(bf16[128,1024]{1,0:T(8,128)(2,1)} %param.8) | copy-start | bytes 786436
  123.7 5.1 %copy-start.5 = (bf16[128,1024]{1,0:T(8,128)(2,1)S(1)}, bf16[128,1024]{1,0:T(8,128)(2,1)}, u32[]{:S(2)}) copy-start(bf16[128,1024]{1,0:T(8,128)(2,1)} %param.11) | copy-start | bytes 786436
  123.7 7.1 %collective-permute-start.9 = (f32[]{:T(128)}, f32[]{:T(128)}, u32[]{:S(2)}, u32[]{:S(2)}) collective-permute-start(f32[]{:T(128)} %add.197), channel_id=1, source_target_pairs={{0,1},{1,0},{2,3},{3,2},{4,5},{5,4},{6,7},{7,6},{8,9},{9,8},{10,11... | collective-permute-start | bytes 20 | tf_op jit(solution)/shard_map/ppermute | solution.py:15
Sparse Core Ops, SparseCore 0:
  10.5 75.3 all-gather.2

commit v16 on v15

--- a/solution.py
+++ b/solution.py
@@ -3,6 +3,8 @@
 import jax
 import jax.numpy as jnp
 from jax import lax
+from jax.experimental import pallas as pl
+from jax.experimental.pallas import tpu as pltpu
 from jax.sharding import PartitionSpec as P
 
 
@@ -26,6 +28,30 @@
     for bits in rounds:
         value = radix_round(value, axis, *bits)
     return value
+
+
+def _take_kernel(slots_ref, blocks_ref, out_ref, sems):
+    count = out_ref.shape[0]
+    copies = [
+        pltpu.make_async_copy(blocks_ref.at[slots_ref[n]], out_ref.at[n], sems.at[n]) for n in range(count)
+    ]
+    for copy in copies:
+        copy.start()
+    for copy in copies:
+        copy.wait()
+
+
+def take_blocks(blocks, slots):
+    count = slots.shape[0]
+    block_bytes = blocks.shape[1] * blocks.shape[2] * blocks.dtype.itemsize
+    return pl.pallas_call(
+        _take_kernel,
+        out_shape=jax.ShapeDtypeStruct((count,) + blocks.shape[1:], blocks.dtype),
+        in_specs=[pl.BlockSpec(memory_space=pltpu.SMEM), pl.BlockSpec(memory_space=pl.ANY)],
+        out_specs=pl.BlockSpec(memory_space=pltpu.VMEM),
+        scratch_shapes=[pltpu.SemaphoreType.DMA((count,))],
+        cost_estimate=pl.CostEstimate(flops=0, bytes_accessed=2 * count * block_bytes, transcendentals=0),
+    )(slots, blocks)
 
 
 def band_select(taps, out_rows, window, lead):
@@ -64,7 +90,7 @@
         valid = (wanted >= 0) & (wanted < spans)
         slots = slot_of[jnp.clip(wanted, 0, spans - 1)].reshape(-1)
         slots = ((slots // per_device) * 2 + which) * per_device + slots % per_device
-        taken = jnp.take(blocks, slots, axis=0).reshape(per_device, halo, span_rows, channels)
+        taken = take_blocks(blocks, slots).reshape(per_device, halo, span_rows, channels)
         return jnp.where(valid[:, :, None, None], taken, jnp.zeros_like(taken))
 
     own_mixed = mixed.reshape(per_device, span_rows, channels)

time: 139 us -> 138 us (level)
  local copies, waits for them, and re-layouts: 20.1 us -> 14 us
  Pallas kernels: 0 us -> 5.23 us
    gather x2 -> x0, local copies, waits for them, and re-layouts: 7.92 us -> none  [pick(): jnp.take(blocks, slots, axis=0)]
    pallas_call x0 -> x2, Pallas kernels: none -> 5.23 us  [take_blocks(): pl.pallas_call(_take_kernel, out_shape=jax.ShapeDtypeStruct((count,) + bl...]
    pallas_call x0 -> x2, local copies, waits for them, and re-layouts: none -> 3.21 us  [take_blocks(): pl.pallas_call(_take_kernel, out_shape=jax.ShapeDtypeStruct((count,) + bl...]
    select_n x2 -> x0, local copies, waits for them, and re-layouts: 1.42 us -> none  [pick(): jnp.take(blocks, slots, axis=0)]
  transfers between devices with their start and end apart: 11 -> 11, of which waited for: 2 -> 2; matrix products, arithmetic and copies ran while one was open for 18% -> 17% of each run, Pallas kernels for 0% -> 2%
where the time goes in v16:
time: 138 us
  waiting for transfers between devices  65 us (47%)
  between operations  17.6 us (13%)
  starting transfers between devices  15.1 us (11%)
  matrix products  14.3 us (10%)
  local copies, waits for them, and re-layouts  14 us (10%)
  other arithmetic  6.49 us (5%)
  Pallas kernels  5.23 us (4%)
    all_gather x1, waiting for transfers between devices, shards(): lax.all_gather(jnp.stack([mixed, gated]), 'seq', axis=0, tiled=False)  63.9 us
    ppermute x10, starting transfers between devices, swap(): return lax.ppermute(value, axis, [(i, i ^ mask) for i in range(size)])  15.1 us
    pallas_call x2, Pallas kernels, take_blocks(): pl.pallas_call(_take_kernel, out_shape=jax.ShapeDtypeStruct((count,) + bl...  5.23 us
    dot_general x1, matrix products, shards(): jnp.einsum('gaw,jaw->gj', corr, select_fwd.astype(jnp.float32), precision...  3.92 us
    dot_general x1, matrix products, shards(): jnp.einsum('gj,jaw->gaw', filters, select_fwd, preferred_element_type=jnp...  3.53 us
    unnamed x20, local copies, waits for them, and re-layouts  3.44 us
    dot_general x1, matrix products, shards(): jnp.einsum('gj,jau->gau', filters, _bwd_select(taps, span_rows, window),...  3.23 us
    pallas_call x2, local copies, waits for them, and re-layouts, take_blocks(): pl.pallas_call(_take_kernel, out_shape=jax.ShapeDtypeStruct((count,) + bl...  3.21 us
  transfers between devices with their start and end apart: 11, of which 2 were waited for; matrix products, arithmetic and copies ran while one was open for 17% of the time, Pallas kernels for 2%

profile of v16, /device:TPU:0, one launch (start us, length us, event | category | flops | bytes accessed | tf_op | source)
XLA Modules:
  0.0 137.7 jit_solution(14392770576785908980)
XLA Ops:
  7.2 1.1 multiply_convert_fusion.4
  8.3 1.1 multiply_convert_fusion.5
  9.4 0.9 pad_maximum_fusion.4
  10.4 0.2 copy.34
  10.5 0.2 copy.31
  11.2 0.2 concatenate.10
  11.6 0.2 reshape_reshape.3
  11.9 0.7 scatter_custom_fusion
  12.6 0.6 gather_fusion
  13.2 0.6 gather_fusion.1
  14.1 3.2 %convert_bitcast_fusion = bf16[64,64,192,1]{2,0,1,3:T(8,128)(2,1)} fusion(bf16[64,128]{1,0:T(8,128)(2,1)S(1)} %copy-done), kind=kOutput, calls=%fused_computation.16 | convolution fusion | flops 205258752 | bytes 1589248 | tf_op jit(solution)/shard_map/gj,jau->gau/dot_general | solution.py:107
  17.4 3.5 %convert_bitcast_fusion.1 = bf16[64,64,192,1]{2,0,1,3:T(8,128)(2,1)} fusion(s32[64]{0:T(128)S(1)} %iota_add_fusion, bf16[64,128]{1,0:T(8,128)(2,1)S(1)} %copy-done), kind=kOutput, calls=%fused_computation.17 | convolution fusion | flops 205258752 | bytes 1589504 | tf_op jit(solution)/shard_map/gj,jaw->gaw/dot_general | solution.py:104
  20.9 0.5 fusion.33.slots_ref
  21.4 0.5 fusion.34.slots_ref
  21.9 63.9 %all-gather.3.cloned.1.call-done = bf16[32,128,1024]{2,1,0:T(8,128)(2,1)} async-done(((bf16[2,128,1024]{2,1,0:T(8,128)(2,1)}), bf16[32,128,1024]{2,1,0:T(8,128)(2,1)}) %all-gather.3.cloned.1.call-update) | async-done | bytes 8388624 | tf_op jit(solution)/shard_map/all_gather | solution.py:80
  85.9 2.6 %shard_map.101 = bf16[4,64,1024]{2,1,0:T(8,128)(2,1)} custom-call(s32[4]{0:T(128)} %fusion.33.slots_ref, bf16[64,64,1024]{2,1,0:T(8,128)(2,1)} %bitcast.42), custom_call_target="tpu_custom_call" | custom-call | bytes 1048576 | tf_op jit(solution)/shard_map/pallas_call | solution.py:47
  88.5 1.6 %copy.32 = bf16[4,64,1024]{1,0,2:T(4,128)(2,1)S(1)} copy(bf16[4,64,1024]{2,1,0:T(8,128)(2,1)} %shard_map.101) | data formatting | bytes 1048576 | tf_op jit(solution)/shard_map/pallas_call | solution.py:47
  90.1 0.5 reshape.185
  90.7 0.8 convolution_bitcast_fusion
  91.5 3.9 %fusion.28 = f32[64,128]{1,0:T(8,128)S(1)} fusion(s32[64]{0:T(128)S(1)} %iota_add_fusion, f32[64,64,192]{2,1,0:T(8,128)S(1)} %convolution_bitcast_fusion), kind=kOutput, calls=%fused_computation.24 | convolution fusion | flops 607125504 | bytes 3178752 | tf_op jit(solution)/shard_map/gaw,jaw->gj/dot_general | solution.py:118
  95.4 0.3 collective-permute-start
  95.7 0.4 collective-permute-start.1
  96.1 2.7 %collective-permute-start.2 = (f32[64,128]{1,0:T(8,128)S(1)}, f32[64,128]{1,0:T(8,128)S(1)}, u32[]{:S(2)}, u32[]{:S(2)}) collective-permute-start(f32[64,128]{1,0:T(8,128)S(1)} %fusion.28), channel_id=1, source_target_pairs={{0,72},{8,64},{16,88},{24,80},{32,104},{40,96},{48,120},{56,112},{... | collective-permute-start | bytes 98312 | tf_op jit(solution)/shard_map/ppermute | solution.py:17
  98.9 1.3 fusion.16
  100.2 0.5 copy.43
  100.8 0.6 reshape.188
  101.4 0.3 collective-permute-start.3
  101.6 2.3 %collective-permute-start.4 = (f32[64,128]{1,0:T(8,128)S(1)}, f32[64,128]{1,0:T(8,128)S(1)}, u32[]{:S(2)}, u32[]{:S(2)}) collective-permute-start(f32[64,128]{1,0:T(8,128)S(1)} %add_add_fusion.1), channel_id=1, source_target_pairs={{0,32},{8,40},{16,48},{24,56},{32,0},{40,8},{48,16},{56,24},{64,96... | collective-permute-start | bytes 98312 | tf_op jit(solution)/shard_map/ppermute | solution.py:17
  103.9 2.2 %collective-permute-start.5 = (f32[64,128]{1,0:T(8,128)S(1)}, f32[64,128]{1,0:T(8,128)S(1)}, u32[]{:S(2)}, u32[]{:S(2)}) collective-permute-start(f32[64,128]{1,0:T(8,128)S(1)} %add_add_fusion.1), channel_id=1, source_target_pairs={{0,48},{8,56},{16,32},{24,40},{32,16},{40,24},{48,0},{56,8},{64,11... | collective-permute-start | bytes 98312 | tf_op jit(solution)/shard_map/ppermute | solution.py:17
  106.2 2.6 %shard_map.102 = bf16[4,64,1024]{2,1,0:T(8,128)(2,1)} custom-call(s32[4]{0:T(128)} %fusion.34.slots_ref, bf16[64,64,1024]{2,1,0:T(8,128)(2,1)} %bitcast.43), custom_call_target="tpu_custom_call" | custom-call | bytes 1048576 | tf_op jit(solution)/shard_map/pallas_call | solution.py:47
  108.8 1.6 %copy.38 = bf16[4,64,1024]{1,0,2:T(4,128)(2,1)S(1)} copy(bf16[4,64,1024]{2,1,0:T(8,128)(2,1)} %shard_map.102) | data formatting | bytes 1048576 | tf_op jit(solution)/shard_map/pallas_call | solution.py:47
  110.4 0.5 reshape.187
  111.0 0.5 pad_maximum_fusion.1
  111.5 0.6 multiply_reduce_fusion
  112.1 3.0 %collective-permute-start.7 = (f32[]{:T(128)}, f32[]{:T(128)}, u32[]{:S(2)}, u32[]{:S(2)}) collective-permute-start(f32[]{:T(128)} %multiply_reduce_fusion), channel_id=1, source_target_pairs={{0,4},{1,5},{2,6},{3,7},{4,0},{5,1},{6,2},{7,3},{8,12},{9,13},{10,... | collective-permute-start | bytes 20 | tf_op jit(solution)/shard_map/ppermute | solution.py:17
  115.1 1.2 collective-permute-start.8
  116.3 1.5 %fusion.25 = f32[2,64,64,16]{1,3,0,2:T(8,128)S(1)} fusion(bf16[2,192,64,16]{1,3,0,2:T(8,128)(2,1)S(1)} %pad_maximum_fusion.1, bf16[64,64,192,1]{2,0,1,3:T(8,128)(2,1)S(1)} %copy-done.1), kind=kOutput, calls=%fused_computation.23 | convolution fusion | flops 50593792 | bytes 2883584 | tf_op jit(solution)/shard_map/gau,sugc->sagc/dot_general | solution.py:129
  117.8 0.5 copy.46
  118.3 0.6 reshape.189
  118.9 1.0 collective-permute-done.6
  122.5 2.7 %collective-permute-start.9 = (f32[]{:T(128)}, f32[]{:T(128)}, u32[]{:S(2)}, u32[]{:S(2)}) collective-permute-start(f32[]{:T(128)} %add.194), channel_id=1, source_target_pairs={{0,1},{1,0},{2,3},{3,2},{4,5},{5,4},{6,7},{7,6},{8,9},{9,8},{10,11... | collective-permute-start | bytes 20 | tf_op jit(solution)/shard_map/ppermute | solution.py:17
  125.4 0.2 copy.48
  125.6 0.9 copy.51
  126.5 0.8 copy.52
  127.5 0.2 copy.44
  127.8 0.9 copy.49
  128.7 0.8 copy.50
  130.2 0.6 broadcast_multiply_fusion
  (52 shorter events, 1.7 us)
Async XLA Ops:
  7.2 7.0 %copy-start = (bf16[64,128]{1,0:T(8,128)(2,1)S(1)}, bf16[64,128]{1,0:T(8,128)(2,1)}, u32[]{:S(2)}) copy-start(bf16[64,128]{1,0:T(8,128)(2,1)} %param.10) | copy-start | bytes 49156
  7.2 3.5 %copy-start.6 = (s32[32]{0:T(128)S(1)}, s32[32]{0:T(128)}, u32[]{:S(2)}) copy-start(s32[32]{0:T(128)} %param.11) | copy-start | bytes 388
  7.2 78.7 %all-gather.3.cloned.1.call-start = ((), (), s32[]{:S(2)}) async-start(), calls=%async_computation | async-start | bytes 8912896 | tf_op jit(solution)/shard_map/all_gather | solution.py:80
  91.5 7.4 %copy-start.7 = (bf16[64,64,192,1]{2,0,1,3:T(8,128)(2,1)S(1)}, bf16[64,64,192,1]{2,0,1,3:T(8,128)(2,1)}, u32[]{:S(2)}) copy-start(bf16[64,64,192,1]{2,0,1,3:T(8,128)(2,1)} %convert_bitcast_fusion.1) | copy-start | bytes 4718596
  95.4 5.9 %collective-permute-start = (f32[64,128]{1,0:T(8,128)S(1)}, f32[64,128]{1,0:T(8,128)S(1)}, u32[]{:S(2)}, u32[]{:S(2)}) collective-permute-start(f32[64,128]{1,0:T(8,128)S(1)} %fusion.28), channel_id=1, source_target_pairs={{0,8},{8,0},{16,24},{24,16},{32,40},{40,32},{48,56},{56,48},{64,72... | collective-permute-start | bytes 98312 | tf_op jit(solution)/shard_map/ppermute | solution.py:17
  95.7 5.6 %collective-permute-start.1 = (f32[64,128]{1,0:T(8,128)S(1)}, f32[64,128]{1,0:T(8,128)S(1)}, u32[]{:S(2)}, u32[]{:S(2)}) collective-permute-start(f32[64,128]{1,0:T(8,128)S(1)} %fusion.28), channel_id=1, source_target_pairs={{0,64},{8,72},{16,80},{24,88},{32,96},{40,104},{48,112},{56,120},{... | collective-permute-start | bytes 98312 | tf_op jit(solution)/shard_map/ppermute | solution.py:17
  96.1 5.3 %collective-permute-start.2 = (f32[64,128]{1,0:T(8,128)S(1)}, f32[64,128]{1,0:T(8,128)S(1)}, u32[]{:S(2)}, u32[]{:S(2)}) collective-permute-start(f32[64,128]{1,0:T(8,128)S(1)} %fusion.28), channel_id=1, source_target_pairs={{0,72},{8,64},{16,88},{24,80},{32,104},{40,96},{48,120},{56,112},{... | collective-permute-start | bytes 98312 | tf_op jit(solution)/shard_map/ppermute | solution.py:17
  101.4 10.1 %collective-permute-start.3 = (f32[64,128]{1,0:T(8,128)S(1)}, f32[64,128]{1,0:T(8,128)S(1)}, u32[]{:S(2)}, u32[]{:S(2)}) collective-permute-start(f32[64,128]{1,0:T(8,128)S(1)} %add_add_fusion.1), channel_id=1, source_target_pairs={{0,16},{8,24},{16,0},{24,8},{32,48},{40,56},{48,32},{56,40},{64,80... | collective-permute-start | bytes 98312 | tf_op jit(solution)/shard_map/ppermute | solution.py:17
  101.6 9.8 %collective-permute-start.4 = (f32[64,128]{1,0:T(8,128)S(1)}, f32[64,128]{1,0:T(8,128)S(1)}, u32[]{:S(2)}, u32[]{:S(2)}) collective-permute-start(f32[64,128]{1,0:T(8,128)S(1)} %add_add_fusion.1), channel_id=1, source_target_pairs={{0,32},{8,40},{16,48},{24,56},{32,0},{40,8},{48,16},{56,24},{64,96... | collective-permute-start | bytes 98312 | tf_op jit(solution)/shard_map/ppermute | solution.py:17
  103.9 7.6 %collective-permute-start.5 = (f32[64,128]{1,0:T(8,128)S(1)}, f32[64,128]{1,0:T(8,128)S(1)}, u32[]{:S(2)}, u32[]{:S(2)}) collective-permute-start(f32[64,128]{1,0:T(8,128)S(1)} %add_add_fusion.1), channel_id=1, source_target_pairs={{0,48},{8,56},{16,32},{24,40},{32,16},{40,24},{48,0},{56,8},{64,11... | collective-permute-start | bytes 98312 | tf_op jit(solution)/shard_map/ppermute | solution.py:17
  110.9 5.4 %copy-start.1 = (bf16[64,64,192,1]{2,0,1,3:T(8,128)(2,1)S(1)}, bf16[64,64,192,1]{2,0,1,3:T(8,128)(2,1)}, u32[]{:S(2)}) copy-start(bf16[64,64,192,1]{2,0,1,3:T(8,128)(2,1)} %convert_bitcast_fusion) | copy-start | bytes 4718596
  112.1 9.1 %collective-permute-start.7 = (f32[]{:T(128)}, f32[]{:T(128)}, u32[]{:S(2)}, u32[]{:S(2)}) collective-permute-start(f32[]{:T(128)} %multiply_reduce_fusion), channel_id=1, source_target_pairs={{0,4},{1,5},{2,6},{3,7},{4,0},{5,1},{6,2},{7,3},{8,12},{9,13},{10,... | collective-permute-start | bytes 20 | tf_op jit(solution)/shard_map/ppermute | solution.py:17
  115.1 6.1 %collective-permute-start.8 = (f32[]{:T(128)}, f32[]{:T(128)}, u32[]{:S(2)}, u32[]{:S(2)}) collective-permute-start(f32[]{:T(128)} %multiply_reduce_fusion), channel_id=1, source_target_pairs={{0,6},{1,7},{2,4},{3,5},{4,2},{5,3},{6,0},{7,1},{8,14},{9,15},{10,... | collective-permute-start | bytes 20 | tf_op jit(solution)/shard_map/ppermute | solution.py:17
  116.3 3.7 %collective-permute-start.6 = (f32[]{:T(128)}, f32[]{:T(128)}, u32[]{:S(2)}, u32[]{:S(2)}) collective-permute-start(f32[]{:T(128)} %multiply_reduce_fusion), channel_id=1, source_target_pairs={{0,2},{1,3},{2,0},{3,1},{4,6},{5,7},{6,4},{7,5},{8,10},{9,11},{10,... | collective-permute-start | bytes 20 | tf_op jit(solution)/shard_map/ppermute | solution.py:17
  117.8 7.4 %copy-start.2 = (bf16[128,1024]{1,0:T(8,128)(2,1)S(1)}, bf16[128,1024]{1,0:T(8,128)(2,1)}, u32[]{:S(2)}) copy-start(bf16[128,1024]{1,0:T(8,128)(2,1)} %param.8) | copy-start | bytes 786436
  117.8 7.6 %copy-start.3 = (bf16[128,1024]{1,0:T(8,128)(2,1)S(1)}, bf16[128,1024]{1,0:T(8,128)(2,1)}, u32[]{:S(2)}) copy-start(bf16[128,1024]{1,0:T(8,128)(2,1)} %param.7) | copy-start | bytes 786436
  118.9 8.4 %copy-start.4 = (bf16[128,1024]{1,0:T(8,128)(2,1)S(1)}, bf16[128,1024]{1,0:T(8,128)(2,1)}, u32[]{:S(2)}) copy-start(bf16[128,1024]{1,0:T(8,128)(2,1)} %param.6) | copy-start | bytes 786436
  122.5 5.1 %copy-start.5 = (bf16[128,1024]{1,0:T(8,128)(2,1)S(1)}, bf16[128,1024]{1,0:T(8,128)(2,1)}, u32[]{:S(2)}) copy-start(bf16[128,1024]{1,0:T(8,128)(2,1)} %param.9) | copy-start | bytes 786436
  122.5 7.0 %collective-permute-start.9 = (f32[]{:T(128)}, f32[]{:T(128)}, u32[]{:S(2)}, u32[]{:S(2)}) collective-permute-start(f32[]{:T(128)} %add.194), channel_id=1, source_target_pairs={{0,1},{1,0},{2,3},{3,2},{4,5},{5,4},{6,7},{7,6},{8,9},{9,8},{10,11... | collective-permute-start | bytes 20 | tf_op jit(solution)/shard_map/ppermute | solution.py:17
Sparse Core Ops, SparseCore 0:
  10.5 75.3 all-gather.2

commit v17 on v15

--- a/solution.py
+++ b/solution.py
@@ -1,8 +1,11 @@
+import functools
 import math
 
 import jax
 import jax.numpy as jnp
 from jax import lax
+from jax.experimental import pallas as pl
+from jax.experimental.pallas import tpu as pltpu
 from jax.sharding import PartitionSpec as P
 
 
@@ -26,6 +29,45 @@
     for bits in rounds:
         value = radix_round(value, axis, *bits)
     return value
+
+
+def _window_kernel(own_first, slots_ref, blocks_ref, own_ref, out_ref, sems):
+    spans, rows = own_ref.shape[0], own_ref.shape[1]
+    halo = slots_ref.shape[0] // spans
+    copies = []
+    for s in range(spans):
+        own_at = 0 if own_first else halo * rows
+        first = rows if own_first else 0
+        copies.append(pltpu.make_async_copy(
+            own_ref.at[s], out_ref.at[s, pl.ds(own_at, rows)], sems.at[s * (halo + 1)]))
+        for h in range(halo):
+            copies.append(pltpu.make_async_copy(
+                blocks_ref.at[slots_ref[s * halo + h]],
+                out_ref.at[s, pl.ds(first + h * rows, rows)],
+                sems.at[s * (halo + 1) + 1 + h],
+            ))
+    for copy in copies:
+        copy.start()
+    for copy in copies:
+        copy.wait()
+
+
+def build_window(blocks, own, slots, own_first):
+    spans, rows, channels = own.shape
+    halo = slots.shape[0] // spans
+    window_bytes = spans * (halo + 1) * rows * channels * own.dtype.itemsize
+    return pl.pallas_call(
+        functools.partial(_window_kernel, own_first),
+        out_shape=jax.ShapeDtypeStruct((spans, (halo + 1) * rows, channels), own.dtype),
+        in_specs=[
+            pl.BlockSpec(memory_space=pltpu.SMEM),
+            pl.BlockSpec(memory_space=pl.ANY),
+            pl.BlockSpec(memory_space=pl.ANY),
+        ],
+        out_specs=pl.BlockSpec(memory_space=pltpu.VMEM),
+        scratch_shapes=[pltpu.SemaphoreType.DMA((spans * (halo + 1),))],
+        cost_estimate=pl.CostEstimate(flops=0, bytes_accessed=2 * window_bytes, transcendentals=0),
+    )(slots, blocks, own)
 
 
 def band_select(taps, out_rows, window, lead):
@@ -60,19 +102,21 @@
     before = mine[:, None] - halo + step[None, :]
     after = mine[:, None] + 1 + step[None, :]
 
-    def pick(blocks, which, wanted):
+    def pick(blocks, which, wanted, own, own_first):
         valid = (wanted >= 0) & (wanted < spans)
         slots = slot_of[jnp.clip(wanted, 0, spans - 1)].reshape(-1)
         slots = ((slots // per_device) * 2 + which) * per_device + slots % per_device
-        taken = jnp.take(blocks, slots, axis=0).reshape(per_device, halo, span_rows, channels)
-        return jnp.where(valid[:, :, None, None], taken, jnp.zeros_like(taken))
+        window_rows = build_window(blocks, own, slots, own_first)
+        keep = jnp.concatenate([jnp.ones((per_device, 1), bool), valid], axis=1) if own_first else (
+            jnp.concatenate([valid, jnp.ones((per_device, 1), bool)], axis=1))
+        keep = jnp.repeat(keep, span_rows, axis=1)
+        return jnp.where(keep[:, :, None], window_rows, jnp.zeros_like(window_rows)).reshape(
+            per_device, window, groups, group_size
+        )
 
     own_mixed = mixed.reshape(per_device, span_rows, channels)
     own_gated = gated.reshape(per_device, span_rows, channels)
-    mixed_window = jnp.concatenate(
-        [pick(blocks, 0, before).reshape(per_device, lead, channels), own_mixed], axis=1
-    )
-    mixed_window = mixed_window.reshape(per_device, window, groups, group_size)
+    mixed_window = pick(blocks, 0, before, own_mixed, False)
 
     select_fwd = band_select(taps, span_rows, window, lead)
     fwd_band = jnp.einsum(
@@ -95,9 +139,7 @@
     seq_rounds = ((0, 3), (1, 2))
     total_grad = radix_round(partial_grad, "seq", *seq_rounds[0])
     total_grad, late_blocks = lax.optimization_barrier((total_grad, blocks))
-    gated_window = jnp.concatenate(
-        [own_gated, pick(late_blocks, 1, after).reshape(per_device, lead, channels)], axis=1
-    ).reshape(per_device, window, groups, group_size)
+    gated_window = pick(late_blocks, 1, after, own_gated, True)
     total_grad = butterfly_sum(total_grad, "seq", seq_rounds[1:])
     total_grad, gated_window = lax.optimization_barrier((total_grad, gated_window))
     adjoint = jnp.einsum("gau,sugc->sagc", bwd_band, gated_window, preferred_element_type=jnp.float32)

time: 139 us -> 138 us (level)
  local copies, waits for them, and re-layouts: 20.1 us -> 10.3 us
  Pallas kernels: 0 us -> 5.67 us
  other arithmetic: 5.74 us -> 9.14 us
  waiting for transfers between devices: 65.9 us -> 63.8 us
  matrix products: 14.3 us -> 16 us
    gather x2 -> x0, local copies, waits for them, and re-layouts: 7.92 us -> none  [pick(): jnp.take(blocks, slots, axis=0)]
    pallas_call x0 -> x2, Pallas kernels: none -> 5.67 us  [build_window(): pl.pallas_call(functools.partial(_window_kernel, own_first), out_shape=ja...]
    select_n x4 -> x2, other arithmetic: 0.38 us -> 2.51 us  [pick(): jnp.where(keep[:, :, None], window_rows, jnp.zeros_like(window_rows))]
    dot_general x1, matrix products: 1.49 us -> 3.08 us  [shards(): jnp.einsum('gau,sugc->sagc', bwd_band, gated_window, preferred_element_ty...]
    unnamed x20 -> x22, local copies, waits for them, and re-layouts: 3.44 us -> 3.45 us
  transfers between devices with their start and end apart: 11 -> 11, of which waited for: 2 -> 1; matrix products, arithmetic and copies ran while one was open for 18% -> 18% of each run, Pallas kernels for 0% -> 2%
where the time goes in v17:
time: 138 us
  waiting for transfers between devices  63.8 us (46%)
  between operations  17.6 us (13%)
  matrix products  16 us (12%)
  starting transfers between devices  14.9 us (11%)
  local copies, waits for them, and re-layouts  10.3 us (7%)
  other arithmetic  9.14 us (7%)
  Pallas kernels  5.67 us (4%)
    all_gather x1, waiting for transfers between devices, shards(): lax.all_gather(jnp.stack([mixed, gated]), 'seq', axis=0, tiled=False)  63.8 us
    ppermute x10, starting transfers between devices, swap(): return lax.ppermute(value, axis, [(i, i ^ mask) for i in range(size)])  14.9 us
    pallas_call x2, Pallas kernels, build_window(): pl.pallas_call(functools.partial(_window_kernel, own_first), out_shape=ja...  5.67 us
    dot_general x1, matrix products, shards(): jnp.einsum('gaw,jaw->gj', corr, select_fwd.astype(jnp.float32), precision...  3.92 us
    dot_general x1, matrix products, shards(): jnp.einsum('gj,jaw->gaw', filters, select_fwd, preferred_element_type=jnp...  3.53 us
    unnamed x22, local copies, waits for them, and re-layouts  3.45 us
    dot_general x1, matrix products, shards(): jnp.einsum('gj,jau->gau', filters, _bwd_select(taps, span_rows, window),...  3.23 us
    dot_general x1, matrix products, shards(): jnp.einsum('gau,sugc->sagc', bwd_band, gated_window, preferred_element_ty...  3.08 us
  transfers between devices with their start and end apart: 11, of which 1 were waited for; matrix products, arithmetic and copies ran while one was open for 18% of the time, Pallas kernels for 2%

profile of v17, /device:TPU:0, one launch (start us, length us, event | category | flops | bytes accessed | tf_op | source)
XLA Modules:
  0.0 137.5 jit_solution(18174010515462450927)
XLA Ops:
  7.2 1.1 multiply_convert_fusion.5
  8.4 1.2 multiply_convert_fusion.4
  9.6 0.9 pad_maximum_fusion
  10.5 0.2 copy.28
  10.7 0.7 broadcast_add_fusion
  11.8 0.2 reshape_reshape.3
  12.2 0.7 scatter_custom_fusion
  12.9 0.6 gather_fusion
  13.5 0.6 gather_fusion.1
  14.4 3.2 %convert_bitcast_fusion = bf16[64,64,192,1]{2,0,1,3:T(8,128)(2,1)} fusion(bf16[64,128]{1,0:T(8,128)(2,1)S(1)} %copy-done), kind=kOutput, calls=%fused_computation.16 | convolution fusion | flops 205258752 | bytes 1589248 | tf_op jit(solution)/shard_map/gj,jau->gau/dot_general | solution.py:125
  17.7 3.5 %convert_bitcast_fusion.1 = bf16[64,64,192,1]{2,0,1,3:T(8,128)(2,1)} fusion(s32[64]{0:T(128)S(1)} %iota_add_fusion, bf16[64,128]{1,0:T(8,128)(2,1)S(1)} %copy-done), kind=kOutput, calls=%fused_computation.17 | convolution fusion | flops 205258752 | bytes 1589504 | tf_op jit(solution)/shard_map/gj,jaw->gaw/dot_general | solution.py:122
  21.2 0.5 fusion.37.slots_ref
  21.7 0.5 fusion.38.slots_ref
  22.2 63.8 %all-gather.3.cloned.1.call-done = bf16[32,128,1024]{2,1,0:T(8,128)(2,1)} async-done(((bf16[2,128,1024]{2,1,0:T(8,128)(2,1)}), bf16[32,128,1024]{2,1,0:T(8,128)(2,1)}) %all-gather.3.cloned.1.call-update) | async-done | bytes 8388624 | tf_op jit(solution)/shard_map/all_gather | solution.py:96
  86.0 2.9 %shard_map.101 = bf16[2,192,1024]{2,1,0:T(8,128)(2,1)} custom-call(s32[4]{0:T(128)} %fusion.37.slots_ref, bf16[64,64,1024]{2,1,0:T(8,128)(2,1)} %bitcast.39, bf16[2,64,1024]{2,1,0:T(8,128)(2,1)} %bitcast.47), custom_call_target="tpu_custom_call" | custom-call | bytes 1572864 | tf_op jit(solution)/shard_map/pallas_call | solution.py:59
  88.9 1.3 broadcast_select_fusion.1
  90.2 0.5 copy.29
  90.7 0.8 convolution_bitcast_fusion
  91.4 3.9 %fusion.28 = f32[64,128]{1,0:T(8,128)S(1)} fusion(s32[64]{0:T(128)S(1)} %iota_add_fusion, f32[64,64,192]{2,1,0:T(8,128)S(1)} %convolution_bitcast_fusion), kind=kOutput, calls=%fused_computation.24 | convolution fusion | flops 607125504 | bytes 3178752 | tf_op jit(solution)/shard_map/gaw,jaw->gj/dot_general | solution.py:136
  95.4 0.3 collective-permute-start
  95.7 0.4 collective-permute-start.1
  96.1 2.7 %collective-permute-start.2 = (f32[64,128]{1,0:T(8,128)S(1)}, f32[64,128]{1,0:T(8,128)S(1)}, u32[]{:S(2)}, u32[]{:S(2)}) collective-permute-start(f32[64,128]{1,0:T(8,128)S(1)} %fusion.28), channel_id=1, source_target_pairs={{0,72},{8,64},{16,88},{24,80},{32,104},{40,96},{48,120},{56,112},{... | collective-permute-start | bytes 98312 | tf_op jit(solution)/shard_map/ppermute | solution.py:18
  98.8 1.5 %fusion.16 = f32[2,64,64,16]{1,3,0,2:T(8,128)S(1)} fusion(bf16[64,64,192,1]{2,0,1,3:T(8,128)(2,1)S(1)} %copy-done.3, bf16[2,192,64,16]{1,3,2,0:T(8,128)(2,1)S(1)} %bitcast.42), kind=kOutput, calls=%fused_computation.20 | convolution fusion | flops 50593792 | bytes 2883584 | tf_op jit(solution)/shard_map/gaw,swgc->sagc/dot_general | solution.py:130
  100.3 0.5 copy.37
  100.9 0.6 reshape.134
  101.5 0.3 collective-permute-start.3
  101.8 2.3 %collective-permute-start.4 = (f32[64,128]{1,0:T(8,128)S(1)}, f32[64,128]{1,0:T(8,128)S(1)}, u32[]{:S(2)}, u32[]{:S(2)}) collective-permute-start(f32[64,128]{1,0:T(8,128)S(1)} %add_add_fusion.1), channel_id=1, source_target_pairs={{0,32},{8,40},{16,48},{24,56},{32,0},{40,8},{48,16},{56,24},{64,96... | collective-permute-start | bytes 98312 | tf_op jit(solution)/shard_map/ppermute | solution.py:18
  104.1 2.2 %collective-permute-start.5 = (f32[64,128]{1,0:T(8,128)S(1)}, f32[64,128]{1,0:T(8,128)S(1)}, u32[]{:S(2)}, u32[]{:S(2)}) collective-permute-start(f32[64,128]{1,0:T(8,128)S(1)} %add_add_fusion.1), channel_id=1, source_target_pairs={{0,48},{8,56},{16,32},{24,40},{32,16},{40,24},{48,0},{56,8},{64,11... | collective-permute-start | bytes 98312 | tf_op jit(solution)/shard_map/ppermute | solution.py:18
  106.3 2.8 %shard_map.102 = bf16[2,192,1024]{2,1,0:T(8,128)(2,1)} custom-call(s32[4]{0:T(128)} %fusion.38.slots_ref, bf16[64,64,1024]{2,1,0:T(8,128)(2,1)} %bitcast.40, bf16[2,64,1024]{2,1,0:T(8,128)(2,1)} %bitcast.44), custom_call_target="tpu_custom_call" | custom-call | bytes 1572864 | tf_op jit(solution)/shard_map/pallas_call | solution.py:59
  109.1 1.3 broadcast_select_fusion
  110.4 0.5 copy.33
  111.0 0.6 multiply_reduce_fusion
  111.6 3.0 %collective-permute-start.7 = (f32[]{:T(128)}, f32[]{:T(128)}, u32[]{:S(2)}, u32[]{:S(2)}) collective-permute-start(f32[]{:T(128)} %multiply_reduce_fusion), channel_id=1, source_target_pairs={{0,4},{1,5},{2,6},{3,7},{4,0},{5,1},{6,2},{7,3},{8,12},{9,13},{10,... | collective-permute-start | bytes 20 | tf_op jit(solution)/shard_map/ppermute | solution.py:18
  114.6 1.2 collective-permute-start.8
  115.7 3.1 %fusion.25 = f32[2,64,64,16]{1,3,0,2:T(8,128)S(1)} fusion(bf16[64,64,192,1]{2,0,1,3:T(8,128)(2,1)} %convert_bitcast_fusion, bf16[2,192,64,16]{1,3,2,0:T(8,128)(2,1)S(1)} %bitcast.45), kind=kOutput, calls=%fused_computation.23 | convolution fusion | flops 50593792 | bytes 2883584 | tf_op jit(solution)/shard_map/gau,sugc->sagc/dot_general | solution.py:145
  118.8 0.5 copy.41
  119.4 0.6 reshape.135
  122.5 2.5 %collective-permute-start.9 = (f32[]{:T(128)}, f32[]{:T(128)}, u32[]{:S(2)}, u32[]{:S(2)}) collective-permute-start(f32[]{:T(128)} %add.186), channel_id=1, source_target_pairs={{0,1},{1,0},{2,3},{3,2},{4,5},{5,4},{6,7},{7,6},{8,9},{9,8},{10,11... | collective-permute-start | bytes 20 | tf_op jit(solution)/shard_map/ppermute | solution.py:18
  125.0 0.2 copy.42
  125.2 0.2 copy.43
  125.4 0.1 multiply_convert_fusion
  125.5 0.9 copy.46
  126.3 0.8 copy.47
  127.2 0.2 copy.34
  127.4 0.2 copy.38
  127.7 0.9 copy.44
  128.5 0.8 copy.45
  130.0 0.6 broadcast_multiply_fusion
  (49 shorter events, 1.0 us)
Async XLA Ops:
  7.2 7.3 %copy-start = (bf16[64,128]{1,0:T(8,128)(2,1)S(1)}, bf16[64,128]{1,0:T(8,128)(2,1)}, u32[]{:S(2)}) copy-start(bf16[64,128]{1,0:T(8,128)(2,1)} %param.10) | copy-start | bytes 49156
  7.2 5.0 %copy-start.8 = (s32[32]{0:T(128)S(1)}, s32[32]{0:T(128)}, u32[]{:S(2)}) copy-start(s32[32]{0:T(128)} %param.11) | copy-start | bytes 388
  7.2 78.8 %all-gather.3.cloned.1.call-start = ((), (), s32[]{:S(2)}) async-start(), calls=%async_computation | async-start | bytes 8912896 | tf_op jit(solution)/shard_map/all_gather | solution.py:96
  8.3 9.3 %copy-start.1 = (bf16[128,1024]{1,0:T(8,128)(2,1)}, bf16[128,1024]{1,0:T(8,128)(2,1)S(1)}, u32[]{:S(2)}) copy-start(bf16[128,1024]{1,0:T(8,128)(2,1)S(1)} %multiply_convert_fusion.5) | copy-start | bytes 786436
  9.5 11.6 %copy-start.2 = (bf16[128,1024]{1,0:T(8,128)(2,1)}, bf16[128,1024]{1,0:T(8,128)(2,1)S(1)}, u32[]{:S(2)}) copy-start(bf16[128,1024]{1,0:T(8,128)(2,1)S(1)} %multiply_convert_fusion.4) | copy-start | bytes 786436
  90.7 8.1 %copy-start.3 = (bf16[64,64,192,1]{2,0,1,3:T(8,128)(2,1)S(1)}, bf16[64,64,192,1]{2,0,1,3:T(8,128)(2,1)}, u32[]{:S(2)}) copy-start(bf16[64,64,192,1]{2,0,1,3:T(8,128)(2,1)} %convert_bitcast_fusion.1) | copy-start | bytes 4718596
  95.4 6.1 %collective-permute-start = (f32[64,128]{1,0:T(8,128)S(1)}, f32[64,128]{1,0:T(8,128)S(1)}, u32[]{:S(2)}, u32[]{:S(2)}) collective-permute-start(f32[64,128]{1,0:T(8,128)S(1)} %fusion.28), channel_id=1, source_target_pairs={{0,8},{8,0},{16,24},{24,16},{32,40},{40,32},{48,56},{56,48},{64,72... | collective-permute-start | bytes 98312 | tf_op jit(solution)/shard_map/ppermute | solution.py:18
  95.7 5.8 %collective-permute-start.1 = (f32[64,128]{1,0:T(8,128)S(1)}, f32[64,128]{1,0:T(8,128)S(1)}, u32[]{:S(2)}, u32[]{:S(2)}) collective-permute-start(f32[64,128]{1,0:T(8,128)S(1)} %fusion.28), channel_id=1, source_target_pairs={{0,64},{8,72},{16,80},{24,88},{32,96},{40,104},{48,112},{56,120},{... | collective-permute-start | bytes 98312 | tf_op jit(solution)/shard_map/ppermute | solution.py:18
  96.1 5.4 %collective-permute-start.2 = (f32[64,128]{1,0:T(8,128)S(1)}, f32[64,128]{1,0:T(8,128)S(1)}, u32[]{:S(2)}, u32[]{:S(2)}) collective-permute-start(f32[64,128]{1,0:T(8,128)S(1)} %fusion.28), channel_id=1, source_target_pairs={{0,72},{8,64},{16,88},{24,80},{32,104},{40,96},{48,120},{56,112},{... | collective-permute-start | bytes 98312 | tf_op jit(solution)/shard_map/ppermute | solution.py:18
  101.5 9.4 %collective-permute-start.3 = (f32[64,128]{1,0:T(8,128)S(1)}, f32[64,128]{1,0:T(8,128)S(1)}, u32[]{:S(2)}, u32[]{:S(2)}) collective-permute-start(f32[64,128]{1,0:T(8,128)S(1)} %add_add_fusion.1), channel_id=1, source_target_pairs={{0,16},{8,24},{16,0},{24,8},{32,48},{40,56},{48,32},{56,40},{64,80... | collective-permute-start | bytes 98312 | tf_op jit(solution)/shard_map/ppermute | solution.py:18
  101.8 9.1 %collective-permute-start.4 = (f32[64,128]{1,0:T(8,128)S(1)}, f32[64,128]{1,0:T(8,128)S(1)}, u32[]{:S(2)}, u32[]{:S(2)}) collective-permute-start(f32[64,128]{1,0:T(8,128)S(1)} %add_add_fusion.1), channel_id=1, source_target_pairs={{0,32},{8,40},{16,48},{24,56},{32,0},{40,8},{48,16},{56,24},{64,96... | collective-permute-start | bytes 98312 | tf_op jit(solution)/shard_map/ppermute | solution.py:18
  104.1 6.9 %collective-permute-start.5 = (f32[64,128]{1,0:T(8,128)S(1)}, f32[64,128]{1,0:T(8,128)S(1)}, u32[]{:S(2)}, u32[]{:S(2)}) collective-permute-start(f32[64,128]{1,0:T(8,128)S(1)} %add_add_fusion.1), channel_id=1, source_target_pairs={{0,48},{8,56},{16,32},{24,40},{32,16},{40,24},{48,0},{56,8},{64,11... | collective-permute-start | bytes 98312 | tf_op jit(solution)/shard_map/ppermute | solution.py:18
  110.9 14.1 %copy-start.4 = (bf16[128,1024]{1,0:T(8,128)(2,1)S(1)}, bf16[128,1024]{1,0:T(8,128)(2,1)}, u32[]{:S(2)}) copy-start(bf16[128,1024]{1,0:T(8,128)(2,1)} %param.8) | copy-start | bytes 786436
  111.6 13.6 %copy-start.5 = (bf16[128,1024]{1,0:T(8,128)(2,1)S(1)}, bf16[128,1024]{1,0:T(8,128)(2,1)}, u32[]{:S(2)}) copy-start(bf16[128,1024]{1,0:T(8,128)(2,1)} %param.7) | copy-start | bytes 786436
  111.6 9.7 %collective-permute-start.7 = (f32[]{:T(128)}, f32[]{:T(128)}, u32[]{:S(2)}, u32[]{:S(2)}) collective-permute-start(f32[]{:T(128)} %multiply_reduce_fusion), channel_id=1, source_target_pairs={{0,4},{1,5},{2,6},{3,7},{4,0},{5,1},{6,2},{7,3},{8,12},{9,13},{10,... | collective-permute-start | bytes 20 | tf_op jit(solution)/shard_map/ppermute | solution.py:18
  114.6 6.7 %collective-permute-start.8 = (f32[]{:T(128)}, f32[]{:T(128)}, u32[]{:S(2)}, u32[]{:S(2)}) collective-permute-start(f32[]{:T(128)} %multiply_reduce_fusion), channel_id=1, source_target_pairs={{0,6},{1,7},{2,4},{3,5},{4,2},{5,3},{6,0},{7,1},{8,14},{9,15},{10,... | collective-permute-start | bytes 20 | tf_op jit(solution)/shard_map/ppermute | solution.py:18
  115.7 4.2 %collective-permute-start.6 = (f32[]{:T(128)}, f32[]{:T(128)}, u32[]{:S(2)}, u32[]{:S(2)}) collective-permute-start(f32[]{:T(128)} %multiply_reduce_fusion), channel_id=1, source_target_pairs={{0,2},{1,3},{2,0},{3,1},{4,6},{5,7},{6,4},{7,5},{8,10},{9,11},{10,... | collective-permute-start | bytes 20 | tf_op jit(solution)/shard_map/ppermute | solution.py:18
  118.8 8.4 %copy-start.6 = (bf16[128,1024]{1,0:T(8,128)(2,1)S(1)}, bf16[128,1024]{1,0:T(8,128)(2,1)}, u32[]{:S(2)}) copy-start(bf16[128,1024]{1,0:T(8,128)(2,1)} %param.6) | copy-start | bytes 786436
  118.8 8.6 %copy-start.7 = (bf16[128,1024]{1,0:T(8,128)(2,1)S(1)}, bf16[128,1024]{1,0:T(8,128)(2,1)}, u32[]{:S(2)}) copy-start(bf16[128,1024]{1,0:T(8,128)(2,1)} %param.9) | copy-start | bytes 786436
  122.5 6.9 %collective-permute-start.9 = (f32[]{:T(128)}, f32[]{:T(128)}, u32[]{:S(2)}, u32[]{:S(2)}) collective-permute-start(f32[]{:T(128)} %add.186), channel_id=1, source_target_pairs={{0,1},{1,0},{2,3},{3,2},{4,5},{5,4},{6,7},{7,6},{8,9},{9,8},{10,11... | collective-permute-start | bytes 20 | tf_op jit(solution)/shard_map/ppermute | solution.py:18
Sparse Core Ops, SparseCore 0:
  10.6 75.3 all-gather.2

commit v18 on v16

--- a/solution.py
+++ b/solution.py
@@ -112,12 +112,12 @@
     conv = jnp.einsum("gaw,swgc->sagc", fwd_band, mixed_window, preferred_element_type=jnp.float32)
     convolved = conv.reshape(rows, channels).astype(jnp.bfloat16)
     own_gated_g = own_gated.reshape(per_device, span_rows, groups, group_size)
-    corr = jnp.einsum(
-        "sagc,swgc->gaw", own_gated_g, mixed_window, preferred_element_type=jnp.float32
-    )
-    partial_grad = jnp.einsum(
-        "gaw,jaw->gj", corr, select_fwd.astype(jnp.float32), precision=lax.Precision.HIGH
-    )
+    def lag_sums(source, select):
+        corr = jnp.einsum("sagc,swgc->gaw", own_gated_g, source, preferred_element_type=jnp.float32)
+        return jnp.einsum("gaw,jaw->gj", corr, select.astype(jnp.float32), precision=lax.Precision.HIGH)
+
+    own_lags = lag_sums(own_mixed.reshape(per_device, span_rows, groups, group_size), select_fwd[:, :, lead:])
+    partial_grad = lag_sums(mixed_window[:, :lead], select_fwd[:, :, :lead]) + own_lags
     seq_rounds = ((0, 3), (1, 2))
     total_grad = radix_round(partial_grad, "seq", *seq_rounds[0])
     total_grad, late_blocks = lax.optimization_barrier((total_grad, blocks))

time: 138 us -> 138 us (level)
  waiting for transfers between devices: 65 us -> 60.5 us
  other arithmetic: 6.49 us -> 9.1 us
    all_gather x1, waiting for transfers between devices: 63.9 us -> 59.5 us  [shards(): lax.all_gather(jnp.stack([mixed, gated]), 'seq', axis=0, tiled=False)]
    eq x0 -> x1, other arithmetic: none -> 2.65 us  [band_select(): return (w == lead + a - j).astype(jnp.bfloat16)]
    unnamed x20 -> x24, local copies, waits for them, and re-layouts: 3.44 us -> 4.48 us
    dot_general x2 -> x4, matrix products: 4.68 us -> 5.67 us  [the longest x2 3.37 us: lag_sums(): jnp.einsum('gaw,jaw->gj', corr, select.astype(jnp.float32), precision=lax...]
  transfers between devices with their start and end apart: 11 -> 11, of which waited for: 2 -> 2; matrix products, arithmetic and copies ran while one was open for 17% -> 20% of each run, Pallas kernels for 2% -> 2%
where the time goes in v18:
time: 138 us
  waiting for transfers between devices  60.5 us (44%)
  between operations  17.7 us (13%)
  matrix products  15.3 us (11%)
  starting transfers between devices  15.1 us (11%)
  local copies, waits for them, and re-layouts  15 us (11%)
  other arithmetic  9.1 us (7%)
  Pallas kernels  5.18 us (4%)
    all_gather x1, waiting for transfers between devices, shards(): lax.all_gather(jnp.stack([mixed, gated]), 'seq', axis=0, tiled=False)  59.5 us
    ppermute x10, starting transfers between devices, swap(): return lax.ppermute(value, axis, [(i, i ^ mask) for i in range(size)])  15.1 us
    pallas_call x2, Pallas kernels, take_blocks(): pl.pallas_call(_take_kernel, out_shape=jax.ShapeDtypeStruct((count,) + bl...  5.18 us
    unnamed x24, local copies, waits for them, and re-layouts  4.48 us
    dot_general x1, matrix products, shards(): jnp.einsum('gj,jaw->gaw', filters, select_fwd, preferred_element_type=jnp...  3.53 us
    dot_general x2, matrix products, lag_sums(): jnp.einsum('gaw,jaw->gj', corr, select.astype(jnp.float32), precision=lax...  3.37 us
    dot_general x1, matrix products, shards(): jnp.einsum('gj,jau->gau', filters, _bwd_select(taps, span_rows, window),...  3.23 us
    pallas_call x2, local copies, waits for them, and re-layouts, take_blocks(): pl.pallas_call(_take_kernel, out_shape=jax.ShapeDtypeStruct((count,) + bl...  3.21 us
  transfers between devices with their start and end apart: 11, of which 2 were waited for; matrix products, arithmetic and copies ran while one was open for 20% of the time, Pallas kernels for 2%

profile of v18, /device:TPU:0, one launch (start us, length us, event | category | flops | bytes accessed | tf_op | source)
XLA Modules:
  0.0 137.8 jit_solution(6378274952576944175)
XLA Ops:
  7.2 1.1 multiply_convert_fusion.4
  8.3 1.1 multiply_convert_fusion.5
  9.4 0.8 pad_maximum_fusion.1
  11.2 0.2 reshape_reshape.6
  11.4 0.2 reshape_reshape.7
  11.8 0.7 scatter_custom_fusion
  12.5 0.6 gather_fusion
  13.1 0.6 gather_fusion.1
  14.1 1.8 %convolution_bitcast_fusion = f32[64,64,64]{2,1,0:T(8,128)} fusion(bf16[2,64,64,16]{1,0,3,2:T(2,128)(2,1)S(1)} %reshape_reshape.7, bf16[2,64,64,16]{1,0,3,2:T(2,128)(2,1)S(1)} %reshape_reshape.6), kind=kOutput, calls=%fused_computation.18 | convolution fusion | flops 16777216 | bytes 1572864 | tf_op jit(solution)/shard_map/sagc,swgc->gaw/dot_general | solution.py:116
  15.9 3.2 %convert_bitcast_fusion = bf16[64,64,192,1]{2,0,1,3:T(8,128)(2,1)} fusion(bf16[64,128]{1,0:T(8,128)(2,1)S(1)} %copy-done), kind=kOutput, calls=%fused_computation.16 | convolution fusion | flops 205258752 | bytes 1589248 | tf_op jit(solution)/shard_map/gj,jau->gau/dot_general | solution.py:107
  19.1 3.5 %convert_bitcast_fusion.1 = bf16[64,64,192,1]{2,0,1,3:T(8,128)(2,1)} fusion(s32[64]{0:T(128)S(1)} %iota_add_fusion, bf16[64,128]{1,0:T(8,128)(2,1)S(1)} %copy-done), kind=kOutput, calls=%fused_computation.17 | convolution fusion | flops 205258752 | bytes 1589504 | tf_op jit(solution)/shard_map/gj,jaw->gaw/dot_general | solution.py:104
  22.7 0.5 fusion.49.slots_ref
  23.2 0.5 fusion.50.slots_ref
  23.7 2.7 %subtract_compare_fusion = pred[128,64,192]{2,0,1:T(32,128)(4,1)} fusion(s32[64]{0:T(128)S(1)} %iota_add_fusion), kind=kLoop, calls=%fused_computation.3 | loop fusion | flops 3145728 | bytes 1573120 | tf_op jit(solution)/shard_map/eq | solution.py:61
  26.4 59.5 %all-gather.3.cloned.1.call-done = bf16[32,128,1024]{2,1,0:T(8,128)(2,1)} async-done(((bf16[2,128,1024]{2,1,0:T(8,128)(2,1)}), bf16[32,128,1024]{2,1,0:T(8,128)(2,1)}) %all-gather.3.cloned.1.call-update) | async-done | bytes 8388624 | tf_op jit(solution)/shard_map/all_gather | solution.py:80
  85.8 2.6 %shard_map.101 = bf16[4,64,1024]{2,1,0:T(8,128)(2,1)} custom-call(s32[4]{0:T(128)} %fusion.49.slots_ref, bf16[64,64,1024]{2,1,0:T(8,128)(2,1)} %bitcast.50), custom_call_target="tpu_custom_call" | custom-call | bytes 1048576 | tf_op jit(solution)/shard_map/pallas_call | solution.py:47
  88.4 1.6 %copy.34 = bf16[4,64,1024]{1,0,2:T(4,128)(2,1)S(1)} copy(bf16[4,64,1024]{2,1,0:T(8,128)(2,1)} %shard_map.101) | data formatting | bytes 1048576 | tf_op jit(solution)/shard_map/pallas_call | solution.py:47
  90.1 0.5 reshape.185
  90.6 0.5 convolution_bitcast_fusion.1
  91.1 1.0 copy-done.2
  92.1 1.6 %fusion.29 = f32[64,128]{1,0:T(8,128)S(1)} fusion(pred[128,64,192]{2,0,1:T(32,128)(4,1)S(1)} %copy-done.2, f32[64,64,128]{2,1,0:T(8,128)S(1)} %convolution_bitcast_fusion.1), kind=kOutput, calls=%fused_computation.26 | convolution fusion | flops 402653184 | bytes 3178496 | tf_op jit(solution)/shard_map/gaw,jaw->gj/dot_general | solution.py:117
  93.7 1.8 %fusion.39 = f32[64,128]{1,0:T(8,128)S(1)} fusion(f32[64,128]{1,0:T(8,128)S(1)} %fusion.29, pred[128,64,192]{2,0,1:T(32,128)(4,1)S(1)} %copy-done.2, f32[64,64,64]{2,1,0:T(8,128)S(1)} %copy-done.1), kind=kOutput, calls=%fused_computation.28 | convolution fusion | flops 201334784 | bytes 3211264 | tf_op jit(solution)/shard_map/gaw,jaw->gj/dot_general | solution.py:117
  95.5 0.3 collective-permute-start
  95.9 0.4 collective-permute-start.1
  96.2 2.7 %collective-permute-start.2 = (f32[64,128]{1,0:T(8,128)S(1)}, f32[64,128]{1,0:T(8,128)S(1)}, u32[]{:S(2)}, u32[]{:S(2)}) collective-permute-start(f32[64,128]{1,0:T(8,128)S(1)} %fusion.39), channel_id=1, source_target_pairs={{0,72},{8,64},{16,88},{24,80},{32,104},{40,96},{48,120},{56,112},{... | collective-permute-start | bytes 98312 | tf_op jit(solution)/shard_map/ppermute | solution.py:17
  99.0 1.3 fusion.17
  100.3 0.5 copy.50
  100.9 0.6 reshape.188
  101.5 0.3 collective-permute-start.3
  101.8 2.3 %collective-permute-start.4 = (f32[64,128]{1,0:T(8,128)S(1)}, f32[64,128]{1,0:T(8,128)S(1)}, u32[]{:S(2)}, u32[]{:S(2)}) collective-permute-start(f32[64,128]{1,0:T(8,128)S(1)} %add_add_fusion.1), channel_id=1, source_target_pairs={{0,32},{8,40},{16,48},{24,56},{32,0},{40,8},{48,16},{56,24},{64,96... | collective-permute-start | bytes 98312 | tf_op jit(solution)/shard_map/ppermute | solution.py:17
  104.0 2.2 %collective-permute-start.5 = (f32[64,128]{1,0:T(8,128)S(1)}, f32[64,128]{1,0:T(8,128)S(1)}, u32[]{:S(2)}, u32[]{:S(2)}) collective-permute-start(f32[64,128]{1,0:T(8,128)S(1)} %add_add_fusion.1), channel_id=1, source_target_pairs={{0,48},{8,56},{16,32},{24,40},{32,16},{40,24},{48,0},{56,8},{64,11... | collective-permute-start | bytes 98312 | tf_op jit(solution)/shard_map/ppermute | solution.py:17
  106.3 2.6 %shard_map.102 = bf16[4,64,1024]{2,1,0:T(8,128)(2,1)} custom-call(s32[4]{0:T(128)} %fusion.50.slots_ref, bf16[64,64,1024]{2,1,0:T(8,128)(2,1)} %bitcast.51), custom_call_target="tpu_custom_call" | custom-call | bytes 1048576 | tf_op jit(solution)/shard_map/pallas_call | solution.py:47
  108.9 1.6 %copy.43 = bf16[4,64,1024]{1,0,2:T(4,128)(2,1)S(1)} copy(bf16[4,64,1024]{2,1,0:T(8,128)(2,1)} %shard_map.102) | data formatting | bytes 1048576 | tf_op jit(solution)/shard_map/pallas_call | solution.py:47
  110.5 0.5 reshape.187
  111.1 0.5 pad_maximum_fusion
  111.6 0.6 multiply_reduce_fusion
  112.2 3.0 %collective-permute-start.7 = (f32[]{:T(128)}, f32[]{:T(128)}, u32[]{:S(2)}, u32[]{:S(2)}) collective-permute-start(f32[]{:T(128)} %multiply_reduce_fusion), channel_id=1, source_target_pairs={{0,4},{1,5},{2,6},{3,7},{4,0},{5,1},{6,2},{7,3},{8,12},{9,13},{10,... | collective-permute-start | bytes 20 | tf_op jit(solution)/shard_map/ppermute | solution.py:17
  115.2 1.2 collective-permute-start.8
  116.4 1.5 %fusion.26 = f32[2,64,64,16]{1,3,0,2:T(8,128)S(1)} fusion(bf16[2,192,64,16]{1,3,0,2:T(8,128)(2,1)S(1)} %pad_maximum_fusion, bf16[64,64,192,1]{2,0,1,3:T(8,128)(2,1)S(1)} %copy-done.3), kind=kOutput, calls=%fused_computation.25 | convolution fusion | flops 50593792 | bytes 2883584 | tf_op jit(solution)/shard_map/gau,sugc->sagc/dot_general | solution.py:129
  117.9 0.5 copy.53
  118.4 0.6 reshape.189
  119.0 1.0 collective-permute-done.6
  122.7 2.7 %collective-permute-start.9 = (f32[]{:T(128)}, f32[]{:T(128)}, u32[]{:S(2)}, u32[]{:S(2)}) collective-permute-start(f32[]{:T(128)} %add.200), channel_id=1, source_target_pairs={{0,1},{1,0},{2,3},{3,2},{4,5},{5,4},{6,7},{7,6},{8,9},{9,8},{10,11... | collective-permute-start | bytes 20 | tf_op jit(solution)/shard_map/ppermute | solution.py:17
  125.8 0.9 copy.58
  126.7 0.8 copy.59
  128.0 0.9 copy.56
  128.9 0.8 copy.57
  130.4 0.6 broadcast_multiply_fusion
  (59 shorter events, 2.4 us)
Async XLA Ops:
  7.2 8.7 %copy-start = (bf16[64,128]{1,0:T(8,128)(2,1)S(1)}, bf16[64,128]{1,0:T(8,128)(2,1)}, u32[]{:S(2)}) copy-start(bf16[64,128]{1,0:T(8,128)(2,1)} %param.10) | copy-start | bytes 49156
  7.2 3.5 %copy-start.8 = (s32[32]{0:T(128)S(1)}, s32[32]{0:T(128)}, u32[]{:S(2)}) copy-start(s32[32]{0:T(128)} %param.11) | copy-start | bytes 388
  7.2 78.7 %all-gather.3.cloned.1.call-start = ((), (), s32[]{:S(2)}) async-start(), calls=%async_computation | async-start | bytes 8912896 | tf_op jit(solution)/shard_map/all_gather | solution.py:80
  90.5 1.6 %copy-start.2 = (pred[128,64,192]{2,0,1:T(32,128)(4,1)S(1)}, pred[128,64,192]{2,0,1:T(32,128)(4,1)}, u32[]{:S(2)}) copy-start(pred[128,64,192]{2,0,1:T(32,128)(4,1)} %subtract_compare_fusion) | copy-start | bytes 4718596
  92.1 1.6 %copy-start.1 = (f32[64,64,64]{2,1,0:T(8,128)S(1)}, f32[64,64,64]{2,1,0:T(8,128)}, u32[]{:S(2)}) copy-start(f32[64,64,64]{2,1,0:T(8,128)} %convolution_bitcast_fusion) | copy-start | bytes 3145732
  93.7 5.3 %copy-start.9 = (bf16[64,64,192,1]{2,0,1,3:T(8,128)(2,1)S(1)}, bf16[64,64,192,1]{2,0,1,3:T(8,128)(2,1)}, u32[]{:S(2)}) copy-start(bf16[64,64,192,1]{2,0,1,3:T(8,128)(2,1)} %convert_bitcast_fusion.1) | copy-start | bytes 4718596
  95.5 5.9 %collective-permute-start = (f32[64,128]{1,0:T(8,128)S(1)}, f32[64,128]{1,0:T(8,128)S(1)}, u32[]{:S(2)}, u32[]{:S(2)}) collective-permute-start(f32[64,128]{1,0:T(8,128)S(1)} %fusion.39), channel_id=1, source_target_pairs={{0,8},{8,0},{16,24},{24,16},{32,40},{40,32},{48,56},{56,48},{64,72... | collective-permute-start | bytes 98312 | tf_op jit(solution)/shard_map/ppermute | solution.py:17
  95.9 5.6 %collective-permute-start.1 = (f32[64,128]{1,0:T(8,128)S(1)}, f32[64,128]{1,0:T(8,128)S(1)}, u32[]{:S(2)}, u32[]{:S(2)}) collective-permute-start(f32[64,128]{1,0:T(8,128)S(1)} %fusion.39), channel_id=1, source_target_pairs={{0,64},{8,72},{16,80},{24,88},{32,96},{40,104},{48,112},{56,120},{... | collective-permute-start | bytes 98312 | tf_op jit(solution)/shard_map/ppermute | solution.py:17
  96.2 5.2 %collective-permute-start.2 = (f32[64,128]{1,0:T(8,128)S(1)}, f32[64,128]{1,0:T(8,128)S(1)}, u32[]{:S(2)}, u32[]{:S(2)}) collective-permute-start(f32[64,128]{1,0:T(8,128)S(1)} %fusion.39), channel_id=1, source_target_pairs={{0,72},{8,64},{16,88},{24,80},{32,104},{40,96},{48,120},{56,112},{... | collective-permute-start | bytes 98312 | tf_op jit(solution)/shard_map/ppermute | solution.py:17
  101.5 10.1 %collective-permute-start.3 = (f32[64,128]{1,0:T(8,128)S(1)}, f32[64,128]{1,0:T(8,128)S(1)}, u32[]{:S(2)}, u32[]{:S(2)}) collective-permute-start(f32[64,128]{1,0:T(8,128)S(1)} %add_add_fusion.1), channel_id=1, source_target_pairs={{0,16},{8,24},{16,0},{24,8},{32,48},{40,56},{48,32},{56,40},{64,80... | collective-permute-start | bytes 98312 | tf_op jit(solution)/shard_map/ppermute | solution.py:17
  101.8 9.8 %collective-permute-start.4 = (f32[64,128]{1,0:T(8,128)S(1)}, f32[64,128]{1,0:T(8,128)S(1)}, u32[]{:S(2)}, u32[]{:S(2)}) collective-permute-start(f32[64,128]{1,0:T(8,128)S(1)} %add_add_fusion.1), channel_id=1, source_target_pairs={{0,32},{8,40},{16,48},{24,56},{32,0},{40,8},{48,16},{56,24},{64,96... | collective-permute-start | bytes 98312 | tf_op jit(solution)/shard_map/ppermute | solution.py:17
  104.0 7.6 %collective-permute-start.5 = (f32[64,128]{1,0:T(8,128)S(1)}, f32[64,128]{1,0:T(8,128)S(1)}, u32[]{:S(2)}, u32[]{:S(2)}) collective-permute-start(f32[64,128]{1,0:T(8,128)S(1)} %add_add_fusion.1), channel_id=1, source_target_pairs={{0,48},{8,56},{16,32},{24,40},{32,16},{40,24},{48,0},{56,8},{64,11... | collective-permute-start | bytes 98312 | tf_op jit(solution)/shard_map/ppermute | solution.py:17
  111.0 5.4 %copy-start.3 = (bf16[64,64,192,1]{2,0,1,3:T(8,128)(2,1)S(1)}, bf16[64,64,192,1]{2,0,1,3:T(8,128)(2,1)}, u32[]{:S(2)}) copy-start(bf16[64,64,192,1]{2,0,1,3:T(8,128)(2,1)} %convert_bitcast_fusion) | copy-start | bytes 4718596
  112.2 9.1 %collective-permute-start.7 = (f32[]{:T(128)}, f32[]{:T(128)}, u32[]{:S(2)}, u32[]{:S(2)}) collective-permute-start(f32[]{:T(128)} %multiply_reduce_fusion), channel_id=1, source_target_pairs={{0,4},{1,5},{2,6},{3,7},{4,0},{5,1},{6,2},{7,3},{8,12},{9,13},{10,... | collective-permute-start | bytes 20 | tf_op jit(solution)/shard_map/ppermute | solution.py:17
  115.2 6.2 %collective-permute-start.8 = (f32[]{:T(128)}, f32[]{:T(128)}, u32[]{:S(2)}, u32[]{:S(2)}) collective-permute-start(f32[]{:T(128)} %multiply_reduce_fusion), channel_id=1, source_target_pairs={{0,6},{1,7},{2,4},{3,5},{4,2},{5,3},{6,0},{7,1},{8,14},{9,15},{10,... | collective-permute-start | bytes 20 | tf_op jit(solution)/shard_map/ppermute | solution.py:17
  116.4 3.7 %collective-permute-start.6 = (f32[]{:T(128)}, f32[]{:T(128)}, u32[]{:S(2)}, u32[]{:S(2)}) collective-permute-start(f32[]{:T(128)} %multiply_reduce_fusion), channel_id=1, source_target_pairs={{0,2},{1,3},{2,0},{3,1},{4,6},{5,7},{6,4},{7,5},{8,10},{9,11},{10,... | collective-permute-start | bytes 20 | tf_op jit(solution)/shard_map/ppermute | solution.py:17
  117.9 7.5 %copy-start.4 = (bf16[128,1024]{1,0:T(8,128)(2,1)S(1)}, bf16[128,1024]{1,0:T(8,128)(2,1)}, u32[]{:S(2)}) copy-start(bf16[128,1024]{1,0:T(8,128)(2,1)} %param.8) | copy-start | bytes 786436
  117.9 7.6 %copy-start.5 = (bf16[128,1024]{1,0:T(8,128)(2,1)S(1)}, bf16[128,1024]{1,0:T(8,128)(2,1)}, u32[]{:S(2)}) copy-start(bf16[128,1024]{1,0:T(8,128)(2,1)} %param.7) | copy-start | bytes 786436
  119.0 8.5 %copy-start.6 = (bf16[128,1024]{1,0:T(8,128)(2,1)S(1)}, bf16[128,1024]{1,0:T(8,128)(2,1)}, u32[]{:S(2)}) copy-start(bf16[128,1024]{1,0:T(8,128)(2,1)} %param.6) | copy-start | bytes 786436
  122.7 5.1 %copy-start.7 = (bf16[128,1024]{1,0:T(8,128)(2,1)S(1)}, bf16[128,1024]{1,0:T(8,128)(2,1)}, u32[]{:S(2)}) copy-start(bf16[128,1024]{1,0:T(8,128)(2,1)} %param.9) | copy-start | bytes 786436
  122.7 7.0 %collective-permute-start.9 = (f32[]{:T(128)}, f32[]{:T(128)}, u32[]{:S(2)}, u32[]{:S(2)}) collective-permute-start(f32[]{:T(128)} %add.200), channel_id=1, source_target_pairs={{0,1},{1,0},{2,3},{3,2},{4,5},{5,4},{6,7},{7,6},{8,9},{9,8},{10,11... | collective-permute-start | bytes 20 | tf_op jit(solution)/shard_map/ppermute | solution.py:17
Sparse Core Ops, SparseCore 0:
  10.4 75.3 all-gather.2

commit v19 on v16

--- a/solution.py
+++ b/solution.py
@@ -128,7 +128,7 @@
     total_grad, gated_window = lax.optimization_barrier((total_grad, gated_window))
     adjoint = jnp.einsum("gau,sugc->sagc", bwd_band, gated_window, preferred_element_type=jnp.float32)
     dmixed = adjoint.reshape(rows, channels).astype(jnp.bfloat16)
-    squares = radix_round(jnp.sum(total_grad * total_grad), "chan", 1, 2)
+    squares = butterfly_sum(jnp.sum(total_grad * total_grad), "chan", ((1,), (2,)))
     squares, late_query, late_key, late_value, late_grad = lax.optimization_barrier(
         (squares, query_rows, key_rows, value_rows, grad_rows)
     )

time: 138 us -> 139 us (level)
  starting transfers between devices: 15.1 us -> 16.5 us
    ppermute x10 -> x9, starting transfers between devices: 15.1 us -> 16.4 us  [swap(): return lax.ppermute(value, axis, [(i, i ^ mask) for i in range(size)])]
  transfers between devices with their start and end apart: 11 -> 10, of which waited for: 2 -> 2; matrix products, arithmetic and copies ran while one was open for 17% -> 17% of each run, Pallas kernels for 2% -> 2%
where the time goes in v19:
time: 139 us; the launch traced here: 138 us
  waiting for transfers between devices  65.2 us (47%)
  between operations  16.9 us (12%)
  starting transfers between devices  16.5 us (12%)
  matrix products  14.3 us (10%)
  local copies, waits for them, and re-layouts  14 us (10%)
  other arithmetic  6.48 us (5%)
  Pallas kernels  5.21 us (4%)
    all_gather x1, waiting for transfers between devices, shards(): lax.all_gather(jnp.stack([mixed, gated]), 'seq', axis=0, tiled=False)  63.9 us
    ppermute x9, starting transfers between devices, swap(): return lax.ppermute(value, axis, [(i, i ^ mask) for i in range(size)])  16.4 us
    pallas_call x2, Pallas kernels, take_blocks(): pl.pallas_call(_take_kernel, out_shape=jax.ShapeDtypeStruct((count,) + bl...  5.21 us
    dot_general x1, matrix products, shards(): jnp.einsum('gaw,jaw->gj', corr, select_fwd.astype(jnp.float32), precision...  3.92 us
    dot_general x1, matrix products, shards(): jnp.einsum('gj,jaw->gaw', filters, select_fwd, preferred_element_type=jnp...  3.53 us
    unnamed x20, local copies, waits for them, and re-layouts  3.44 us
    dot_general x1, matrix products, shards(): jnp.einsum('gj,jau->gau', filters, _bwd_select(taps, span_rows, window),...  3.23 us
    pallas_call x2, local copies, waits for them, and re-layouts, take_blocks(): pl.pallas_call(_take_kernel, out_shape=jax.ShapeDtypeStruct((count,) + bl...  3.21 us
  transfers between devices with their start and end apart: 10, of which 2 were waited for; matrix products, arithmetic and copies ran while one was open for 17% of the time, Pallas kernels for 2%

profile of v19, /device:TPU:0, one launch (start us, length us, event | category | flops | bytes accessed | tf_op | source)
XLA Modules:
  0.0 138.4 jit_solution(13089627914388401119)
XLA Ops:
  7.2 1.1 multiply_convert_fusion.4
  8.3 1.1 multiply_convert_fusion.5
  9.4 0.9 pad_maximum_fusion.4
  10.4 0.2 copy.34
  10.5 0.2 copy.31
  11.2 0.2 concatenate.10
  11.5 0.2 reshape_reshape.3
  11.9 0.7 scatter_custom_fusion
  12.6 0.6 gather_fusion
  13.2 0.6 gather_fusion.1
  14.1 3.2 %convert_bitcast_fusion = bf16[64,64,192,1]{2,0,1,3:T(8,128)(2,1)} fusion(bf16[64,128]{1,0:T(8,128)(2,1)S(1)} %copy-done), kind=kOutput, calls=%fused_computation.16 | convolution fusion | flops 205258752 | bytes 1589248 | tf_op jit(solution)/shard_map/gj,jau->gau/dot_general | solution.py:107
  17.4 3.5 %convert_bitcast_fusion.1 = bf16[64,64,192,1]{2,0,1,3:T(8,128)(2,1)} fusion(s32[64]{0:T(128)S(1)} %iota_add_fusion, bf16[64,128]{1,0:T(8,128)(2,1)S(1)} %copy-done), kind=kOutput, calls=%fused_computation.17 | convolution fusion | flops 205258752 | bytes 1589504 | tf_op jit(solution)/shard_map/gj,jaw->gaw/dot_general | solution.py:104
  20.9 0.5 fusion.33.slots_ref
  21.4 0.5 fusion.34.slots_ref
  21.9 63.9 %all-gather.3.cloned.1.call-done = bf16[32,128,1024]{2,1,0:T(8,128)(2,1)} async-done(((bf16[2,128,1024]{2,1,0:T(8,128)(2,1)}), bf16[32,128,1024]{2,1,0:T(8,128)(2,1)}) %all-gather.3.cloned.1.call-update) | async-done | bytes 8388624 | tf_op jit(solution)/shard_map/all_gather | solution.py:80
  85.9 2.6 %shard_map.101 = bf16[4,64,1024]{2,1,0:T(8,128)(2,1)} custom-call(s32[4]{0:T(128)} %fusion.33.slots_ref, bf16[64,64,1024]{2,1,0:T(8,128)(2,1)} %bitcast.42), custom_call_target="tpu_custom_call" | custom-call | bytes 1048576 | tf_op jit(solution)/shard_map/pallas_call | solution.py:47
  88.5 1.6 %copy.32 = bf16[4,64,1024]{1,0,2:T(4,128)(2,1)S(1)} copy(bf16[4,64,1024]{2,1,0:T(8,128)(2,1)} %shard_map.101) | data formatting | bytes 1048576 | tf_op jit(solution)/shard_map/pallas_call | solution.py:47
  90.1 0.5 reshape.185
  90.7 0.8 convolution_bitcast_fusion
  91.5 3.9 %fusion.28 = f32[64,128]{1,0:T(8,128)S(1)} fusion(s32[64]{0:T(128)S(1)} %iota_add_fusion, f32[64,64,192]{2,1,0:T(8,128)S(1)} %convolution_bitcast_fusion), kind=kOutput, calls=%fused_computation.24 | convolution fusion | flops 607125504 | bytes 3178752 | tf_op jit(solution)/shard_map/gaw,jaw->gj/dot_general | solution.py:118
  95.4 0.3 collective-permute-start
  95.7 0.4 collective-permute-start.1
  96.1 2.7 %collective-permute-start.2 = (f32[64,128]{1,0:T(8,128)S(1)}, f32[64,128]{1,0:T(8,128)S(1)}, u32[]{:S(2)}, u32[]{:S(2)}) collective-permute-start(f32[64,128]{1,0:T(8,128)S(1)} %fusion.28), channel_id=1, source_target_pairs={{0,72},{8,64},{16,88},{24,80},{32,104},{40,96},{48,120},{56,112},{... | collective-permute-start | bytes 98312 | tf_op jit(solution)/shard_map/ppermute | solution.py:17
  98.8 1.3 fusion.16
  100.2 0.5 copy.43
  100.7 0.6 reshape.188
  101.4 0.3 collective-permute-start.3
  101.6 2.3 %collective-permute-start.4 = (f32[64,128]{1,0:T(8,128)S(1)}, f32[64,128]{1,0:T(8,128)S(1)}, u32[]{:S(2)}, u32[]{:S(2)}) collective-permute-start(f32[64,128]{1,0:T(8,128)S(1)} %add_add_fusion.1), channel_id=1, source_target_pairs={{0,32},{8,40},{16,48},{24,56},{32,0},{40,8},{48,16},{56,24},{64,96... | collective-permute-start | bytes 98312 | tf_op jit(solution)/shard_map/ppermute | solution.py:17
  103.9 2.2 %collective-permute-start.5 = (f32[64,128]{1,0:T(8,128)S(1)}, f32[64,128]{1,0:T(8,128)S(1)}, u32[]{:S(2)}, u32[]{:S(2)}) collective-permute-start(f32[64,128]{1,0:T(8,128)S(1)} %add_add_fusion.1), channel_id=1, source_target_pairs={{0,48},{8,56},{16,32},{24,40},{32,16},{40,24},{48,0},{56,8},{64,11... | collective-permute-start | bytes 98312 | tf_op jit(solution)/shard_map/ppermute | solution.py:17
  106.1 2.6 %shard_map.102 = bf16[4,64,1024]{2,1,0:T(8,128)(2,1)} custom-call(s32[4]{0:T(128)} %fusion.34.slots_ref, bf16[64,64,1024]{2,1,0:T(8,128)(2,1)} %bitcast.43), custom_call_target="tpu_custom_call" | custom-call | bytes 1048576 | tf_op jit(solution)/shard_map/pallas_call | solution.py:47
  108.7 1.6 %copy.38 = bf16[4,64,1024]{1,0,2:T(4,128)(2,1)S(1)} copy(bf16[4,64,1024]{2,1,0:T(8,128)(2,1)} %shard_map.102) | data formatting | bytes 1048576 | tf_op jit(solution)/shard_map/pallas_call | solution.py:47
  110.3 0.5 reshape.187
  110.9 0.5 pad_maximum_fusion.1
  111.5 0.6 multiply_reduce_fusion
  112.1 1.5 %collective-permute-start.6 = (f32[]{:T(128)}, f32[]{:T(128)}, u32[]{:S(2)}, u32[]{:S(2)}) collective-permute-start(f32[]{:T(128)} %multiply_reduce_fusion), channel_id=1, source_target_pairs={{0,2},{1,3},{2,0},{3,1},{4,6},{5,7},{6,4},{7,5},{8,10},{9,11},{10,... | collective-permute-start | bytes 20 | tf_op jit(solution)/shard_map/ppermute | solution.py:17
  113.6 1.5 %fusion.25 = f32[2,64,64,16]{1,3,0,2:T(8,128)S(1)} fusion(bf16[2,192,64,16]{1,3,0,2:T(8,128)(2,1)S(1)} %pad_maximum_fusion.1, bf16[64,64,192,1]{2,0,1,3:T(8,128)(2,1)S(1)} %copy-done.1), kind=kOutput, calls=%fused_computation.23 | convolution fusion | flops 50593792 | bytes 2883584 | tf_op jit(solution)/shard_map/gau,sugc->sagc/dot_general | solution.py:129
  115.1 0.5 copy.46
  115.6 0.6 reshape.189
  117.5 4.1 %collective-permute-start.7 = (f32[]{:T(128)}, f32[]{:T(128)}, u32[]{:S(2)}, u32[]{:S(2)}) collective-permute-start(f32[]{:T(128)} %add.189), channel_id=1, source_target_pairs={{0,4},{1,5},{2,6},{3,7},{4,0},{5,1},{6,2},{7,3},{8,12},{9,13},{10,... | collective-permute-start | bytes 20 | tf_op jit(solution)/shard_map/ppermute | solution.py:17
  121.5 1.2 collective-permute-done.7
  123.3 2.7 %collective-permute-start.8 = (f32[]{:T(128)}, f32[]{:T(128)}, u32[]{:S(2)}, u32[]{:S(2)}) collective-permute-start(f32[]{:T(128)} %add.190), channel_id=1, source_target_pairs={{0,1},{1,0},{2,3},{3,2},{4,5},{5,4},{6,7},{7,6},{8,9},{9,8},{10,11... | collective-permute-start | bytes 20 | tf_op jit(solution)/shard_map/ppermute | solution.py:17
  126.2 0.2 copy.48
  126.5 0.9 copy.51
  127.3 0.8 copy.52
  128.3 0.2 copy.44
  128.6 0.9 copy.49
  129.5 0.8 copy.50
  130.9 0.6 broadcast_multiply_fusion
  (50 shorter events, 1.7 us)
Async XLA Ops:
  7.2 7.0 %copy-start = (bf16[64,128]{1,0:T(8,128)(2,1)S(1)}, bf16[64,128]{1,0:T(8,128)(2,1)}, u32[]{:S(2)}) copy-start(bf16[64,128]{1,0:T(8,128)(2,1)} %param.10) | copy-start | bytes 49156
  7.2 3.5 %copy-start.6 = (s32[32]{0:T(128)S(1)}, s32[32]{0:T(128)}, u32[]{:S(2)}) copy-start(s32[32]{0:T(128)} %param.11) | copy-start | bytes 388
  7.2 78.7 %all-gather.3.cloned.1.call-start = ((), (), s32[]{:S(2)}) async-start(), calls=%async_computation | async-start | bytes 8912896 | tf_op jit(solution)/shard_map/all_gather | solution.py:80
  91.4 7.4 %copy-start.7 = (bf16[64,64,192,1]{2,0,1,3:T(8,128)(2,1)S(1)}, bf16[64,64,192,1]{2,0,1,3:T(8,128)(2,1)}, u32[]{:S(2)}) copy-start(bf16[64,64,192,1]{2,0,1,3:T(8,128)(2,1)} %convert_bitcast_fusion.1) | copy-start | bytes 4718596
  95.4 5.9 %collective-permute-start = (f32[64,128]{1,0:T(8,128)S(1)}, f32[64,128]{1,0:T(8,128)S(1)}, u32[]{:S(2)}, u32[]{:S(2)}) collective-permute-start(f32[64,128]{1,0:T(8,128)S(1)} %fusion.28), channel_id=1, source_target_pairs={{0,8},{8,0},{16,24},{24,16},{32,40},{40,32},{48,56},{56,48},{64,72... | collective-permute-start | bytes 98312 | tf_op jit(solution)/shard_map/ppermute | solution.py:17
  95.7 5.6 %collective-permute-start.1 = (f32[64,128]{1,0:T(8,128)S(1)}, f32[64,128]{1,0:T(8,128)S(1)}, u32[]{:S(2)}, u32[]{:S(2)}) collective-permute-start(f32[64,128]{1,0:T(8,128)S(1)} %fusion.28), channel_id=1, source_target_pairs={{0,64},{8,72},{16,80},{24,88},{32,96},{40,104},{48,112},{56,120},{... | collective-permute-start | bytes 98312 | tf_op jit(solution)/shard_map/ppermute | solution.py:17
  96.1 5.3 %collective-permute-start.2 = (f32[64,128]{1,0:T(8,128)S(1)}, f32[64,128]{1,0:T(8,128)S(1)}, u32[]{:S(2)}, u32[]{:S(2)}) collective-permute-start(f32[64,128]{1,0:T(8,128)S(1)} %fusion.28), channel_id=1, source_target_pairs={{0,72},{8,64},{16,88},{24,80},{32,104},{40,96},{48,120},{56,112},{... | collective-permute-start | bytes 98312 | tf_op jit(solution)/shard_map/ppermute | solution.py:17
  101.4 10.1 %collective-permute-start.3 = (f32[64,128]{1,0:T(8,128)S(1)}, f32[64,128]{1,0:T(8,128)S(1)}, u32[]{:S(2)}, u32[]{:S(2)}) collective-permute-start(f32[64,128]{1,0:T(8,128)S(1)} %add_add_fusion.1), channel_id=1, source_target_pairs={{0,16},{8,24},{16,0},{24,8},{32,48},{40,56},{48,32},{56,40},{64,80... | collective-permute-start | bytes 98312 | tf_op jit(solution)/shard_map/ppermute | solution.py:17
  101.6 9.8 %collective-permute-start.4 = (f32[64,128]{1,0:T(8,128)S(1)}, f32[64,128]{1,0:T(8,128)S(1)}, u32[]{:S(2)}, u32[]{:S(2)}) collective-permute-start(f32[64,128]{1,0:T(8,128)S(1)} %add_add_fusion.1), channel_id=1, source_target_pairs={{0,32},{8,40},{16,48},{24,56},{32,0},{40,8},{48,16},{56,24},{64,96... | collective-permute-start | bytes 98312 | tf_op jit(solution)/shard_map/ppermute | solution.py:17
  103.9 7.6 %collective-permute-start.5 = (f32[64,128]{1,0:T(8,128)S(1)}, f32[64,128]{1,0:T(8,128)S(1)}, u32[]{:S(2)}, u32[]{:S(2)}) collective-permute-start(f32[64,128]{1,0:T(8,128)S(1)} %add_add_fusion.1), channel_id=1, source_target_pairs={{0,48},{8,56},{16,32},{24,40},{32,16},{40,24},{48,0},{56,8},{64,11... | collective-permute-start | bytes 98312 | tf_op jit(solution)/shard_map/ppermute | solution.py:17
  110.8 2.7 %copy-start.1 = (bf16[64,64,192,1]{2,0,1,3:T(8,128)(2,1)S(1)}, bf16[64,64,192,1]{2,0,1,3:T(8,128)(2,1)}, u32[]{:S(2)}) copy-start(bf16[64,64,192,1]{2,0,1,3:T(8,128)(2,1)} %convert_bitcast_fusion) | copy-start | bytes 4718596
  112.1 4.1 %collective-permute-start.6 = (f32[]{:T(128)}, f32[]{:T(128)}, u32[]{:S(2)}, u32[]{:S(2)}) collective-permute-start(f32[]{:T(128)} %multiply_reduce_fusion), channel_id=1, source_target_pairs={{0,2},{1,3},{2,0},{3,1},{4,6},{5,7},{6,4},{7,5},{8,10},{9,11},{10,... | collective-permute-start | bytes 20 | tf_op jit(solution)/shard_map/ppermute | solution.py:17
  115.1 10.9 %copy-start.2 = (bf16[128,1024]{1,0:T(8,128)(2,1)S(1)}, bf16[128,1024]{1,0:T(8,128)(2,1)}, u32[]{:S(2)}) copy-start(bf16[128,1024]{1,0:T(8,128)(2,1)} %param.8) | copy-start | bytes 786436
  115.1 11.1 %copy-start.3 = (bf16[128,1024]{1,0:T(8,128)(2,1)S(1)}, bf16[128,1024]{1,0:T(8,128)(2,1)}, u32[]{:S(2)}) copy-start(bf16[128,1024]{1,0:T(8,128)(2,1)} %param.7) | copy-start | bytes 786436
  116.2 12.0 %copy-start.4 = (bf16[128,1024]{1,0:T(8,128)(2,1)S(1)}, bf16[128,1024]{1,0:T(8,128)(2,1)}, u32[]{:S(2)}) copy-start(bf16[128,1024]{1,0:T(8,128)(2,1)} %param.6) | copy-start | bytes 786436
  117.5 5.3 %collective-permute-start.7 = (f32[]{:T(128)}, f32[]{:T(128)}, u32[]{:S(2)}, u32[]{:S(2)}) collective-permute-start(f32[]{:T(128)} %add.189), channel_id=1, source_target_pairs={{0,4},{1,5},{2,6},{3,7},{4,0},{5,1},{6,2},{7,3},{8,12},{9,13},{10,... | collective-permute-start | bytes 20 | tf_op jit(solution)/shard_map/ppermute | solution.py:17
  123.3 5.0 %copy-start.5 = (bf16[128,1024]{1,0:T(8,128)(2,1)S(1)}, bf16[128,1024]{1,0:T(8,128)(2,1)}, u32[]{:S(2)}) copy-start(bf16[128,1024]{1,0:T(8,128)(2,1)} %param.9) | copy-start | bytes 786436
  123.3 7.0 %collective-permute-start.8 = (f32[]{:T(128)}, f32[]{:T(128)}, u32[]{:S(2)}, u32[]{:S(2)}) collective-permute-start(f32[]{:T(128)} %add.190), channel_id=1, source_target_pairs={{0,1},{1,0},{2,3},{3,2},{4,5},{5,4},{6,7},{7,6},{8,9},{9,8},{10,11... | collective-permute-start | bytes 20 | tf_op jit(solution)/shard_map/ppermute | solution.py:17
Sparse Core Ops, SparseCore 0:
  10.5 75.3 all-gather.2
